TPU v7x, 32 devices: a whole 2x2x4 slice. The times are simulated.
32 devices in a mesh: rows: 8 (over z, x), cols: 4 (over y, core).
Axes of the slice: x: 2, y: 2, z: 4, core: 2. Of those that a mesh axis runs over, the one named last changes fastest.
Arguments:
- matrix: float32 [1, 256, 6144], P(None, 'cols', 'rows'), may hold values from -110 to 110, as said below
Outputs:
- updated: float32 [1, 256, 6144], P(None, 'cols', 'rows')
Inputs may be any that keep to these rules, and one draw needn't show every extreme that they name: Every 64-column panel has full column rank, and for each panel k the matrix I - top_k has all singular values at least 0.5.
All inputs are finite; a program needn't handle non-finite values.
Results may differ from a plain program's by a relative error of at most 0.00019.
Values sent between devices are 32-bit elements; how exact they have to be, the bound alone decides.
No kernel may reach another device: no remote copies, remote signals or barrier semaphores. Data moves between devices by JAX's collectives and lax.ppermute only.
A program may use at most 64 MiB of HBM per device.

v0:
```python
import jax
import jax.numpy as jnp
from jax import lax
from jax.sharding import PartitionSpec as P

HIGHEST_PRECISION = lax.Precision.HIGHEST


def spread(x, axis, root):
    mine = lax.axis_index(axis) == root
    return lax.psum(jnp.where(mine, x, jnp.zeros_like(x)), axis)


def inner_rows(left, right):
    return lax.dot_general(left, right, (((1,), (1,)), ((), ())), precision=HIGHEST_PRECISION)


def apply_left(square, right_side):
    return jnp.dot(square, right_side, precision=HIGHEST_PRECISION)


def factor_inverse(square):
    factor = jnp.linalg.cholesky(square)
    identity = jnp.eye(square.shape[0], dtype=jnp.float32)
    return lax.linalg.triangular_solve(factor, identity, left_side=True, lower=True)


def invert(square):
    normal = jnp.dot(square.T, square, precision=HIGHEST_PRECISION)
    lower_inv = factor_inverse(normal)
    normal_inv = jnp.dot(lower_inv.T, lower_inv, precision=HIGHEST_PRECISION)
    return jnp.dot(normal_inv, square.T, precision=HIGHEST_PRECISION)


def local(matrix):
    block_count, width, local_rows = matrix.shape
    current = matrix.reshape(block_count * width, local_rows)
    global_rows = lax.axis_index("rows") * local_rows + jnp.arange(local_rows, dtype=jnp.int32)
    identity = jnp.eye(width, dtype=jnp.float32)
    for panel_index in range(2):
        offset = panel_index * width
        live_rows = global_rows >= offset
        relative = global_rows - offset
        unit_rows = (jnp.arange(width, dtype=jnp.int32)[:, None] == relative[None, :]).astype(
            jnp.float32
        )
        panel = jnp.where(live_rows[None, :], current, jnp.zeros_like(current))
        panel = spread(panel, "cols", panel_index)
        gram = inner_rows(panel, panel)
        top_rows = inner_rows(panel, unit_rows)
        gram = lax.psum(gram, "rows")
        lower_inv = factor_inverse(gram)
        basis = apply_left(lower_inv, panel)
        top_block = apply_left(lower_inv, top_rows)
        inverse = invert(identity - top_block.T)
        inverse = spread(inverse, "rows", 0)
        reflect = unit_rows - basis
        products = lax.psum(inner_rows(reflect, current), "rows")
        mixed = jnp.dot(inverse, products, precision=HIGHEST_PRECISION)
        current = current - jnp.dot(mixed.T, reflect, precision=HIGHEST_PRECISION)
    return current.reshape(matrix.shape)


def solution(mesh):
    return jax.shard_map(
        local,
        mesh=mesh,
        in_specs=(P(None, "cols", "rows"),),
        out_specs=P(None, "cols", "rows"),
        check_vma=False,
    )
```

profile of v0, /device:TPU:0, one launch (start us, length us, event | category | flops | bytes accessed | tf_op | source)
XLA Modules:
  0.0 281.0 jit_solution(3133846450142442208)
XLA Ops:
  6.5 1.6 fusion.3
  8.3 35.8 %all-reduce.5.cloned.1.call-done = f32[64,768]{1,0:T(8,128)} async-done(((f32[64,768]{1,0:T(8,128)}), f32[64,768]{1,0:T(8,128)}) %all-reduce.5.cloned.1.call-update) | async-done | bytes 196624 | tf_op jit(solution)/shard_map/psum | solution.py:11
  44.1 1.3 fusion.33
  45.4 37.2 %psum.57 = f32[64,64]{0,1:T(8,128)S(1)} all-reduce(f32[64,64]{0,1:T(8,128)S(1)} %fusion.33), channel_id=1, replica_groups=mesh['rows'=8,'cols'=4] {'rows'}, use_global_device_ids=true, to_apply=%region_1.2 | all-reduce | flops 4096 | bytes 32768 | tf_op jit(solution)/shard_map/psum | solution.py:51
  82.7 5.8 %cholesky.74 = f32[64,64]{1,0:T(8,128)S(1)} custom-call(f32[64,64]{1,0:T(8,128)S(1)} %fusion.27), custom_call_target="Cholesky" | custom-call | tf_op jit(solution)/shard_map/jit(cholesky)/cholesky | solution.py:23
  88.6 0.6 compare_reduce_fusion.3
  89.3 0.7 fusion.16
  89.9 4.9 %custom-call.8 = f32[1,64,64]{1,2,0:T(8,128)S(1)} custom-call(f32[1,64,64]{2,1,0:T(8,128)S(1)} %fusion.16), custom_call_target="InvertDiagBlocksLowerTriangular" | custom-call | tf_op jit(solution)/shard_map/triangular_solve/custom-call.0 | solution.py:25
  95.9 5.8 %cholesky.85 = f32[64,64]{1,0:T(8,128)S(1)} custom-call(f32[64,64]{1,0:T(8,128)S(1)} %fusion.25), custom_call_target="Cholesky" | custom-call | tf_op jit(solution)/shard_map/jit(cholesky)/cholesky | solution.py:23
  101.8 0.6 compare_reduce_fusion.2
  102.5 0.7 fusion.17
  103.1 4.9 %custom-call.9 = f32[1,64,64]{1,2,0:T(8,128)S(1)} custom-call(f32[1,64,64]{2,1,0:T(8,128)S(1)} %fusion.17), custom_call_target="InvertDiagBlocksLowerTriangular" | custom-call | tf_op jit(solution)/shard_map/triangular_solve/custom-call.0 | solution.py:25
  108.5 0.3 convolution_subtract_fusion.3
  108.8 0.6 copy-done.2
  109.5 0.3 fusion.1
  110.0 33.4 %all-reduce.1 = (f32[64,64]{1,0:T(8,128)S(1)}, f32[64,64]{1,0:T(8,128)S(1)}) all-reduce(f32[64,64]{1,0:T(8,128)S(1)} %convolution_select_fusion.1, f32[64,64]{1,0:T(8,128)S(1)} %fusion.1), channel_id=1, replica_groups=mesh['rows'=8,'cols'=4] {'rows'}, use_global_device_ids=true, to_apply=%region_4.7 | all-reduce | flops 8192 | bytes 65536 | tf_op jit(solution)/shard_map/psum | solution.py:11
  143.5 1.1 select_select_fusion
  144.6 29.6 %all-reduce.7.cloned.1.call-done = f32[64,768]{1,0:T(8,128)} async-done(((f32[64,768]{1,0:T(8,128)}), f32[64,768]{1,0:T(8,128)}) %all-reduce.7.cloned.1.call-update) | async-done | bytes 196624 | tf_op jit(solution)/shard_map/psum | solution.py:11
  174.2 1.3 fusion.37
  175.6 37.2 %psum.61 = f32[64,64]{0,1:T(8,128)S(1)} all-reduce(f32[64,64]{0,1:T(8,128)S(1)} %fusion.37), channel_id=1, replica_groups=mesh['rows'=8,'cols'=4] {'rows'}, use_global_device_ids=true, to_apply=%region_7.10 | all-reduce | flops 4096 | bytes 32768 | tf_op jit(solution)/shard_map/psum | solution.py:51
  212.9 5.8 %cholesky.96 = f32[64,64]{1,0:T(8,128)S(1)} custom-call(f32[64,64]{1,0:T(8,128)S(1)} %fusion.23), custom_call_target="Cholesky" | custom-call | tf_op jit(solution)/shard_map/jit(cholesky)/cholesky | solution.py:23
  218.8 0.6 compare_reduce_fusion.1
  219.4 0.7 fusion.18
  220.1 4.9 %custom-call.10 = f32[1,64,64]{1,2,0:T(8,128)S(1)} custom-call(f32[1,64,64]{2,1,0:T(8,128)S(1)} %fusion.18), custom_call_target="InvertDiagBlocksLowerTriangular" | custom-call | tf_op jit(solution)/shard_map/triangular_solve/custom-call.0 | solution.py:25
  226.1 5.8 %cholesky.107 = f32[64,64]{1,0:T(8,128)S(1)} custom-call(f32[64,64]{1,0:T(8,128)S(1)} %fusion.21), custom_call_target="Cholesky" | custom-call | tf_op jit(solution)/shard_map/jit(cholesky)/cholesky | solution.py:23
  232.0 0.6 compare_reduce_fusion
  232.6 0.7 fusion.19
  233.3 4.9 %custom-call.11 = f32[1,64,64]{1,2,0:T(8,128)S(1)} custom-call(f32[1,64,64]{2,1,0:T(8,128)S(1)} %fusion.19), custom_call_target="InvertDiagBlocksLowerTriangular" | custom-call | tf_op jit(solution)/shard_map/triangular_solve/custom-call.0 | solution.py:25
  238.9 0.3 convolution_subtract_fusion.1
  239.2 0.3 fusion.40
  239.5 33.4 %all-reduce = (f32[64,64]{1,0:T(8,128)S(1)}, f32[64,64]{1,0:T(8,128)S(1)}) all-reduce(f32[64,64]{1,0:T(8,128)S(1)} %convolution_select_fusion, f32[64,64]{1,0:T(8,128)S(1)} %fusion.40), channel_id=1, replica_groups=mesh['rows'=8,'cols'=4] {'rows'}, use_global_device_ids=true, to_apply=%region_8.11 | all-reduce | flops 8192 | bytes 65536 | tf_op jit(solution)/shard_map/psum | solution.py:11
  273.1 1.1 fusion
  (41 shorter events, 4.2 us)
Async XLA Ops:
  6.5 37.6 %all-reduce.5.cloned.1.call-start = ((), (), s32[]{:S(2)}) async-start(), calls=%async_computation | async-start | bytes 393216 | tf_op jit(solution)/shard_map/psum | solution.py:11
  8.2 166.1 %all-reduce.7.cloned.1.call-start = ((), (), s32[]{:S(2)}) async-start(), calls=%async_computation.1 | async-start | bytes 393216 | tf_op jit(solution)/shard_map/psum | solution.py:11
  45.4 49.7 %copy-start = (f32[64,768]{1,0:T(8,128)S(1)}, f32[64,768]{1,0:T(8,128)}, u32[]{:S(2)}) copy-start(f32[64,768]{1,0:T(8,128)} %all-reduce.5.cloned.1.call-done) | copy-start | bytes 589828
  108.5 0.9 copy-start.2
  175.6 49.7 %copy-start.1 = (f32[64,768]{1,0:T(8,128)S(1)}, f32[64,768]{1,0:T(8,128)}, u32[]{:S(2)}) copy-start(f32[64,768]{1,0:T(8,128)} %all-reduce.7.cloned.1.call-done) | copy-start | bytes 589828
Sparse Core Ops, SparseCore 0:
  9.7 34.3 all-reduce.4
  144.7 29.4 all-reduce.6
where the time goes:
time: 281 us
  blocking collectives  141 us (50%)
  waiting for transfers between devices  65.5 us (23%)
  other arithmetic  50 us (18%)
  between operations  13.8 us (5%)
  matrix products  9.61 us (3%)
    psum x2, blocking collectives, local(): gram = lax.psum(gram, 'rows')  74.4 us
    psum x2, blocking collectives, spread(): return lax.psum(jnp.where(mine, x, jnp.zeros_like(x)), axis)  66.8 us
    psum x2, waiting for transfers between devices, spread(): return lax.psum(jnp.where(mine, x, jnp.zeros_like(x)), axis)  65.4 us
    another operation x12, other arithmetic, factor_inverse(): factor = jnp.linalg.cholesky(square)  26.1 us
    another operation x8, other arithmetic, factor_inverse(): lax.linalg.triangular_solve(factor, identity, left_side=True, lower=True)  22.2 us
  transfers between devices with their start and end apart: 2, of which 2 were waited for; matrix products, arithmetic and copies ran while one was open for 0% of the time, Pallas kernels for 0%

commit v1 on v0

v1 whole, which is shorter than its diff:
```python
import jax
import jax.numpy as jnp
from jax import lax
from jax.sharding import PartitionSpec as P

HIGHEST_PRECISION = lax.Precision.HIGHEST


def inner_rows(left, right):
    return lax.dot_general(left, right, (((1,), (1,)), ((), ())), precision=HIGHEST_PRECISION)


def apply_left(square, right_side):
    return jnp.dot(square, right_side, precision=HIGHEST_PRECISION)


def butterfly_sum(x, axis, size):
    if size & (size - 1):
        return lax.psum(x, axis)
    step = 1
    while step < size:
        x = x + lax.ppermute(x, axis, [(i, i ^ step) for i in range(size)])
        step *= 2
    return x


def invert_near_identity(square):
    identity = jnp.eye(square.shape[0], dtype=jnp.float32)
    approx = square.T * (2.0 / 4.25)
    for _ in range(9):
        approx = apply_left(approx, 2.0 * identity - apply_left(square, approx))
    return approx


def lower_inverse(gram):
    factor = jnp.linalg.cholesky(gram)
    identity = jnp.eye(gram.shape[0], dtype=jnp.float32)
    return lax.linalg.triangular_solve(factor, identity, left_side=True, lower=True)


def make_local(rows_size):
    def local(matrix):
        block_count, width, local_rows = matrix.shape
        current = matrix.reshape(block_count * width, local_rows)
        global_rows = lax.axis_index("rows") * local_rows + jnp.arange(local_rows, dtype=jnp.int32)
        identity = jnp.eye(width, dtype=jnp.float32)
        lanes = jnp.arange(width, dtype=jnp.int32)[:, None]
        units = [
            (lanes == (global_rows - k * width)[None, :]).astype(jnp.float32) for k in range(2)
        ]

        gathered = lax.all_gather(current, "cols")
        panel_0 = gathered[0]
        second = gathered[1]

        sums = jnp.stack([
            inner_rows(panel_0, panel_0),
            inner_rows(panel_0, units[0]),
            inner_rows(panel_0, current),
            inner_rows(units[0], current),
            inner_rows(panel_0, second),
            inner_rows(units[0], second),
        ])
        sums = butterfly_sum(sums, "rows", rows_size)
        gram, top_rows, basis_cur, unit_cur, basis_sec, unit_sec = (sums[i] for i in range(6))
        lower_inv = lower_inverse(gram)
        top_block = apply_left(lower_inv, top_rows)
        inverse = invert_near_identity(identity - top_block.T)
        reflect = units[0] - apply_left(lower_inv, panel_0)
        mixed = apply_left(inverse, unit_cur - apply_left(lower_inv, basis_cur))
        mixed_sec = apply_left(inverse, unit_sec - apply_left(lower_inv, basis_sec))
        current = current - jnp.dot(mixed.T, reflect, precision=HIGHEST_PRECISION)
        second = second - jnp.dot(mixed_sec.T, reflect, precision=HIGHEST_PRECISION)

        panel_1 = jnp.where((global_rows >= width)[None, :], second, jnp.zeros_like(second))
        sums = jnp.stack([
            inner_rows(panel_1, panel_1),
            inner_rows(panel_1, units[1]),
            inner_rows(panel_1, current),
            inner_rows(units[1], current),
        ])
        sums = butterfly_sum(sums, "rows", rows_size)
        gram, top_rows, basis_cur, unit_cur = (sums[i] for i in range(4))
        lower_inv = lower_inverse(gram)
        top_block = apply_left(lower_inv, top_rows)
        inverse = invert_near_identity(identity - top_block.T)
        reflect = units[1] - apply_left(lower_inv, panel_1)
        mixed = apply_left(inverse, unit_cur - apply_left(lower_inv, basis_cur))
        current = current - jnp.dot(mixed.T, reflect, precision=HIGHEST_PRECISION)
        return current.reshape(matrix.shape)

    return local


def solution(mesh):
    return jax.shard_map(
        make_local(mesh.shape["rows"]),
        mesh=mesh,
        in_specs=(P(None, "cols", "rows"),),
        out_specs=P(None, "cols", "rows"),
        check_vma=False,
    )
```

time: 281 us -> 90.7 us (0.32)
  blocking collectives: 141 us -> 10.3 us
  waiting for transfers between devices: 65.5 us -> 30.8 us
  other arithmetic: 50 us -> 24.3 us
  between operations: 13.8 us -> 0.57 us
  starting transfers between devices: 0.04 us -> 10.9 us
  matrix products: 9.61 us -> 13.2 us
    psum x4 -> x0, blocking collectives: 141 us -> none  [the longest x2 74.4 us: local(): gram = lax.psum(gram, 'rows')]
    psum x2 -> x0, waiting for transfers between devices: 65.4 us -> none  [spread(): return lax.psum(jnp.where(mine, x, jnp.zeros_like(x)), axis)]
    ppermute x0 -> x6, waiting for transfers between devices: none -> 30.8 us  [butterfly_sum(): x = x + lax.ppermute(x, axis, [(i, i ^ step) for i in range(size)])]
    another operation x20 -> x11, other arithmetic: 48.3 us -> 24.2 us  [the longest x6 13 us: lower_inverse(): factor = jnp.linalg.cholesky(gram)]
    ppermute x0 -> x6, starting transfers between devices: none -> 10.9 us  [butterfly_sum(): x = x + lax.ppermute(x, axis, [(i, i ^ step) for i in range(size)])]
    all_gather x0 -> x1, blocking collectives: none -> 10.3 us  [local(): gathered = lax.all_gather(current, 'cols')]
    dot_general x4 -> x46, matrix products: 1.08 us -> 8.12 us  [apply_left(): return jnp.dot(square, right_side, precision=HIGHEST_PRECISION)]
  transfers between devices with their start and end apart: 2 -> 6, of which waited for: 2 -> 6; matrix products, arithmetic and copies ran while one was open for 0% -> 0% of each run, Pallas kernels for 0% -> 0%
where the time goes in v1:
time: 90.7 us; the launch traced here: 90.5 us
  waiting for transfers between devices  30.8 us (34%)
  other arithmetic  24.3 us (27%)
  matrix products  13.2 us (15%)
  starting transfers between devices  10.9 us (12%)
  blocking collectives  10.3 us (11%)
    ppermute x6, waiting for transfers between devices, butterfly_sum(): x = x + lax.ppermute(x, axis, [(i, i ^ step) for i in range(size)])  30.8 us
    another operation x6, other arithmetic, lower_inverse(): factor = jnp.linalg.cholesky(gram)  13 us
    another operation x4, other arithmetic, lower_inverse(): lax.linalg.triangular_solve(factor, identity, left_side=True, lower=True)  11.1 us
    ppermute x6, starting transfers between devices, butterfly_sum(): x = x + lax.ppermute(x, axis, [(i, i ^ step) for i in range(size)])  10.9 us
    all_gather x1, blocking collectives, local(): gathered = lax.all_gather(current, 'cols')  10.3 us
    dot_general x46, matrix products, apply_left(): return jnp.dot(square, right_side, precision=HIGHEST_PRECISION)  8.12 us
    dot_general x10, matrix products, inner_rows(): lax.dot_general(left, right, (((1,), (1,)), ((), ())), precision=HIGHEST_...  2.79 us
  transfers between devices with their start and end apart: 6, of which 6 were waited for; matrix products, arithmetic and copies ran while one was open for 0% of the time, Pallas kernels for 0%

profile of v1, /device:TPU:0, one launch (start us, length us, event | category | flops | bytes accessed | tf_op | source)
XLA Modules:
  0.0 90.5 jit_solution(12831783000609917317)
XLA Ops:
  0.0 10.3 %all_gather.3 = f32[4,64,768]{2,1,0:T(8,128)S(1)} all-gather(f32[1,64,768]{2,1,0:T(8,128)} %param.4), channel_id=1, replica_groups=mesh['rows'=8,'cols'=4] {'cols'}, dimensions={0}, use_global_device_ids=true | all-gather | bytes 983040 | tf_op jit(solution)/shard_map/all_gather | solution.py:52
  10.3 0.3 fusion.7
  10.9 0.3 copy-done
  11.2 0.3 fusion.6
  11.8 0.3 fusion.5
  12.3 1.6 %collective-permute-start = (f32[6,64,64]{1,2,0:T(8,128)S(1)}, f32[6,64,64]{1,2,0:T(8,128)S(1)}, u32[]{:S(2)}, u32[]{:S(2)}) collective-permute-start(f32[6,64,64]{1,2,0:T(8,128)S(1)} %fusion.2), channel_id=1, source_target_pairs={{0,4},{4,0},{8,12},{12,8},{16,20},{20,16},{24,28},{28,24},{1,5},{5... | collective-permute-start | bytes 294920 | tf_op jit(solution)/shard_map/ppermute | solution.py:22
  13.9 5.7 %collective-permute-done = f32[6,64,64]{1,2,0:T(8,128)S(1)} collective-permute-done((f32[6,64,64]{1,2,0:T(8,128)S(1)}, f32[6,64,64]{1,2,0:T(8,128)S(1)}, u32[]{:S(2)}, u32[]{:S(2)}) %collective-permute-start) | collective-permute-done | bytes 98336 | tf_op jit(solution)/shard_map/ppermute | solution.py:22
  19.6 1.6 %collective-permute-start.1 = (f32[6,64,64]{1,2,0:T(8,128)S(1)}, f32[6,64,64]{1,2,0:T(8,128)S(1)}, u32[]{:S(2)}, u32[]{:S(2)}) collective-permute-start(f32[6,64,64]{1,2,0:T(8,128)S(1)} %add.49), channel_id=1, source_target_pairs={{0,8},{4,12},{8,0},{12,4},{16,24},{20,28},{24,16},{28,20},{1,9},{5... | collective-permute-start | bytes 294920 | tf_op jit(solution)/shard_map/ppermute | solution.py:22
  21.2 4.8 %collective-permute-done.1 = f32[6,64,64]{1,2,0:T(8,128)S(1)} collective-permute-done((f32[6,64,64]{1,2,0:T(8,128)S(1)}, f32[6,64,64]{1,2,0:T(8,128)S(1)}, u32[]{:S(2)}, u32[]{:S(2)}) %collective-permute-start.1) | collective-permute-done | bytes 98336 | tf_op jit(solution)/shard_map/ppermute | solution.py:22
  26.0 2.7 %collective-permute-start.2 = (f32[6,64,64]{1,2,0:T(8,128)S(1)}, f32[6,64,64]{1,2,0:T(8,128)S(1)}, u32[]{:S(2)}, u32[]{:S(2)}) collective-permute-start(f32[6,64,64]{1,2,0:T(8,128)S(1)} %add.50), channel_id=1, source_target_pairs={{0,16},{4,20},{8,24},{12,28},{16,0},{20,4},{24,8},{28,12},{1,17},{... | collective-permute-start | bytes 294920 | tf_op jit(solution)/shard_map/ppermute | solution.py:22
  28.7 8.0 %collective-permute-done.2 = f32[6,64,64]{1,2,0:T(8,128)S(1)} collective-permute-done((f32[6,64,64]{1,2,0:T(8,128)S(1)}, f32[6,64,64]{1,2,0:T(8,128)S(1)}, u32[]{:S(2)}, u32[]{:S(2)}) %collective-permute-start.2) | collective-permute-done | bytes 98336 | tf_op jit(solution)/shard_map/ppermute | solution.py:22
  36.8 5.8 %cholesky.44 = f32[64,64]{1,0:T(8,128)S(1)} custom-call(f32[64,64]{1,0:T(8,128)S(1)} %fusion.38), custom_call_target="Cholesky" | custom-call | tf_op jit(solution)/shard_map/jit(cholesky)/cholesky | solution.py:36
  42.7 0.6 compare_reduce_fusion.1
  43.3 0.7 fusion.19
  44.0 4.9 %custom-call.6 = f32[1,64,64]{1,2,0:T(8,128)S(1)} custom-call(f32[1,64,64]{2,1,0:T(8,128)S(1)} %fusion.19), custom_call_target="InvertDiagBlocksLowerTriangular" | custom-call | tf_op jit(solution)/shard_map/triangular_solve/custom-call.0 | solution.py:38
  49.7 0.3 convolution_subtract_fusion.4
  53.6 0.4 convolution_subtract_fusion.3
  53.9 0.4 fusion.1
  54.6 0.3 convolution_bitcast_fusion.5
  55.2 0.3 convolution_bitcast_fusion.6
  55.5 1.6 %collective-permute-start.3 = (f32[4,64,64]{1,2,0:T(8,128)S(1)}, f32[4,64,64]{1,2,0:T(8,128)S(1)}, u32[]{:S(2)}, u32[]{:S(2)}) collective-permute-start(f32[4,64,64]{1,2,0:T(8,128)S(1)} %pad_maximum_fusion), channel_id=1, source_target_pairs={{0,4},{4,0},{8,12},{12,8},{16,20},{20,16},{24,28},{28,24},{1,5},{5... | collective-permute-start | bytes 196616 | tf_op jit(solution)/shard_map/ppermute | solution.py:22
  57.1 3.5 %collective-permute-done.3 = f32[4,64,64]{1,2,0:T(8,128)S(1)} collective-permute-done((f32[4,64,64]{1,2,0:T(8,128)S(1)}, f32[4,64,64]{1,2,0:T(8,128)S(1)}, u32[]{:S(2)}, u32[]{:S(2)}) %collective-permute-start.3) | collective-permute-done | bytes 65568 | tf_op jit(solution)/shard_map/ppermute | solution.py:22
  60.6 1.0 %collective-permute-start.4 = (f32[4,64,64]{1,2,0:T(8,128)S(1)}, f32[4,64,64]{1,2,0:T(8,128)S(1)}, u32[]{:S(2)}, u32[]{:S(2)}) collective-permute-start(f32[4,64,64]{1,2,0:T(8,128)S(1)} %fusion.57), channel_id=1, source_target_pairs={{0,8},{4,12},{8,0},{12,4},{16,24},{20,28},{24,16},{28,20},{1,9},{5... | collective-permute-start | bytes 196616 | tf_op jit(solution)/shard_map/ppermute | solution.py:22
  61.6 4.0 %collective-permute-done.4 = f32[4,64,64]{1,2,0:T(8,128)S(1)} collective-permute-done((f32[4,64,64]{1,2,0:T(8,128)S(1)}, f32[4,64,64]{1,2,0:T(8,128)S(1)}, u32[]{:S(2)}, u32[]{:S(2)}) %collective-permute-start.4) | collective-permute-done | bytes 65568 | tf_op jit(solution)/shard_map/ppermute | solution.py:22
  65.6 2.4 %collective-permute-start.5 = (f32[4,64,64]{1,2,0:T(8,128)S(1)}, f32[4,64,64]{1,2,0:T(8,128)S(1)}, u32[]{:S(2)}, u32[]{:S(2)}) collective-permute-start(f32[4,64,64]{1,2,0:T(8,128)S(1)} %fusion.147), channel_id=1, source_target_pairs={{0,16},{4,20},{8,24},{12,28},{16,0},{20,4},{24,8},{28,12},{1,17},{... | collective-permute-start | bytes 196616 | tf_op jit(solution)/shard_map/ppermute | solution.py:22
  68.0 4.9 %collective-permute-done.5 = f32[4,64,64]{1,2,0:T(8,128)S(1)} collective-permute-done((f32[4,64,64]{1,2,0:T(8,128)S(1)}, f32[4,64,64]{1,2,0:T(8,128)S(1)}, u32[]{:S(2)}, u32[]{:S(2)}) %collective-permute-start.5) | collective-permute-done | bytes 65568 | tf_op jit(solution)/shard_map/ppermute | solution.py:22
  73.1 5.8 %cholesky.55 = f32[64,64]{1,0:T(8,128)S(1)} custom-call(f32[64,64]{1,0:T(8,128)S(1)} %fusion.37), custom_call_target="Cholesky" | custom-call | tf_op jit(solution)/shard_map/jit(cholesky)/cholesky | solution.py:36
  79.0 0.6 compare_reduce_fusion
  79.6 0.7 fusion.20
  80.3 4.9 %custom-call.7 = f32[1,64,64]{1,2,0:T(8,128)S(1)} custom-call(f32[1,64,64]{2,1,0:T(8,128)S(1)} %fusion.20), custom_call_target="InvertDiagBlocksLowerTriangular" | custom-call | tf_op jit(solution)/shard_map/triangular_solve/custom-call.0 | solution.py:38
  85.4 0.3 convolution_subtract_fusion.1
  89.5 1.1 %fusion = f32[1,64,768]{2,1,0:T(8,128)} fusion(f32[64,768]{1,0:T(8,128)S(1)} %convolution_subtract_fusion.3, f32[64,64]{1,0:T(8,128)S(1)} %fusion.25, f32[64,768]{1,0:T(8,128)S(1)} %convolution_subtract_fusion.1), kind=kOutput, calls=%fused_computation.1 | convolution fusion | flops 37797888 | bytes 606208 | tf_op jit(solution)/shard_map/dot_general | solution.py:89
  (70 shorter events, 9.7 us)
Async XLA Ops:
  10.3 0.9 %copy-start = (f32[1,64,768]{2,1,0:T(8,128)S(1)}, f32[1,64,768]{2,1,0:T(8,128)}, u32[]{:S(2)}) copy-start(f32[1,64,768]{2,1,0:T(8,128)} %param.4) | copy-start | bytes 589828
  12.3 7.2 %collective-permute-start = (f32[6,64,64]{1,2,0:T(8,128)S(1)}, f32[6,64,64]{1,2,0:T(8,128)S(1)}, u32[]{:S(2)}, u32[]{:S(2)}) collective-permute-start(f32[6,64,64]{1,2,0:T(8,128)S(1)} %fusion.2), channel_id=1, source_target_pairs={{0,4},{4,0},{8,12},{12,8},{16,20},{20,16},{24,28},{28,24},{1,5},{5... | collective-permute-start | bytes 294920 | tf_op jit(solution)/shard_map/ppermute | solution.py:22
  19.6 6.4 %collective-permute-start.1 = (f32[6,64,64]{1,2,0:T(8,128)S(1)}, f32[6,64,64]{1,2,0:T(8,128)S(1)}, u32[]{:S(2)}, u32[]{:S(2)}) collective-permute-start(f32[6,64,64]{1,2,0:T(8,128)S(1)} %add.49), channel_id=1, source_target_pairs={{0,8},{4,12},{8,0},{12,4},{16,24},{20,28},{24,16},{28,20},{1,9},{5... | collective-permute-start | bytes 294920 | tf_op jit(solution)/shard_map/ppermute | solution.py:22
  26.0 10.6 %collective-permute-start.2 = (f32[6,64,64]{1,2,0:T(8,128)S(1)}, f32[6,64,64]{1,2,0:T(8,128)S(1)}, u32[]{:S(2)}, u32[]{:S(2)}) collective-permute-start(f32[6,64,64]{1,2,0:T(8,128)S(1)} %add.50), channel_id=1, source_target_pairs={{0,16},{4,20},{8,24},{12,28},{16,0},{20,4},{24,8},{28,12},{1,17},{... | collective-permute-start | bytes 294920 | tf_op jit(solution)/shard_map/ppermute | solution.py:22
  55.5 5.0 %collective-permute-start.3 = (f32[4,64,64]{1,2,0:T(8,128)S(1)}, f32[4,64,64]{1,2,0:T(8,128)S(1)}, u32[]{:S(2)}, u32[]{:S(2)}) collective-permute-start(f32[4,64,64]{1,2,0:T(8,128)S(1)} %pad_maximum_fusion), channel_id=1, source_target_pairs={{0,4},{4,0},{8,12},{12,8},{16,20},{20,16},{24,28},{28,24},{1,5},{5... | collective-permute-start | bytes 196616 | tf_op jit(solution)/shard_map/ppermute | solution.py:22
  60.6 5.0 %collective-permute-start.4 = (f32[4,64,64]{1,2,0:T(8,128)S(1)}, f32[4,64,64]{1,2,0:T(8,128)S(1)}, u32[]{:S(2)}, u32[]{:S(2)}) collective-permute-start(f32[4,64,64]{1,2,0:T(8,128)S(1)} %fusion.57), channel_id=1, source_target_pairs={{0,8},{4,12},{8,0},{12,4},{16,24},{20,28},{24,16},{28,20},{1,9},{5... | collective-permute-start | bytes 196616 | tf_op jit(solution)/shard_map/ppermute | solution.py:22
  65.6 7.3 %collective-permute-start.5 = (f32[4,64,64]{1,2,0:T(8,128)S(1)}, f32[4,64,64]{1,2,0:T(8,128)S(1)}, u32[]{:S(2)}, u32[]{:S(2)}) collective-permute-start(f32[4,64,64]{1,2,0:T(8,128)S(1)} %fusion.147), channel_id=1, source_target_pairs={{0,16},{4,20},{8,24},{12,28},{16,0},{20,4},{24,8},{28,12},{1,17},{... | collective-permute-start | bytes 196616 | tf_op jit(solution)/shard_map/ppermute | solution.py:22

commit v2 on v1

--- a/solution.py
+++ b/solution.py
@@ -1,6 +1,7 @@
 import jax
 import jax.numpy as jnp
 from jax import lax
+from jax.experimental import pallas as pl
 from jax.sharding import PartitionSpec as P
 
 HIGHEST_PRECISION = lax.Precision.HIGHEST
@@ -32,10 +33,32 @@
     return approx
 
 
+def _eliminate_kernel(aug_ref, out_ref):
+    size, wide = aug_ref.shape
+    rows = lax.broadcasted_iota(jnp.int32, (size, wide), 0)
+    lanes = lax.broadcasted_iota(jnp.int32, (size, wide), 1)
+    row_ids = lax.broadcasted_iota(jnp.int32, (size, 1), 0)
+
+    def step(j, work):
+        column = jnp.sum(jnp.where(lanes == j, work, 0.0), axis=1, keepdims=True)
+        row = jnp.sum(jnp.where(rows == j, work, 0.0), axis=0, keepdims=True)
+        pivot = jnp.sum(jnp.where(row_ids == j, column, 0.0), axis=0, keepdims=True)
+        scale = 1.0 / jnp.sqrt(pivot)
+        scaled = row * scale
+        weight = jnp.where(row_ids > j, column * scale, 0.0)
+        work = work - weight * scaled
+        return jnp.where(rows == j, scaled, work)
+
+    out_ref[...] = lax.fori_loop(0, size, step, aug_ref[...], unroll=4)
+
+
 def lower_inverse(gram):
-    factor = jnp.linalg.cholesky(gram)
-    identity = jnp.eye(gram.shape[0], dtype=jnp.float32)
-    return lax.linalg.triangular_solve(factor, identity, left_side=True, lower=True)
+    size = gram.shape[0]
+    aug = jnp.concatenate([gram, jnp.eye(size, dtype=jnp.float32)], axis=1)
+    out = pl.pallas_call(
+        _eliminate_kernel, out_shape=jax.ShapeDtypeStruct(aug.shape, jnp.float32)
+    )(aug)
+    return out[:, size:]
 
 
 def make_local(rows_size):

time: 90.7 us -> 86.3 us (0.951)
  other arithmetic: 24.3 us -> 1.57 us
  Pallas kernels: 0 us -> 16.8 us
  matrix products: 13.2 us -> 14.7 us
    another operation x10 -> x0, other arithmetic: 24.1 us -> none  [the longest x6 13 us: lower_inverse(): factor = jnp.linalg.cholesky(gram)]
    pallas_call x0 -> x2, Pallas kernels: none -> 16.8 us  [lower_inverse(): pl.pallas_call(_eliminate_kernel, out_shape=jax.ShapeDtypeStruct(aug.shap...]
    dot_general x46, matrix products: 8.12 us -> 10.1 us  [apply_left(): return jnp.dot(square, right_side, precision=HIGHEST_PRECISION)]
    concatenate x0 -> x2, other arithmetic: none -> 1.39 us  [lower_inverse(): aug = jnp.concatenate([gram, jnp.eye(size, dtype=jnp.float32)], axis=1)]
where the time goes in v2:
time: 86.3 us; the launch traced here: 85.8 us
  waiting for transfers between devices  30.8 us (36%)
  Pallas kernels  16.8 us (19%)
  matrix products  14.7 us (17%)
  starting transfers between devices  10.9 us (13%)
  blocking collectives  10.3 us (12%)
  other arithmetic  1.57 us (2%)
    ppermute x6, waiting for transfers between devices, butterfly_sum(): x = x + lax.ppermute(x, axis, [(i, i ^ step) for i in range(size)])  30.8 us
    pallas_call x2, Pallas kernels, lower_inverse(): pl.pallas_call(_eliminate_kernel, out_shape=jax.ShapeDtypeStruct(aug.shap...  16.8 us
    ppermute x6, starting transfers between devices, butterfly_sum(): x = x + lax.ppermute(x, axis, [(i, i ^ step) for i in range(size)])  10.9 us
    all_gather x1, blocking collectives, local(): gathered = lax.all_gather(current, 'cols')  10.3 us
    dot_general x46, matrix products, apply_left(): return jnp.dot(square, right_side, precision=HIGHEST_PRECISION)  10.1 us
    dot_general x10, matrix products, inner_rows(): lax.dot_general(left, right, (((1,), (1,)), ((), ())), precision=HIGHEST_...  2.8 us
  transfers between devices with their start and end apart: 6, of which 6 were waited for; matrix products, arithmetic and copies ran while one was open for 0% of the time, Pallas kernels for 0%

profile of v2, /device:TPU:0, one launch (start us, length us, event | category | flops | bytes accessed | tf_op | source)
XLA Modules:
  0.0 85.8 jit_solution(9909205370666295153)
XLA Ops:
  0.0 10.3 %all_gather.3 = f32[4,64,768]{2,1,0:T(8,128)S(1)} all-gather(f32[1,64,768]{2,1,0:T(8,128)} %param.1), channel_id=1, replica_groups=mesh['rows'=8,'cols'=4] {'cols'}, dimensions={0}, use_global_device_ids=true | all-gather | bytes 983040 | tf_op jit(solution)/shard_map/all_gather | solution.py:75
  10.3 0.3 fusion.7
  10.8 0.4 copy-done
  11.2 0.3 fusion.6
  11.8 0.3 fusion.5
  12.1 0.2 fusion.2
  12.4 1.6 %collective-permute-start = (f32[6,64,64]{2,1,0:T(8,128)S(1)}, f32[6,64,64]{2,1,0:T(8,128)S(1)}, u32[]{:S(2)}, u32[]{:S(2)}) collective-permute-start(f32[6,64,64]{2,1,0:T(8,128)S(1)} %fusion.2), channel_id=1, source_target_pairs={{0,4},{4,0},{8,12},{12,8},{16,20},{20,16},{24,28},{28,24},{1,5},{5... | collective-permute-start | bytes 294920 | tf_op jit(solution)/shard_map/ppermute | solution.py:23
  13.9 5.7 %collective-permute-done = f32[6,64,64]{2,1,0:T(8,128)S(1)} collective-permute-done((f32[6,64,64]{2,1,0:T(8,128)S(1)}, f32[6,64,64]{2,1,0:T(8,128)S(1)}, u32[]{:S(2)}, u32[]{:S(2)}) %collective-permute-start) | collective-permute-done | bytes 98336 | tf_op jit(solution)/shard_map/ppermute | solution.py:23
  19.6 1.6 %collective-permute-start.1 = (f32[6,64,64]{2,1,0:T(8,128)S(1)}, f32[6,64,64]{2,1,0:T(8,128)S(1)}, u32[]{:S(2)}, u32[]{:S(2)}) collective-permute-start(f32[6,64,64]{2,1,0:T(8,128)S(1)} %add.41), channel_id=1, source_target_pairs={{0,8},{4,12},{8,0},{12,4},{16,24},{20,28},{24,16},{28,20},{1,9},{5... | collective-permute-start | bytes 294920 | tf_op jit(solution)/shard_map/ppermute | solution.py:23
  21.3 4.8 %collective-permute-done.1 = f32[6,64,64]{2,1,0:T(8,128)S(1)} collective-permute-done((f32[6,64,64]{2,1,0:T(8,128)S(1)}, f32[6,64,64]{2,1,0:T(8,128)S(1)}, u32[]{:S(2)}, u32[]{:S(2)}) %collective-permute-start.1) | collective-permute-done | bytes 98336 | tf_op jit(solution)/shard_map/ppermute | solution.py:23
  26.0 2.7 %collective-permute-start.2 = (f32[6,64,64]{2,1,0:T(8,128)S(1)}, f32[6,64,64]{2,1,0:T(8,128)S(1)}, u32[]{:S(2)}, u32[]{:S(2)}) collective-permute-start(f32[6,64,64]{2,1,0:T(8,128)S(1)} %add.42), channel_id=1, source_target_pairs={{0,16},{4,20},{8,24},{12,28},{16,0},{20,4},{24,8},{28,12},{1,17},{... | collective-permute-start | bytes 294920 | tf_op jit(solution)/shard_map/ppermute | solution.py:23
  28.7 8.0 %collective-permute-done.2 = f32[6,64,64]{2,1,0:T(8,128)S(1)} collective-permute-done((f32[6,64,64]{2,1,0:T(8,128)S(1)}, f32[6,64,64]{2,1,0:T(8,128)S(1)}, u32[]{:S(2)}, u32[]{:S(2)}) %collective-permute-start.2) | collective-permute-done | bytes 98336 | tf_op jit(solution)/shard_map/ppermute | solution.py:23
  36.7 0.7 pad_maximum_fusion.1.aug_ref
  37.4 8.4 %shard_map.17 = f32[64,128]{1,0:T(8,128)} custom-call(f32[64,128]{1,0:T(8,128)} %pad_maximum_fusion.1.aug_ref), custom_call_target="tpu_custom_call" | custom-call | tf_op jit(solution)/shard_map/pallas_call | solution.py:58
  45.8 1.1 %fusion.30 = f32[64,64]{1,0:T(8,128)S(1)} fusion(f32[6,64,64]{2,1,0:T(8,128)S(1)} %add.43, f32[64,128]{1,0:T(8,128)} %shard_map.17), kind=kOutput, calls=%fused_computation.77 | convolution fusion | flops 3145728 | bytes 81920 | tf_op jit(solution)/shard_map/dot_general | solution.py:15
  47.4 0.4 convolution_subtract_fusion.4
  51.2 0.4 convolution_subtract_fusion.3
  51.6 0.4 fusion.1
  52.0 0.3 convolution_bitcast_fusion
  52.3 0.3 convolution_bitcast_fusion.5
  52.8 0.3 convolution_bitcast_fusion.6
  53.2 1.6 %collective-permute-start.3 = (f32[4,64,64]{2,1,0:T(8,128)S(1)}, f32[4,64,64]{2,1,0:T(8,128)S(1)}, u32[]{:S(2)}, u32[]{:S(2)}) collective-permute-start(f32[4,64,64]{2,1,0:T(8,128)S(1)} %pad_maximum_fusion), channel_id=1, source_target_pairs={{0,4},{4,0},{8,12},{12,8},{16,20},{20,16},{24,28},{28,24},{1,5},{5... | collective-permute-start | bytes 196616 | tf_op jit(solution)/shard_map/ppermute | solution.py:23
  54.7 3.5 %collective-permute-done.3 = f32[4,64,64]{2,1,0:T(8,128)S(1)} collective-permute-done((f32[4,64,64]{2,1,0:T(8,128)S(1)}, f32[4,64,64]{2,1,0:T(8,128)S(1)}, u32[]{:S(2)}, u32[]{:S(2)}) %collective-permute-start.3) | collective-permute-done | bytes 65568 | tf_op jit(solution)/shard_map/ppermute | solution.py:23
  58.2 1.1 %collective-permute-start.4 = (f32[4,64,64]{2,1,0:T(8,128)S(1)}, f32[4,64,64]{2,1,0:T(8,128)S(1)}, u32[]{:S(2)}, u32[]{:S(2)}) collective-permute-start(f32[4,64,64]{2,1,0:T(8,128)S(1)} %fusion.75), channel_id=1, source_target_pairs={{0,8},{4,12},{8,0},{12,4},{16,24},{20,28},{24,16},{28,20},{1,9},{5... | collective-permute-start | bytes 196616 | tf_op jit(solution)/shard_map/ppermute | solution.py:23
  59.3 4.0 %collective-permute-done.4 = f32[4,64,64]{2,1,0:T(8,128)S(1)} collective-permute-done((f32[4,64,64]{2,1,0:T(8,128)S(1)}, f32[4,64,64]{2,1,0:T(8,128)S(1)}, u32[]{:S(2)}, u32[]{:S(2)}) %collective-permute-start.4) | collective-permute-done | bytes 65568 | tf_op jit(solution)/shard_map/ppermute | solution.py:23
  63.3 2.4 %collective-permute-start.5 = (f32[4,64,64]{2,1,0:T(8,128)S(1)}, f32[4,64,64]{2,1,0:T(8,128)S(1)}, u32[]{:S(2)}, u32[]{:S(2)}) collective-permute-start(f32[4,64,64]{2,1,0:T(8,128)S(1)} %fusion.158), channel_id=1, source_target_pairs={{0,16},{4,20},{8,24},{12,28},{16,0},{20,4},{24,8},{28,12},{1,17},{... | collective-permute-start | bytes 196616 | tf_op jit(solution)/shard_map/ppermute | solution.py:23
  65.7 4.9 %collective-permute-done.5 = f32[4,64,64]{2,1,0:T(8,128)S(1)} collective-permute-done((f32[4,64,64]{2,1,0:T(8,128)S(1)}, f32[4,64,64]{2,1,0:T(8,128)S(1)}, u32[]{:S(2)}, u32[]{:S(2)}) %collective-permute-start.5) | collective-permute-done | bytes 65568 | tf_op jit(solution)/shard_map/ppermute | solution.py:23
  70.7 0.7 pad_maximum_fusion.2.aug_ref
  71.4 8.4 %shard_map.18 = f32[64,128]{1,0:T(8,128)} custom-call(f32[64,128]{1,0:T(8,128)} %pad_maximum_fusion.2.aug_ref), custom_call_target="tpu_custom_call" | custom-call | tf_op jit(solution)/shard_map/pallas_call | solution.py:58
  79.7 1.2 %convolution_subtract_fusion.1 = f32[64,768]{1,0:T(8,128)S(1)} fusion(f32[64,768]{1,0:T(8,128)S(1)} %fusion.1, s32[768]{0:T(1024)S(1)} %fusion.51, f32[64,128]{1,0:T(8,128)} %shard_map.18), kind=kOutput, calls=%fused_computation.2 | convolution fusion | flops 37896192 | bytes 429056 | tf_op jit(solution)/shard_map/dot_general | solution.py:15
  81.0 0.3 fusion.21
  84.8 1.1 %fusion = f32[1,64,768]{2,1,0:T(8,128)} fusion(f32[64,768]{1,0:T(8,128)S(1)} %convolution_subtract_fusion.3, f32[64,64]{1,0:T(8,128)S(1)} %fusion.19, f32[64,768]{1,0:T(8,128)S(1)} %convolution_subtract_fusion.1), kind=kOutput, calls=%fused_computation.1 | convolution fusion | flops 37797888 | bytes 606208 | tf_op jit(solution)/shard_map/dot_general | solution.py:112
  (63 shorter events, 8.1 us)
Async XLA Ops:
  10.3 0.9 %copy-start = (f32[1,64,768]{2,1,0:T(8,128)S(1)}, f32[1,64,768]{2,1,0:T(8,128)}, u32[]{:S(2)}) copy-start(f32[1,64,768]{2,1,0:T(8,128)} %param.1) | copy-start | bytes 589828
  12.4 7.2 %collective-permute-start = (f32[6,64,64]{2,1,0:T(8,128)S(1)}, f32[6,64,64]{2,1,0:T(8,128)S(1)}, u32[]{:S(2)}, u32[]{:S(2)}) collective-permute-start(f32[6,64,64]{2,1,0:T(8,128)S(1)} %fusion.2), channel_id=1, source_target_pairs={{0,4},{4,0},{8,12},{12,8},{16,20},{20,16},{24,28},{28,24},{1,5},{5... | collective-permute-start | bytes 294920 | tf_op jit(solution)/shard_map/ppermute | solution.py:23
  19.6 6.4 %collective-permute-start.1 = (f32[6,64,64]{2,1,0:T(8,128)S(1)}, f32[6,64,64]{2,1,0:T(8,128)S(1)}, u32[]{:S(2)}, u32[]{:S(2)}) collective-permute-start(f32[6,64,64]{2,1,0:T(8,128)S(1)} %add.41), channel_id=1, source_target_pairs={{0,8},{4,12},{8,0},{12,4},{16,24},{20,28},{24,16},{28,20},{1,9},{5... | collective-permute-start | bytes 294920 | tf_op jit(solution)/shard_map/ppermute | solution.py:23
  26.0 10.6 %collective-permute-start.2 = (f32[6,64,64]{2,1,0:T(8,128)S(1)}, f32[6,64,64]{2,1,0:T(8,128)S(1)}, u32[]{:S(2)}, u32[]{:S(2)}) collective-permute-start(f32[6,64,64]{2,1,0:T(8,128)S(1)} %add.42), channel_id=1, source_target_pairs={{0,16},{4,20},{8,24},{12,28},{16,0},{20,4},{24,8},{28,12},{1,17},{... | collective-permute-start | bytes 294920 | tf_op jit(solution)/shard_map/ppermute | solution.py:23
  45.8 1.1 %copy-start.1 = (f32[64,128]{1,0:T(8,128)S(1)}, f32[64,128]{1,0:T(8,128)}, u32[]{:S(2)}) copy-start(f32[64,128]{1,0:T(8,128)} %shard_map.17) | copy-start | bytes 98308
  53.2 5.0 %collective-permute-start.3 = (f32[4,64,64]{2,1,0:T(8,128)S(1)}, f32[4,64,64]{2,1,0:T(8,128)S(1)}, u32[]{:S(2)}, u32[]{:S(2)}) collective-permute-start(f32[4,64,64]{2,1,0:T(8,128)S(1)} %pad_maximum_fusion), channel_id=1, source_target_pairs={{0,4},{4,0},{8,12},{12,8},{16,20},{20,16},{24,28},{28,24},{1,5},{5... | collective-permute-start | bytes 196616 | tf_op jit(solution)/shard_map/ppermute | solution.py:23
  58.2 5.0 %collective-permute-start.4 = (f32[4,64,64]{2,1,0:T(8,128)S(1)}, f32[4,64,64]{2,1,0:T(8,128)S(1)}, u32[]{:S(2)}, u32[]{:S(2)}) collective-permute-start(f32[4,64,64]{2,1,0:T(8,128)S(1)} %fusion.75), channel_id=1, source_target_pairs={{0,8},{4,12},{8,0},{12,4},{16,24},{20,28},{24,16},{28,20},{1,9},{5... | collective-permute-start | bytes 196616 | tf_op jit(solution)/shard_map/ppermute | solution.py:23
  63.3 7.3 %collective-permute-start.5 = (f32[4,64,64]{2,1,0:T(8,128)S(1)}, f32[4,64,64]{2,1,0:T(8,128)S(1)}, u32[]{:S(2)}, u32[]{:S(2)}) collective-permute-start(f32[4,64,64]{2,1,0:T(8,128)S(1)} %fusion.158), channel_id=1, source_target_pairs={{0,16},{4,20},{8,24},{12,28},{16,0},{20,4},{24,8},{28,12},{1,17},{... | collective-permute-start | bytes 196616 | tf_op jit(solution)/shard_map/ppermute | solution.py:23
  79.7 1.2 %copy-start.2 = (f32[64,128]{1,0:T(8,128)S(1)}, f32[64,128]{1,0:T(8,128)}, u32[]{:S(2)}) copy-start(f32[64,128]{1,0:T(8,128)} %shard_map.18) | copy-start | bytes 98308

commit v3 on v2

--- a/solution.py
+++ b/solution.py
@@ -28,7 +28,7 @@
 def invert_near_identity(square):
     identity = jnp.eye(square.shape[0], dtype=jnp.float32)
     approx = square.T * (2.0 / 4.25)
-    for _ in range(9):
+    for _ in range(8):
         approx = apply_left(approx, 2.0 * identity - apply_left(square, approx))
     return approx
 
@@ -76,16 +76,18 @@
         panel_0 = gathered[0]
         second = gathered[1]
 
-        sums = jnp.stack([
+        head = butterfly_sum(jnp.stack([
             inner_rows(panel_0, panel_0),
             inner_rows(panel_0, units[0]),
+        ]), "rows", rows_size)
+        tail = butterfly_sum(jnp.stack([
             inner_rows(panel_0, current),
             inner_rows(units[0], current),
             inner_rows(panel_0, second),
             inner_rows(units[0], second),
-        ])
-        sums = butterfly_sum(sums, "rows", rows_size)
-        gram, top_rows, basis_cur, unit_cur, basis_sec, unit_sec = (sums[i] for i in range(6))
+        ]), "rows", rows_size)
+        gram, top_rows = head[0], head[1]
+        basis_cur, unit_cur, basis_sec, unit_sec = (tail[i] for i in range(4))
         lower_inv = lower_inverse(gram)
         top_block = apply_left(lower_inv, top_rows)
         inverse = invert_near_identity(identity - top_block.T)
@@ -96,14 +98,16 @@
         second = second - jnp.dot(mixed_sec.T, reflect, precision=HIGHEST_PRECISION)
 
         panel_1 = jnp.where((global_rows >= width)[None, :], second, jnp.zeros_like(second))
-        sums = jnp.stack([
+        head = butterfly_sum(jnp.stack([
             inner_rows(panel_1, panel_1),
             inner_rows(panel_1, units[1]),
+        ]), "rows", rows_size)
+        tail = butterfly_sum(jnp.stack([
             inner_rows(panel_1, current),
             inner_rows(units[1], current),
-        ])
-        sums = butterfly_sum(sums, "rows", rows_size)
-        gram, top_rows, basis_cur, unit_cur = (sums[i] for i in range(4))
+        ]), "rows", rows_size)
+        gram, top_rows = head[0], head[1]
+        basis_cur, unit_cur = tail[0], tail[1]
         lower_inv = lower_inverse(gram)
         top_block = apply_left(lower_inv, top_rows)
         inverse = invert_near_identity(identity - top_block.T)

time: 86.3 us -> 78.5 us (0.910)
  waiting for transfers between devices: 30.8 us -> 15.4 us
  starting transfers between devices: 10.9 us -> 19.4 us
    ppermute x6 -> x12, waiting for transfers between devices: 30.8 us -> 15.4 us  [butterfly_sum(): x = x + lax.ppermute(x, axis, [(i, i ^ step) for i in range(size)])]
    ppermute x6 -> x12, starting transfers between devices: 10.9 us -> 19.4 us  [butterfly_sum(): x = x + lax.ppermute(x, axis, [(i, i ^ step) for i in range(size)])]
    dot_general x46 -> x42, matrix products: 10.1 us -> 9.47 us  [apply_left(): return jnp.dot(square, right_side, precision=HIGHEST_PRECISION)]
  transfers between devices with their start and end apart: 6 -> 12, of which waited for: 6 -> 8; matrix products, arithmetic and copies ran while one was open for 0% -> 11% of each run, Pallas kernels for 0% -> 21%
where the time goes in v3:
time: 78.5 us; the launch traced here: 78.1 us
  starting transfers between devices  19.4 us (25%)
  Pallas kernels  16.7 us (21%)
  waiting for transfers between devices  15.4 us (20%)
  matrix products  14.1 us (18%)
  blocking collectives  10.3 us (13%)
  other arithmetic  1.61 us (2%)
    ppermute x12, starting transfers between devices, butterfly_sum(): x = x + lax.ppermute(x, axis, [(i, i ^ step) for i in range(size)])  19.4 us
    pallas_call x2, Pallas kernels, lower_inverse(): pl.pallas_call(_eliminate_kernel, out_shape=jax.ShapeDtypeStruct(aug.shap...  16.7 us
    ppermute x12, waiting for transfers between devices, butterfly_sum(): x = x + lax.ppermute(x, axis, [(i, i ^ step) for i in range(size)])  15.4 us
    all_gather x1, blocking collectives, local(): gathered = lax.all_gather(current, 'cols')  10.3 us
    dot_general x42, matrix products, apply_left(): return jnp.dot(square, right_side, precision=HIGHEST_PRECISION)  9.47 us
    dot_general x10, matrix products, inner_rows(): lax.dot_general(left, right, (((1,), (1,)), ((), ())), precision=HIGHEST_...  2.79 us
  transfers between devices with their start and end apart: 12, of which 8 were waited for; matrix products, arithmetic and copies ran while one was open for 11% of the time, Pallas kernels for 21%

profile of v3, /device:TPU:0, one launch (start us, length us, event | category | flops | bytes accessed | tf_op | source)
XLA Modules:
  0.0 78.1 jit_solution(6301536935260249696)
XLA Ops:
  0.0 10.3 %all_gather.3 = f32[4,64,768]{2,1,0:T(8,128)S(1)} all-gather(f32[1,64,768]{2,1,0:T(8,128)} %param.1), channel_id=1, replica_groups=mesh['rows'=8,'cols'=4] {'cols'}, dimensions={0}, use_global_device_ids=true | all-gather | bytes 983040 | tf_op jit(solution)/shard_map/all_gather | solution.py:75
  10.9 1.6 %collective-permute-start = (f32[2,64,64]{2,1,0:T(8,128)S(1)}, f32[2,64,64]{2,1,0:T(8,128)S(1)}, u32[]{:S(2)}, u32[]{:S(2)}) collective-permute-start(f32[2,64,64]{2,1,0:T(8,128)S(1)} %pad_maximum_fusion.1), channel_id=1, source_target_pairs={{0,4},{4,0},{8,12},{12,8},{16,20},{20,16},{24,28},{28,24},{1,5},{5... | collective-permute-start | bytes 98312 | tf_op jit(solution)/shard_map/ppermute | solution.py:23
  13.6 0.6 collective-permute-start.3
  14.3 1.0 %collective-permute-done = f32[2,64,64]{2,1,0:T(8,128)S(1)} collective-permute-done((f32[2,64,64]{2,1,0:T(8,128)S(1)}, f32[2,64,64]{2,1,0:T(8,128)S(1)}, u32[]{:S(2)}, u32[]{:S(2)}) %collective-permute-start) | collective-permute-done | bytes 32800 | tf_op jit(solution)/shard_map/ppermute | solution.py:23
  15.3 1.6 %collective-permute-start.1 = (f32[2,64,64]{2,1,0:T(8,128)S(1)}, f32[2,64,64]{2,1,0:T(8,128)S(1)}, u32[]{:S(2)}, u32[]{:S(2)}) collective-permute-start(f32[2,64,64]{2,1,0:T(8,128)S(1)} %fusion.69), channel_id=1, source_target_pairs={{0,8},{4,12},{8,0},{12,4},{16,24},{20,28},{24,16},{28,20},{1,9},{5... | collective-permute-start | bytes 98312 | tf_op jit(solution)/shard_map/ppermute | solution.py:23
  16.9 2.7 %collective-permute-done.1 = f32[2,64,64]{2,1,0:T(8,128)S(1)} collective-permute-done((f32[2,64,64]{2,1,0:T(8,128)S(1)}, f32[2,64,64]{2,1,0:T(8,128)S(1)}, u32[]{:S(2)}, u32[]{:S(2)}) %collective-permute-start.1) | collective-permute-done | bytes 32800 | tf_op jit(solution)/shard_map/ppermute | solution.py:23
  19.6 2.7 %collective-permute-start.2 = (f32[2,64,64]{2,1,0:T(8,128)S(1)}, f32[2,64,64]{2,1,0:T(8,128)S(1)}, u32[]{:S(2)}, u32[]{:S(2)}) collective-permute-start(f32[2,64,64]{2,1,0:T(8,128)S(1)} %fusion.148), channel_id=1, source_target_pairs={{0,16},{4,20},{8,24},{12,28},{16,0},{20,4},{24,8},{28,12},{1,17},{... | collective-permute-start | bytes 98312 | tf_op jit(solution)/shard_map/ppermute | solution.py:23
  22.3 1.6 %collective-permute-start.4 = (f32[4,64,64]{2,1,0:T(8,128)S(1)}, f32[4,64,64]{2,1,0:T(8,128)S(1)}, u32[]{:S(2)}, u32[]{:S(2)}) collective-permute-start(f32[4,64,64]{2,1,0:T(8,128)S(1)} %fusion.70), channel_id=1, source_target_pairs={{0,8},{4,12},{8,0},{12,4},{16,24},{20,28},{24,16},{28,20},{1,9},{5... | collective-permute-start | bytes 196616 | tf_op jit(solution)/shard_map/ppermute | solution.py:23
  24.0 1.0 %collective-permute-done.2 = f32[2,64,64]{2,1,0:T(8,128)S(1)} collective-permute-done((f32[2,64,64]{2,1,0:T(8,128)S(1)}, f32[2,64,64]{2,1,0:T(8,128)S(1)}, u32[]{:S(2)}, u32[]{:S(2)}) %collective-permute-start.2) | collective-permute-done | bytes 32800 | tf_op jit(solution)/shard_map/ppermute | solution.py:23
  25.0 0.7 pad_maximum_fusion.4.aug_ref
  25.7 8.4 %shard_map.17 = f32[64,128]{1,0:T(8,128)} custom-call(f32[64,128]{1,0:T(8,128)} %pad_maximum_fusion.4.aug_ref), custom_call_target="tpu_custom_call" | custom-call | tf_op jit(solution)/shard_map/pallas_call | solution.py:58
  34.1 1.1 %fusion.24 = f32[64,64]{1,0:T(8,128)S(1)} fusion(f32[2,64,64]{2,1,0:T(8,128)S(1)} %add.61, f32[64,128]{1,0:T(8,128)} %shard_map.17), kind=kOutput, calls=%fused_computation.72 | convolution fusion | flops 3145728 | bytes 81920 | tf_op jit(solution)/shard_map/dot_general | solution.py:15
  35.2 0.4 convolution_subtract_fusion.4
  38.3 3.2 %collective-permute-start.5 = (f32[4,64,64]{2,1,0:T(8,128)S(1)}, f32[4,64,64]{2,1,0:T(8,128)S(1)}, u32[]{:S(2)}, u32[]{:S(2)}) collective-permute-start(f32[4,64,64]{2,1,0:T(8,128)S(1)} %fusion.147), channel_id=1, source_target_pairs={{0,16},{4,20},{8,24},{12,28},{16,0},{20,4},{24,8},{28,12},{1,17},{... | collective-permute-start | bytes 196616 | tf_op jit(solution)/shard_map/ppermute | solution.py:23
  41.6 4.2 %collective-permute-done.5 = f32[4,64,64]{2,1,0:T(8,128)S(1)} collective-permute-done((f32[4,64,64]{2,1,0:T(8,128)S(1)}, f32[4,64,64]{2,1,0:T(8,128)S(1)}, u32[]{:S(2)}, u32[]{:S(2)}) %collective-permute-start.5) | collective-permute-done | bytes 65568 | tf_op jit(solution)/shard_map/ppermute | solution.py:23
  46.6 0.4 convolution_subtract_fusion.3
  47.0 0.4 fusion.1
  47.6 0.3 convolution_bitcast_fusion.5
  48.5 1.6 %collective-permute-start.6 = (f32[2,64,64]{2,1,0:T(8,128)S(1)}, f32[2,64,64]{2,1,0:T(8,128)S(1)}, u32[]{:S(2)}, u32[]{:S(2)}) collective-permute-start(f32[2,64,64]{2,1,0:T(8,128)S(1)} %pad_maximum_fusion.2), channel_id=1, source_target_pairs={{0,4},{4,0},{8,12},{12,8},{16,20},{20,16},{24,28},{28,24},{1,5},{5... | collective-permute-start | bytes 98312 | tf_op jit(solution)/shard_map/ppermute | solution.py:23
  50.1 0.6 collective-permute-start.9
  50.7 2.2 %collective-permute-done.6 = f32[2,64,64]{2,1,0:T(8,128)S(1)} collective-permute-done((f32[2,64,64]{2,1,0:T(8,128)S(1)}, f32[2,64,64]{2,1,0:T(8,128)S(1)}, u32[]{:S(2)}, u32[]{:S(2)}) %collective-permute-start.6) | collective-permute-done | bytes 32800 | tf_op jit(solution)/shard_map/ppermute | solution.py:23
  52.9 1.1 %collective-permute-start.7 = (f32[2,64,64]{2,1,0:T(8,128)S(1)}, f32[2,64,64]{2,1,0:T(8,128)S(1)}, u32[]{:S(2)}, u32[]{:S(2)}) collective-permute-start(f32[2,64,64]{2,1,0:T(8,128)S(1)} %fusion.68), channel_id=1, source_target_pairs={{0,8},{4,12},{8,0},{12,4},{16,24},{20,28},{24,16},{28,20},{1,9},{5... | collective-permute-start | bytes 98312 | tf_op jit(solution)/shard_map/ppermute | solution.py:23
  53.9 0.5 collective-permute-done.9
  54.4 1.1 %collective-permute-start.10 = (f32[2,64,64]{2,1,0:T(8,128)S(1)}, f32[2,64,64]{2,1,0:T(8,128)S(1)}, u32[]{:S(2)}, u32[]{:S(2)}) collective-permute-start(f32[2,64,64]{2,1,0:T(8,128)S(1)} %fusion.67), channel_id=1, source_target_pairs={{0,8},{4,12},{8,0},{12,4},{16,24},{20,28},{24,16},{28,20},{1,9},{5... | collective-permute-start | bytes 98312 | tf_op jit(solution)/shard_map/ppermute | solution.py:23
  55.5 2.4 %collective-permute-done.7 = f32[2,64,64]{2,1,0:T(8,128)S(1)} collective-permute-done((f32[2,64,64]{2,1,0:T(8,128)S(1)}, f32[2,64,64]{2,1,0:T(8,128)S(1)}, u32[]{:S(2)}, u32[]{:S(2)}) %collective-permute-start.7) | collective-permute-done | bytes 32800 | tf_op jit(solution)/shard_map/ppermute | solution.py:23
  57.9 2.1 %collective-permute-start.8 = (f32[2,64,64]{2,1,0:T(8,128)S(1)}, f32[2,64,64]{2,1,0:T(8,128)S(1)}, u32[]{:S(2)}, u32[]{:S(2)}) collective-permute-start(f32[2,64,64]{2,1,0:T(8,128)S(1)} %fusion.146), channel_id=1, source_target_pairs={{0,16},{4,20},{8,24},{12,28},{16,0},{20,4},{24,8},{28,12},{1,17},{... | collective-permute-start | bytes 98312 | tf_op jit(solution)/shard_map/ppermute | solution.py:23
  60.0 1.7 %collective-permute-start.11 = (f32[2,64,64]{2,1,0:T(8,128)S(1)}, f32[2,64,64]{2,1,0:T(8,128)S(1)}, u32[]{:S(2)}, u32[]{:S(2)}) collective-permute-start(f32[2,64,64]{2,1,0:T(8,128)S(1)} %fusion.145), channel_id=1, source_target_pairs={{0,16},{4,20},{8,24},{12,28},{16,0},{20,4},{24,8},{28,12},{1,17},{... | collective-permute-start | bytes 98312 | tf_op jit(solution)/shard_map/ppermute | solution.py:23
  61.8 1.4 %collective-permute-done.8 = f32[2,64,64]{2,1,0:T(8,128)S(1)} collective-permute-done((f32[2,64,64]{2,1,0:T(8,128)S(1)}, f32[2,64,64]{2,1,0:T(8,128)S(1)}, u32[]{:S(2)}, u32[]{:S(2)}) %collective-permute-start.8) | collective-permute-done | bytes 32800 | tf_op jit(solution)/shard_map/ppermute | solution.py:23
  63.2 0.7 pad_maximum_fusion.5.aug_ref
  63.9 8.4 %shard_map.18 = f32[64,128]{1,0:T(8,128)} custom-call(f32[64,128]{1,0:T(8,128)} %pad_maximum_fusion.5.aug_ref), custom_call_target="tpu_custom_call" | custom-call | tf_op jit(solution)/shard_map/pallas_call | solution.py:58
  72.3 1.2 %convolution_subtract_fusion.1 = f32[64,768]{1,0:T(8,128)S(1)} fusion(f32[64,768]{1,0:T(8,128)S(1)} %fusion.1, s32[768]{0:T(1024)S(1)} %get-tuple-element.6, f32[64,128]{1,0:T(8,128)} %shard_map.18), kind=kOutput, calls=%fused_computation.2 | convolution fusion | flops 37896192 | bytes 429056 | tf_op jit(solution)/shard_map/dot_general | solution.py:15
  77.0 1.1 %fusion = f32[1,64,768]{2,1,0:T(8,128)} fusion(f32[64,768]{1,0:T(8,128)S(1)} %convolution_subtract_fusion.3, f32[64,64]{1,0:T(8,128)S(1)} %fusion.13, f32[64,768]{1,0:T(8,128)S(1)} %convolution_subtract_fusion.1), kind=kOutput, calls=%fused_computation.1 | convolution fusion | flops 37797888 | bytes 606208 | tf_op jit(solution)/shard_map/dot_general | solution.py:116
  (79 shorter events, 9.5 us)
Async XLA Ops:
  10.6 1.8 %copy-start = (f32[1,64,768]{2,1,0:T(8,128)S(1)}, f32[1,64,768]{2,1,0:T(8,128)}, u32[]{:S(2)}) copy-start(f32[1,64,768]{2,1,0:T(8,128)} %param.1) | copy-start | bytes 589828
  10.9 4.4 %collective-permute-start = (f32[2,64,64]{2,1,0:T(8,128)S(1)}, f32[2,64,64]{2,1,0:T(8,128)S(1)}, u32[]{:S(2)}, u32[]{:S(2)}) collective-permute-start(f32[2,64,64]{2,1,0:T(8,128)S(1)} %pad_maximum_fusion.1), channel_id=1, source_target_pairs={{0,4},{4,0},{8,12},{12,8},{16,20},{20,16},{24,28},{28,24},{1,5},{5... | collective-permute-start | bytes 98312 | tf_op jit(solution)/shard_map/ppermute | solution.py:23
  13.6 8.7 %collective-permute-start.3 = (f32[4,64,64]{2,1,0:T(8,128)S(1)}, f32[4,64,64]{2,1,0:T(8,128)S(1)}, u32[]{:S(2)}, u32[]{:S(2)}) collective-permute-start(f32[4,64,64]{2,1,0:T(8,128)S(1)} %pad_maximum_fusion), channel_id=1, source_target_pairs={{0,4},{4,0},{8,12},{12,8},{16,20},{20,16},{24,28},{28,24},{1,5},{5... | collective-permute-start | bytes 196616 | tf_op jit(solution)/shard_map/ppermute | solution.py:23
  15.3 4.3 %collective-permute-start.1 = (f32[2,64,64]{2,1,0:T(8,128)S(1)}, f32[2,64,64]{2,1,0:T(8,128)S(1)}, u32[]{:S(2)}, u32[]{:S(2)}) collective-permute-start(f32[2,64,64]{2,1,0:T(8,128)S(1)} %fusion.69), channel_id=1, source_target_pairs={{0,8},{4,12},{8,0},{12,4},{16,24},{20,28},{24,16},{28,20},{1,9},{5... | collective-permute-start | bytes 98312 | tf_op jit(solution)/shard_map/ppermute | solution.py:23
  19.6 5.3 %collective-permute-start.2 = (f32[2,64,64]{2,1,0:T(8,128)S(1)}, f32[2,64,64]{2,1,0:T(8,128)S(1)}, u32[]{:S(2)}, u32[]{:S(2)}) collective-permute-start(f32[2,64,64]{2,1,0:T(8,128)S(1)} %fusion.148), channel_id=1, source_target_pairs={{0,16},{4,20},{8,24},{12,28},{16,0},{20,4},{24,8},{28,12},{1,17},{... | collective-permute-start | bytes 98312 | tf_op jit(solution)/shard_map/ppermute | solution.py:23
  22.3 15.9 %collective-permute-start.4 = (f32[4,64,64]{2,1,0:T(8,128)S(1)}, f32[4,64,64]{2,1,0:T(8,128)S(1)}, u32[]{:S(2)}, u32[]{:S(2)}) collective-permute-start(f32[4,64,64]{2,1,0:T(8,128)S(1)} %fusion.70), channel_id=1, source_target_pairs={{0,8},{4,12},{8,0},{12,4},{16,24},{20,28},{24,16},{28,20},{1,9},{5... | collective-permute-start | bytes 196616 | tf_op jit(solution)/shard_map/ppermute | solution.py:23
  34.1 1.1 %copy-start.1 = (f32[64,128]{1,0:T(8,128)S(1)}, f32[64,128]{1,0:T(8,128)}, u32[]{:S(2)}) copy-start(f32[64,128]{1,0:T(8,128)} %shard_map.17) | copy-start | bytes 98308
  38.3 7.5 %collective-permute-start.5 = (f32[4,64,64]{2,1,0:T(8,128)S(1)}, f32[4,64,64]{2,1,0:T(8,128)S(1)}, u32[]{:S(2)}, u32[]{:S(2)}) collective-permute-start(f32[4,64,64]{2,1,0:T(8,128)S(1)} %fusion.147), channel_id=1, source_target_pairs={{0,16},{4,20},{8,24},{12,28},{16,0},{20,4},{24,8},{28,12},{1,17},{... | collective-permute-start | bytes 196616 | tf_op jit(solution)/shard_map/ppermute | solution.py:23
  48.5 4.3 %collective-permute-start.6 = (f32[2,64,64]{2,1,0:T(8,128)S(1)}, f32[2,64,64]{2,1,0:T(8,128)S(1)}, u32[]{:S(2)}, u32[]{:S(2)}) collective-permute-start(f32[2,64,64]{2,1,0:T(8,128)S(1)} %pad_maximum_fusion.2), channel_id=1, source_target_pairs={{0,4},{4,0},{8,12},{12,8},{16,20},{20,16},{24,28},{28,24},{1,5},{5... | collective-permute-start | bytes 98312 | tf_op jit(solution)/shard_map/ppermute | solution.py:23
  50.1 4.3 %collective-permute-start.9 = (f32[2,64,64]{2,1,0:T(8,128)S(1)}, f32[2,64,64]{2,1,0:T(8,128)S(1)}, u32[]{:S(2)}, u32[]{:S(2)}) collective-permute-start(f32[2,64,64]{2,1,0:T(8,128)S(1)} %pad_maximum_fusion.3), channel_id=1, source_target_pairs={{0,4},{4,0},{8,12},{12,8},{16,20},{20,16},{24,28},{28,24},{1,5},{5... | collective-permute-start | bytes 98312 | tf_op jit(solution)/shard_map/ppermute | solution.py:23
  52.9 5.0 %collective-permute-start.7 = (f32[2,64,64]{2,1,0:T(8,128)S(1)}, f32[2,64,64]{2,1,0:T(8,128)S(1)}, u32[]{:S(2)}, u32[]{:S(2)}) collective-permute-start(f32[2,64,64]{2,1,0:T(8,128)S(1)} %fusion.68), channel_id=1, source_target_pairs={{0,8},{4,12},{8,0},{12,4},{16,24},{20,28},{24,16},{28,20},{1,9},{5... | collective-permute-start | bytes 98312 | tf_op jit(solution)/shard_map/ppermute | solution.py:23
  54.4 5.6 %collective-permute-start.10 = (f32[2,64,64]{2,1,0:T(8,128)S(1)}, f32[2,64,64]{2,1,0:T(8,128)S(1)}, u32[]{:S(2)}, u32[]{:S(2)}) collective-permute-start(f32[2,64,64]{2,1,0:T(8,128)S(1)} %fusion.67), channel_id=1, source_target_pairs={{0,8},{4,12},{8,0},{12,4},{16,24},{20,28},{24,16},{28,20},{1,9},{5... | collective-permute-start | bytes 98312 | tf_op jit(solution)/shard_map/ppermute | solution.py:23
  57.9 5.2 %collective-permute-start.8 = (f32[2,64,64]{2,1,0:T(8,128)S(1)}, f32[2,64,64]{2,1,0:T(8,128)S(1)}, u32[]{:S(2)}, u32[]{:S(2)}) collective-permute-start(f32[2,64,64]{2,1,0:T(8,128)S(1)} %fusion.146), channel_id=1, source_target_pairs={{0,16},{4,20},{8,24},{12,28},{16,0},{20,4},{24,8},{28,12},{1,17},{... | collective-permute-start | bytes 98312 | tf_op jit(solution)/shard_map/ppermute | solution.py:23
  60.0 13.7 %collective-permute-start.11 = (f32[2,64,64]{2,1,0:T(8,128)S(1)}, f32[2,64,64]{2,1,0:T(8,128)S(1)}, u32[]{:S(2)}, u32[]{:S(2)}) collective-permute-start(f32[2,64,64]{2,1,0:T(8,128)S(1)} %fusion.145), channel_id=1, source_target_pairs={{0,16},{4,20},{8,24},{12,28},{16,0},{20,4},{24,8},{28,12},{1,17},{... | collective-permute-start | bytes 98312 | tf_op jit(solution)/shard_map/ppermute | solution.py:23
  72.3 1.2 %copy-start.2 = (f32[64,128]{1,0:T(8,128)S(1)}, f32[64,128]{1,0:T(8,128)}, u32[]{:S(2)}) copy-start(f32[64,128]{1,0:T(8,128)} %shard_map.18) | copy-start | bytes 98308

commit v4 on v2

--- a/solution.py
+++ b/solution.py
@@ -28,7 +28,7 @@
 def invert_near_identity(square):
     identity = jnp.eye(square.shape[0], dtype=jnp.float32)
     approx = square.T * (2.0 / 4.25)
-    for _ in range(9):
+    for _ in range(8):
         approx = apply_left(approx, 2.0 * identity - apply_left(square, approx))
     return approx
 
@@ -76,40 +76,41 @@
         panel_0 = gathered[0]
         second = gathered[1]
 
-        sums = jnp.stack([
-            inner_rows(panel_0, panel_0),
-            inner_rows(panel_0, units[0]),
-            inner_rows(panel_0, current),
-            inner_rows(units[0], current),
-            inner_rows(panel_0, second),
-            inner_rows(units[0], second),
-        ])
-        sums = butterfly_sum(sums, "rows", rows_size)
-        gram, top_rows, basis_cur, unit_cur, basis_sec, unit_sec = (sums[i] for i in range(6))
+        def reduce_rows(*pairs):
+            return butterfly_sum(
+                jnp.stack([inner_rows(a, b) for a, b in pairs]), "rows", rows_size
+            )
+
+        gram = reduce_rows((panel_0, panel_0))[0]
+        tail = reduce_rows((panel_0, units[0]), (panel_0, second), (units[0], second))
+        late = reduce_rows((panel_0, current), (units[0], current))
         lower_inv = lower_inverse(gram)
-        top_block = apply_left(lower_inv, top_rows)
+        top_block = apply_left(lower_inv, tail[0])
         inverse = invert_near_identity(identity - top_block.T)
         reflect = units[0] - apply_left(lower_inv, panel_0)
-        mixed = apply_left(inverse, unit_cur - apply_left(lower_inv, basis_cur))
-        mixed_sec = apply_left(inverse, unit_sec - apply_left(lower_inv, basis_sec))
-        current = current - jnp.dot(mixed.T, reflect, precision=HIGHEST_PRECISION)
+        mixed_sec = apply_left(inverse, tail[2] - apply_left(lower_inv, tail[1]))
         second = second - jnp.dot(mixed_sec.T, reflect, precision=HIGHEST_PRECISION)
 
         panel_1 = jnp.where((global_rows >= width)[None, :], second, jnp.zeros_like(second))
-        sums = jnp.stack([
-            inner_rows(panel_1, panel_1),
-            inner_rows(panel_1, units[1]),
-            inner_rows(panel_1, current),
-            inner_rows(units[1], current),
-        ])
-        sums = butterfly_sum(sums, "rows", rows_size)
-        gram, top_rows, basis_cur, unit_cur = (sums[i] for i in range(4))
-        lower_inv = lower_inverse(gram)
-        top_block = apply_left(lower_inv, top_rows)
-        inverse = invert_near_identity(identity - top_block.T)
-        reflect = units[1] - apply_left(lower_inv, panel_1)
-        mixed = apply_left(inverse, unit_cur - apply_left(lower_inv, basis_cur))
+        gram_1 = reduce_rows((panel_1, panel_1))[0]
+        tail_1 = reduce_rows(
+            (panel_1, units[1]),
+            (panel_1, current),
+            (units[1], current),
+            (panel_1, panel_0),
+            (units[1], panel_0),
+        )
+        mixed = apply_left(inverse, late[1] - apply_left(lower_inv, late[0]))
+        back = jnp.dot(lower_inv.T, mixed, precision=HIGHEST_PRECISION)
+        basis_cur = tail_1[1] + apply_left(tail_1[3], back)
+        unit_cur = tail_1[2] + apply_left(tail_1[4], back)
+        lower_inv_1 = lower_inverse(gram_1)
+        top_block = apply_left(lower_inv_1, tail_1[0])
+        inverse_1 = invert_near_identity(identity - top_block.T)
+        reflect_1 = units[1] - apply_left(lower_inv_1, panel_1)
+        mixed_1 = apply_left(inverse_1, unit_cur - apply_left(lower_inv_1, basis_cur))
         current = current - jnp.dot(mixed.T, reflect, precision=HIGHEST_PRECISION)
+        current = current - jnp.dot(mixed_1.T, reflect_1, precision=HIGHEST_PRECISION)
         return current.reshape(matrix.shape)
 
     return local

time: 86.3 us -> 90.4 us (1.048)
  starting transfers between devices: 10.9 us -> 19.9 us
  waiting for transfers between devices: 30.8 us -> 27.3 us
  matrix products: 14.7 us -> 13.6 us
    ppermute x6 -> x15, starting transfers between devices: 10.9 us -> 19.9 us  [butterfly_sum(): x = x + lax.ppermute(x, axis, [(i, i ^ step) for i in range(size)])]
    ppermute x6 -> x15, waiting for transfers between devices: 30.8 us -> 27.3 us  [butterfly_sum(): x = x + lax.ppermute(x, axis, [(i, i ^ step) for i in range(size)])]
    dot_general x46 -> x44, matrix products: 10.1 us -> 8.19 us  [apply_left(): return jnp.dot(square, right_side, precision=HIGHEST_PRECISION)]
    dot_general x0 -> x2, matrix products: none -> 1.35 us  [the longest x1 1.05 us: local(): jnp.dot(mixed_1.T, reflect_1, precision=HIGHEST_PRECISION)]
    dot_general x2 -> x1, matrix products: 1.42 us -> 0.37 us  [local(): current = current - jnp.dot(mixed.T, reflect, precision=HIGHEST_PRECISION)]
    dot_general x10 -> x12, matrix products: 2.8 us -> 3.35 us  [inner_rows(): lax.dot_general(left, right, (((1,), (1,)), ((), ())), precision=HIGHEST_...]
  transfers between devices with their start and end apart: 6 -> 15, of which waited for: 6 -> 9; matrix products, arithmetic and copies ran while one was open for 0% -> 6% of each run, Pallas kernels for 0% -> 19%
where the time goes in v4:
time: 90.4 us; the launch traced here: 90.1 us
  waiting for transfers between devices  27.3 us (30%)
  starting transfers between devices  19.9 us (22%)
  Pallas kernels  16.8 us (19%)
  matrix products  13.6 us (15%)
  blocking collectives  10.3 us (11%)
  other arithmetic  1.62 us (2%)
    ppermute x15, waiting for transfers between devices, butterfly_sum(): x = x + lax.ppermute(x, axis, [(i, i ^ step) for i in range(size)])  27.3 us
    ppermute x15, starting transfers between devices, butterfly_sum(): x = x + lax.ppermute(x, axis, [(i, i ^ step) for i in range(size)])  19.9 us
    pallas_call x2, Pallas kernels, lower_inverse(): pl.pallas_call(_eliminate_kernel, out_shape=jax.ShapeDtypeStruct(aug.shap...  16.8 us
    all_gather x1, blocking collectives, local(): gathered = lax.all_gather(current, 'cols')  10.3 us
    dot_general x44, matrix products, apply_left(): return jnp.dot(square, right_side, precision=HIGHEST_PRECISION)  8.19 us
    dot_general x12, matrix products, inner_rows(): lax.dot_general(left, right, (((1,), (1,)), ((), ())), precision=HIGHEST_...  3.35 us
  transfers between devices with their start and end apart: 15, of which 9 were waited for; matrix products, arithmetic and copies ran while one was open for 6% of the time, Pallas kernels for 19%

profile of v4, /device:TPU:0, one launch (start us, length us, event | category | flops | bytes accessed | tf_op | source)
XLA Modules:
  0.0 90.1 jit_solution(469378442869485008)
XLA Ops:
  0.0 10.3 %all_gather.3 = f32[4,64,768]{2,1,0:T(8,128)S(1)} all-gather(f32[1,64,768]{2,1,0:T(8,128)} %param.1), channel_id=1, replica_groups=mesh['rows'=8,'cols'=4] {'cols'}, dimensions={0}, use_global_device_ids=true | all-gather | bytes 983040 | tf_op jit(solution)/shard_map/all_gather | solution.py:75
  10.6 1.6 %collective-permute-start.3 = (f32[1,64,64]{2,1,0:T(8,128)S(1)}, f32[1,64,64]{2,1,0:T(8,128)S(1)}, u32[]{:S(2)}, u32[]{:S(2)}) collective-permute-start(f32[1,64,64]{2,1,0:T(8,128)S(1)} %convolution_bitcast_fusion.10), channel_id=1, source_target_pairs={{0,4},{4,0},{8,12},{12,8},{16,20},{20,16},{24,28},{28,24},{1,5},{5... | collective-permute-start | bytes 49160 | tf_op jit(solution)/shard_map/ppermute | solution.py:23
  12.8 0.6 collective-permute-start.6
  14.2 1.5 %collective-permute-start = (f32[3,64,64]{1,2,0:T(8,128)S(1)}, f32[3,64,64]{1,2,0:T(8,128)S(1)}, u32[]{:S(2)}, u32[]{:S(2)}) collective-permute-start(f32[3,64,64]{1,2,0:T(8,128)S(1)} %pad_maximum_fusion), channel_id=1, source_target_pairs={{0,4},{4,0},{8,12},{12,8},{16,20},{20,16},{24,28},{28,24},{1,5},{5... | collective-permute-start | bytes 147464 | tf_op jit(solution)/shard_map/ppermute | solution.py:23
  15.8 1.6 %collective-permute-start.4 = (f32[1,64,64]{2,1,0:T(8,128)S(1)}, f32[1,64,64]{2,1,0:T(8,128)S(1)}, u32[]{:S(2)}, u32[]{:S(2)}) collective-permute-start(f32[1,64,64]{2,1,0:T(8,128)S(1)} %add.77), channel_id=1, source_target_pairs={{0,8},{4,12},{8,0},{12,4},{16,24},{20,28},{24,16},{28,20},{1,9},{5... | collective-permute-start | bytes 49160 | tf_op jit(solution)/shard_map/ppermute | solution.py:23
  17.4 2.3 %collective-permute-done.4 = f32[1,64,64]{2,1,0:T(8,128)S(1)} collective-permute-done((f32[1,64,64]{2,1,0:T(8,128)S(1)}, f32[1,64,64]{2,1,0:T(8,128)S(1)}, u32[]{:S(2)}, u32[]{:S(2)}) %collective-permute-start.4) | collective-permute-done | bytes 16416 | tf_op jit(solution)/shard_map/ppermute | solution.py:23
  19.8 2.6 %collective-permute-start.5 = (f32[1,64,64]{2,1,0:T(8,128)S(1)}, f32[1,64,64]{2,1,0:T(8,128)S(1)}, u32[]{:S(2)}, u32[]{:S(2)}) collective-permute-start(f32[1,64,64]{2,1,0:T(8,128)S(1)} %add.78), channel_id=1, source_target_pairs={{0,16},{4,20},{8,24},{12,28},{16,0},{20,4},{24,8},{28,12},{1,17},{... | collective-permute-start | bytes 49160 | tf_op jit(solution)/shard_map/ppermute | solution.py:23
  22.4 1.6 %collective-permute-start.7 = (f32[2,64,64]{2,1,0:T(8,128)S(1)}, f32[2,64,64]{2,1,0:T(8,128)S(1)}, u32[]{:S(2)}, u32[]{:S(2)}) collective-permute-start(f32[2,64,64]{2,1,0:T(8,128)S(1)} %fusion.82), channel_id=1, source_target_pairs={{0,8},{4,12},{8,0},{12,4},{16,24},{20,28},{24,16},{28,20},{1,9},{5... | collective-permute-start | bytes 98312 | tf_op jit(solution)/shard_map/ppermute | solution.py:23
  24.0 0.6 collective-permute-done.5
  24.6 0.7 pad_maximum_fusion.2.aug_ref
  25.3 8.4 %shard_map.17 = f32[64,128]{1,0:T(8,128)} custom-call(f32[64,128]{1,0:T(8,128)} %pad_maximum_fusion.2.aug_ref), custom_call_target="tpu_custom_call" | custom-call | tf_op jit(solution)/shard_map/pallas_call | solution.py:58
  33.7 1.6 %collective-permute-start.1 = (f32[3,64,64]{1,2,0:T(8,128)S(1)}, f32[3,64,64]{1,2,0:T(8,128)S(1)}, u32[]{:S(2)}, u32[]{:S(2)}) collective-permute-start(f32[3,64,64]{1,2,0:T(8,128)S(1)} %fusion.83), channel_id=1, source_target_pairs={{0,8},{4,12},{8,0},{12,4},{16,24},{20,28},{24,16},{28,20},{1,9},{5... | collective-permute-start | bytes 147464 | tf_op jit(solution)/shard_map/ppermute | solution.py:23
  35.4 2.9 %collective-permute-start.8 = (f32[2,64,64]{2,1,0:T(8,128)S(1)}, f32[2,64,64]{2,1,0:T(8,128)S(1)}, u32[]{:S(2)}, u32[]{:S(2)}) collective-permute-start(f32[2,64,64]{2,1,0:T(8,128)S(1)} %fusion.160), channel_id=1, source_target_pairs={{0,16},{4,20},{8,24},{12,28},{16,0},{20,4},{24,8},{28,12},{1,17},{... | collective-permute-start | bytes 98312 | tf_op jit(solution)/shard_map/ppermute | solution.py:23
  38.3 0.4 convolution_subtract_fusion.4
  38.6 3.9 %collective-permute-done.8 = f32[2,64,64]{2,1,0:T(8,128)S(1)} collective-permute-done((f32[2,64,64]{2,1,0:T(8,128)S(1)}, f32[2,64,64]{2,1,0:T(8,128)S(1)}, u32[]{:S(2)}, u32[]{:S(2)}) %collective-permute-start.8) | collective-permute-done | bytes 32800 | tf_op jit(solution)/shard_map/ppermute | solution.py:23
  42.6 1.4 %collective-permute-start.2 = (f32[3,64,64]{1,2,0:T(8,128)S(1)}, f32[3,64,64]{1,2,0:T(8,128)S(1)}, u32[]{:S(2)}, u32[]{:S(2)}) collective-permute-start(f32[3,64,64]{1,2,0:T(8,128)S(1)} %fusion.161), channel_id=1, source_target_pairs={{0,16},{4,20},{8,24},{12,28},{16,0},{20,4},{24,8},{28,12},{1,17},{... | collective-permute-start | bytes 147464 | tf_op jit(solution)/shard_map/ppermute | solution.py:23
  44.3 3.9 %collective-permute-done.2 = f32[3,64,64]{1,2,0:T(8,128)S(1)} collective-permute-done((f32[3,64,64]{1,2,0:T(8,128)S(1)}, f32[3,64,64]{1,2,0:T(8,128)S(1)}, u32[]{:S(2)}, u32[]{:S(2)}) %collective-permute-start.2) | collective-permute-done | bytes 49184 | tf_op jit(solution)/shard_map/ppermute | solution.py:23
  51.9 0.4 convolution_subtract_fusion.3
  52.3 0.4 fusion.1
  53.0 0.6 collective-permute-start.12
  54.8 2.2 %collective-permute-done.12 = f32[1,64,64]{2,1,0:T(8,128)S(1)} collective-permute-done((f32[1,64,64]{2,1,0:T(8,128)S(1)}, f32[1,64,64]{2,1,0:T(8,128)S(1)}, u32[]{:S(2)}, u32[]{:S(2)}) %collective-permute-start.12) | collective-permute-done | bytes 16416 | tf_op jit(solution)/shard_map/ppermute | solution.py:23
  57.2 3.6 %collective-permute-done.13 = f32[1,64,64]{2,1,0:T(8,128)S(1)} collective-permute-done((f32[1,64,64]{2,1,0:T(8,128)S(1)}, f32[1,64,64]{2,1,0:T(8,128)S(1)}, u32[]{:S(2)}, u32[]{:S(2)}) %collective-permute-start.13) | collective-permute-done | bytes 16416 | tf_op jit(solution)/shard_map/ppermute | solution.py:23
  60.9 1.4 %collective-permute-start.14 = (f32[1,64,64]{2,1,0:T(8,128)S(1)}, f32[1,64,64]{2,1,0:T(8,128)S(1)}, u32[]{:S(2)}, u32[]{:S(2)}) collective-permute-start(f32[1,64,64]{2,1,0:T(8,128)S(1)} %add.87), channel_id=1, source_target_pairs={{0,16},{4,20},{8,24},{12,28},{16,0},{20,4},{24,8},{28,12},{1,17},{... | collective-permute-start | bytes 49160 | tf_op jit(solution)/shard_map/ppermute | solution.py:23
  62.6 0.6 collective-permute-start.9
  63.2 2.5 %collective-permute-done.14 = f32[1,64,64]{2,1,0:T(8,128)S(1)} collective-permute-done((f32[1,64,64]{2,1,0:T(8,128)S(1)}, f32[1,64,64]{2,1,0:T(8,128)S(1)}, u32[]{:S(2)}, u32[]{:S(2)}) %collective-permute-start.14) | collective-permute-done | bytes 16416 | tf_op jit(solution)/shard_map/ppermute | solution.py:23
  65.7 2.3 %collective-permute-done.9 = f32[5,64,64]{2,1,0:T(8,128)S(1)} collective-permute-done((f32[5,64,64]{2,1,0:T(8,128)S(1)}, f32[5,64,64]{2,1,0:T(8,128)S(1)}, u32[]{:S(2)}, u32[]{:S(2)}) %collective-permute-start.9) | collective-permute-done | bytes 81952 | tf_op jit(solution)/shard_map/ppermute | solution.py:23
  68.1 0.7 pad_maximum_fusion.3.aug_ref
  68.8 8.4 %shard_map.18 = f32[64,128]{1,0:T(8,128)} custom-call(f32[64,128]{1,0:T(8,128)} %pad_maximum_fusion.3.aug_ref), custom_call_target="tpu_custom_call" | custom-call | tf_op jit(solution)/shard_map/pallas_call | solution.py:58
  77.2 1.6 %collective-permute-start.11 = (f32[5,64,64]{2,1,0:T(8,128)S(1)}, f32[5,64,64]{2,1,0:T(8,128)S(1)}, u32[]{:S(2)}, u32[]{:S(2)}) collective-permute-start(f32[5,64,64]{2,1,0:T(8,128)S(1)} %add.84), channel_id=1, source_target_pairs={{0,16},{4,20},{8,24},{12,28},{16,0},{20,4},{24,8},{28,12},{1,17},{... | collective-permute-start | bytes 245768 | tf_op jit(solution)/shard_map/ppermute | solution.py:23
  78.8 0.4 convolution_subtract_fusion.1
  79.2 6.0 %collective-permute-done.11 = f32[5,64,64]{2,1,0:T(8,128)S(1)} collective-permute-done((f32[5,64,64]{2,1,0:T(8,128)S(1)}, f32[5,64,64]{2,1,0:T(8,128)S(1)}, u32[]{:S(2)}, u32[]{:S(2)}) %collective-permute-start.11) | collective-permute-done | bytes 81952 | tf_op jit(solution)/shard_map/ppermute | solution.py:23
  89.1 1.1 %fusion = f32[1,64,768]{2,1,0:T(8,128)} fusion(f32[64,768]{1,0:T(8,128)S(1)} %convolution_subtract_fusion.3, f32[64,64]{1,0:T(8,128)S(1)} %fusion.26, f32[64,768]{1,0:T(8,128)S(1)} %convolution_subtract_fusion.1), kind=kOutput, calls=%fused_computation.1 | convolution fusion | flops 37797888 | bytes 606208 | tf_op jit(solution)/shard_map/dot_general | solution.py:113
  (90 shorter events, 11.4 us)
Async XLA Ops:
  10.3 1.9 %copy-start = (f32[1,64,768]{2,1,0:T(8,128)S(1)}, f32[1,64,768]{2,1,0:T(8,128)}, u32[]{:S(2)}) copy-start(f32[1,64,768]{2,1,0:T(8,128)} %param.1) | copy-start | bytes 589828
  10.6 5.2 %collective-permute-start.3 = (f32[1,64,64]{2,1,0:T(8,128)S(1)}, f32[1,64,64]{2,1,0:T(8,128)S(1)}, u32[]{:S(2)}, u32[]{:S(2)}) collective-permute-start(f32[1,64,64]{2,1,0:T(8,128)S(1)} %convolution_bitcast_fusion.10), channel_id=1, source_target_pairs={{0,4},{4,0},{8,12},{12,8},{16,20},{20,16},{24,28},{28,24},{1,5},{5... | collective-permute-start | bytes 49160 | tf_op jit(solution)/shard_map/ppermute | solution.py:23
  12.8 9.6 %collective-permute-start.6 = (f32[2,64,64]{2,1,0:T(8,128)S(1)}, f32[2,64,64]{2,1,0:T(8,128)S(1)}, u32[]{:S(2)}, u32[]{:S(2)}) collective-permute-start(f32[2,64,64]{2,1,0:T(8,128)S(1)} %pad_maximum_fusion.1), channel_id=1, source_target_pairs={{0,4},{4,0},{8,12},{12,8},{16,20},{20,16},{24,28},{28,24},{1,5},{5... | collective-permute-start | bytes 98312 | tf_op jit(solution)/shard_map/ppermute | solution.py:23
  14.2 19.5 %collective-permute-start = (f32[3,64,64]{1,2,0:T(8,128)S(1)}, f32[3,64,64]{1,2,0:T(8,128)S(1)}, u32[]{:S(2)}, u32[]{:S(2)}) collective-permute-start(f32[3,64,64]{1,2,0:T(8,128)S(1)} %pad_maximum_fusion), channel_id=1, source_target_pairs={{0,4},{4,0},{8,12},{12,8},{16,20},{20,16},{24,28},{28,24},{1,5},{5... | collective-permute-start | bytes 147464 | tf_op jit(solution)/shard_map/ppermute | solution.py:23
  15.8 4.0 %collective-permute-start.4 = (f32[1,64,64]{2,1,0:T(8,128)S(1)}, f32[1,64,64]{2,1,0:T(8,128)S(1)}, u32[]{:S(2)}, u32[]{:S(2)}) collective-permute-start(f32[1,64,64]{2,1,0:T(8,128)S(1)} %add.77), channel_id=1, source_target_pairs={{0,8},{4,12},{8,0},{12,4},{16,24},{20,28},{24,16},{28,20},{1,9},{5... | collective-permute-start | bytes 49160 | tf_op jit(solution)/shard_map/ppermute | solution.py:23
  19.8 4.8 %collective-permute-start.5 = (f32[1,64,64]{2,1,0:T(8,128)S(1)}, f32[1,64,64]{2,1,0:T(8,128)S(1)}, u32[]{:S(2)}, u32[]{:S(2)}) collective-permute-start(f32[1,64,64]{2,1,0:T(8,128)S(1)} %add.78), channel_id=1, source_target_pairs={{0,16},{4,20},{8,24},{12,28},{16,0},{20,4},{24,8},{28,12},{1,17},{... | collective-permute-start | bytes 49160 | tf_op jit(solution)/shard_map/ppermute | solution.py:23
  22.4 13.0 %collective-permute-start.7 = (f32[2,64,64]{2,1,0:T(8,128)S(1)}, f32[2,64,64]{2,1,0:T(8,128)S(1)}, u32[]{:S(2)}, u32[]{:S(2)}) collective-permute-start(f32[2,64,64]{2,1,0:T(8,128)S(1)} %fusion.82), channel_id=1, source_target_pairs={{0,8},{4,12},{8,0},{12,4},{16,24},{20,28},{24,16},{28,20},{1,9},{5... | collective-permute-start | bytes 98312 | tf_op jit(solution)/shard_map/ppermute | solution.py:23
  33.7 4.6 %copy-start.1 = (f32[64,128]{1,0:T(8,128)S(1)}, f32[64,128]{1,0:T(8,128)}, u32[]{:S(2)}) copy-start(f32[64,128]{1,0:T(8,128)} %shard_map.17) | copy-start | bytes 98308
  33.7 8.9 %collective-permute-start.1 = (f32[3,64,64]{1,2,0:T(8,128)S(1)}, f32[3,64,64]{1,2,0:T(8,128)S(1)}, u32[]{:S(2)}, u32[]{:S(2)}) collective-permute-start(f32[3,64,64]{1,2,0:T(8,128)S(1)} %fusion.83), channel_id=1, source_target_pairs={{0,8},{4,12},{8,0},{12,4},{16,24},{20,28},{24,16},{28,20},{1,9},{5... | collective-permute-start | bytes 147464 | tf_op jit(solution)/shard_map/ppermute | solution.py:23
  35.4 7.2 %collective-permute-start.8 = (f32[2,64,64]{2,1,0:T(8,128)S(1)}, f32[2,64,64]{2,1,0:T(8,128)S(1)}, u32[]{:S(2)}, u32[]{:S(2)}) collective-permute-start(f32[2,64,64]{2,1,0:T(8,128)S(1)} %fusion.160), channel_id=1, source_target_pairs={{0,16},{4,20},{8,24},{12,28},{16,0},{20,4},{24,8},{28,12},{1,17},{... | collective-permute-start | bytes 98312 | tf_op jit(solution)/shard_map/ppermute | solution.py:23
  42.6 5.6 %collective-permute-start.2 = (f32[3,64,64]{1,2,0:T(8,128)S(1)}, f32[3,64,64]{1,2,0:T(8,128)S(1)}, u32[]{:S(2)}, u32[]{:S(2)}) collective-permute-start(f32[3,64,64]{1,2,0:T(8,128)S(1)} %fusion.161), channel_id=1, source_target_pairs={{0,16},{4,20},{8,24},{12,28},{16,0},{20,4},{24,8},{28,12},{1,17},{... | collective-permute-start | bytes 147464 | tf_op jit(solution)/shard_map/ppermute | solution.py:23
  53.0 4.0 %collective-permute-start.12 = (f32[1,64,64]{2,1,0:T(8,128)S(1)}, f32[1,64,64]{2,1,0:T(8,128)S(1)}, u32[]{:S(2)}, u32[]{:S(2)}) collective-permute-start(f32[1,64,64]{2,1,0:T(8,128)S(1)} %convolution_bitcast_fusion.6), channel_id=1, source_target_pairs={{0,4},{4,0},{8,12},{12,8},{16,20},{20,16},{24,28},{28,24},{1,5},{5... | collective-permute-start | bytes 49160 | tf_op jit(solution)/shard_map/ppermute | solution.py:23
  57.0 3.9 %collective-permute-start.13 = (f32[1,64,64]{2,1,0:T(8,128)S(1)}, f32[1,64,64]{2,1,0:T(8,128)S(1)}, u32[]{:S(2)}, u32[]{:S(2)}) collective-permute-start(f32[1,64,64]{2,1,0:T(8,128)S(1)} %add.86), channel_id=1, source_target_pairs={{0,8},{4,12},{8,0},{12,4},{16,24},{20,28},{24,16},{28,20},{1,9},{5... | collective-permute-start | bytes 49160 | tf_op jit(solution)/shard_map/ppermute | solution.py:23
  60.9 4.8 %collective-permute-start.14 = (f32[1,64,64]{2,1,0:T(8,128)S(1)}, f32[1,64,64]{2,1,0:T(8,128)S(1)}, u32[]{:S(2)}, u32[]{:S(2)}) collective-permute-start(f32[1,64,64]{2,1,0:T(8,128)S(1)} %add.87), channel_id=1, source_target_pairs={{0,16},{4,20},{8,24},{12,28},{16,0},{20,4},{24,8},{28,12},{1,17},{... | collective-permute-start | bytes 49160 | tf_op jit(solution)/shard_map/ppermute | solution.py:23
  62.6 5.4 %collective-permute-start.9 = (f32[5,64,64]{2,1,0:T(8,128)S(1)}, f32[5,64,64]{2,1,0:T(8,128)S(1)}, u32[]{:S(2)}, u32[]{:S(2)}) collective-permute-start(f32[5,64,64]{2,1,0:T(8,128)S(1)} %fusion.2), channel_id=1, source_target_pairs={{0,4},{4,0},{8,12},{12,8},{16,20},{20,16},{24,28},{28,24},{1,5},{5... | collective-permute-start | bytes 245768 | tf_op jit(solution)/shard_map/ppermute | solution.py:23
  68.0 9.2 %collective-permute-start.10 = (f32[5,64,64]{2,1,0:T(8,128)S(1)}, f32[5,64,64]{2,1,0:T(8,128)S(1)}, u32[]{:S(2)}, u32[]{:S(2)}) collective-permute-start(f32[5,64,64]{2,1,0:T(8,128)S(1)} %add.83), channel_id=1, source_target_pairs={{0,8},{4,12},{8,0},{12,4},{16,24},{20,28},{24,16},{28,20},{1,9},{5... | collective-permute-start | bytes 245768 | tf_op jit(solution)/shard_map/ppermute | solution.py:23
  77.1 1.6 %copy-start.2 = (f32[64,128]{1,0:T(8,128)S(1)}, f32[64,128]{1,0:T(8,128)}, u32[]{:S(2)}) copy-start(f32[64,128]{1,0:T(8,128)} %shard_map.18) | copy-start | bytes 98308
  77.2 8.0 %collective-permute-start.11 = (f32[5,64,64]{2,1,0:T(8,128)S(1)}, f32[5,64,64]{2,1,0:T(8,128)S(1)}, u32[]{:S(2)}, u32[]{:S(2)}) collective-permute-start(f32[5,64,64]{2,1,0:T(8,128)S(1)} %add.84), channel_id=1, source_target_pairs={{0,16},{4,20},{8,24},{12,28},{16,0},{20,4},{24,8},{28,12},{1,17},{... | collective-permute-start | bytes 245768 | tf_op jit(solution)/shard_map/ppermute | solution.py:23

commit v5 on v3

--- a/solution.py
+++ b/solution.py
@@ -23,6 +23,21 @@
         x = x + lax.ppermute(x, axis, [(i, i ^ step) for i in range(size)])
         step *= 2
     return x
+
+
+def paired_sums(head, tail, axis, size):
+    if size & (size - 1) or size < 2:
+        return lax.psum(head, axis), lax.psum(tail, axis)
+    step = 1
+    while step < size:
+        head = head + lax.ppermute(head, axis, [(i, i ^ step) for i in range(size)])
+        if 2 * step < size:
+            tail = tail + lax.ppermute(tail, axis, [(i, i ^ step) for i in range(size)])
+            head, tail = lax.optimization_barrier((head, tail))
+        step *= 2
+    step //= 2
+    tail = tail + lax.ppermute(tail, axis, [(i, i ^ step) for i in range(size)])
+    return head, tail
 
 
 def invert_near_identity(square):
@@ -76,16 +91,17 @@
         panel_0 = gathered[0]
         second = gathered[1]
 
-        head = butterfly_sum(jnp.stack([
-            inner_rows(panel_0, panel_0),
-            inner_rows(panel_0, units[0]),
-        ]), "rows", rows_size)
-        tail = butterfly_sum(jnp.stack([
-            inner_rows(panel_0, current),
-            inner_rows(units[0], current),
-            inner_rows(panel_0, second),
-            inner_rows(units[0], second),
-        ]), "rows", rows_size)
+        head, tail = paired_sums(
+            jnp.stack([inner_rows(panel_0, panel_0), inner_rows(panel_0, units[0])]),
+            jnp.stack([
+                inner_rows(panel_0, current),
+                inner_rows(units[0], current),
+                inner_rows(panel_0, second),
+                inner_rows(units[0], second),
+            ]),
+            "rows",
+            rows_size,
+        )
         gram, top_rows = head[0], head[1]
         basis_cur, unit_cur, basis_sec, unit_sec = (tail[i] for i in range(4))
         lower_inv = lower_inverse(gram)
@@ -98,14 +114,12 @@
         second = second - jnp.dot(mixed_sec.T, reflect, precision=HIGHEST_PRECISION)
 
         panel_1 = jnp.where((global_rows >= width)[None, :], second, jnp.zeros_like(second))
-        head = butterfly_sum(jnp.stack([
-            inner_rows(panel_1, panel_1),
-            inner_rows(panel_1, units[1]),
-        ]), "rows", rows_size)
-        tail = butterfly_sum(jnp.stack([
-            inner_rows(panel_1, current),
-            inner_rows(units[1], current),
-        ]), "rows", rows_size)
+        head, tail = paired_sums(
+            jnp.stack([inner_rows(panel_1, panel_1), inner_rows(panel_1, units[1])]),
+            jnp.stack([inner_rows(panel_1, current), inner_rows(units[1], current)]),
+            "rows",
+            rows_size,
+        )
         gram, top_rows = head[0], head[1]
         basis_cur, unit_cur = tail[0], tail[1]
         lower_inv = lower_inverse(gram)

time: 78.5 us -> 82.5 us (1.051)
  waiting for transfers between devices: 15.4 us -> 24.3 us
  starting transfers between devices: 19.4 us -> 14.5 us
    ppermute x12, waiting for transfers between devices: 15.4 us -> 24.3 us  [the longest x6 15.9 us: paired_sums(): head = head + lax.ppermute(head, axis, [(i, i ^ step) for i in range(size)])]
    ppermute x12, starting transfers between devices: 19.4 us -> 14.5 us  [the longest x6 9.6 us: paired_sums(): head = head + lax.ppermute(head, axis, [(i, i ^ step) for i in range(size)])]
  transfers between devices with their start and end apart: 12 -> 12, of which waited for: 8 -> 10; matrix products, arithmetic and copies ran while one was open for 11% -> 13% of each run, Pallas kernels for 21% -> 20%
where the time goes in v5:
time: 82.5 us; the launch traced here: 82.1 us
  waiting for transfers between devices  24.3 us (29%)
  Pallas kernels  16.7 us (20%)
  starting transfers between devices  14.5 us (18%)
  matrix products  14.1 us (17%)
  blocking collectives  10.3 us (12%)
  other arithmetic  1.59 us (2%)
    pallas_call x2, Pallas kernels, lower_inverse(): pl.pallas_call(_eliminate_kernel, out_shape=jax.ShapeDtypeStruct(aug.shap...  16.7 us
    ppermute x6, waiting for transfers between devices, paired_sums(): head = head + lax.ppermute(head, axis, [(i, i ^ step) for i in range(size)])  15.9 us
    all_gather x1, blocking collectives, local(): gathered = lax.all_gather(current, 'cols')  10.3 us
    ppermute x6, starting transfers between devices, paired_sums(): head = head + lax.ppermute(head, axis, [(i, i ^ step) for i in range(size)])  9.6 us
    dot_general x42, matrix products, apply_left(): return jnp.dot(square, right_side, precision=HIGHEST_PRECISION)  9.48 us
    ppermute x6, waiting for transfers between devices, paired_sums(): tail = tail + lax.ppermute(tail, axis, [(i, i ^ step) for i in range(size)])  8.43 us
    ppermute x6, starting transfers between devices, paired_sums(): tail = tail + lax.ppermute(tail, axis, [(i, i ^ step) for i in range(size)])  4.91 us
    dot_general x10, matrix products, inner_rows(): lax.dot_general(left, right, (((1,), (1,)), ((), ())), precision=HIGHEST_...  2.8 us
  transfers between devices with their start and end apart: 12, of which 10 were waited for; matrix products, arithmetic and copies ran while one was open for 13% of the time, Pallas kernels for 20%

profile of v5, /device:TPU:0, one launch (start us, length us, event | category | flops | bytes accessed | tf_op | source)
XLA Modules:
  0.0 82.1 jit_solution(8797746026066299542)
XLA Ops:
  0.0 10.3 %all_gather.3 = f32[4,64,768]{2,1,0:T(8,128)S(1)} all-gather(f32[1,64,768]{2,1,0:T(8,128)} %param.1), channel_id=1, replica_groups=mesh['rows'=8,'cols'=4] {'cols'}, dimensions={0}, use_global_device_ids=true | all-gather | bytes 983040 | tf_op jit(solution)/shard_map/all_gather | solution.py:90
  10.9 1.6 %collective-permute-start = (f32[2,64,64]{2,1,0:T(8,128)S(1)}, f32[2,64,64]{2,1,0:T(8,128)S(1)}, u32[]{:S(2)}, u32[]{:S(2)}) collective-permute-start(f32[2,64,64]{2,1,0:T(8,128)S(1)} %pad_maximum_fusion.1), channel_id=1, source_target_pairs={{0,4},{4,0},{8,12},{12,8},{16,20},{20,16},{24,28},{28,24},{1,5},{5... | collective-permute-start | bytes 98312 | tf_op jit(solution)/shard_map/ppermute | solution.py:33
  13.6 0.6 collective-permute-start.1
  14.3 1.0 %collective-permute-done = f32[2,64,64]{2,1,0:T(8,128)S(1)} collective-permute-done((f32[2,64,64]{2,1,0:T(8,128)S(1)}, f32[2,64,64]{2,1,0:T(8,128)S(1)}, u32[]{:S(2)}, u32[]{:S(2)}) %collective-permute-start) | collective-permute-done | bytes 32800 | tf_op jit(solution)/shard_map/ppermute | solution.py:33
  15.3 3.8 %collective-permute-done.1 = f32[4,64,64]{2,1,0:T(8,128)S(1)} collective-permute-done((f32[4,64,64]{2,1,0:T(8,128)S(1)}, f32[4,64,64]{2,1,0:T(8,128)S(1)}, u32[]{:S(2)}, u32[]{:S(2)}) %collective-permute-start.1) | collective-permute-done | bytes 65568 | tf_op jit(solution)/shard_map/ppermute | solution.py:35
  19.2 1.6 %collective-permute-start.2 = (f32[2,64,64]{2,1,0:T(8,128)S(1)}, f32[2,64,64]{2,1,0:T(8,128)S(1)}, u32[]{:S(2)}, u32[]{:S(2)}) collective-permute-start(f32[2,64,64]{2,1,0:T(8,128)S(1)} %fusion.69), channel_id=1, source_target_pairs={{0,8},{4,12},{8,0},{12,4},{16,24},{20,28},{24,16},{28,20},{1,9},{5... | collective-permute-start | bytes 98312 | tf_op jit(solution)/shard_map/ppermute | solution.py:33
  20.8 0.5 collective-permute-start.3
  21.3 2.9 %collective-permute-done.2 = f32[2,64,64]{2,1,0:T(8,128)S(1)} collective-permute-done((f32[2,64,64]{2,1,0:T(8,128)S(1)}, f32[2,64,64]{2,1,0:T(8,128)S(1)}, u32[]{:S(2)}, u32[]{:S(2)}) %collective-permute-start.2) | collective-permute-done | bytes 32800 | tf_op jit(solution)/shard_map/ppermute | solution.py:33
  24.1 1.7 %collective-permute-done.3 = f32[4,64,64]{2,1,0:T(8,128)S(1)} collective-permute-done((f32[4,64,64]{2,1,0:T(8,128)S(1)}, f32[4,64,64]{2,1,0:T(8,128)S(1)}, u32[]{:S(2)}, u32[]{:S(2)}) %collective-permute-start.3) | collective-permute-done | bytes 65568 | tf_op jit(solution)/shard_map/ppermute | solution.py:35
  25.9 2.7 %collective-permute-start.4 = (f32[2,64,64]{2,1,0:T(8,128)S(1)}, f32[2,64,64]{2,1,0:T(8,128)S(1)}, u32[]{:S(2)}, u32[]{:S(2)}) collective-permute-start(f32[2,64,64]{2,1,0:T(8,128)S(1)} %add.61), channel_id=1, source_target_pairs={{0,16},{4,20},{8,24},{12,28},{16,0},{20,4},{24,8},{28,12},{1,17},{... | collective-permute-start | bytes 98312 | tf_op jit(solution)/shard_map/ppermute | solution.py:33
  28.9 6.4 %collective-permute-done.4 = f32[2,64,64]{2,1,0:T(8,128)S(1)} collective-permute-done((f32[2,64,64]{2,1,0:T(8,128)S(1)}, f32[2,64,64]{2,1,0:T(8,128)S(1)}, u32[]{:S(2)}, u32[]{:S(2)}) %collective-permute-start.4) | collective-permute-done | bytes 32800 | tf_op jit(solution)/shard_map/ppermute | solution.py:33
  35.3 0.7 pad_maximum_fusion.4.aug_ref
  36.0 8.4 %shard_map.17 = f32[64,128]{1,0:T(8,128)} custom-call(f32[64,128]{1,0:T(8,128)} %pad_maximum_fusion.4.aug_ref), custom_call_target="tpu_custom_call" | custom-call | tf_op jit(solution)/shard_map/pallas_call | solution.py:73
  44.3 1.1 %fusion.24 = f32[64,64]{1,0:T(8,128)S(1)} fusion(f32[2,64,64]{2,1,0:T(8,128)S(1)} %add.63, f32[64,128]{1,0:T(8,128)} %shard_map.17), kind=kOutput, calls=%fused_computation.72 | convolution fusion | flops 3145728 | bytes 81920 | tf_op jit(solution)/shard_map/dot_general | solution.py:15
  45.4 0.4 convolution_subtract_fusion.4
  49.5 0.4 convolution_subtract_fusion.3
  49.9 0.4 fusion.1
  51.4 1.0 %collective-permute-start.7 = (f32[2,64,64]{2,1,0:T(8,128)S(1)}, f32[2,64,64]{2,1,0:T(8,128)S(1)}, u32[]{:S(2)}, u32[]{:S(2)}) collective-permute-start(f32[2,64,64]{2,1,0:T(8,128)S(1)} %pad_maximum_fusion.3), channel_id=1, source_target_pairs={{0,4},{4,0},{8,12},{12,8},{16,20},{20,16},{24,28},{28,24},{1,5},{5... | collective-permute-start | bytes 98312 | tf_op jit(solution)/shard_map/ppermute | solution.py:35
  52.4 1.1 %collective-permute-start.6 = (f32[2,64,64]{2,1,0:T(8,128)S(1)}, f32[2,64,64]{2,1,0:T(8,128)S(1)}, u32[]{:S(2)}, u32[]{:S(2)}) collective-permute-start(f32[2,64,64]{2,1,0:T(8,128)S(1)} %pad_maximum_fusion.2), channel_id=1, source_target_pairs={{0,4},{4,0},{8,12},{12,8},{16,20},{20,16},{24,28},{28,24},{1,5},{5... | collective-permute-start | bytes 98312 | tf_op jit(solution)/shard_map/ppermute | solution.py:33
  53.6 2.2 %collective-permute-done.7 = f32[2,64,64]{2,1,0:T(8,128)S(1)} collective-permute-done((f32[2,64,64]{2,1,0:T(8,128)S(1)}, f32[2,64,64]{2,1,0:T(8,128)S(1)}, u32[]{:S(2)}, u32[]{:S(2)}) %collective-permute-start.7) | collective-permute-done | bytes 32800 | tf_op jit(solution)/shard_map/ppermute | solution.py:35
  55.8 1.0 %collective-permute-done.6 = f32[2,64,64]{2,1,0:T(8,128)S(1)} collective-permute-done((f32[2,64,64]{2,1,0:T(8,128)S(1)}, f32[2,64,64]{2,1,0:T(8,128)S(1)}, u32[]{:S(2)}, u32[]{:S(2)}) %collective-permute-start.6) | collective-permute-done | bytes 32800 | tf_op jit(solution)/shard_map/ppermute | solution.py:33
  56.9 2.0 %collective-permute-start.9 = (f32[2,64,64]{2,1,0:T(8,128)S(1)}, f32[2,64,64]{2,1,0:T(8,128)S(1)}, u32[]{:S(2)}, u32[]{:S(2)}) collective-permute-start(f32[2,64,64]{2,1,0:T(8,128)S(1)} %fusion.67), channel_id=1, source_target_pairs={{0,8},{4,12},{8,0},{12,4},{16,24},{20,28},{24,16},{28,20},{1,9},{5... | collective-permute-start | bytes 98312 | tf_op jit(solution)/shard_map/ppermute | solution.py:35
  58.9 2.4 %collective-permute-done.8 = f32[2,64,64]{2,1,0:T(8,128)S(1)} collective-permute-done((f32[2,64,64]{2,1,0:T(8,128)S(1)}, f32[2,64,64]{2,1,0:T(8,128)S(1)}, u32[]{:S(2)}, u32[]{:S(2)}) %collective-permute-start.8) | collective-permute-done | bytes 32800 | tf_op jit(solution)/shard_map/ppermute | solution.py:33
  61.3 0.7 collective-permute-done.9
  62.0 2.5 %collective-permute-start.10 = (f32[2,64,64]{2,1,0:T(8,128)S(1)}, f32[2,64,64]{2,1,0:T(8,128)S(1)}, u32[]{:S(2)}, u32[]{:S(2)}) collective-permute-start(f32[2,64,64]{2,1,0:T(8,128)S(1)} %add.67), channel_id=1, source_target_pairs={{0,16},{4,20},{8,24},{12,28},{16,0},{20,4},{24,8},{28,12},{1,17},{... | collective-permute-start | bytes 98312 | tf_op jit(solution)/shard_map/ppermute | solution.py:33
  64.5 0.5 collective-permute-start.11
  65.0 2.2 %collective-permute-done.10 = f32[2,64,64]{2,1,0:T(8,128)S(1)} collective-permute-done((f32[2,64,64]{2,1,0:T(8,128)S(1)}, f32[2,64,64]{2,1,0:T(8,128)S(1)}, u32[]{:S(2)}, u32[]{:S(2)}) %collective-permute-start.10) | collective-permute-done | bytes 32800 | tf_op jit(solution)/shard_map/ppermute | solution.py:33
  67.2 0.7 pad_maximum_fusion.5.aug_ref
  67.9 8.4 %shard_map.18 = f32[64,128]{1,0:T(8,128)} custom-call(f32[64,128]{1,0:T(8,128)} %pad_maximum_fusion.5.aug_ref), custom_call_target="tpu_custom_call" | custom-call | tf_op jit(solution)/shard_map/pallas_call | solution.py:73
  76.3 1.1 %fusion.15 = f32[64,64]{1,0:T(8,128)S(1)} fusion(f32[2,64,64]{2,1,0:T(8,128)S(1)} %add.69, f32[64,128]{1,0:T(8,128)} %shard_map.18), kind=kOutput, calls=%fused_computation.59 | convolution fusion | flops 3145728 | bytes 81920 | tf_op jit(solution)/shard_map/dot_general | solution.py:15
  77.4 0.4 convolution_subtract_fusion.1
  81.0 1.1 %fusion = f32[1,64,768]{2,1,0:T(8,128)} fusion(f32[64,768]{1,0:T(8,128)S(1)} %convolution_subtract_fusion.3, f32[64,64]{1,0:T(8,128)S(1)} %fusion.13, f32[64,768]{1,0:T(8,128)S(1)} %convolution_subtract_fusion.1), kind=kOutput, calls=%fused_computation.1 | convolution fusion | flops 37797888 | bytes 606208 | tf_op jit(solution)/shard_map/dot_general | solution.py:130
  (79 shorter events, 10.0 us)
Async XLA Ops:
  10.6 1.8 %copy-start = (f32[1,64,768]{2,1,0:T(8,128)S(1)}, f32[1,64,768]{2,1,0:T(8,128)}, u32[]{:S(2)}) copy-start(f32[1,64,768]{2,1,0:T(8,128)} %param.1) | copy-start | bytes 589828
  10.9 4.4 %collective-permute-start = (f32[2,64,64]{2,1,0:T(8,128)S(1)}, f32[2,64,64]{2,1,0:T(8,128)S(1)}, u32[]{:S(2)}, u32[]{:S(2)}) collective-permute-start(f32[2,64,64]{2,1,0:T(8,128)S(1)} %pad_maximum_fusion.1), channel_id=1, source_target_pairs={{0,4},{4,0},{8,12},{12,8},{16,20},{20,16},{24,28},{28,24},{1,5},{5... | collective-permute-start | bytes 98312 | tf_op jit(solution)/shard_map/ppermute | solution.py:33
  13.6 5.5 %collective-permute-start.1 = (f32[4,64,64]{2,1,0:T(8,128)S(1)}, f32[4,64,64]{2,1,0:T(8,128)S(1)}, u32[]{:S(2)}, u32[]{:S(2)}) collective-permute-start(f32[4,64,64]{2,1,0:T(8,128)S(1)} %pad_maximum_fusion), channel_id=1, source_target_pairs={{0,4},{4,0},{8,12},{12,8},{16,20},{20,16},{24,28},{28,24},{1,5},{5... | collective-permute-start | bytes 196616 | tf_op jit(solution)/shard_map/ppermute | solution.py:35
  19.2 5.0 %collective-permute-start.2 = (f32[2,64,64]{2,1,0:T(8,128)S(1)}, f32[2,64,64]{2,1,0:T(8,128)S(1)}, u32[]{:S(2)}, u32[]{:S(2)}) collective-permute-start(f32[2,64,64]{2,1,0:T(8,128)S(1)} %fusion.69), channel_id=1, source_target_pairs={{0,8},{4,12},{8,0},{12,4},{16,24},{20,28},{24,16},{28,20},{1,9},{5... | collective-permute-start | bytes 98312 | tf_op jit(solution)/shard_map/ppermute | solution.py:33
  20.8 5.1 %collective-permute-start.3 = (f32[4,64,64]{2,1,0:T(8,128)S(1)}, f32[4,64,64]{2,1,0:T(8,128)S(1)}, u32[]{:S(2)}, u32[]{:S(2)}) collective-permute-start(f32[4,64,64]{2,1,0:T(8,128)S(1)} %fusion.70), channel_id=1, source_target_pairs={{0,8},{4,12},{8,0},{12,4},{16,24},{20,28},{24,16},{28,20},{1,9},{5... | collective-permute-start | bytes 196616 | tf_op jit(solution)/shard_map/ppermute | solution.py:35
  25.9 9.4 %collective-permute-start.4 = (f32[2,64,64]{2,1,0:T(8,128)S(1)}, f32[2,64,64]{2,1,0:T(8,128)S(1)}, u32[]{:S(2)}, u32[]{:S(2)}) collective-permute-start(f32[2,64,64]{2,1,0:T(8,128)S(1)} %add.61), channel_id=1, source_target_pairs={{0,16},{4,20},{8,24},{12,28},{16,0},{20,4},{24,8},{28,12},{1,17},{... | collective-permute-start | bytes 98312 | tf_op jit(solution)/shard_map/ppermute | solution.py:33
  28.5 20.1 %collective-permute-start.5 = (f32[4,64,64]{2,1,0:T(8,128)S(1)}, f32[4,64,64]{2,1,0:T(8,128)S(1)}, u32[]{:S(2)}, u32[]{:S(2)}) collective-permute-start(f32[4,64,64]{2,1,0:T(8,128)S(1)} %add.62), channel_id=1, source_target_pairs={{0,16},{4,20},{8,24},{12,28},{16,0},{20,4},{24,8},{28,12},{1,17},{... | collective-permute-start | bytes 196616 | tf_op jit(solution)/shard_map/ppermute | solution.py:39
  44.3 1.1 %copy-start.1 = (f32[64,128]{1,0:T(8,128)S(1)}, f32[64,128]{1,0:T(8,128)}, u32[]{:S(2)}) copy-start(f32[64,128]{1,0:T(8,128)} %shard_map.17) | copy-start | bytes 98308
  51.4 4.3 %collective-permute-start.7 = (f32[2,64,64]{2,1,0:T(8,128)S(1)}, f32[2,64,64]{2,1,0:T(8,128)S(1)}, u32[]{:S(2)}, u32[]{:S(2)}) collective-permute-start(f32[2,64,64]{2,1,0:T(8,128)S(1)} %pad_maximum_fusion.3), channel_id=1, source_target_pairs={{0,4},{4,0},{8,12},{12,8},{16,20},{20,16},{24,28},{28,24},{1,5},{5... | collective-permute-start | bytes 98312 | tf_op jit(solution)/shard_map/ppermute | solution.py:35
  52.4 4.3 %collective-permute-start.6 = (f32[2,64,64]{2,1,0:T(8,128)S(1)}, f32[2,64,64]{2,1,0:T(8,128)S(1)}, u32[]{:S(2)}, u32[]{:S(2)}) collective-permute-start(f32[2,64,64]{2,1,0:T(8,128)S(1)} %pad_maximum_fusion.2), channel_id=1, source_target_pairs={{0,4},{4,0},{8,12},{12,8},{16,20},{20,16},{24,28},{28,24},{1,5},{5... | collective-permute-start | bytes 98312 | tf_op jit(solution)/shard_map/ppermute | solution.py:33
  56.8 4.5 %collective-permute-start.8 = (f32[2,64,64]{2,1,0:T(8,128)S(1)}, f32[2,64,64]{2,1,0:T(8,128)S(1)}, u32[]{:S(2)}, u32[]{:S(2)}) collective-permute-start(f32[2,64,64]{2,1,0:T(8,128)S(1)} %fusion.68), channel_id=1, source_target_pairs={{0,8},{4,12},{8,0},{12,4},{16,24},{20,28},{24,16},{28,20},{1,9},{5... | collective-permute-start | bytes 98312 | tf_op jit(solution)/shard_map/ppermute | solution.py:33
  56.9 5.1 %collective-permute-start.9 = (f32[2,64,64]{2,1,0:T(8,128)S(1)}, f32[2,64,64]{2,1,0:T(8,128)S(1)}, u32[]{:S(2)}, u32[]{:S(2)}) collective-permute-start(f32[2,64,64]{2,1,0:T(8,128)S(1)} %fusion.67), channel_id=1, source_target_pairs={{0,8},{4,12},{8,0},{12,4},{16,24},{20,28},{24,16},{28,20},{1,9},{5... | collective-permute-start | bytes 98312 | tf_op jit(solution)/shard_map/ppermute | solution.py:35
  62.0 5.2 %collective-permute-start.10 = (f32[2,64,64]{2,1,0:T(8,128)S(1)}, f32[2,64,64]{2,1,0:T(8,128)S(1)}, u32[]{:S(2)}, u32[]{:S(2)}) collective-permute-start(f32[2,64,64]{2,1,0:T(8,128)S(1)} %add.67), channel_id=1, source_target_pairs={{0,16},{4,20},{8,24},{12,28},{16,0},{20,4},{24,8},{28,12},{1,17},{... | collective-permute-start | bytes 98312 | tf_op jit(solution)/shard_map/ppermute | solution.py:33
  64.5 16.1 %collective-permute-start.11 = (f32[2,64,64]{2,1,0:T(8,128)S(1)}, f32[2,64,64]{2,1,0:T(8,128)S(1)}, u32[]{:S(2)}, u32[]{:S(2)}) collective-permute-start(f32[2,64,64]{2,1,0:T(8,128)S(1)} %add.68), channel_id=1, source_target_pairs={{0,16},{4,20},{8,24},{12,28},{16,0},{20,4},{24,8},{28,12},{1,17},{... | collective-permute-start | bytes 98312 | tf_op jit(solution)/shard_map/ppermute | solution.py:39
  76.3 1.1 %copy-start.2 = (f32[64,128]{1,0:T(8,128)S(1)}, f32[64,128]{1,0:T(8,128)}, u32[]{:S(2)}) copy-start(f32[64,128]{1,0:T(8,128)} %shard_map.18) | copy-start | bytes 98308

commit v6 on v2

--- a/solution.py
+++ b/solution.py
@@ -28,7 +28,7 @@
 def invert_near_identity(square):
     identity = jnp.eye(square.shape[0], dtype=jnp.float32)
     approx = square.T * (2.0 / 4.25)
-    for _ in range(9):
+    for _ in range(8):
         approx = apply_left(approx, 2.0 * identity - apply_left(square, approx))
     return approx
 
@@ -76,16 +76,19 @@
         panel_0 = gathered[0]
         second = gathered[1]
 
-        sums = jnp.stack([
-            inner_rows(panel_0, panel_0),
-            inner_rows(panel_0, units[0]),
-            inner_rows(panel_0, current),
-            inner_rows(units[0], current),
-            inner_rows(panel_0, second),
-            inner_rows(units[0], second),
-        ])
-        sums = butterfly_sum(sums, "rows", rows_size)
-        gram, top_rows, basis_cur, unit_cur, basis_sec, unit_sec = (sums[i] for i in range(6))
+        head = butterfly_sum(
+            inner_rows(panel_0, jnp.concatenate([panel_0, units[0]])), "rows", rows_size
+        )
+        both = jnp.concatenate([current, second])
+        tail = butterfly_sum(
+            jnp.concatenate([inner_rows(panel_0, both), inner_rows(units[0], both)], axis=1),
+            "rows",
+            rows_size,
+        )
+        gram, top_rows = head[:, :width], head[:, width:]
+        basis_cur, basis_sec, unit_cur, unit_sec = (
+            tail[:, i * width:(i + 1) * width] for i in range(4)
+        )
         lower_inv = lower_inverse(gram)
         top_block = apply_left(lower_inv, top_rows)
         inverse = invert_near_identity(identity - top_block.T)
@@ -96,14 +99,16 @@
         second = second - jnp.dot(mixed_sec.T, reflect, precision=HIGHEST_PRECISION)
 
         panel_1 = jnp.where((global_rows >= width)[None, :], second, jnp.zeros_like(second))
-        sums = jnp.stack([
-            inner_rows(panel_1, panel_1),
-            inner_rows(panel_1, units[1]),
-            inner_rows(panel_1, current),
-            inner_rows(units[1], current),
-        ])
-        sums = butterfly_sum(sums, "rows", rows_size)
-        gram, top_rows, basis_cur, unit_cur = (sums[i] for i in range(4))
+        head = butterfly_sum(
+            inner_rows(panel_1, jnp.concatenate([panel_1, units[1]])), "rows", rows_size
+        )
+        tail = butterfly_sum(
+            jnp.concatenate([inner_rows(panel_1, current), inner_rows(units[1], current)], axis=1),
+            "rows",
+            rows_size,
+        )
+        gram, top_rows = head[:, :width], head[:, width:]
+        basis_cur, unit_cur = tail[:, :width], tail[:, width:]
         lower_inv = lower_inverse(gram)
         top_block = apply_left(lower_inv, top_rows)
         inverse = invert_near_identity(identity - top_block.T)

time: 86.3 us -> 76.6 us (0.89)
  waiting for transfers between devices: 30.8 us -> 12.4 us
  starting transfers between devices: 10.9 us -> 19.6 us
    ppermute x6 -> x12, waiting for transfers between devices: 30.8 us -> 12.4 us  [butterfly_sum(): x = x + lax.ppermute(x, axis, [(i, i ^ step) for i in range(size)])]
    ppermute x6 -> x12, starting transfers between devices: 10.9 us -> 19.6 us  [butterfly_sum(): x = x + lax.ppermute(x, axis, [(i, i ^ step) for i in range(size)])]
    dot_general x46 -> x42, matrix products: 10.1 us -> 9.71 us  [apply_left(): return jnp.dot(square, right_side, precision=HIGHEST_PRECISION)]
    dot_general x10 -> x6, matrix products: 2.8 us -> 2.51 us  [inner_rows(): lax.dot_general(left, right, (((1,), (1,)), ((), ())), precision=HIGHEST_...]
  transfers between devices with their start and end apart: 6 -> 12, of which waited for: 6 -> 7; matrix products, arithmetic and copies ran while one was open for 0% -> 10% of each run, Pallas kernels for 0% -> 22%
where the time goes in v6:
time: 76.6 us; the launch traced here: 76.1 us
  starting transfers between devices  19.6 us (26%)
  Pallas kernels  16.7 us (22%)
  matrix products  14 us (18%)
  waiting for transfers between devices  12.4 us (16%)
  blocking collectives  10.3 us (13%)
  other arithmetic  1.68 us (2%)
  local copies, waits for them, and re-layouts  0.91 us (1%)
    ppermute x12, starting transfers between devices, butterfly_sum(): x = x + lax.ppermute(x, axis, [(i, i ^ step) for i in range(size)])  19.6 us
    pallas_call x2, Pallas kernels, lower_inverse(): pl.pallas_call(_eliminate_kernel, out_shape=jax.ShapeDtypeStruct(aug.shap...  16.7 us
    ppermute x12, waiting for transfers between devices, butterfly_sum(): x = x + lax.ppermute(x, axis, [(i, i ^ step) for i in range(size)])  12.4 us
    all_gather x1, blocking collectives, local(): gathered = lax.all_gather(current, 'cols')  10.3 us
    dot_general x42, matrix products, apply_left(): return jnp.dot(square, right_side, precision=HIGHEST_PRECISION)  9.71 us
    dot_general x6, matrix products, inner_rows(): lax.dot_general(left, right, (((1,), (1,)), ((), ())), precision=HIGHEST_...  2.51 us
  transfers between devices with their start and end apart: 12, of which 7 were waited for; matrix products, arithmetic and copies ran while one was open for 10% of the time, Pallas kernels for 22%

profile of v6, /device:TPU:0, one launch (start us, length us, event | category | flops | bytes accessed | tf_op | source)
XLA Modules:
  0.0 76.1 jit_solution(15727063701303024643)
XLA Ops:
  0.0 10.3 %all_gather.3 = f32[4,64,768]{2,1,0:T(8,128)S(1)} all-gather(f32[1,64,768]{2,1,0:T(8,128)} %param.1), channel_id=1, replica_groups=mesh['rows'=8,'cols'=4] {'cols'}, dimensions={0}, use_global_device_ids=true | all-gather | bytes 983040 | tf_op jit(solution)/shard_map/all_gather | solution.py:75
  10.3 0.9 %copy-done = f32[1,64,768]{2,1,0:T(8,128)S(1)} copy-done((f32[1,64,768]{2,1,0:T(8,128)S(1)}, f32[1,64,768]{2,1,0:T(8,128)}, u32[]{:S(2)}) %copy-start) | copy-done | bytes 196632
  11.2 0.5 convolution_bitcast_fusion
  12.1 1.6 %collective-permute-start.3 = (f32[64,256]{1,0:T(8,128)S(1)}, f32[64,256]{1,0:T(8,128)S(1)}, u32[]{:S(2)}, u32[]{:S(2)}) collective-permute-start(f32[64,256]{1,0:T(8,128)S(1)} %pad_maximum_fusion.3), channel_id=1, source_target_pairs={{0,4},{4,0},{8,12},{12,8},{16,20},{20,16},{24,28},{28,24},{1,5},{5... | collective-permute-start | bytes 196616 | tf_op jit(solution)/shard_map/ppermute | solution.py:23
  13.7 0.5 convolution_bitcast_fusion.1
  14.2 0.6 collective-permute-start
  14.9 3.3 %collective-permute-done = f32[64,128]{1,0:T(8,128)S(1)} collective-permute-done((f32[64,128]{1,0:T(8,128)S(1)}, f32[64,128]{1,0:T(8,128)S(1)}, u32[]{:S(2)}, u32[]{:S(2)}) %collective-permute-start) | collective-permute-done | bytes 32800 | tf_op jit(solution)/shard_map/ppermute | solution.py:23
  18.2 1.6 %collective-permute-start.1 = (f32[64,128]{1,0:T(8,128)S(1)}, f32[64,128]{1,0:T(8,128)S(1)}, u32[]{:S(2)}, u32[]{:S(2)}) collective-permute-start(f32[64,128]{1,0:T(8,128)S(1)} %add.59), channel_id=1, source_target_pairs={{0,8},{4,12},{8,0},{12,4},{16,24},{20,28},{24,16},{28,20},{1,9},{5... | collective-permute-start | bytes 98312 | tf_op jit(solution)/shard_map/ppermute | solution.py:23
  19.8 2.3 %collective-permute-done.1 = f32[64,128]{1,0:T(8,128)S(1)} collective-permute-done((f32[64,128]{1,0:T(8,128)S(1)}, f32[64,128]{1,0:T(8,128)S(1)}, u32[]{:S(2)}, u32[]{:S(2)}) %collective-permute-start.1) | collective-permute-done | bytes 32800 | tf_op jit(solution)/shard_map/ppermute | solution.py:23
  22.1 2.6 %collective-permute-start.2 = (f32[64,128]{1,0:T(8,128)S(1)}, f32[64,128]{1,0:T(8,128)S(1)}, u32[]{:S(2)}, u32[]{:S(2)}) collective-permute-start(f32[64,128]{1,0:T(8,128)S(1)} %add.60), channel_id=1, source_target_pairs={{0,16},{4,20},{8,24},{12,28},{16,0},{20,4},{24,8},{28,12},{1,17},{... | collective-permute-start | bytes 98312 | tf_op jit(solution)/shard_map/ppermute | solution.py:23
  24.7 1.6 %collective-permute-start.4 = (f32[64,256]{1,0:T(8,128)S(1)}, f32[64,256]{1,0:T(8,128)S(1)}, u32[]{:S(2)}, u32[]{:S(2)}) collective-permute-start(f32[64,256]{1,0:T(8,128)S(1)} %fusion.76), channel_id=1, source_target_pairs={{0,8},{4,12},{8,0},{12,4},{16,24},{20,28},{24,16},{28,20},{1,9},{5... | collective-permute-start | bytes 196616 | tf_op jit(solution)/shard_map/ppermute | solution.py:23
  26.4 0.6 collective-permute-done.2
  26.9 0.7 pad_maximum_fusion.4.aug_ref
  27.6 8.4 %shard_map.17 = f32[64,128]{1,0:T(8,128)} custom-call(f32[64,128]{1,0:T(8,128)} %pad_maximum_fusion.4.aug_ref), custom_call_target="tpu_custom_call" | custom-call | tf_op jit(solution)/shard_map/pallas_call | solution.py:58
  36.0 1.1 %fusion.28 = f32[64,64]{1,0:T(8,128)S(1)} fusion(f32[64,128]{1,0:T(8,128)S(1)} %add.61, f32[64,128]{1,0:T(8,128)} %shard_map.17), kind=kOutput, calls=%fused_computation.62 | convolution fusion | flops 3145728 | bytes 81920 | tf_op jit(solution)/shard_map/dot_general | solution.py:15
  37.2 0.4 convolution_subtract_fusion.4
  40.2 2.7 %collective-permute-start.5 = (f32[64,256]{1,0:T(8,128)S(1)}, f32[64,256]{1,0:T(8,128)S(1)}, u32[]{:S(2)}, u32[]{:S(2)}) collective-permute-start(f32[64,256]{1,0:T(8,128)S(1)} %add.63), channel_id=1, source_target_pairs={{0,16},{4,20},{8,24},{12,28},{16,0},{20,4},{24,8},{28,12},{1,17},{... | collective-permute-start | bytes 196616 | tf_op jit(solution)/shard_map/ppermute | solution.py:23
  43.1 2.4 %collective-permute-done.5 = f32[64,256]{1,0:T(8,128)S(1)} collective-permute-done((f32[64,256]{1,0:T(8,128)S(1)}, f32[64,256]{1,0:T(8,128)S(1)}, u32[]{:S(2)}, u32[]{:S(2)}) %collective-permute-start.5) | collective-permute-done | bytes 65568 | tf_op jit(solution)/shard_map/ppermute | solution.py:23
  47.0 0.4 fusion.1
  47.7 0.5 fusion.5
  48.2 0.6 collective-permute-start.6
  48.9 1.5 %collective-permute-start.9 = (f32[64,128]{1,0:T(8,128)S(1)}, f32[64,128]{1,0:T(8,128)S(1)}, u32[]{:S(2)}, u32[]{:S(2)}) collective-permute-start(f32[64,128]{1,0:T(8,128)S(1)} %pad_maximum_fusion.6), channel_id=1, source_target_pairs={{0,4},{4,0},{8,12},{12,8},{16,20},{20,16},{24,28},{28,24},{1,5},{5... | collective-permute-start | bytes 98312 | tf_op jit(solution)/shard_map/ppermute | solution.py:23
  50.4 1.8 %collective-permute-done.6 = f32[64,128]{1,0:T(8,128)S(1)} collective-permute-done((f32[64,128]{1,0:T(8,128)S(1)}, f32[64,128]{1,0:T(8,128)S(1)}, u32[]{:S(2)}, u32[]{:S(2)}) %collective-permute-start.6) | collective-permute-done | bytes 32800 | tf_op jit(solution)/shard_map/ppermute | solution.py:23
  52.2 1.6 %collective-permute-start.7 = (f32[64,128]{1,0:T(8,128)S(1)}, f32[64,128]{1,0:T(8,128)S(1)}, u32[]{:S(2)}, u32[]{:S(2)}) collective-permute-start(f32[64,128]{1,0:T(8,128)S(1)} %add.65), channel_id=1, source_target_pairs={{0,8},{4,12},{8,0},{12,4},{16,24},{20,28},{24,16},{28,20},{1,9},{5... | collective-permute-start | bytes 98312 | tf_op jit(solution)/shard_map/ppermute | solution.py:23
  53.9 0.6 collective-permute-start.10
  54.5 1.8 %collective-permute-done.7 = f32[64,128]{1,0:T(8,128)S(1)} collective-permute-done((f32[64,128]{1,0:T(8,128)S(1)}, f32[64,128]{1,0:T(8,128)S(1)}, u32[]{:S(2)}, u32[]{:S(2)}) %collective-permute-start.7) | collective-permute-done | bytes 32800 | tf_op jit(solution)/shard_map/ppermute | solution.py:23
  56.3 2.6 %collective-permute-start.8 = (f32[64,128]{1,0:T(8,128)S(1)}, f32[64,128]{1,0:T(8,128)S(1)}, u32[]{:S(2)}, u32[]{:S(2)}) collective-permute-start(f32[64,128]{1,0:T(8,128)S(1)} %add.66), channel_id=1, source_target_pairs={{0,16},{4,20},{8,24},{12,28},{16,0},{20,4},{24,8},{28,12},{1,17},{... | collective-permute-start | bytes 98312 | tf_op jit(solution)/shard_map/ppermute | solution.py:23
  58.9 2.1 %collective-permute-start.11 = (f32[64,128]{1,0:T(8,128)S(1)}, f32[64,128]{1,0:T(8,128)S(1)}, u32[]{:S(2)}, u32[]{:S(2)}) collective-permute-start(f32[64,128]{1,0:T(8,128)S(1)} %add.69), channel_id=1, source_target_pairs={{0,16},{4,20},{8,24},{12,28},{16,0},{20,4},{24,8},{28,12},{1,17},{... | collective-permute-start | bytes 98312 | tf_op jit(solution)/shard_map/ppermute | solution.py:23
  61.2 0.7 pad_maximum_fusion.5.aug_ref
  61.8 8.4 %shard_map.18 = f32[64,128]{1,0:T(8,128)} custom-call(f32[64,128]{1,0:T(8,128)} %pad_maximum_fusion.5.aug_ref), custom_call_target="tpu_custom_call" | custom-call | tf_op jit(solution)/shard_map/pallas_call | solution.py:58
  70.2 1.2 %convolution_subtract_fusion.1 = f32[64,768]{1,0:T(8,128)S(1)} fusion(f32[64,768]{1,0:T(8,128)S(1)} %fusion.1, s32[768]{0:T(1024)S(1)} %fusion.66, f32[64,128]{1,0:T(8,128)} %shard_map.18), kind=kOutput, calls=%fused_computation.2 | convolution fusion | flops 37896192 | bytes 429056 | tf_op jit(solution)/shard_map/dot_general | solution.py:15
  75.1 1.1 %fusion = f32[1,64,768]{2,1,0:T(8,128)} fusion(f32[64,768]{1,0:T(8,128)S(1)} %convolution_subtract_fusion.3, f32[64,64]{1,0:T(8,128)S(1)} %fusion.19, f32[64,768]{1,0:T(8,128)S(1)} %convolution_subtract_fusion.1), kind=kOutput, calls=%fused_computation.1 | convolution fusion | flops 37797888 | bytes 606208 | tf_op jit(solution)/shard_map/dot_general | solution.py:117
  (75 shorter events, 8.8 us)
Async XLA Ops:
  10.3 0.9 %copy-start = (f32[1,64,768]{2,1,0:T(8,128)S(1)}, f32[1,64,768]{2,1,0:T(8,128)}, u32[]{:S(2)}) copy-start(f32[1,64,768]{2,1,0:T(8,128)} %param.1) | copy-start | bytes 589828
  12.1 12.6 %collective-permute-start.3 = (f32[64,256]{1,0:T(8,128)S(1)}, f32[64,256]{1,0:T(8,128)S(1)}, u32[]{:S(2)}, u32[]{:S(2)}) collective-permute-start(f32[64,256]{1,0:T(8,128)S(1)} %pad_maximum_fusion.3), channel_id=1, source_target_pairs={{0,4},{4,0},{8,12},{12,8},{16,20},{20,16},{24,28},{28,24},{1,5},{5... | collective-permute-start | bytes 196616 | tf_op jit(solution)/shard_map/ppermute | solution.py:23
  14.2 4.0 %collective-permute-start = (f32[64,128]{1,0:T(8,128)S(1)}, f32[64,128]{1,0:T(8,128)S(1)}, u32[]{:S(2)}, u32[]{:S(2)}) collective-permute-start(f32[64,128]{1,0:T(8,128)S(1)} %convolution_bitcast_fusion.1), channel_id=1, source_target_pairs={{0,4},{4,0},{8,12},{12,8},{16,20},{20,16},{24,28},{28,24},{1,5},{5... | collective-permute-start | bytes 98312 | tf_op jit(solution)/shard_map/ppermute | solution.py:23
  18.2 3.9 %collective-permute-start.1 = (f32[64,128]{1,0:T(8,128)S(1)}, f32[64,128]{1,0:T(8,128)S(1)}, u32[]{:S(2)}, u32[]{:S(2)}) collective-permute-start(f32[64,128]{1,0:T(8,128)S(1)} %add.59), channel_id=1, source_target_pairs={{0,8},{4,12},{8,0},{12,4},{16,24},{20,28},{24,16},{28,20},{1,9},{5... | collective-permute-start | bytes 98312 | tf_op jit(solution)/shard_map/ppermute | solution.py:23
  22.1 4.8 %collective-permute-start.2 = (f32[64,128]{1,0:T(8,128)S(1)}, f32[64,128]{1,0:T(8,128)S(1)}, u32[]{:S(2)}, u32[]{:S(2)}) collective-permute-start(f32[64,128]{1,0:T(8,128)S(1)} %add.60), channel_id=1, source_target_pairs={{0,16},{4,20},{8,24},{12,28},{16,0},{20,4},{24,8},{28,12},{1,17},{... | collective-permute-start | bytes 98312 | tf_op jit(solution)/shard_map/ppermute | solution.py:23
  24.7 15.5 %collective-permute-start.4 = (f32[64,256]{1,0:T(8,128)S(1)}, f32[64,256]{1,0:T(8,128)S(1)}, u32[]{:S(2)}, u32[]{:S(2)}) collective-permute-start(f32[64,256]{1,0:T(8,128)S(1)} %fusion.76), channel_id=1, source_target_pairs={{0,8},{4,12},{8,0},{12,4},{16,24},{20,28},{24,16},{28,20},{1,9},{5... | collective-permute-start | bytes 196616 | tf_op jit(solution)/shard_map/ppermute | solution.py:23
  36.0 1.1 %copy-start.1 = (f32[64,128]{1,0:T(8,128)S(1)}, f32[64,128]{1,0:T(8,128)}, u32[]{:S(2)}) copy-start(f32[64,128]{1,0:T(8,128)} %shard_map.17) | copy-start | bytes 98308
  40.2 5.2 %collective-permute-start.5 = (f32[64,256]{1,0:T(8,128)S(1)}, f32[64,256]{1,0:T(8,128)S(1)}, u32[]{:S(2)}, u32[]{:S(2)}) collective-permute-start(f32[64,256]{1,0:T(8,128)S(1)} %add.63), channel_id=1, source_target_pairs={{0,16},{4,20},{8,24},{12,28},{16,0},{20,4},{24,8},{28,12},{1,17},{... | collective-permute-start | bytes 196616 | tf_op jit(solution)/shard_map/ppermute | solution.py:23
  48.2 4.0 %collective-permute-start.6 = (f32[64,128]{1,0:T(8,128)S(1)}, f32[64,128]{1,0:T(8,128)S(1)}, u32[]{:S(2)}, u32[]{:S(2)}) collective-permute-start(f32[64,128]{1,0:T(8,128)S(1)} %fusion.5), channel_id=1, source_target_pairs={{0,4},{4,0},{8,12},{12,8},{16,20},{20,16},{24,28},{28,24},{1,5},{5... | collective-permute-start | bytes 98312 | tf_op jit(solution)/shard_map/ppermute | solution.py:23
  48.9 4.9 %collective-permute-start.9 = (f32[64,128]{1,0:T(8,128)S(1)}, f32[64,128]{1,0:T(8,128)S(1)}, u32[]{:S(2)}, u32[]{:S(2)}) collective-permute-start(f32[64,128]{1,0:T(8,128)S(1)} %pad_maximum_fusion.6), channel_id=1, source_target_pairs={{0,4},{4,0},{8,12},{12,8},{16,20},{20,16},{24,28},{28,24},{1,5},{5... | collective-permute-start | bytes 98312 | tf_op jit(solution)/shard_map/ppermute | solution.py:23
  52.2 4.1 %collective-permute-start.7 = (f32[64,128]{1,0:T(8,128)S(1)}, f32[64,128]{1,0:T(8,128)S(1)}, u32[]{:S(2)}, u32[]{:S(2)}) collective-permute-start(f32[64,128]{1,0:T(8,128)S(1)} %add.65), channel_id=1, source_target_pairs={{0,8},{4,12},{8,0},{12,4},{16,24},{20,28},{24,16},{28,20},{1,9},{5... | collective-permute-start | bytes 98312 | tf_op jit(solution)/shard_map/ppermute | solution.py:23
  53.9 5.0 %collective-permute-start.10 = (f32[64,128]{1,0:T(8,128)S(1)}, f32[64,128]{1,0:T(8,128)S(1)}, u32[]{:S(2)}, u32[]{:S(2)}) collective-permute-start(f32[64,128]{1,0:T(8,128)S(1)} %fusion.151), channel_id=1, source_target_pairs={{0,8},{4,12},{8,0},{12,4},{16,24},{20,28},{24,16},{28,20},{1,9},{5... | collective-permute-start | bytes 98312 | tf_op jit(solution)/shard_map/ppermute | solution.py:23
  56.3 4.8 %collective-permute-start.8 = (f32[64,128]{1,0:T(8,128)S(1)}, f32[64,128]{1,0:T(8,128)S(1)}, u32[]{:S(2)}, u32[]{:S(2)}) collective-permute-start(f32[64,128]{1,0:T(8,128)S(1)} %add.66), channel_id=1, source_target_pairs={{0,16},{4,20},{8,24},{12,28},{16,0},{20,4},{24,8},{28,12},{1,17},{... | collective-permute-start | bytes 98312 | tf_op jit(solution)/shard_map/ppermute | solution.py:23
  58.9 12.9 %collective-permute-start.11 = (f32[64,128]{1,0:T(8,128)S(1)}, f32[64,128]{1,0:T(8,128)S(1)}, u32[]{:S(2)}, u32[]{:S(2)}) collective-permute-start(f32[64,128]{1,0:T(8,128)S(1)} %add.69), channel_id=1, source_target_pairs={{0,16},{4,20},{8,24},{12,28},{16,0},{20,4},{24,8},{28,12},{1,17},{... | collective-permute-start | bytes 98312 | tf_op jit(solution)/shard_map/ppermute | solution.py:23
  70.2 1.2 %copy-start.2 = (f32[64,128]{1,0:T(8,128)S(1)}, f32[64,128]{1,0:T(8,128)}, u32[]{:S(2)}) copy-start(f32[64,128]{1,0:T(8,128)} %shard_map.18) | copy-start | bytes 98308

commit v7 on v6

--- a/solution.py
+++ b/solution.py
@@ -15,13 +15,18 @@
     return jnp.dot(square, right_side, precision=HIGHEST_PRECISION)
 
 
-def butterfly_sum(x, axis, size):
-    if size & (size - 1):
-        return lax.psum(x, axis)
-    step = 1
-    while step < size:
+def butterfly_steps(size):
+    if size < 2 or size & (size - 1):
+        return None
+    return [1 << k for k in range(size.bit_length() - 1)]
+
+
+def butterfly_sum(x, axis, size, steps=None):
+    every = butterfly_steps(size)
+    if every is None:
+        return x if steps == [] else lax.psum(x, axis)
+    for step in every if steps is None else steps:
         x = x + lax.ppermute(x, axis, [(i, i ^ step) for i in range(size)])
-        step *= 2
     return x
 
 
@@ -36,20 +41,17 @@
 def _eliminate_kernel(aug_ref, out_ref):
     size, wide = aug_ref.shape
     rows = lax.broadcasted_iota(jnp.int32, (size, wide), 0)
-    lanes = lax.broadcasted_iota(jnp.int32, (size, wide), 1)
     row_ids = lax.broadcasted_iota(jnp.int32, (size, 1), 0)
-
-    def step(j, work):
-        column = jnp.sum(jnp.where(lanes == j, work, 0.0), axis=1, keepdims=True)
-        row = jnp.sum(jnp.where(rows == j, work, 0.0), axis=0, keepdims=True)
-        pivot = jnp.sum(jnp.where(row_ids == j, column, 0.0), axis=0, keepdims=True)
-        scale = 1.0 / jnp.sqrt(pivot)
+    work = aug_ref[...]
+    for j in range(size):
+        row = work[j:j + 1, :]
+        pivot = row[:, j:j + 1]
+        scale = lax.rsqrt(pivot)
+        scale = scale * (1.5 - 0.5 * pivot * scale * scale)
         scaled = row * scale
-        weight = jnp.where(row_ids > j, column * scale, 0.0)
-        work = work - weight * scaled
-        return jnp.where(rows == j, scaled, work)
-
-    out_ref[...] = lax.fori_loop(0, size, step, aug_ref[...], unroll=4)
+        weight = jnp.where(row_ids > j, work[:, j:j + 1] * scale, 0.0)
+        work = jnp.where(rows == j, scaled, work - weight * scaled)
+    out_ref[...] = work
 
 
 def lower_inverse(gram):
@@ -80,16 +82,15 @@
             inner_rows(panel_0, jnp.concatenate([panel_0, units[0]])), "rows", rows_size
         )
         both = jnp.concatenate([current, second])
-        tail = butterfly_sum(
-            jnp.concatenate([inner_rows(panel_0, both), inner_rows(units[0], both)], axis=1),
-            "rows",
-            rows_size,
-        )
-        gram, top_rows = head[:, :width], head[:, width:]
+        tail = jnp.concatenate([inner_rows(panel_0, both), inner_rows(units[0], both)], axis=1)
+        steps = butterfly_steps(rows_size)
+        tail = butterfly_sum(tail, "rows", rows_size, None if steps is None else steps[:-1])
+        lower_inv, tail = lax.optimization_barrier((lower_inverse(head[:, :width]), tail))
+        tail = butterfly_sum(tail, "rows", rows_size, None if steps is None else steps[-1:])
+        top_rows = head[:, width:]
         basis_cur, basis_sec, unit_cur, unit_sec = (
             tail[:, i * width:(i + 1) * width] for i in range(4)
         )
-        lower_inv = lower_inverse(gram)
         top_block = apply_left(lower_inv, top_rows)
         inverse = invert_near_identity(identity - top_block.T)
         reflect = units[0] - apply_left(lower_inv, panel_0)

time: 76.6 us -> 71.6 us (0.935)
  waiting for transfers between devices: 12.4 us -> 9.98 us
  Pallas kernels: 16.7 us -> 14.3 us
  matrix products: 14 us -> 13.1 us
  local copies, waits for them, and re-layouts: 0.91 us -> 1.74 us
    ppermute x12, waiting for transfers between devices: 12.4 us -> 9.98 us  [butterfly_sum(): x = x + lax.ppermute(x, axis, [(i, i ^ step) for i in range(size)])]
    pallas_call x2, Pallas kernels: 16.7 us -> 14.3 us  [lower_inverse(): pl.pallas_call(_eliminate_kernel, out_shape=jax.ShapeDtypeStruct(aug.shap...]
    dot_general x42, matrix products: 9.71 us -> 8.75 us  [apply_left(): return jnp.dot(square, right_side, precision=HIGHEST_PRECISION)]
    slice x0 -> x1, local copies, waits for them, and re-layouts: none -> 0.83 us  [lower_inverse(): return out[:, size:]]
  transfers between devices with their start and end apart: 12 -> 12, of which waited for: 7 -> 6; matrix products, arithmetic and copies ran while one was open for 10% -> 10% of each run, Pallas kernels for 22% -> 20%
where the time goes in v7:
time: 71.6 us; the launch traced here: 71.1 us
  starting transfers between devices  19.6 us (27%)
  Pallas kernels  14.3 us (20%)
  matrix products  13.1 us (18%)
  blocking collectives  10.3 us (14%)
  waiting for transfers between devices  9.98 us (14%)
  local copies, waits for them, and re-layouts  1.74 us (2%)
  other arithmetic  1.69 us (2%)
    ppermute x12, starting transfers between devices, butterfly_sum(): x = x + lax.ppermute(x, axis, [(i, i ^ step) for i in range(size)])  19.6 us
    pallas_call x2, Pallas kernels, lower_inverse(): pl.pallas_call(_eliminate_kernel, out_shape=jax.ShapeDtypeStruct(aug.shap...  14.3 us
    all_gather x1, blocking collectives, local(): gathered = lax.all_gather(current, 'cols')  10.3 us
    ppermute x12, waiting for transfers between devices, butterfly_sum(): x = x + lax.ppermute(x, axis, [(i, i ^ step) for i in range(size)])  9.98 us
    dot_general x42, matrix products, apply_left(): return jnp.dot(square, right_side, precision=HIGHEST_PRECISION)  8.75 us
    dot_general x6, matrix products, inner_rows(): lax.dot_general(left, right, (((1,), (1,)), ((), ())), precision=HIGHEST_...  2.52 us
  transfers between devices with their start and end apart: 12, of which 6 were waited for; matrix products, arithmetic and copies ran while one was open for 10% of the time, Pallas kernels for 20%

profile of v7, /device:TPU:0, one launch (start us, length us, event | category | flops | bytes accessed | tf_op | source)
XLA Modules:
  0.0 71.1 jit_solution(3079645022896408086)
XLA Ops:
  0.0 10.3 %all_gather.3 = f32[4,64,768]{2,1,0:T(8,128)S(1)} all-gather(f32[1,64,768]{2,1,0:T(8,128)} %param.1), channel_id=1, replica_groups=mesh['rows'=8,'cols'=4] {'cols'}, dimensions={0}, use_global_device_ids=true | all-gather | bytes 983040 | tf_op jit(solution)/shard_map/all_gather | solution.py:77
  10.3 0.9 %copy-done = f32[1,64,768]{2,1,0:T(8,128)S(1)} copy-done((f32[1,64,768]{2,1,0:T(8,128)S(1)}, f32[1,64,768]{2,1,0:T(8,128)}, u32[]{:S(2)}) %copy-start) | copy-done | bytes 196632
  11.2 0.5 convolution_bitcast_fusion
  12.1 1.6 %collective-permute-start.3 = (f32[64,256]{1,0:T(8,128)S(1)}, f32[64,256]{1,0:T(8,128)S(1)}, u32[]{:S(2)}, u32[]{:S(2)}) collective-permute-start(f32[64,256]{1,0:T(8,128)S(1)} %pad_maximum_fusion.3), channel_id=1, source_target_pairs={{0,4},{4,0},{8,12},{12,8},{16,20},{20,16},{24,28},{28,24},{1,5},{5... | collective-permute-start | bytes 196616 | tf_op jit(solution)/shard_map/ppermute | solution.py:29
  13.7 0.5 convolution_bitcast_fusion.1
  14.2 0.6 collective-permute-start
  14.9 3.3 %collective-permute-done = f32[64,128]{1,0:T(8,128)S(1)} collective-permute-done((f32[64,128]{1,0:T(8,128)S(1)}, f32[64,128]{1,0:T(8,128)S(1)}, u32[]{:S(2)}, u32[]{:S(2)}) %collective-permute-start) | collective-permute-done | bytes 32800 | tf_op jit(solution)/shard_map/ppermute | solution.py:29
  18.2 1.6 %collective-permute-start.1 = (f32[64,128]{1,0:T(8,128)S(1)}, f32[64,128]{1,0:T(8,128)S(1)}, u32[]{:S(2)}, u32[]{:S(2)}) collective-permute-start(f32[64,128]{1,0:T(8,128)S(1)} %add.59), channel_id=1, source_target_pairs={{0,8},{4,12},{8,0},{12,4},{16,24},{20,28},{24,16},{28,20},{1,9},{5... | collective-permute-start | bytes 98312 | tf_op jit(solution)/shard_map/ppermute | solution.py:29
  19.8 2.3 %collective-permute-done.1 = f32[64,128]{1,0:T(8,128)S(1)} collective-permute-done((f32[64,128]{1,0:T(8,128)S(1)}, f32[64,128]{1,0:T(8,128)S(1)}, u32[]{:S(2)}, u32[]{:S(2)}) %collective-permute-start.1) | collective-permute-done | bytes 32800 | tf_op jit(solution)/shard_map/ppermute | solution.py:29
  22.1 2.6 %collective-permute-start.2 = (f32[64,128]{1,0:T(8,128)S(1)}, f32[64,128]{1,0:T(8,128)S(1)}, u32[]{:S(2)}, u32[]{:S(2)}) collective-permute-start(f32[64,128]{1,0:T(8,128)S(1)} %add.60), channel_id=1, source_target_pairs={{0,16},{4,20},{8,24},{12,28},{16,0},{20,4},{24,8},{28,12},{1,17},{... | collective-permute-start | bytes 98312 | tf_op jit(solution)/shard_map/ppermute | solution.py:29
  24.7 1.6 %collective-permute-start.4 = (f32[64,256]{1,0:T(8,128)S(1)}, f32[64,256]{1,0:T(8,128)S(1)}, u32[]{:S(2)}, u32[]{:S(2)}) collective-permute-start(f32[64,256]{1,0:T(8,128)S(1)} %fusion.72), channel_id=1, source_target_pairs={{0,8},{4,12},{8,0},{12,4},{16,24},{20,28},{24,16},{28,20},{1,9},{5... | collective-permute-start | bytes 196616 | tf_op jit(solution)/shard_map/ppermute | solution.py:29
  26.4 0.6 collective-permute-done.2
  26.9 0.7 pad_maximum_fusion.4.aug_ref
  27.6 7.2 %shard_map.17 = f32[64,128]{1,0:T(8,128)} custom-call(f32[64,128]{1,0:T(8,128)} %pad_maximum_fusion.4.aug_ref), custom_call_target="tpu_custom_call" | custom-call | tf_op jit(solution)/shard_map/pallas_call | solution.py:60
  34.8 0.8 %slice.59 = f32[64,64]{1,0:T(8,128)S(1)} slice(f32[64,128]{1,0:T(8,128)} %shard_map.17), slice={[0:64], [64:128]} | slice | bytes 32768 | tf_op jit(solution)/shard_map/slice | solution.py:63
  36.3 2.7 %collective-permute-start.5 = (f32[64,256]{1,0:T(8,128)S(1)}, f32[64,256]{1,0:T(8,128)S(1)}, u32[]{:S(2)}, u32[]{:S(2)}) collective-permute-start(f32[64,256]{1,0:T(8,128)S(1)} %add.63), channel_id=1, source_target_pairs={{0,16},{4,20},{8,24},{12,28},{16,0},{20,4},{24,8},{28,12},{1,17},{... | collective-permute-start | bytes 196616 | tf_op jit(solution)/shard_map/ppermute | solution.py:29
  42.6 0.4 convolution_subtract_fusion.3
  43.3 0.4 fusion.1
  44.0 0.5 fusion.5
  44.5 0.6 collective-permute-start.6
  45.2 1.5 %collective-permute-start.9 = (f32[64,128]{1,0:T(8,128)S(1)}, f32[64,128]{1,0:T(8,128)S(1)}, u32[]{:S(2)}, u32[]{:S(2)}) collective-permute-start(f32[64,128]{1,0:T(8,128)S(1)} %pad_maximum_fusion.6), channel_id=1, source_target_pairs={{0,4},{4,0},{8,12},{12,8},{16,20},{20,16},{24,28},{28,24},{1,5},{5... | collective-permute-start | bytes 98312 | tf_op jit(solution)/shard_map/ppermute | solution.py:29
  46.7 1.8 %collective-permute-done.6 = f32[64,128]{1,0:T(8,128)S(1)} collective-permute-done((f32[64,128]{1,0:T(8,128)S(1)}, f32[64,128]{1,0:T(8,128)S(1)}, u32[]{:S(2)}, u32[]{:S(2)}) %collective-permute-start.6) | collective-permute-done | bytes 32800 | tf_op jit(solution)/shard_map/ppermute | solution.py:29
  48.5 1.8 %collective-permute-start.7 = (f32[64,128]{1,0:T(8,128)S(1)}, f32[64,128]{1,0:T(8,128)S(1)}, u32[]{:S(2)}, u32[]{:S(2)}) collective-permute-start(f32[64,128]{1,0:T(8,128)S(1)} %add.65), channel_id=1, source_target_pairs={{0,8},{4,12},{8,0},{12,4},{16,24},{20,28},{24,16},{28,20},{1,9},{5... | collective-permute-start | bytes 98312 | tf_op jit(solution)/shard_map/ppermute | solution.py:29
  50.4 0.6 collective-permute-start.10
  51.0 1.6 %collective-permute-done.7 = f32[64,128]{1,0:T(8,128)S(1)} collective-permute-done((f32[64,128]{1,0:T(8,128)S(1)}, f32[64,128]{1,0:T(8,128)S(1)}, u32[]{:S(2)}, u32[]{:S(2)}) %collective-permute-start.7) | collective-permute-done | bytes 32800 | tf_op jit(solution)/shard_map/ppermute | solution.py:29
  52.5 2.3 %collective-permute-start.8 = (f32[64,128]{1,0:T(8,128)S(1)}, f32[64,128]{1,0:T(8,128)S(1)}, u32[]{:S(2)}, u32[]{:S(2)}) collective-permute-start(f32[64,128]{1,0:T(8,128)S(1)} %add.66), channel_id=1, source_target_pairs={{0,16},{4,20},{8,24},{12,28},{16,0},{20,4},{24,8},{28,12},{1,17},{... | collective-permute-start | bytes 98312 | tf_op jit(solution)/shard_map/ppermute | solution.py:29
  54.9 2.1 %collective-permute-start.11 = (f32[64,128]{1,0:T(8,128)S(1)}, f32[64,128]{1,0:T(8,128)S(1)}, u32[]{:S(2)}, u32[]{:S(2)}) collective-permute-start(f32[64,128]{1,0:T(8,128)S(1)} %add.69), channel_id=1, source_target_pairs={{0,16},{4,20},{8,24},{12,28},{16,0},{20,4},{24,8},{28,12},{1,17},{... | collective-permute-start | bytes 98312 | tf_op jit(solution)/shard_map/ppermute | solution.py:29
  57.0 0.4 collective-permute-done.8
  57.4 0.7 pad_maximum_fusion.5.aug_ref
  58.1 7.2 %shard_map.18 = f32[64,128]{1,0:T(8,128)} custom-call(f32[64,128]{1,0:T(8,128)} %pad_maximum_fusion.5.aug_ref), custom_call_target="tpu_custom_call" | custom-call | tf_op jit(solution)/shard_map/pallas_call | solution.py:60
  65.2 1.2 %convolution_subtract_fusion.1 = f32[64,768]{1,0:T(8,128)S(1)} fusion(f32[64,768]{1,0:T(8,128)S(1)} %fusion.1, s32[768]{0:T(1024)S(1)} %fusion.62, f32[64,128]{1,0:T(8,128)} %shard_map.18), kind=kOutput, calls=%fused_computation.2 | convolution fusion | flops 37896192 | bytes 429056 | tf_op jit(solution)/shard_map/dot_general | solution.py:15
  70.1 1.1 %fusion = f32[1,64,768]{2,1,0:T(8,128)} fusion(f32[64,768]{1,0:T(8,128)S(1)} %convolution_subtract_fusion.3, f32[64,64]{1,0:T(8,128)S(1)} %fusion.19, f32[64,768]{1,0:T(8,128)S(1)} %convolution_subtract_fusion.1), kind=kOutput, calls=%fused_computation.1 | convolution fusion | flops 37797888 | bytes 606208 | tf_op jit(solution)/shard_map/dot_general | solution.py:118
  (74 shorter events, 8.8 us)
Async XLA Ops:
  10.3 0.9 %copy-start = (f32[1,64,768]{2,1,0:T(8,128)S(1)}, f32[1,64,768]{2,1,0:T(8,128)}, u32[]{:S(2)}) copy-start(f32[1,64,768]{2,1,0:T(8,128)} %param.1) | copy-start | bytes 589828
  12.1 12.6 %collective-permute-start.3 = (f32[64,256]{1,0:T(8,128)S(1)}, f32[64,256]{1,0:T(8,128)S(1)}, u32[]{:S(2)}, u32[]{:S(2)}) collective-permute-start(f32[64,256]{1,0:T(8,128)S(1)} %pad_maximum_fusion.3), channel_id=1, source_target_pairs={{0,4},{4,0},{8,12},{12,8},{16,20},{20,16},{24,28},{28,24},{1,5},{5... | collective-permute-start | bytes 196616 | tf_op jit(solution)/shard_map/ppermute | solution.py:29
  14.2 4.0 %collective-permute-start = (f32[64,128]{1,0:T(8,128)S(1)}, f32[64,128]{1,0:T(8,128)S(1)}, u32[]{:S(2)}, u32[]{:S(2)}) collective-permute-start(f32[64,128]{1,0:T(8,128)S(1)} %convolution_bitcast_fusion.1), channel_id=1, source_target_pairs={{0,4},{4,0},{8,12},{12,8},{16,20},{20,16},{24,28},{28,24},{1,5},{5... | collective-permute-start | bytes 98312 | tf_op jit(solution)/shard_map/ppermute | solution.py:29
  18.2 3.9 %collective-permute-start.1 = (f32[64,128]{1,0:T(8,128)S(1)}, f32[64,128]{1,0:T(8,128)S(1)}, u32[]{:S(2)}, u32[]{:S(2)}) collective-permute-start(f32[64,128]{1,0:T(8,128)S(1)} %add.59), channel_id=1, source_target_pairs={{0,8},{4,12},{8,0},{12,4},{16,24},{20,28},{24,16},{28,20},{1,9},{5... | collective-permute-start | bytes 98312 | tf_op jit(solution)/shard_map/ppermute | solution.py:29
  22.1 4.8 %collective-permute-start.2 = (f32[64,128]{1,0:T(8,128)S(1)}, f32[64,128]{1,0:T(8,128)S(1)}, u32[]{:S(2)}, u32[]{:S(2)}) collective-permute-start(f32[64,128]{1,0:T(8,128)S(1)} %add.60), channel_id=1, source_target_pairs={{0,16},{4,20},{8,24},{12,28},{16,0},{20,4},{24,8},{28,12},{1,17},{... | collective-permute-start | bytes 98312 | tf_op jit(solution)/shard_map/ppermute | solution.py:29
  24.7 10.9 %collective-permute-start.4 = (f32[64,256]{1,0:T(8,128)S(1)}, f32[64,256]{1,0:T(8,128)S(1)}, u32[]{:S(2)}, u32[]{:S(2)}) collective-permute-start(f32[64,256]{1,0:T(8,128)S(1)} %fusion.72), channel_id=1, source_target_pairs={{0,8},{4,12},{8,0},{12,4},{16,24},{20,28},{24,16},{28,20},{1,9},{5... | collective-permute-start | bytes 196616 | tf_op jit(solution)/shard_map/ppermute | solution.py:29
  36.3 5.5 %collective-permute-start.5 = (f32[64,256]{1,0:T(8,128)S(1)}, f32[64,256]{1,0:T(8,128)S(1)}, u32[]{:S(2)}, u32[]{:S(2)}) collective-permute-start(f32[64,256]{1,0:T(8,128)S(1)} %add.63), channel_id=1, source_target_pairs={{0,16},{4,20},{8,24},{12,28},{16,0},{20,4},{24,8},{28,12},{1,17},{... | collective-permute-start | bytes 196616 | tf_op jit(solution)/shard_map/ppermute | solution.py:29
  44.5 4.0 %collective-permute-start.6 = (f32[64,128]{1,0:T(8,128)S(1)}, f32[64,128]{1,0:T(8,128)S(1)}, u32[]{:S(2)}, u32[]{:S(2)}) collective-permute-start(f32[64,128]{1,0:T(8,128)S(1)} %fusion.5), channel_id=1, source_target_pairs={{0,4},{4,0},{8,12},{12,8},{16,20},{20,16},{24,28},{28,24},{1,5},{5... | collective-permute-start | bytes 98312 | tf_op jit(solution)/shard_map/ppermute | solution.py:29
  45.2 5.1 %collective-permute-start.9 = (f32[64,128]{1,0:T(8,128)S(1)}, f32[64,128]{1,0:T(8,128)S(1)}, u32[]{:S(2)}, u32[]{:S(2)}) collective-permute-start(f32[64,128]{1,0:T(8,128)S(1)} %pad_maximum_fusion.6), channel_id=1, source_target_pairs={{0,4},{4,0},{8,12},{12,8},{16,20},{20,16},{24,28},{28,24},{1,5},{5... | collective-permute-start | bytes 98312 | tf_op jit(solution)/shard_map/ppermute | solution.py:29
  48.5 4.0 %collective-permute-start.7 = (f32[64,128]{1,0:T(8,128)S(1)}, f32[64,128]{1,0:T(8,128)S(1)}, u32[]{:S(2)}, u32[]{:S(2)}) collective-permute-start(f32[64,128]{1,0:T(8,128)S(1)} %add.65), channel_id=1, source_target_pairs={{0,8},{4,12},{8,0},{12,4},{16,24},{20,28},{24,16},{28,20},{1,9},{5... | collective-permute-start | bytes 98312 | tf_op jit(solution)/shard_map/ppermute | solution.py:29
  50.4 4.5 %collective-permute-start.10 = (f32[64,128]{1,0:T(8,128)S(1)}, f32[64,128]{1,0:T(8,128)S(1)}, u32[]{:S(2)}, u32[]{:S(2)}) collective-permute-start(f32[64,128]{1,0:T(8,128)S(1)} %fusion.151), channel_id=1, source_target_pairs={{0,8},{4,12},{8,0},{12,4},{16,24},{20,28},{24,16},{28,20},{1,9},{5... | collective-permute-start | bytes 98312 | tf_op jit(solution)/shard_map/ppermute | solution.py:29
  52.5 4.8 %collective-permute-start.8 = (f32[64,128]{1,0:T(8,128)S(1)}, f32[64,128]{1,0:T(8,128)S(1)}, u32[]{:S(2)}, u32[]{:S(2)}) collective-permute-start(f32[64,128]{1,0:T(8,128)S(1)} %add.66), channel_id=1, source_target_pairs={{0,16},{4,20},{8,24},{12,28},{16,0},{20,4},{24,8},{28,12},{1,17},{... | collective-permute-start | bytes 98312 | tf_op jit(solution)/shard_map/ppermute | solution.py:29
  54.9 11.9 %collective-permute-start.11 = (f32[64,128]{1,0:T(8,128)S(1)}, f32[64,128]{1,0:T(8,128)S(1)}, u32[]{:S(2)}, u32[]{:S(2)}) collective-permute-start(f32[64,128]{1,0:T(8,128)S(1)} %add.69), channel_id=1, source_target_pairs={{0,16},{4,20},{8,24},{12,28},{16,0},{20,4},{24,8},{28,12},{1,17},{... | collective-permute-start | bytes 98312 | tf_op jit(solution)/shard_map/ppermute | solution.py:29
  65.2 1.2 %copy-start.1 = (f32[64,128]{1,0:T(8,128)S(1)}, f32[64,128]{1,0:T(8,128)}, u32[]{:S(2)}) copy-start(f32[64,128]{1,0:T(8,128)} %shard_map.18) | copy-start | bytes 98308

commit v8 on v7

--- a/solution.py
+++ b/solution.py
@@ -38,11 +38,14 @@
     return approx
 
 
-def _eliminate_kernel(aug_ref, out_ref):
-    size, wide = aug_ref.shape
+def _eliminate_kernel(head_ref, out_ref):
+    size = out_ref.shape[0]
+    wide = 2 * size
     rows = lax.broadcasted_iota(jnp.int32, (size, wide), 0)
+    lanes = lax.broadcasted_iota(jnp.int32, (size, wide), 1)
     row_ids = lax.broadcasted_iota(jnp.int32, (size, 1), 0)
-    work = aug_ref[...]
+    work = head_ref[:, :wide]
+    work = jnp.where(lanes < size, work, (lanes == rows + size).astype(jnp.float32))
     for j in range(size):
         row = work[j:j + 1, :]
         pivot = row[:, j:j + 1]
@@ -51,16 +54,14 @@
         scaled = row * scale
         weight = jnp.where(row_ids > j, work[:, j:j + 1] * scale, 0.0)
         work = jnp.where(rows == j, scaled, work - weight * scaled)
-    out_ref[...] = work
+    out_ref[...] = work[:, size:]
 
 
-def lower_inverse(gram):
-    size = gram.shape[0]
-    aug = jnp.concatenate([gram, jnp.eye(size, dtype=jnp.float32)], axis=1)
-    out = pl.pallas_call(
-        _eliminate_kernel, out_shape=jax.ShapeDtypeStruct(aug.shape, jnp.float32)
-    )(aug)
-    return out[:, size:]
+def lower_inverse(head):
+    size = head.shape[0]
+    return pl.pallas_call(
+        _eliminate_kernel, out_shape=jax.ShapeDtypeStruct((size, size), jnp.float32)
+    )(head)
 
 
 def make_local(rows_size):
@@ -85,7 +86,7 @@
         tail = jnp.concatenate([inner_rows(panel_0, both), inner_rows(units[0], both)], axis=1)
         steps = butterfly_steps(rows_size)
         tail = butterfly_sum(tail, "rows", rows_size, None if steps is None else steps[:-1])
-        lower_inv, tail = lax.optimization_barrier((lower_inverse(head[:, :width]), tail))
+        lower_inv, tail = lax.optimization_barrier((lower_inverse(head), tail))
         tail = butterfly_sum(tail, "rows", rows_size, None if steps is None else steps[-1:])
         top_rows = head[:, width:]
         basis_cur, basis_sec, unit_cur, unit_sec = (
@@ -108,9 +109,9 @@
             "rows",
             rows_size,
         )
-        gram, top_rows = head[:, :width], head[:, width:]
+        top_rows = head[:, width:]
         basis_cur, unit_cur = tail[:, :width], tail[:, width:]
-        lower_inv = lower_inverse(gram)
+        lower_inv = lower_inverse(head)
         top_block = apply_left(lower_inv, top_rows)
         inverse = invert_near_identity(identity - top_block.T)
         reflect = units[1] - apply_left(lower_inv, panel_1)

time: 71.6 us -> 71.3 us (level)
  waiting for transfers between devices: 9.98 us -> 11 us
  starting transfers between devices: 19.6 us -> 18.6 us
    concatenate x2 -> x0, other arithmetic: 1.39 us -> none  [lower_inverse(): aug = jnp.concatenate([gram, jnp.eye(size, dtype=jnp.float32)], axis=1)]
    add x12, other arithmetic: 0.15 us -> 1.38 us  [butterfly_sum(): x = x + lax.ppermute(x, axis, [(i, i ^ step) for i in range(size)])]
    ppermute x12, waiting for transfers between devices: 9.98 us -> 11 us  [butterfly_sum(): x = x + lax.ppermute(x, axis, [(i, i ^ step) for i in range(size)])]
    ppermute x12, starting transfers between devices: 19.6 us -> 18.6 us  [butterfly_sum(): x = x + lax.ppermute(x, axis, [(i, i ^ step) for i in range(size)])]
    slice x1 -> x0, local copies, waits for them, and re-layouts: 0.83 us -> none  [lower_inverse(): return out[:, size:]]
    unnamed x4 -> x10, local copies, waits for them, and re-layouts: 0.88 us -> 1.64 us
  transfers between devices with their start and end apart: 12 -> 12, of which waited for: 6 -> 6; matrix products, arithmetic and copies ran while one was open for 10% -> 9% of each run, Pallas kernels for 20% -> 20%
where the time goes in v8:
time: 71.3 us; the launch traced here: 70.9 us
  starting transfers between devices  18.6 us (26%)
  Pallas kernels  14.5 us (20%)
  matrix products  12.9 us (18%)
  waiting for transfers between devices  11 us (15%)
  blocking collectives  10.3 us (14%)
  local copies, waits for them, and re-layouts  1.67 us (2%)
  other arithmetic  1.52 us (2%)
    ppermute x12, starting transfers between devices, butterfly_sum(): x = x + lax.ppermute(x, axis, [(i, i ^ step) for i in range(size)])  18.6 us
    pallas_call x2, Pallas kernels, lower_inverse(): pl.pallas_call(_eliminate_kernel, out_shape=jax.ShapeDtypeStruct((size, s...  14.5 us
    ppermute x12, waiting for transfers between devices, butterfly_sum(): x = x + lax.ppermute(x, axis, [(i, i ^ step) for i in range(size)])  11 us
    all_gather x1, blocking collectives, local(): gathered = lax.all_gather(current, 'cols')  10.3 us
    dot_general x42, matrix products, apply_left(): return jnp.dot(square, right_side, precision=HIGHEST_PRECISION)  8.61 us
    dot_general x6, matrix products, inner_rows(): lax.dot_general(left, right, (((1,), (1,)), ((), ())), precision=HIGHEST_...  2.51 us
    unnamed x10, local copies, waits for them, and re-layouts  1.64 us
  transfers between devices with their start and end apart: 12, of which 6 were waited for; matrix products, arithmetic and copies ran while one was open for 9% of the time, Pallas kernels for 20%

profile of v8, /device:TPU:0, one launch (start us, length us, event | category | flops | bytes accessed | tf_op | source)
XLA Modules:
  0.0 70.9 jit_solution(18225059006701572103)
XLA Ops:
  0.0 10.3 %all_gather.3 = f32[4,64,768]{2,1,0:T(8,128)S(1)} all-gather(f32[1,64,768]{2,1,0:T(8,128)} %param.1), channel_id=1, replica_groups=mesh['rows'=8,'cols'=4] {'cols'}, dimensions={0}, use_global_device_ids=true | all-gather | bytes 983040 | tf_op jit(solution)/shard_map/all_gather | solution.py:78
  10.3 0.9 %copy-done = f32[1,64,768]{2,1,0:T(8,128)S(1)} copy-done((f32[1,64,768]{2,1,0:T(8,128)S(1)}, f32[1,64,768]{2,1,0:T(8,128)}, u32[]{:S(2)}) %copy-start) | copy-done | bytes 196632
  11.2 0.5 convolution_bitcast_fusion
  11.7 0.4 fusion.9
  12.1 1.6 %collective-permute-start.3 = (f32[64,256]{1,0:T(8,128)S(1)}, f32[64,256]{1,0:T(8,128)S(1)}, u32[]{:S(2)}, u32[]{:S(2)}) collective-permute-start(f32[64,256]{1,0:T(8,128)S(1)} %pad_maximum_fusion.3), channel_id=1, source_target_pairs={{0,4},{4,0},{8,12},{12,8},{16,20},{20,16},{24,28},{28,24},{1,5},{5... | collective-permute-start | bytes 196616 | tf_op jit(solution)/shard_map/ppermute | solution.py:29
  13.7 0.5 convolution_bitcast_fusion.1
  14.2 0.6 collective-permute-start
  14.8 3.4 %collective-permute-done = f32[64,128]{1,0:T(8,128)S(1)} collective-permute-done((f32[64,128]{1,0:T(8,128)S(1)}, f32[64,128]{1,0:T(8,128)S(1)}, u32[]{:S(2)}, u32[]{:S(2)}) %collective-permute-start) | collective-permute-done | bytes 32800 | tf_op jit(solution)/shard_map/ppermute | solution.py:29
  18.2 1.6 %collective-permute-start.1 = (f32[64,128]{1,0:T(8,128)S(1)}, f32[64,128]{1,0:T(8,128)S(1)}, u32[]{:S(2)}, u32[]{:S(2)}) collective-permute-start(f32[64,128]{1,0:T(8,128)S(1)} %add.59), channel_id=1, source_target_pairs={{0,8},{4,12},{8,0},{12,4},{16,24},{20,28},{24,16},{28,20},{1,9},{5... | collective-permute-start | bytes 98312 | tf_op jit(solution)/shard_map/ppermute | solution.py:29
  19.8 0.5 collective-permute-start.4
  20.3 1.8 %collective-permute-done.1 = f32[64,128]{1,0:T(8,128)S(1)} collective-permute-done((f32[64,128]{1,0:T(8,128)S(1)}, f32[64,128]{1,0:T(8,128)S(1)}, u32[]{:S(2)}, u32[]{:S(2)}) %collective-permute-start.1) | collective-permute-done | bytes 32800 | tf_op jit(solution)/shard_map/ppermute | solution.py:29
  22.2 2.6 %collective-permute-start.2 = (f32[64,128]{1,0:T(8,128)S(1)}, f32[64,128]{1,0:T(8,128)S(1)}, u32[]{:S(2)}, u32[]{:S(2)}) collective-permute-start(f32[64,128]{1,0:T(8,128)S(1)} %add.60), channel_id=1, source_target_pairs={{0,16},{4,20},{8,24},{12,28},{16,0},{20,4},{24,8},{28,12},{1,17},{... | collective-permute-start | bytes 98312 | tf_op jit(solution)/shard_map/ppermute | solution.py:29
  24.8 2.2 %collective-permute-done.2 = f32[64,128]{1,0:T(8,128)S(1)} collective-permute-done((f32[64,128]{1,0:T(8,128)S(1)}, f32[64,128]{1,0:T(8,128)S(1)}, u32[]{:S(2)}, u32[]{:S(2)}) %collective-permute-start.2) | collective-permute-done | bytes 32800 | tf_op jit(solution)/shard_map/ppermute | solution.py:29
  27.0 0.6 add.61.head_ref
  27.6 7.2 %shard_map.17 = f32[64,64]{1,0:T(8,128)} custom-call(f32[64,128]{1,0:T(8,128)} %add.61.head_ref), custom_call_target="tpu_custom_call" | custom-call | tf_op jit(solution)/shard_map/pallas_call | solution.py:62
  34.9 0.7 %copy-done.1 = f32[64,64]{1,0:T(8,128)S(1)} copy-done((f32[64,64]{1,0:T(8,128)S(1)}, f32[64,64]{1,0:T(8,128)}, u32[]{:S(2)}) %copy-start.1) | copy-done | bytes 16408
  36.2 2.7 %collective-permute-start.5 = (f32[64,256]{1,0:T(8,128)S(1)}, f32[64,256]{1,0:T(8,128)S(1)}, u32[]{:S(2)}, u32[]{:S(2)}) collective-permute-start(f32[64,256]{1,0:T(8,128)S(1)} %add.63), channel_id=1, source_target_pairs={{0,16},{4,20},{8,24},{12,28},{16,0},{20,4},{24,8},{28,12},{1,17},{... | collective-permute-start | bytes 196616 | tf_op jit(solution)/shard_map/ppermute | solution.py:29
  42.6 0.4 convolution_subtract_fusion.3
  43.2 0.4 fusion.1
  43.9 0.5 fusion.5
  44.4 1.0 %collective-permute-start.6 = (f32[64,128]{1,0:T(8,128)S(1)}, f32[64,128]{1,0:T(8,128)S(1)}, u32[]{:S(2)}, u32[]{:S(2)}) collective-permute-start(f32[64,128]{1,0:T(8,128)S(1)} %fusion.5), channel_id=1, source_target_pairs={{0,4},{4,0},{8,12},{12,8},{16,20},{20,16},{24,28},{28,24},{1,5},{5... | collective-permute-start | bytes 98312 | tf_op jit(solution)/shard_map/ppermute | solution.py:29
  45.5 1.1 %collective-permute-start.9 = (f32[64,128]{1,0:T(8,128)S(1)}, f32[64,128]{1,0:T(8,128)S(1)}, u32[]{:S(2)}, u32[]{:S(2)}) collective-permute-start(f32[64,128]{1,0:T(8,128)S(1)} %pad_maximum_fusion.4), channel_id=1, source_target_pairs={{0,4},{4,0},{8,12},{12,8},{16,20},{20,16},{24,28},{28,24},{1,5},{5... | collective-permute-start | bytes 98312 | tf_op jit(solution)/shard_map/ppermute | solution.py:29
  46.6 1.8 %collective-permute-done.6 = f32[64,128]{1,0:T(8,128)S(1)} collective-permute-done((f32[64,128]{1,0:T(8,128)S(1)}, f32[64,128]{1,0:T(8,128)S(1)}, u32[]{:S(2)}, u32[]{:S(2)}) %collective-permute-start.6) | collective-permute-done | bytes 32800 | tf_op jit(solution)/shard_map/ppermute | solution.py:29
  48.4 1.8 %collective-permute-start.7 = (f32[64,128]{1,0:T(8,128)S(1)}, f32[64,128]{1,0:T(8,128)S(1)}, u32[]{:S(2)}, u32[]{:S(2)}) collective-permute-start(f32[64,128]{1,0:T(8,128)S(1)} %add.65), channel_id=1, source_target_pairs={{0,8},{4,12},{8,0},{12,4},{16,24},{20,28},{24,16},{28,20},{1,9},{5... | collective-permute-start | bytes 98312 | tf_op jit(solution)/shard_map/ppermute | solution.py:29
  50.3 0.7 %collective-permute-start.10 = (f32[64,128]{1,0:T(8,128)S(1)}, f32[64,128]{1,0:T(8,128)S(1)}, u32[]{:S(2)}, u32[]{:S(2)}) collective-permute-start(f32[64,128]{1,0:T(8,128)S(1)} %fusion.132), channel_id=1, source_target_pairs={{0,8},{4,12},{8,0},{12,4},{16,24},{20,28},{24,16},{28,20},{1,9},{5... | collective-permute-start | bytes 98312 | tf_op jit(solution)/shard_map/ppermute | solution.py:29
  51.0 1.4 %collective-permute-done.7 = f32[64,128]{1,0:T(8,128)S(1)} collective-permute-done((f32[64,128]{1,0:T(8,128)S(1)}, f32[64,128]{1,0:T(8,128)S(1)}, u32[]{:S(2)}, u32[]{:S(2)}) %collective-permute-start.7) | collective-permute-done | bytes 32800 | tf_op jit(solution)/shard_map/ppermute | solution.py:29
  52.5 2.4 %collective-permute-start.8 = (f32[64,128]{1,0:T(8,128)S(1)}, f32[64,128]{1,0:T(8,128)S(1)}, u32[]{:S(2)}, u32[]{:S(2)}) collective-permute-start(f32[64,128]{1,0:T(8,128)S(1)} %add.66), channel_id=1, source_target_pairs={{0,16},{4,20},{8,24},{12,28},{16,0},{20,4},{24,8},{28,12},{1,17},{... | collective-permute-start | bytes 98312 | tf_op jit(solution)/shard_map/ppermute | solution.py:29
  54.8 2.1 %collective-permute-start.11 = (f32[64,128]{1,0:T(8,128)S(1)}, f32[64,128]{1,0:T(8,128)S(1)}, u32[]{:S(2)}, u32[]{:S(2)}) collective-permute-start(f32[64,128]{1,0:T(8,128)S(1)} %add.69), channel_id=1, source_target_pairs={{0,16},{4,20},{8,24},{12,28},{16,0},{20,4},{24,8},{28,12},{1,17},{... | collective-permute-start | bytes 98312 | tf_op jit(solution)/shard_map/ppermute | solution.py:29
  57.3 0.6 add.67.head_ref
  57.9 7.2 %shard_map.18 = f32[64,64]{1,0:T(8,128)} custom-call(f32[64,128]{1,0:T(8,128)} %add.67.head_ref), custom_call_target="tpu_custom_call" | custom-call | tf_op jit(solution)/shard_map/pallas_call | solution.py:62
  65.1 1.1 %convolution_subtract_fusion.1 = f32[64,768]{1,0:T(8,128)S(1)} fusion(f32[64,64]{1,0:T(8,128)} %shard_map.18, f32[64,768]{1,0:T(8,128)S(1)} %fusion.1, s32[768]{0:T(1024)S(1)} %fusion.40), kind=kOutput, calls=%fused_computation.2 | convolution fusion | flops 37896192 | bytes 412672 | tf_op jit(solution)/shard_map/dot_general | solution.py:15
  69.9 1.1 %fusion = f32[1,64,768]{2,1,0:T(8,128)} fusion(f32[64,768]{1,0:T(8,128)S(1)} %convolution_subtract_fusion.3, f32[64,64]{1,0:T(8,128)S(1)} %fusion.19, f32[64,768]{1,0:T(8,128)S(1)} %convolution_subtract_fusion.1), kind=kOutput, calls=%fused_computation.1 | convolution fusion | flops 37797888 | bytes 606208 | tf_op jit(solution)/shard_map/dot_general | solution.py:119
  (76 shorter events, 8.7 us)
Async XLA Ops:
  10.3 0.9 %copy-start = (f32[1,64,768]{2,1,0:T(8,128)S(1)}, f32[1,64,768]{2,1,0:T(8,128)}, u32[]{:S(2)}) copy-start(f32[1,64,768]{2,1,0:T(8,128)} %param.1) | copy-start | bytes 589828
  12.1 7.7 %collective-permute-start.3 = (f32[64,256]{1,0:T(8,128)S(1)}, f32[64,256]{1,0:T(8,128)S(1)}, u32[]{:S(2)}, u32[]{:S(2)}) collective-permute-start(f32[64,256]{1,0:T(8,128)S(1)} %pad_maximum_fusion.3), channel_id=1, source_target_pairs={{0,4},{4,0},{8,12},{12,8},{16,20},{20,16},{24,28},{28,24},{1,5},{5... | collective-permute-start | bytes 196616 | tf_op jit(solution)/shard_map/ppermute | solution.py:29
  14.2 4.0 %collective-permute-start = (f32[64,128]{1,0:T(8,128)S(1)}, f32[64,128]{1,0:T(8,128)S(1)}, u32[]{:S(2)}, u32[]{:S(2)}) collective-permute-start(f32[64,128]{1,0:T(8,128)S(1)} %convolution_bitcast_fusion.1), channel_id=1, source_target_pairs={{0,4},{4,0},{8,12},{12,8},{16,20},{20,16},{24,28},{28,24},{1,5},{5... | collective-permute-start | bytes 98312 | tf_op jit(solution)/shard_map/ppermute | solution.py:29
  18.2 3.9 %collective-permute-start.1 = (f32[64,128]{1,0:T(8,128)S(1)}, f32[64,128]{1,0:T(8,128)S(1)}, u32[]{:S(2)}, u32[]{:S(2)}) collective-permute-start(f32[64,128]{1,0:T(8,128)S(1)} %add.59), channel_id=1, source_target_pairs={{0,8},{4,12},{8,0},{12,4},{16,24},{20,28},{24,16},{28,20},{1,9},{5... | collective-permute-start | bytes 98312 | tf_op jit(solution)/shard_map/ppermute | solution.py:29
  19.8 15.0 %collective-permute-start.4 = (f32[64,256]{1,0:T(8,128)S(1)}, f32[64,256]{1,0:T(8,128)S(1)}, u32[]{:S(2)}, u32[]{:S(2)}) collective-permute-start(f32[64,256]{1,0:T(8,128)S(1)} %fusion.50), channel_id=1, source_target_pairs={{0,8},{4,12},{8,0},{12,4},{16,24},{20,28},{24,16},{28,20},{1,9},{5... | collective-permute-start | bytes 196616 | tf_op jit(solution)/shard_map/ppermute | solution.py:29
  22.2 4.8 %collective-permute-start.2 = (f32[64,128]{1,0:T(8,128)S(1)}, f32[64,128]{1,0:T(8,128)S(1)}, u32[]{:S(2)}, u32[]{:S(2)}) collective-permute-start(f32[64,128]{1,0:T(8,128)S(1)} %add.60), channel_id=1, source_target_pairs={{0,16},{4,20},{8,24},{12,28},{16,0},{20,4},{24,8},{28,12},{1,17},{... | collective-permute-start | bytes 98312 | tf_op jit(solution)/shard_map/ppermute | solution.py:29
  34.8 0.8 %copy-start.1 = (f32[64,64]{1,0:T(8,128)S(1)}, f32[64,64]{1,0:T(8,128)}, u32[]{:S(2)}) copy-start(f32[64,64]{1,0:T(8,128)} %shard_map.17) | copy-start | bytes 49156
  34.8 0.8 %copy-start.3 = (f32[64,128]{1,0:T(8,128)S(1)}, f32[64,128]{1,0:T(8,128)}, u32[]{:S(2)}) copy-start(f32[64,128]{1,0:T(8,128)} %add.61.head_ref) | copy-start | bytes 98308
  36.2 5.5 %collective-permute-start.5 = (f32[64,256]{1,0:T(8,128)S(1)}, f32[64,256]{1,0:T(8,128)S(1)}, u32[]{:S(2)}, u32[]{:S(2)}) collective-permute-start(f32[64,256]{1,0:T(8,128)S(1)} %add.63), channel_id=1, source_target_pairs={{0,16},{4,20},{8,24},{12,28},{16,0},{20,4},{24,8},{28,12},{1,17},{... | collective-permute-start | bytes 196616 | tf_op jit(solution)/shard_map/ppermute | solution.py:29
  44.4 4.0 %collective-permute-start.6 = (f32[64,128]{1,0:T(8,128)S(1)}, f32[64,128]{1,0:T(8,128)S(1)}, u32[]{:S(2)}, u32[]{:S(2)}) collective-permute-start(f32[64,128]{1,0:T(8,128)S(1)} %fusion.5), channel_id=1, source_target_pairs={{0,4},{4,0},{8,12},{12,8},{16,20},{20,16},{24,28},{28,24},{1,5},{5... | collective-permute-start | bytes 98312 | tf_op jit(solution)/shard_map/ppermute | solution.py:29
  45.5 4.7 %collective-permute-start.9 = (f32[64,128]{1,0:T(8,128)S(1)}, f32[64,128]{1,0:T(8,128)S(1)}, u32[]{:S(2)}, u32[]{:S(2)}) collective-permute-start(f32[64,128]{1,0:T(8,128)S(1)} %pad_maximum_fusion.4), channel_id=1, source_target_pairs={{0,4},{4,0},{8,12},{12,8},{16,20},{20,16},{24,28},{28,24},{1,5},{5... | collective-permute-start | bytes 98312 | tf_op jit(solution)/shard_map/ppermute | solution.py:29
  48.4 4.0 %collective-permute-start.7 = (f32[64,128]{1,0:T(8,128)S(1)}, f32[64,128]{1,0:T(8,128)S(1)}, u32[]{:S(2)}, u32[]{:S(2)}) collective-permute-start(f32[64,128]{1,0:T(8,128)S(1)} %add.65), channel_id=1, source_target_pairs={{0,8},{4,12},{8,0},{12,4},{16,24},{20,28},{24,16},{28,20},{1,9},{5... | collective-permute-start | bytes 98312 | tf_op jit(solution)/shard_map/ppermute | solution.py:29
  50.3 4.5 %collective-permute-start.10 = (f32[64,128]{1,0:T(8,128)S(1)}, f32[64,128]{1,0:T(8,128)S(1)}, u32[]{:S(2)}, u32[]{:S(2)}) collective-permute-start(f32[64,128]{1,0:T(8,128)S(1)} %fusion.132), channel_id=1, source_target_pairs={{0,8},{4,12},{8,0},{12,4},{16,24},{20,28},{24,16},{28,20},{1,9},{5... | collective-permute-start | bytes 98312 | tf_op jit(solution)/shard_map/ppermute | solution.py:29
  52.5 4.8 %collective-permute-start.8 = (f32[64,128]{1,0:T(8,128)S(1)}, f32[64,128]{1,0:T(8,128)S(1)}, u32[]{:S(2)}, u32[]{:S(2)}) collective-permute-start(f32[64,128]{1,0:T(8,128)S(1)} %add.66), channel_id=1, source_target_pairs={{0,16},{4,20},{8,24},{12,28},{16,0},{20,4},{24,8},{28,12},{1,17},{... | collective-permute-start | bytes 98312 | tf_op jit(solution)/shard_map/ppermute | solution.py:29
  54.8 11.8 %collective-permute-start.11 = (f32[64,128]{1,0:T(8,128)S(1)}, f32[64,128]{1,0:T(8,128)S(1)}, u32[]{:S(2)}, u32[]{:S(2)}) collective-permute-start(f32[64,128]{1,0:T(8,128)S(1)} %add.69), channel_id=1, source_target_pairs={{0,16},{4,20},{8,24},{12,28},{16,0},{20,4},{24,8},{28,12},{1,17},{... | collective-permute-start | bytes 98312 | tf_op jit(solution)/shard_map/ppermute | solution.py:29
  65.1 1.1 %copy-start.2 = (f32[64,64]{1,0:T(8,128)S(1)}, f32[64,64]{1,0:T(8,128)}, u32[]{:S(2)}) copy-start(f32[64,64]{1,0:T(8,128)} %shard_map.18) | copy-start | bytes 49156
  65.1 1.2 %copy-start.4 = (f32[64,128]{1,0:T(8,128)S(1)}, f32[64,128]{1,0:T(8,128)}, u32[]{:S(2)}) copy-start(f32[64,128]{1,0:T(8,128)} %add.67.head_ref) | copy-start | bytes 98308

commit v9 on v8

--- a/solution.py
+++ b/solution.py
@@ -64,7 +64,34 @@
     )(head)
 
 
-def make_local(rows_size):
+def spread_pair(block, axis, size):
+    index = lax.axis_index(axis)
+    have = block
+    dist = size // 2
+    while dist >= 2:
+        got = lax.ppermute(
+            have, axis, [(i, i + dist) for i in range(size) if i % (2 * dist) < 2]
+        )
+        have = jnp.where(index % (2 * dist) >= dist, got, have)
+        dist //= 2
+    other = lax.ppermute(have, axis, [(i, i ^ 1) for i in range(size)])
+    even = index % 2 == 0
+    return jnp.where(even, have, other), jnp.where(even, other, have)
+
+
+def spread_root(value, axis, size):
+    index = lax.axis_index(axis)
+    dist = size // 2
+    while dist >= 1:
+        got = lax.ppermute(
+            value, axis, [(i, i + dist) for i in range(size) if i % (2 * dist) == 0]
+        )
+        value = jnp.where(index % (2 * dist) == dist, got, value)
+        dist //= 2
+    return value
+
+
+def make_local(rows_size, cols_size):
     def local(matrix):
         block_count, width, local_rows = matrix.shape
         current = matrix.reshape(block_count * width, local_rows)
@@ -75,13 +102,20 @@
             (lanes == (global_rows - k * width)[None, :]).astype(jnp.float32) for k in range(2)
         ]
 
-        gathered = lax.all_gather(current, "cols")
-        panel_0 = gathered[0]
-        second = gathered[1]
+        if butterfly_steps(cols_size) is None:
+            gathered = lax.all_gather(current, "cols")
+            panel_0 = gathered[0]
+            second = gathered[1]
+            head = butterfly_sum(
+                inner_rows(panel_0, jnp.concatenate([panel_0, units[0]])), "rows", rows_size
+            )
+        else:
+            head = butterfly_sum(
+                inner_rows(current, jnp.concatenate([current, units[0]])), "rows", rows_size
+            )
+            panel_0, second = spread_pair(current, "cols", cols_size)
+            head = spread_root(head, "cols", cols_size)
 
-        head = butterfly_sum(
-            inner_rows(panel_0, jnp.concatenate([panel_0, units[0]])), "rows", rows_size
-        )
         both = jnp.concatenate([current, second])
         tail = jnp.concatenate([inner_rows(panel_0, both), inner_rows(units[0], both)], axis=1)
         steps = butterfly_steps(rows_size)
@@ -124,7 +158,7 @@
 
 def solution(mesh):
     return jax.shard_map(
-        make_local(mesh.shape["rows"]),
+        make_local(mesh.shape["rows"], mesh.shape["cols"]),
         mesh=mesh,
         in_specs=(P(None, "cols", "rows"),),
         out_specs=P(None, "cols", "rows"),

time: 71.3 us -> 70.6 us (level)
  blocking collectives: 10.3 us -> 0 us
  starting transfers between devices: 18.6 us -> 26.1 us
  waiting for transfers between devices: 11 us -> 14.5 us
  local copies, waits for them, and re-layouts: 1.67 us -> 0.02 us
    all_gather x1 -> x0, blocking collectives: 10.3 us -> none  [local(): gathered = lax.all_gather(current, 'cols')]
    ppermute x0 -> x4, starting transfers between devices: none -> 7.7 us  [the longest x1 5 us: spread_pair(): lax.ppermute(have, axis, [(i, i + dist) for i in range(size) if i % (2 *...]
    ppermute x12, waiting for transfers between devices: 11 us -> 14.5 us  [butterfly_sum(): x = x + lax.ppermute(x, axis, [(i, i ^ step) for i in range(size)])]
    unnamed x10, local copies, waits for them, and re-layouts: 1.64 us -> 0.02 us
  transfers between devices with their start and end apart: 12 -> 16, of which waited for: 6 -> 8; matrix products, arithmetic and copies ran while one was open for 9% -> 11% of each run, Pallas kernels for 20% -> 21%
where the time goes in v9:
time: 70.6 us; the launch traced here: 70.2 us
  starting transfers between devices  26.1 us (37%)
  waiting for transfers between devices  14.5 us (21%)
  Pallas kernels  14.5 us (21%)
  matrix products  12.9 us (18%)
  other arithmetic  1.57 us (2%)
    ppermute x12, starting transfers between devices, butterfly_sum(): x = x + lax.ppermute(x, axis, [(i, i ^ step) for i in range(size)])  18.5 us
    ppermute x12, waiting for transfers between devices, butterfly_sum(): x = x + lax.ppermute(x, axis, [(i, i ^ step) for i in range(size)])  14.5 us
    pallas_call x2, Pallas kernels, lower_inverse(): pl.pallas_call(_eliminate_kernel, out_shape=jax.ShapeDtypeStruct((size, s...  14.5 us
    dot_general x42, matrix products, apply_left(): return jnp.dot(square, right_side, precision=HIGHEST_PRECISION)  8.63 us
    ppermute x1, starting transfers between devices, spread_pair(): lax.ppermute(have, axis, [(i, i + dist) for i in range(size) if i % (2 *...  5 us
    ppermute x2, starting transfers between devices, spread_root(): lax.ppermute(value, axis, [(i, i + dist) for i in range(size) if i % (2 *...  2.62 us
    dot_general x6, matrix products, inner_rows(): lax.dot_general(left, right, (((1,), (1,)), ((), ())), precision=HIGHEST_...  2.52 us
    dot_general x2, matrix products, local(): current = current - jnp.dot(mixed.T, reflect, precision=HIGHEST_PRECISION)  1.43 us
  transfers between devices with their start and end apart: 16, of which 8 were waited for; matrix products, arithmetic and copies ran while one was open for 11% of the time, Pallas kernels for 21%

profile of v9, /device:TPU:0, one launch (start us, length us, event | category | flops | bytes accessed | tf_op | source)
XLA Modules:
  0.0 70.2 jit_solution(3543929163291104563)
XLA Ops:
  0.0 5.0 %collective-permute-start.5 = (f32[64,768]{1,0:T(8,128)}, f32[64,768]{1,0:T(8,128)S(1)}, u32[]{:S(2)}, u32[]{:S(2)}) collective-permute-start(f32[64,768]{1,0:T(8,128)} %bitcast.81), channel_id=1, source_target_pairs={{0,2},{1,3},{4,6},{5,7},{8,10},{9,11},{12,14},{13,15},{16,18},{17,... | collective-permute-start | bytes 589832 | tf_op jit(solution)/shard_map/ppermute | solution.py:72
  5.1 0.5 convolution_bitcast_fusion
  5.6 1.6 %collective-permute-start = (f32[64,128]{1,0:T(8,128)S(1)}, f32[64,128]{1,0:T(8,128)S(1)}, u32[]{:S(2)}, u32[]{:S(2)}) collective-permute-start(f32[64,128]{1,0:T(8,128)S(1)} %convolution_bitcast_fusion), channel_id=1, source_target_pairs={{0,4},{4,0},{8,12},{12,8},{16,20},{20,16},{24,28},{28,24},{1,5},{5... | collective-permute-start | bytes 98312 | tf_op jit(solution)/shard_map/ppermute | solution.py:29
  7.2 2.4 %collective-permute-done = f32[64,128]{1,0:T(8,128)S(1)} collective-permute-done((f32[64,128]{1,0:T(8,128)S(1)}, f32[64,128]{1,0:T(8,128)S(1)}, u32[]{:S(2)}, u32[]{:S(2)}) %collective-permute-start) | collective-permute-done | bytes 32800 | tf_op jit(solution)/shard_map/ppermute | solution.py:29
  9.6 1.6 %collective-permute-start.1 = (f32[64,128]{1,0:T(8,128)S(1)}, f32[64,128]{1,0:T(8,128)S(1)}, u32[]{:S(2)}, u32[]{:S(2)}) collective-permute-start(f32[64,128]{1,0:T(8,128)S(1)} %add.70), channel_id=1, source_target_pairs={{0,8},{4,12},{8,0},{12,4},{16,24},{20,28},{24,16},{28,20},{1,9},{5... | collective-permute-start | bytes 98312 | tf_op jit(solution)/shard_map/ppermute | solution.py:29
  11.3 2.2 %collective-permute-done.1 = f32[64,128]{1,0:T(8,128)S(1)} collective-permute-done((f32[64,128]{1,0:T(8,128)S(1)}, f32[64,128]{1,0:T(8,128)S(1)}, u32[]{:S(2)}, u32[]{:S(2)}) %collective-permute-start.1) | collective-permute-done | bytes 32800 | tf_op jit(solution)/shard_map/ppermute | solution.py:29
  13.5 2.8 %collective-permute-start.2 = (f32[64,128]{1,0:T(8,128)S(1)}, f32[64,128]{1,0:T(8,128)S(1)}, u32[]{:S(2)}, u32[]{:S(2)}) collective-permute-start(f32[64,128]{1,0:T(8,128)S(1)} %add.71), channel_id=1, source_target_pairs={{0,16},{4,20},{8,24},{12,28},{16,0},{20,4},{24,8},{28,12},{1,17},{... | collective-permute-start | bytes 98312 | tf_op jit(solution)/shard_map/ppermute | solution.py:29
  16.3 2.0 %collective-permute-done.2 = f32[64,128]{1,0:T(8,128)S(1)} collective-permute-done((f32[64,128]{1,0:T(8,128)S(1)}, f32[64,128]{1,0:T(8,128)S(1)}, u32[]{:S(2)}, u32[]{:S(2)}) %collective-permute-start.2) | collective-permute-done | bytes 32800 | tf_op jit(solution)/shard_map/ppermute | solution.py:29
  18.3 1.3 %collective-permute-start.3 = (f32[64,128]{1,0:T(8,128)S(1)}, f32[64,128]{1,0:T(8,128)S(1)}, u32[]{:S(2)}, u32[]{:S(2)}) collective-permute-start(f32[64,128]{1,0:T(8,128)S(1)} %add.72), channel_id=1, source_target_pairs={{0,2},{4,6},{8,10},{12,14},{16,18},{20,22},{24,26},{28,30}} | collective-permute-start | bytes 98312 | tf_op jit(solution)/shard_map/ppermute | solution.py:86
  20.1 0.5 fusion.8
  20.6 1.6 %collective-permute-start.7 = (f32[64,256]{1,0:T(8,128)S(1)}, f32[64,256]{1,0:T(8,128)S(1)}, u32[]{:S(2)}, u32[]{:S(2)}) collective-permute-start(f32[64,256]{1,0:T(8,128)S(1)} %pad_maximum_fusion.5), channel_id=1, source_target_pairs={{0,4},{4,0},{8,12},{12,8},{16,20},{20,16},{24,28},{28,24},{1,5},{5... | collective-permute-start | bytes 196616 | tf_op jit(solution)/shard_map/ppermute | solution.py:29
  22.2 1.3 %collective-permute-start.4 = (f32[64,128]{1,0:T(8,128)S(1)}, f32[64,128]{1,0:T(8,128)S(1)}, u32[]{:S(2)}, u32[]{:S(2)}) collective-permute-start(f32[64,128]{1,0:T(8,128)S(1)} %broadcast_select_fusion.5), channel_id=1, source_target_pairs={{0,1},{2,3},{4,5},{6,7},{8,9},{10,11},{12,13},{14,15},{16,17},{18,... | collective-permute-start | bytes 98312 | tf_op jit(solution)/shard_map/ppermute | solution.py:86
  23.5 1.5 %collective-permute-done.7 = f32[64,256]{1,0:T(8,128)S(1)} collective-permute-done((f32[64,256]{1,0:T(8,128)S(1)}, f32[64,256]{1,0:T(8,128)S(1)}, u32[]{:S(2)}, u32[]{:S(2)}) %collective-permute-start.7) | collective-permute-done | bytes 65568 | tf_op jit(solution)/shard_map/ppermute | solution.py:29
  25.0 1.6 %collective-permute-start.8 = (f32[64,256]{1,0:T(8,128)S(1)}, f32[64,256]{1,0:T(8,128)S(1)}, u32[]{:S(2)}, u32[]{:S(2)}) collective-permute-start(f32[64,256]{1,0:T(8,128)S(1)} %fusion.49), channel_id=1, source_target_pairs={{0,8},{4,12},{8,0},{12,4},{16,24},{20,28},{24,16},{28,20},{1,9},{5... | collective-permute-start | bytes 196616 | tf_op jit(solution)/shard_map/ppermute | solution.py:29
  26.6 0.6 broadcast_select_fusion.6.head_ref
  27.2 7.2 %shard_map.17 = f32[64,64]{1,0:T(8,128)} custom-call(f32[64,128]{1,0:T(8,128)} %broadcast_select_fusion.6.head_ref), custom_call_target="tpu_custom_call" | custom-call | tf_op jit(solution)/shard_map/pallas_call | solution.py:62
  34.4 3.0 %collective-permute-start.9 = (f32[64,256]{1,0:T(8,128)S(1)}, f32[64,256]{1,0:T(8,128)S(1)}, u32[]{:S(2)}, u32[]{:S(2)}) collective-permute-start(f32[64,256]{1,0:T(8,128)S(1)} %add.74), channel_id=1, source_target_pairs={{0,16},{4,20},{8,24},{12,28},{16,0},{20,4},{24,8},{28,12},{1,17},{... | collective-permute-start | bytes 196616 | tf_op jit(solution)/shard_map/ppermute | solution.py:29
  43.1 0.5 fusion.3
  43.6 1.6 %collective-permute-start.10 = (f32[64,128]{1,0:T(8,128)S(1)}, f32[64,128]{1,0:T(8,128)S(1)}, u32[]{:S(2)}, u32[]{:S(2)}) collective-permute-start(f32[64,128]{1,0:T(8,128)S(1)} %fusion.3), channel_id=1, source_target_pairs={{0,4},{4,0},{8,12},{12,8},{16,20},{20,16},{24,28},{28,24},{1,5},{5... | collective-permute-start | bytes 98312 | tf_op jit(solution)/shard_map/ppermute | solution.py:29
  45.3 0.5 collective-permute-start.13
  45.8 1.8 %collective-permute-done.10 = f32[64,128]{1,0:T(8,128)S(1)} collective-permute-done((f32[64,128]{1,0:T(8,128)S(1)}, f32[64,128]{1,0:T(8,128)S(1)}, u32[]{:S(2)}, u32[]{:S(2)}) %collective-permute-start.10) | collective-permute-done | bytes 32800 | tf_op jit(solution)/shard_map/ppermute | solution.py:29
  47.6 0.4 collective-permute-start.11
  48.1 1.1 %collective-permute-done.13 = f32[64,128]{1,0:T(8,128)S(1)} collective-permute-done((f32[64,128]{1,0:T(8,128)S(1)}, f32[64,128]{1,0:T(8,128)S(1)}, u32[]{:S(2)}, u32[]{:S(2)}) %collective-permute-start.13) | collective-permute-done | bytes 32800 | tf_op jit(solution)/shard_map/ppermute | solution.py:29
  49.3 0.5 collective-permute-start.14
  49.7 1.8 %collective-permute-done.11 = f32[64,128]{1,0:T(8,128)S(1)} collective-permute-done((f32[64,128]{1,0:T(8,128)S(1)}, f32[64,128]{1,0:T(8,128)S(1)}, u32[]{:S(2)}, u32[]{:S(2)}) %collective-permute-start.11) | collective-permute-done | bytes 32800 | tf_op jit(solution)/shard_map/ppermute | solution.py:29
  51.5 1.7 %collective-permute-start.12 = (f32[64,128]{1,0:T(8,128)S(1)}, f32[64,128]{1,0:T(8,128)S(1)}, u32[]{:S(2)}, u32[]{:S(2)}) collective-permute-start(f32[64,128]{1,0:T(8,128)S(1)} %add.77), channel_id=1, source_target_pairs={{0,16},{4,20},{8,24},{12,28},{16,0},{20,4},{24,8},{28,12},{1,17},{... | collective-permute-start | bytes 98312 | tf_op jit(solution)/shard_map/ppermute | solution.py:29
  53.2 1.6 %collective-permute-start.15 = (f32[64,128]{1,0:T(8,128)S(1)}, f32[64,128]{1,0:T(8,128)S(1)}, u32[]{:S(2)}, u32[]{:S(2)}) collective-permute-start(f32[64,128]{1,0:T(8,128)S(1)} %add.80), channel_id=1, source_target_pairs={{0,16},{4,20},{8,24},{12,28},{16,0},{20,4},{24,8},{28,12},{1,17},{... | collective-permute-start | bytes 98312 | tf_op jit(solution)/shard_map/ppermute | solution.py:29
  54.9 1.7 %collective-permute-done.12 = f32[64,128]{1,0:T(8,128)S(1)} collective-permute-done((f32[64,128]{1,0:T(8,128)S(1)}, f32[64,128]{1,0:T(8,128)S(1)}, u32[]{:S(2)}, u32[]{:S(2)}) %collective-permute-start.12) | collective-permute-done | bytes 32800 | tf_op jit(solution)/shard_map/ppermute | solution.py:29
  56.6 0.6 add.78.head_ref
  57.2 7.2 %shard_map.18 = f32[64,64]{1,0:T(8,128)} custom-call(f32[64,128]{1,0:T(8,128)} %add.78.head_ref), custom_call_target="tpu_custom_call" | custom-call | tf_op jit(solution)/shard_map/pallas_call | solution.py:62
  64.5 1.1 %convolution_subtract_fusion.1 = f32[64,768]{1,0:T(8,128)S(1)} fusion(f32[64,64]{1,0:T(8,128)} %shard_map.18, f32[64,768]{1,0:T(8,128)S(1)} %fusion.1, s32[768]{0:T(1024)S(1)} %fusion.39), kind=kOutput, calls=%fused_computation.2 | convolution fusion | flops 37896192 | bytes 412672 | tf_op jit(solution)/shard_map/dot_general | solution.py:15
  69.2 1.1 %fusion = f32[1,64,768]{2,1,0:T(8,128)} fusion(f32[64,768]{1,0:T(8,128)S(1)} %convolution_subtract_fusion.3, f32[64,64]{1,0:T(8,128)S(1)} %fusion.18, f32[64,768]{1,0:T(8,128)S(1)} %convolution_subtract_fusion.1), kind=kOutput, calls=%fused_computation.1 | convolution fusion | flops 37797888 | bytes 606208 | tf_op jit(solution)/shard_map/dot_general | solution.py:153
  (86 shorter events, 9.6 us)
Async XLA Ops:
  0.0 5.1 %copy-start = (f32[1,64,768]{2,1,0:T(8,128)S(1)}, f32[1,64,768]{2,1,0:T(8,128)}, u32[]{:S(2)}) copy-start(f32[1,64,768]{2,1,0:T(8,128)} %param.1) | copy-start | bytes 589828
  0.0 11.2 %collective-permute-start.5 = (f32[64,768]{1,0:T(8,128)}, f32[64,768]{1,0:T(8,128)S(1)}, u32[]{:S(2)}, u32[]{:S(2)}) collective-permute-start(f32[64,768]{1,0:T(8,128)} %bitcast.81), channel_id=1, source_target_pairs={{0,2},{1,3},{4,6},{5,7},{8,10},{9,11},{12,14},{13,15},{16,18},{17,... | collective-permute-start | bytes 589832 | tf_op jit(solution)/shard_map/ppermute | solution.py:72
  5.6 4.0 %collective-permute-start = (f32[64,128]{1,0:T(8,128)S(1)}, f32[64,128]{1,0:T(8,128)S(1)}, u32[]{:S(2)}, u32[]{:S(2)}) collective-permute-start(f32[64,128]{1,0:T(8,128)S(1)} %convolution_bitcast_fusion), channel_id=1, source_target_pairs={{0,4},{4,0},{8,12},{12,8},{16,20},{20,16},{24,28},{28,24},{1,5},{5... | collective-permute-start | bytes 98312 | tf_op jit(solution)/shard_map/ppermute | solution.py:29
  9.6 3.9 %collective-permute-start.1 = (f32[64,128]{1,0:T(8,128)S(1)}, f32[64,128]{1,0:T(8,128)S(1)}, u32[]{:S(2)}, u32[]{:S(2)}) collective-permute-start(f32[64,128]{1,0:T(8,128)S(1)} %add.70), channel_id=1, source_target_pairs={{0,8},{4,12},{8,0},{12,4},{16,24},{20,28},{24,16},{28,20},{1,9},{5... | collective-permute-start | bytes 98312 | tf_op jit(solution)/shard_map/ppermute | solution.py:29
  11.2 8.5 %collective-permute-start.6 = (f32[64,768]{1,0:T(8,128)S(1)}, f32[64,768]{1,0:T(8,128)S(1)}, u32[]{:S(2)}, u32[]{:S(2)}) collective-permute-start(f32[64,768]{1,0:T(8,128)S(1)} %broadcast_select_fusion), channel_id=1, source_target_pairs={{0,1},{1,0},{2,3},{3,2},{4,5},{5,4},{6,7},{7,6},{8,9},{9,8},{10,11... | collective-permute-start | bytes 589832 | tf_op jit(solution)/shard_map/ppermute | solution.py:77
  13.5 4.8 %collective-permute-start.2 = (f32[64,128]{1,0:T(8,128)S(1)}, f32[64,128]{1,0:T(8,128)S(1)}, u32[]{:S(2)}, u32[]{:S(2)}) collective-permute-start(f32[64,128]{1,0:T(8,128)S(1)} %add.71), channel_id=1, source_target_pairs={{0,16},{4,20},{8,24},{12,28},{16,0},{20,4},{24,8},{28,12},{1,17},{... | collective-permute-start | bytes 98312 | tf_op jit(solution)/shard_map/ppermute | solution.py:29
  18.3 3.9 %collective-permute-start.3 = (f32[64,128]{1,0:T(8,128)S(1)}, f32[64,128]{1,0:T(8,128)S(1)}, u32[]{:S(2)}, u32[]{:S(2)}) collective-permute-start(f32[64,128]{1,0:T(8,128)S(1)} %add.72), channel_id=1, source_target_pairs={{0,2},{4,6},{8,10},{12,14},{16,18},{20,22},{24,26},{28,30}} | collective-permute-start | bytes 98312 | tf_op jit(solution)/shard_map/ppermute | solution.py:86
  20.6 4.3 %collective-permute-start.7 = (f32[64,256]{1,0:T(8,128)S(1)}, f32[64,256]{1,0:T(8,128)S(1)}, u32[]{:S(2)}, u32[]{:S(2)}) collective-permute-start(f32[64,256]{1,0:T(8,128)S(1)} %pad_maximum_fusion.5), channel_id=1, source_target_pairs={{0,4},{4,0},{8,12},{12,8},{16,20},{20,16},{24,28},{28,24},{1,5},{5... | collective-permute-start | bytes 196616 | tf_op jit(solution)/shard_map/ppermute | solution.py:29
  22.2 4.4 %collective-permute-start.4 = (f32[64,128]{1,0:T(8,128)S(1)}, f32[64,128]{1,0:T(8,128)S(1)}, u32[]{:S(2)}, u32[]{:S(2)}) collective-permute-start(f32[64,128]{1,0:T(8,128)S(1)} %broadcast_select_fusion.5), channel_id=1, source_target_pairs={{0,1},{2,3},{4,5},{6,7},{8,9},{10,11},{12,13},{14,15},{16,17},{18,... | collective-permute-start | bytes 98312 | tf_op jit(solution)/shard_map/ppermute | solution.py:86
  25.0 9.5 %collective-permute-start.8 = (f32[64,256]{1,0:T(8,128)S(1)}, f32[64,256]{1,0:T(8,128)S(1)}, u32[]{:S(2)}, u32[]{:S(2)}) collective-permute-start(f32[64,256]{1,0:T(8,128)S(1)} %fusion.49), channel_id=1, source_target_pairs={{0,8},{4,12},{8,0},{12,4},{16,24},{20,28},{24,16},{28,20},{1,9},{5... | collective-permute-start | bytes 196616 | tf_op jit(solution)/shard_map/ppermute | solution.py:29
  34.4 3.0 %copy-start.1 = (f32[64,64]{1,0:T(8,128)S(1)}, f32[64,64]{1,0:T(8,128)}, u32[]{:S(2)}) copy-start(f32[64,64]{1,0:T(8,128)} %shard_map.17) | copy-start | bytes 49156
  34.4 3.0 %copy-start.3 = (f32[64,128]{1,0:T(8,128)S(1)}, f32[64,128]{1,0:T(8,128)}, u32[]{:S(2)}) copy-start(f32[64,128]{1,0:T(8,128)} %broadcast_select_fusion.6.head_ref) | copy-start | bytes 98308
  34.4 6.5 %collective-permute-start.9 = (f32[64,256]{1,0:T(8,128)S(1)}, f32[64,256]{1,0:T(8,128)S(1)}, u32[]{:S(2)}, u32[]{:S(2)}) collective-permute-start(f32[64,256]{1,0:T(8,128)S(1)} %add.74), channel_id=1, source_target_pairs={{0,16},{4,20},{8,24},{12,28},{16,0},{20,4},{24,8},{28,12},{1,17},{... | collective-permute-start | bytes 196616 | tf_op jit(solution)/shard_map/ppermute | solution.py:29
  43.6 4.0 %collective-permute-start.10 = (f32[64,128]{1,0:T(8,128)S(1)}, f32[64,128]{1,0:T(8,128)S(1)}, u32[]{:S(2)}, u32[]{:S(2)}) collective-permute-start(f32[64,128]{1,0:T(8,128)S(1)} %fusion.3), channel_id=1, source_target_pairs={{0,4},{4,0},{8,12},{12,8},{16,20},{20,16},{24,28},{28,24},{1,5},{5... | collective-permute-start | bytes 98312 | tf_op jit(solution)/shard_map/ppermute | solution.py:29
  45.3 3.9 %collective-permute-start.13 = (f32[64,128]{1,0:T(8,128)S(1)}, f32[64,128]{1,0:T(8,128)S(1)}, u32[]{:S(2)}, u32[]{:S(2)}) collective-permute-start(f32[64,128]{1,0:T(8,128)S(1)} %pad_maximum_fusion.6), channel_id=1, source_target_pairs={{0,4},{4,0},{8,12},{12,8},{16,20},{20,16},{24,28},{28,24},{1,5},{5... | collective-permute-start | bytes 98312 | tf_op jit(solution)/shard_map/ppermute | solution.py:29
  47.6 3.9 %collective-permute-start.11 = (f32[64,128]{1,0:T(8,128)S(1)}, f32[64,128]{1,0:T(8,128)S(1)}, u32[]{:S(2)}, u32[]{:S(2)}) collective-permute-start(f32[64,128]{1,0:T(8,128)S(1)} %add.76), channel_id=1, source_target_pairs={{0,8},{4,12},{8,0},{12,4},{16,24},{20,28},{24,16},{28,20},{1,9},{5... | collective-permute-start | bytes 98312 | tf_op jit(solution)/shard_map/ppermute | solution.py:29
  49.3 4.0 %collective-permute-start.14 = (f32[64,128]{1,0:T(8,128)S(1)}, f32[64,128]{1,0:T(8,128)S(1)}, u32[]{:S(2)}, u32[]{:S(2)}) collective-permute-start(f32[64,128]{1,0:T(8,128)S(1)} %fusion.131), channel_id=1, source_target_pairs={{0,8},{4,12},{8,0},{12,4},{16,24},{20,28},{24,16},{28,20},{1,9},{5... | collective-permute-start | bytes 98312 | tf_op jit(solution)/shard_map/ppermute | solution.py:29
  51.5 5.0 %collective-permute-start.12 = (f32[64,128]{1,0:T(8,128)S(1)}, f32[64,128]{1,0:T(8,128)S(1)}, u32[]{:S(2)}, u32[]{:S(2)}) collective-permute-start(f32[64,128]{1,0:T(8,128)S(1)} %add.77), channel_id=1, source_target_pairs={{0,16},{4,20},{8,24},{12,28},{16,0},{20,4},{24,8},{28,12},{1,17},{... | collective-permute-start | bytes 98312 | tf_op jit(solution)/shard_map/ppermute | solution.py:29
  53.2 12.7 %collective-permute-start.15 = (f32[64,128]{1,0:T(8,128)S(1)}, f32[64,128]{1,0:T(8,128)S(1)}, u32[]{:S(2)}, u32[]{:S(2)}) collective-permute-start(f32[64,128]{1,0:T(8,128)S(1)} %add.80), channel_id=1, source_target_pairs={{0,16},{4,20},{8,24},{12,28},{16,0},{20,4},{24,8},{28,12},{1,17},{... | collective-permute-start | bytes 98312 | tf_op jit(solution)/shard_map/ppermute | solution.py:29
  64.5 1.1 %copy-start.2 = (f32[64,64]{1,0:T(8,128)S(1)}, f32[64,64]{1,0:T(8,128)}, u32[]{:S(2)}) copy-start(f32[64,64]{1,0:T(8,128)} %shard_map.18) | copy-start | bytes 49156
  64.5 1.2 %copy-start.4 = (f32[64,128]{1,0:T(8,128)S(1)}, f32[64,128]{1,0:T(8,128)}, u32[]{:S(2)}) copy-start(f32[64,128]{1,0:T(8,128)} %add.78.head_ref) | copy-start | bytes 98308

commit v10 on v9

--- a/solution.py
+++ b/solution.py
@@ -79,15 +79,11 @@
     return jnp.where(even, have, other), jnp.where(even, other, have)
 
 
-def spread_root(value, axis, size):
+def from_root(value, axis, size):
     index = lax.axis_index(axis)
-    dist = size // 2
-    while dist >= 1:
-        got = lax.ppermute(
-            value, axis, [(i, i + dist) for i in range(size) if i % (2 * dist) == 0]
-        )
-        value = jnp.where(index % (2 * dist) == dist, got, value)
-        dist //= 2
+    for k in range(1, size):
+        got = lax.ppermute(value, axis, [(0, k)])
+        value = jnp.where(index == k, got, value)
     return value
 
 
@@ -110,11 +106,9 @@
                 inner_rows(panel_0, jnp.concatenate([panel_0, units[0]])), "rows", rows_size
             )
         else:
-            head = butterfly_sum(
-                inner_rows(current, jnp.concatenate([current, units[0]])), "rows", rows_size
-            )
+            head = inner_rows(current, jnp.concatenate([current, units[0]]))
+            head = butterfly_sum(from_root(head, "cols", cols_size), "rows", rows_size)
             panel_0, second = spread_pair(current, "cols", cols_size)
-            head = spread_root(head, "cols", cols_size)
 
         both = jnp.concatenate([current, second])
         tail = jnp.concatenate([inner_rows(panel_0, both), inner_rows(units[0], both)], axis=1)

time: 70.6 us -> 69.6 us (0.986)
  waiting for transfers between devices: 14.5 us -> 9.99 us
  starting transfers between devices: 26.1 us -> 28.7 us
  local copies, waits for them, and re-layouts: 0.02 us -> 0.91 us
    ppermute x12, waiting for transfers between devices: 14.5 us -> 6.37 us  [butterfly_sum(): x = x + lax.ppermute(x, axis, [(i, i ^ step) for i in range(size)])]
    ppermute x1, starting transfers between devices: 5 us -> 1.3 us  [spread_pair(): lax.ppermute(have, axis, [(i, i + dist) for i in range(size) if i % (2 *...]
    ppermute x2 -> x3, starting transfers between devices: 2.62 us -> 6 us  [from_root(): got = lax.ppermute(value, axis, [(0, k)])]
    ppermute x12, starting transfers between devices: 18.5 us -> 21.3 us  [butterfly_sum(): x = x + lax.ppermute(x, axis, [(i, i ^ step) for i in range(size)])]
    ppermute x1, waiting for transfers between devices: 0.01 us -> 2.18 us  [spread_pair(): lax.ppermute(have, axis, [(i, i + dist) for i in range(size) if i % (2 *...]
    ppermute x2 -> x3, waiting for transfers between devices: 0.01 us -> 1.44 us  [from_root(): got = lax.ppermute(value, axis, [(0, k)])]
    unnamed x10, local copies, waits for them, and re-layouts: 0.02 us -> 0.91 us
  transfers between devices with their start and end apart: 16 -> 17, of which waited for: 8 -> 10; matrix products, arithmetic and copies ran while one was open for 11% -> 10% of each run, Pallas kernels for 21% -> 21%
where the time goes in v10:
time: 69.6 us; the launch traced here: 69.1 us
  starting transfers between devices  28.7 us (41%)
  Pallas kernels  14.5 us (21%)
  matrix products  12.9 us (19%)
  waiting for transfers between devices  9.99 us (14%)
  other arithmetic  1.58 us (2%)
  local copies, waits for them, and re-layouts  0.91 us (1%)
    ppermute x12, starting transfers between devices, butterfly_sum(): x = x + lax.ppermute(x, axis, [(i, i ^ step) for i in range(size)])  21.3 us
    pallas_call x2, Pallas kernels, lower_inverse(): pl.pallas_call(_eliminate_kernel, out_shape=jax.ShapeDtypeStruct((size, s...  14.5 us
    dot_general x42, matrix products, apply_left(): return jnp.dot(square, right_side, precision=HIGHEST_PRECISION)  8.63 us
    ppermute x12, waiting for transfers between devices, butterfly_sum(): x = x + lax.ppermute(x, axis, [(i, i ^ step) for i in range(size)])  6.37 us
    ppermute x3, starting transfers between devices, from_root(): got = lax.ppermute(value, axis, [(0, k)])  6 us
    dot_general x6, matrix products, inner_rows(): lax.dot_general(left, right, (((1,), (1,)), ((), ())), precision=HIGHEST_...  2.51 us
    ppermute x1, waiting for transfers between devices, spread_pair(): lax.ppermute(have, axis, [(i, i + dist) for i in range(size) if i % (2 *...  2.18 us
    ppermute x3, waiting for transfers between devices, from_root(): got = lax.ppermute(value, axis, [(0, k)])  1.44 us
  transfers between devices with their start and end apart: 17, of which 10 were waited for; matrix products, arithmetic and copies ran while one was open for 10% of the time, Pallas kernels for 21%

profile of v10, /device:TPU:0, one launch (start us, length us, event | category | flops | bytes accessed | tf_op | source)
XLA Modules:
  0.0 69.1 jit_solution(14798422681614632144)
XLA Ops:
  0.0 0.9 %copy-done = f32[1,64,768]{2,1,0:T(8,128)S(1)} copy-done((f32[1,64,768]{2,1,0:T(8,128)S(1)}, f32[1,64,768]{2,1,0:T(8,128)}, u32[]{:S(2)}) %copy-start) | copy-done | bytes 196632
  0.9 0.5 convolution_bitcast_fusion
  1.5 2.4 %collective-permute-start = (f32[64,128]{1,0:T(8,128)S(1)}, f32[64,128]{1,0:T(8,128)S(1)}, u32[]{:S(2)}, u32[]{:S(2)}) collective-permute-start(f32[64,128]{1,0:T(8,128)S(1)} %convolution_bitcast_fusion), channel_id=1, source_target_pairs={{0,1},{4,5},{8,9},{12,13},{16,17},{20,21},{24,25},{28,29}} | collective-permute-start | bytes 98312 | tf_op jit(solution)/shard_map/ppermute | solution.py:85
  3.8 0.8 %collective-permute-done = f32[64,128]{1,0:T(8,128)S(1)} collective-permute-done((f32[64,128]{1,0:T(8,128)S(1)}, f32[64,128]{1,0:T(8,128)S(1)}, u32[]{:S(2)}, u32[]{:S(2)}) %collective-permute-start) | collective-permute-done | bytes 32800 | tf_op jit(solution)/shard_map/ppermute | solution.py:85
  4.7 2.4 %collective-permute-start.1 = (f32[64,128]{1,0:T(8,128)S(1)}, f32[64,128]{1,0:T(8,128)S(1)}, u32[]{:S(2)}, u32[]{:S(2)}) collective-permute-start(f32[64,128]{1,0:T(8,128)S(1)} %broadcast_select_fusion.5), channel_id=1, source_target_pairs={{0,2},{4,6},{8,10},{12,14},{16,18},{20,22},{24,26},{28,30}} | collective-permute-start | bytes 98312 | tf_op jit(solution)/shard_map/ppermute | solution.py:85
  7.0 1.3 %collective-permute-start.6 = (f32[64,768]{1,0:T(8,128)S(1)}, f32[64,768]{1,0:T(8,128)S(1)}, u32[]{:S(2)}, u32[]{:S(2)}) collective-permute-start(f32[64,768]{1,0:T(8,128)S(1)} %bitcast.82), channel_id=1, source_target_pairs={{0,2},{1,3},{4,6},{5,7},{8,10},{9,11},{12,14},{13,15},{16,18},{17,... | collective-permute-start | bytes 589832 | tf_op jit(solution)/shard_map/ppermute | solution.py:72
  8.7 1.3 %collective-permute-start.2 = (f32[64,128]{1,0:T(8,128)S(1)}, f32[64,128]{1,0:T(8,128)S(1)}, u32[]{:S(2)}, u32[]{:S(2)}) collective-permute-start(f32[64,128]{1,0:T(8,128)S(1)} %broadcast_select_fusion.6), channel_id=1, source_target_pairs={{0,3},{4,7},{8,11},{12,15},{16,19},{20,23},{24,27},{28,31}} | collective-permute-start | bytes 98312 | tf_op jit(solution)/shard_map/ppermute | solution.py:85
  10.0 2.2 %collective-permute-done.6 = f32[64,768]{1,0:T(8,128)S(1)} collective-permute-done((f32[64,768]{1,0:T(8,128)S(1)}, f32[64,768]{1,0:T(8,128)S(1)}, u32[]{:S(2)}, u32[]{:S(2)}) %collective-permute-start.6) | collective-permute-done | bytes 196640 | tf_op jit(solution)/shard_map/ppermute | solution.py:72
  12.6 2.0 %collective-permute-start.3 = (f32[64,128]{1,0:T(8,128)S(1)}, f32[64,128]{1,0:T(8,128)S(1)}, u32[]{:S(2)}, u32[]{:S(2)}) collective-permute-start(f32[64,128]{1,0:T(8,128)S(1)} %broadcast_select_fusion.7), channel_id=1, source_target_pairs={{0,4},{4,0},{8,12},{12,8},{16,20},{20,16},{24,28},{28,24},{1,5},{5... | collective-permute-start | bytes 98312 | tf_op jit(solution)/shard_map/ppermute | solution.py:29
  14.5 2.0 %collective-permute-done.3 = f32[64,128]{1,0:T(8,128)S(1)} collective-permute-done((f32[64,128]{1,0:T(8,128)S(1)}, f32[64,128]{1,0:T(8,128)S(1)}, u32[]{:S(2)}, u32[]{:S(2)}) %collective-permute-start.3) | collective-permute-done | bytes 32800 | tf_op jit(solution)/shard_map/ppermute | solution.py:29
  16.5 2.0 %collective-permute-start.4 = (f32[64,128]{1,0:T(8,128)S(1)}, f32[64,128]{1,0:T(8,128)S(1)}, u32[]{:S(2)}, u32[]{:S(2)}) collective-permute-start(f32[64,128]{1,0:T(8,128)S(1)} %add.66), channel_id=1, source_target_pairs={{0,8},{4,12},{8,0},{12,4},{16,24},{20,28},{24,16},{28,20},{1,9},{5... | collective-permute-start | bytes 98312 | tf_op jit(solution)/shard_map/ppermute | solution.py:29
  18.9 0.5 fusion.8
  19.5 1.6 %collective-permute-start.8 = (f32[64,256]{1,0:T(8,128)S(1)}, f32[64,256]{1,0:T(8,128)S(1)}, u32[]{:S(2)}, u32[]{:S(2)}) collective-permute-start(f32[64,256]{1,0:T(8,128)S(1)} %pad_maximum_fusion.5), channel_id=1, source_target_pairs={{0,4},{4,0},{8,12},{12,8},{16,20},{20,16},{24,28},{28,24},{1,5},{5... | collective-permute-start | bytes 196616 | tf_op jit(solution)/shard_map/ppermute | solution.py:29
  21.1 2.7 %collective-permute-start.5 = (f32[64,128]{1,0:T(8,128)S(1)}, f32[64,128]{1,0:T(8,128)S(1)}, u32[]{:S(2)}, u32[]{:S(2)}) collective-permute-start(f32[64,128]{1,0:T(8,128)S(1)} %add.67), channel_id=1, source_target_pairs={{0,16},{4,20},{8,24},{12,28},{16,0},{20,4},{24,8},{28,12},{1,17},{... | collective-permute-start | bytes 98312 | tf_op jit(solution)/shard_map/ppermute | solution.py:29
  23.8 1.3 %collective-permute-start.9 = (f32[64,256]{1,0:T(8,128)S(1)}, f32[64,256]{1,0:T(8,128)S(1)}, u32[]{:S(2)}, u32[]{:S(2)}) collective-permute-start(f32[64,256]{1,0:T(8,128)S(1)} %fusion.49), channel_id=1, source_target_pairs={{0,8},{4,12},{8,0},{12,4},{16,24},{20,28},{24,16},{28,20},{1,9},{5... | collective-permute-start | bytes 196616 | tf_op jit(solution)/shard_map/ppermute | solution.py:29
  25.1 0.8 %collective-permute-done.5 = f32[64,128]{1,0:T(8,128)S(1)} collective-permute-done((f32[64,128]{1,0:T(8,128)S(1)}, f32[64,128]{1,0:T(8,128)S(1)}, u32[]{:S(2)}, u32[]{:S(2)}) %collective-permute-start.5) | collective-permute-done | bytes 32800 | tf_op jit(solution)/shard_map/ppermute | solution.py:29
  25.9 0.6 add.68.head_ref
  26.6 7.2 %shard_map.17 = f32[64,64]{1,0:T(8,128)} custom-call(f32[64,128]{1,0:T(8,128)} %add.68.head_ref), custom_call_target="tpu_custom_call" | custom-call | tf_op jit(solution)/shard_map/pallas_call | solution.py:62
  33.8 2.8 %collective-permute-start.10 = (f32[64,256]{1,0:T(8,128)S(1)}, f32[64,256]{1,0:T(8,128)S(1)}, u32[]{:S(2)}, u32[]{:S(2)}) collective-permute-start(f32[64,256]{1,0:T(8,128)S(1)} %add.72), channel_id=1, source_target_pairs={{0,16},{4,20},{8,24},{12,28},{16,0},{20,4},{24,8},{28,12},{1,17},{... | collective-permute-start | bytes 196616 | tf_op jit(solution)/shard_map/ppermute | solution.py:29
  42.8 1.2 %collective-permute-start.11 = (f32[64,128]{1,0:T(8,128)S(1)}, f32[64,128]{1,0:T(8,128)S(1)}, u32[]{:S(2)}, u32[]{:S(2)}) collective-permute-start(f32[64,128]{1,0:T(8,128)S(1)} %fusion.3), channel_id=1, source_target_pairs={{0,4},{4,0},{8,12},{12,8},{16,20},{20,16},{24,28},{28,24},{1,5},{5... | collective-permute-start | bytes 98312 | tf_op jit(solution)/shard_map/ppermute | solution.py:29
  44.1 0.9 %collective-permute-start.14 = (f32[64,128]{1,0:T(8,128)S(1)}, f32[64,128]{1,0:T(8,128)S(1)}, u32[]{:S(2)}, u32[]{:S(2)}) collective-permute-start(f32[64,128]{1,0:T(8,128)S(1)} %pad_maximum_fusion.6), channel_id=1, source_target_pairs={{0,4},{4,0},{8,12},{12,8},{16,20},{20,16},{24,28},{28,24},{1,5},{5... | collective-permute-start | bytes 98312 | tf_op jit(solution)/shard_map/ppermute | solution.py:29
  44.9 1.8 %collective-permute-done.11 = f32[64,128]{1,0:T(8,128)S(1)} collective-permute-done((f32[64,128]{1,0:T(8,128)S(1)}, f32[64,128]{1,0:T(8,128)S(1)}, u32[]{:S(2)}, u32[]{:S(2)}) %collective-permute-start.11) | collective-permute-done | bytes 32800 | tf_op jit(solution)/shard_map/ppermute | solution.py:29
  46.8 1.6 %collective-permute-start.12 = (f32[64,128]{1,0:T(8,128)S(1)}, f32[64,128]{1,0:T(8,128)S(1)}, u32[]{:S(2)}, u32[]{:S(2)}) collective-permute-start(f32[64,128]{1,0:T(8,128)S(1)} %add.74), channel_id=1, source_target_pairs={{0,8},{4,12},{8,0},{12,4},{16,24},{20,28},{24,16},{28,20},{1,9},{5... | collective-permute-start | bytes 98312 | tf_op jit(solution)/shard_map/ppermute | solution.py:29
  48.4 1.5 %collective-permute-start.15 = (f32[64,128]{1,0:T(8,128)S(1)}, f32[64,128]{1,0:T(8,128)S(1)}, u32[]{:S(2)}, u32[]{:S(2)}) collective-permute-start(f32[64,128]{1,0:T(8,128)S(1)} %fusion.131), channel_id=1, source_target_pairs={{0,8},{4,12},{8,0},{12,4},{16,24},{20,28},{24,16},{28,20},{1,9},{5... | collective-permute-start | bytes 98312 | tf_op jit(solution)/shard_map/ppermute | solution.py:29
  49.9 0.8 %collective-permute-done.12 = f32[64,128]{1,0:T(8,128)S(1)} collective-permute-done((f32[64,128]{1,0:T(8,128)S(1)}, f32[64,128]{1,0:T(8,128)S(1)}, u32[]{:S(2)}, u32[]{:S(2)}) %collective-permute-start.12) | collective-permute-done | bytes 32800 | tf_op jit(solution)/shard_map/ppermute | solution.py:29
  50.7 1.8 %collective-permute-start.13 = (f32[64,128]{1,0:T(8,128)S(1)}, f32[64,128]{1,0:T(8,128)S(1)}, u32[]{:S(2)}, u32[]{:S(2)}) collective-permute-start(f32[64,128]{1,0:T(8,128)S(1)} %add.75), channel_id=1, source_target_pairs={{0,16},{4,20},{8,24},{12,28},{16,0},{20,4},{24,8},{28,12},{1,17},{... | collective-permute-start | bytes 98312 | tf_op jit(solution)/shard_map/ppermute | solution.py:29
  52.5 2.1 %collective-permute-start.16 = (f32[64,128]{1,0:T(8,128)S(1)}, f32[64,128]{1,0:T(8,128)S(1)}, u32[]{:S(2)}, u32[]{:S(2)}) collective-permute-start(f32[64,128]{1,0:T(8,128)S(1)} %add.78), channel_id=1, source_target_pairs={{0,16},{4,20},{8,24},{12,28},{16,0},{20,4},{24,8},{28,12},{1,17},{... | collective-permute-start | bytes 98312 | tf_op jit(solution)/shard_map/ppermute | solution.py:29
  54.6 0.9 %collective-permute-done.13 = f32[64,128]{1,0:T(8,128)S(1)} collective-permute-done((f32[64,128]{1,0:T(8,128)S(1)}, f32[64,128]{1,0:T(8,128)S(1)}, u32[]{:S(2)}, u32[]{:S(2)}) %collective-permute-start.13) | collective-permute-done | bytes 32800 | tf_op jit(solution)/shard_map/ppermute | solution.py:29
  55.5 0.6 add.76.head_ref
  56.1 7.2 %shard_map.18 = f32[64,64]{1,0:T(8,128)} custom-call(f32[64,128]{1,0:T(8,128)} %add.76.head_ref), custom_call_target="tpu_custom_call" | custom-call | tf_op jit(solution)/shard_map/pallas_call | solution.py:62
  63.4 1.1 %convolution_subtract_fusion.1 = f32[64,768]{1,0:T(8,128)S(1)} fusion(f32[64,64]{1,0:T(8,128)} %shard_map.18, f32[64,768]{1,0:T(8,128)S(1)} %fusion.1, s32[768]{0:T(1024)S(1)} %fusion.39), kind=kOutput, calls=%fused_computation.2 | convolution fusion | flops 37896192 | bytes 412672 | tf_op jit(solution)/shard_map/dot_general | solution.py:15
  68.1 1.1 %fusion = f32[1,64,768]{2,1,0:T(8,128)} fusion(f32[64,768]{1,0:T(8,128)S(1)} %convolution_subtract_fusion.3, f32[64,64]{1,0:T(8,128)S(1)} %fusion.18, f32[64,768]{1,0:T(8,128)S(1)} %convolution_subtract_fusion.1), kind=kOutput, calls=%fused_computation.1 | convolution fusion | flops 37797888 | bytes 606208 | tf_op jit(solution)/shard_map/dot_general | solution.py:147
  (89 shorter events, 10.8 us)
Async XLA Ops:
  0.0 0.9 %copy-start = (f32[1,64,768]{2,1,0:T(8,128)S(1)}, f32[1,64,768]{2,1,0:T(8,128)}, u32[]{:S(2)}) copy-start(f32[1,64,768]{2,1,0:T(8,128)} %param.1) | copy-start | bytes 589828
  1.5 3.2 %collective-permute-start = (f32[64,128]{1,0:T(8,128)S(1)}, f32[64,128]{1,0:T(8,128)S(1)}, u32[]{:S(2)}, u32[]{:S(2)}) collective-permute-start(f32[64,128]{1,0:T(8,128)S(1)} %convolution_bitcast_fusion), channel_id=1, source_target_pairs={{0,1},{4,5},{8,9},{12,13},{16,17},{20,21},{24,25},{28,29}} | collective-permute-start | bytes 98312 | tf_op jit(solution)/shard_map/ppermute | solution.py:85
  4.7 4.1 %collective-permute-start.1 = (f32[64,128]{1,0:T(8,128)S(1)}, f32[64,128]{1,0:T(8,128)S(1)}, u32[]{:S(2)}, u32[]{:S(2)}) collective-permute-start(f32[64,128]{1,0:T(8,128)S(1)} %broadcast_select_fusion.5), channel_id=1, source_target_pairs={{0,2},{4,6},{8,10},{12,14},{16,18},{20,22},{24,26},{28,30}} | collective-permute-start | bytes 98312 | tf_op jit(solution)/shard_map/ppermute | solution.py:85
  7.0 5.2 %collective-permute-start.6 = (f32[64,768]{1,0:T(8,128)S(1)}, f32[64,768]{1,0:T(8,128)S(1)}, u32[]{:S(2)}, u32[]{:S(2)}) collective-permute-start(f32[64,768]{1,0:T(8,128)S(1)} %bitcast.82), channel_id=1, source_target_pairs={{0,2},{1,3},{4,6},{5,7},{8,10},{9,11},{12,14},{13,15},{16,18},{17,... | collective-permute-start | bytes 589832 | tf_op jit(solution)/shard_map/ppermute | solution.py:72
  8.7 3.8 %collective-permute-start.2 = (f32[64,128]{1,0:T(8,128)S(1)}, f32[64,128]{1,0:T(8,128)S(1)}, u32[]{:S(2)}, u32[]{:S(2)}) collective-permute-start(f32[64,128]{1,0:T(8,128)S(1)} %broadcast_select_fusion.6), channel_id=1, source_target_pairs={{0,3},{4,7},{8,11},{12,15},{16,19},{20,23},{24,27},{28,31}} | collective-permute-start | bytes 98312 | tf_op jit(solution)/shard_map/ppermute | solution.py:85
  12.2 6.3 %collective-permute-start.7 = (f32[64,768]{1,0:T(8,128)S(1)}, f32[64,768]{1,0:T(8,128)S(1)}, u32[]{:S(2)}, u32[]{:S(2)}) collective-permute-start(f32[64,768]{1,0:T(8,128)S(1)} %broadcast_select_fusion), channel_id=1, source_target_pairs={{0,1},{1,0},{2,3},{3,2},{4,5},{5,4},{6,7},{7,6},{8,9},{9,8},{10,11... | collective-permute-start | bytes 589832 | tf_op jit(solution)/shard_map/ppermute | solution.py:77
  12.6 3.9 %collective-permute-start.3 = (f32[64,128]{1,0:T(8,128)S(1)}, f32[64,128]{1,0:T(8,128)S(1)}, u32[]{:S(2)}, u32[]{:S(2)}) collective-permute-start(f32[64,128]{1,0:T(8,128)S(1)} %broadcast_select_fusion.7), channel_id=1, source_target_pairs={{0,4},{4,0},{8,12},{12,8},{16,20},{20,16},{24,28},{28,24},{1,5},{5... | collective-permute-start | bytes 98312 | tf_op jit(solution)/shard_map/ppermute | solution.py:29
  16.5 4.6 %collective-permute-start.4 = (f32[64,128]{1,0:T(8,128)S(1)}, f32[64,128]{1,0:T(8,128)S(1)}, u32[]{:S(2)}, u32[]{:S(2)}) collective-permute-start(f32[64,128]{1,0:T(8,128)S(1)} %add.66), channel_id=1, source_target_pairs={{0,8},{4,12},{8,0},{12,4},{16,24},{20,28},{24,16},{28,20},{1,9},{5... | collective-permute-start | bytes 98312 | tf_op jit(solution)/shard_map/ppermute | solution.py:29
  19.5 4.3 %collective-permute-start.8 = (f32[64,256]{1,0:T(8,128)S(1)}, f32[64,256]{1,0:T(8,128)S(1)}, u32[]{:S(2)}, u32[]{:S(2)}) collective-permute-start(f32[64,256]{1,0:T(8,128)S(1)} %pad_maximum_fusion.5), channel_id=1, source_target_pairs={{0,4},{4,0},{8,12},{12,8},{16,20},{20,16},{24,28},{28,24},{1,5},{5... | collective-permute-start | bytes 196616 | tf_op jit(solution)/shard_map/ppermute | solution.py:29
  21.1 4.9 %collective-permute-start.5 = (f32[64,128]{1,0:T(8,128)S(1)}, f32[64,128]{1,0:T(8,128)S(1)}, u32[]{:S(2)}, u32[]{:S(2)}) collective-permute-start(f32[64,128]{1,0:T(8,128)S(1)} %add.67), channel_id=1, source_target_pairs={{0,16},{4,20},{8,24},{12,28},{16,0},{20,4},{24,8},{28,12},{1,17},{... | collective-permute-start | bytes 98312 | tf_op jit(solution)/shard_map/ppermute | solution.py:29
  23.8 10.0 %collective-permute-start.9 = (f32[64,256]{1,0:T(8,128)S(1)}, f32[64,256]{1,0:T(8,128)S(1)}, u32[]{:S(2)}, u32[]{:S(2)}) collective-permute-start(f32[64,256]{1,0:T(8,128)S(1)} %fusion.49), channel_id=1, source_target_pairs={{0,8},{4,12},{8,0},{12,4},{16,24},{20,28},{24,16},{28,20},{1,9},{5... | collective-permute-start | bytes 196616 | tf_op jit(solution)/shard_map/ppermute | solution.py:29
  33.8 2.8 %copy-start.1 = (f32[64,64]{1,0:T(8,128)S(1)}, f32[64,64]{1,0:T(8,128)}, u32[]{:S(2)}) copy-start(f32[64,64]{1,0:T(8,128)} %shard_map.17) | copy-start | bytes 49156
  33.8 2.8 %copy-start.3 = (f32[64,128]{1,0:T(8,128)S(1)}, f32[64,128]{1,0:T(8,128)}, u32[]{:S(2)}) copy-start(f32[64,128]{1,0:T(8,128)} %add.68.head_ref) | copy-start | bytes 98308
  33.8 6.2 %collective-permute-start.10 = (f32[64,256]{1,0:T(8,128)S(1)}, f32[64,256]{1,0:T(8,128)S(1)}, u32[]{:S(2)}, u32[]{:S(2)}) collective-permute-start(f32[64,256]{1,0:T(8,128)S(1)} %add.72), channel_id=1, source_target_pairs={{0,16},{4,20},{8,24},{12,28},{16,0},{20,4},{24,8},{28,12},{1,17},{... | collective-permute-start | bytes 196616 | tf_op jit(solution)/shard_map/ppermute | solution.py:29
  42.8 4.0 %collective-permute-start.11 = (f32[64,128]{1,0:T(8,128)S(1)}, f32[64,128]{1,0:T(8,128)S(1)}, u32[]{:S(2)}, u32[]{:S(2)}) collective-permute-start(f32[64,128]{1,0:T(8,128)S(1)} %fusion.3), channel_id=1, source_target_pairs={{0,4},{4,0},{8,12},{12,8},{16,20},{20,16},{24,28},{28,24},{1,5},{5... | collective-permute-start | bytes 98312 | tf_op jit(solution)/shard_map/ppermute | solution.py:29
  44.1 4.3 %collective-permute-start.14 = (f32[64,128]{1,0:T(8,128)S(1)}, f32[64,128]{1,0:T(8,128)S(1)}, u32[]{:S(2)}, u32[]{:S(2)}) collective-permute-start(f32[64,128]{1,0:T(8,128)S(1)} %pad_maximum_fusion.6), channel_id=1, source_target_pairs={{0,4},{4,0},{8,12},{12,8},{16,20},{20,16},{24,28},{28,24},{1,5},{5... | collective-permute-start | bytes 98312 | tf_op jit(solution)/shard_map/ppermute | solution.py:29
  46.8 3.9 %collective-permute-start.12 = (f32[64,128]{1,0:T(8,128)S(1)}, f32[64,128]{1,0:T(8,128)S(1)}, u32[]{:S(2)}, u32[]{:S(2)}) collective-permute-start(f32[64,128]{1,0:T(8,128)S(1)} %add.74), channel_id=1, source_target_pairs={{0,8},{4,12},{8,0},{12,4},{16,24},{20,28},{24,16},{28,20},{1,9},{5... | collective-permute-start | bytes 98312 | tf_op jit(solution)/shard_map/ppermute | solution.py:29
  48.4 4.1 %collective-permute-start.15 = (f32[64,128]{1,0:T(8,128)S(1)}, f32[64,128]{1,0:T(8,128)S(1)}, u32[]{:S(2)}, u32[]{:S(2)}) collective-permute-start(f32[64,128]{1,0:T(8,128)S(1)} %fusion.131), channel_id=1, source_target_pairs={{0,8},{4,12},{8,0},{12,4},{16,24},{20,28},{24,16},{28,20},{1,9},{5... | collective-permute-start | bytes 98312 | tf_op jit(solution)/shard_map/ppermute | solution.py:29
  50.7 4.8 %collective-permute-start.13 = (f32[64,128]{1,0:T(8,128)S(1)}, f32[64,128]{1,0:T(8,128)S(1)}, u32[]{:S(2)}, u32[]{:S(2)}) collective-permute-start(f32[64,128]{1,0:T(8,128)S(1)} %add.75), channel_id=1, source_target_pairs={{0,16},{4,20},{8,24},{12,28},{16,0},{20,4},{24,8},{28,12},{1,17},{... | collective-permute-start | bytes 98312 | tf_op jit(solution)/shard_map/ppermute | solution.py:29
  52.5 12.3 %collective-permute-start.16 = (f32[64,128]{1,0:T(8,128)S(1)}, f32[64,128]{1,0:T(8,128)S(1)}, u32[]{:S(2)}, u32[]{:S(2)}) collective-permute-start(f32[64,128]{1,0:T(8,128)S(1)} %add.78), channel_id=1, source_target_pairs={{0,16},{4,20},{8,24},{12,28},{16,0},{20,4},{24,8},{28,12},{1,17},{... | collective-permute-start | bytes 98312 | tf_op jit(solution)/shard_map/ppermute | solution.py:29
  63.4 1.1 %copy-start.2 = (f32[64,64]{1,0:T(8,128)S(1)}, f32[64,64]{1,0:T(8,128)}, u32[]{:S(2)}) copy-start(f32[64,64]{1,0:T(8,128)} %shard_map.18) | copy-start | bytes 49156
  63.4 1.2 %copy-start.4 = (f32[64,128]{1,0:T(8,128)S(1)}, f32[64,128]{1,0:T(8,128)}, u32[]{:S(2)}) copy-start(f32[64,128]{1,0:T(8,128)} %add.76.head_ref) | copy-start | bytes 98308

commit v11 on v10

--- a/solution.py
+++ b/solution.py
@@ -30,22 +30,14 @@
     return x
 
 
-def invert_near_identity(square):
-    identity = jnp.eye(square.shape[0], dtype=jnp.float32)
-    approx = square.T * (2.0 / 4.25)
-    for _ in range(8):
-        approx = apply_left(approx, 2.0 * identity - apply_left(square, approx))
-    return approx
-
-
-def _eliminate_kernel(head_ref, out_ref):
-    size = out_ref.shape[0]
+def _eliminate_kernel(head_ref, lower_ref, inverse_ref):
+    size = lower_ref.shape[0]
     wide = 2 * size
     rows = lax.broadcasted_iota(jnp.int32, (size, wide), 0)
     lanes = lax.broadcasted_iota(jnp.int32, (size, wide), 1)
     row_ids = lax.broadcasted_iota(jnp.int32, (size, 1), 0)
-    work = head_ref[:, :wide]
-    work = jnp.where(lanes < size, work, (lanes == rows + size).astype(jnp.float32))
+    head = head_ref[...]
+    work = jnp.where(lanes < size, head, (lanes == rows + size).astype(jnp.float32))
     for j in range(size):
         row = work[j:j + 1, :]
         pivot = row[:, j:j + 1]
@@ -54,14 +46,25 @@
         scaled = row * scale
         weight = jnp.where(row_ids > j, work[:, j:j + 1] * scale, 0.0)
         work = jnp.where(rows == j, scaled, work - weight * scaled)
-    out_ref[...] = work[:, size:]
+    lower_inv = work[:, size:]
+    lower_ref[...] = lower_inv
+
+    def dot(a, b):
+        return jnp.dot(a, b, precision=HIGHEST_PRECISION, preferred_element_type=jnp.float32)
+
+    identity = (rows[:, :size] == lanes[:, :size]).astype(jnp.float32)
+    top_block = dot(lower_inv, head[:, size:])
+    square = identity - top_block.T
+    approx = square.T * (2.0 / 4.25)
+    for _ in range(8):
+        approx = dot(approx, 2.0 * identity - dot(square, approx))
+    inverse_ref[...] = approx
 
 
-def lower_inverse(head):
+def factor_and_inverse(head):
     size = head.shape[0]
-    return pl.pallas_call(
-        _eliminate_kernel, out_shape=jax.ShapeDtypeStruct((size, size), jnp.float32)
-    )(head)
+    square = jax.ShapeDtypeStruct((size, size), jnp.float32)
+    return pl.pallas_call(_eliminate_kernel, out_shape=(square, square))(head)
 
 
 def spread_pair(block, axis, size):
@@ -92,7 +95,6 @@
         block_count, width, local_rows = matrix.shape
         current = matrix.reshape(block_count * width, local_rows)
         global_rows = lax.axis_index("rows") * local_rows + jnp.arange(local_rows, dtype=jnp.int32)
-        identity = jnp.eye(width, dtype=jnp.float32)
         lanes = jnp.arange(width, dtype=jnp.int32)[:, None]
         units = [
             (lanes == (global_rows - k * width)[None, :]).astype(jnp.float32) for k in range(2)
@@ -114,14 +116,11 @@
         tail = jnp.concatenate([inner_rows(panel_0, both), inner_rows(units[0], both)], axis=1)
         steps = butterfly_steps(rows_size)
         tail = butterfly_sum(tail, "rows", rows_size, None if steps is None else steps[:-1])
-        lower_inv, tail = lax.optimization_barrier((lower_inverse(head), tail))
+        lower_inv, inverse, tail = lax.optimization_barrier((*factor_and_inverse(head), tail))
         tail = butterfly_sum(tail, "rows", rows_size, None if steps is None else steps[-1:])
-        top_rows = head[:, width:]
         basis_cur, basis_sec, unit_cur, unit_sec = (
             tail[:, i * width:(i + 1) * width] for i in range(4)
         )
-        top_block = apply_left(lower_inv, top_rows)
-        inverse = invert_near_identity(identity - top_block.T)
         reflect = units[0] - apply_left(lower_inv, panel_0)
         mixed = apply_left(inverse, unit_cur - apply_left(lower_inv, basis_cur))
         mixed_sec = apply_left(inverse, unit_sec - apply_left(lower_inv, basis_sec))
@@ -137,11 +136,8 @@
             "rows",
             rows_size,
         )
-        top_rows = head[:, width:]
         basis_cur, unit_cur = tail[:, :width], tail[:, width:]
-        lower_inv = lower_inverse(head)
-        top_block = apply_left(lower_inv, top_rows)
-        inverse = invert_near_identity(identity - top_block.T)
+        lower_inv, inverse = factor_and_inverse(head)
         reflect = units[1] - apply_left(lower_inv, panel_1)
         mixed = apply_left(inverse, unit_cur - apply_left(lower_inv, basis_cur))
         current = current - jnp.dot(mixed.T, reflect, precision=HIGHEST_PRECISION)

time: 69.6 us -> 73.5 us (1.056)
  matrix products: 12.9 us -> 6.88 us
  Pallas kernels: 14.5 us -> 20.4 us
  local copies, waits for them, and re-layouts: 0.91 us -> 2.8 us
  starting transfers between devices: 28.7 us -> 29.9 us
  waiting for transfers between devices: 9.99 us -> 11.1 us
    dot_general x42 -> x8, matrix products: 8.63 us -> 2.57 us  [apply_left(): return jnp.dot(square, right_side, precision=HIGHEST_PRECISION)]
    pallas_call x2, Pallas kernels: 14.5 us -> 20.4 us  [factor_and_inverse(): return pl.pallas_call(_eliminate_kernel, out_shape=(square, square))(head)]
    unnamed x10, local copies, waits for them, and re-layouts: 0.91 us -> 2.8 us
    ppermute x12, starting transfers between devices: 21.3 us -> 22.5 us  [butterfly_sum(): x = x + lax.ppermute(x, axis, [(i, i ^ step) for i in range(size)])]
    ppermute x12, waiting for transfers between devices: 6.37 us -> 7.43 us  [butterfly_sum(): x = x + lax.ppermute(x, axis, [(i, i ^ step) for i in range(size)])]
  transfers between devices with their start and end apart: 17 -> 17, of which waited for: 10 -> 10; matrix products, arithmetic and copies ran while one was open for 10% -> 5% of each run, Pallas kernels for 21% -> 28%
where the time goes in v11:
time: 73.5 us; the launch traced here: 72.9 us
  starting transfers between devices  29.9 us (41%)
  Pallas kernels  20.4 us (28%)
  waiting for transfers between devices  11.1 us (15%)
  matrix products  6.88 us (9%)
  local copies, waits for them, and re-layouts  2.8 us (4%)
  other arithmetic  1.58 us (2%)
    ppermute x12, starting transfers between devices, butterfly_sum(): x = x + lax.ppermute(x, axis, [(i, i ^ step) for i in range(size)])  22.5 us
    pallas_call x2, Pallas kernels, factor_and_inverse(): return pl.pallas_call(_eliminate_kernel, out_shape=(square, square))(head)  20.4 us
    ppermute x12, waiting for transfers between devices, butterfly_sum(): x = x + lax.ppermute(x, axis, [(i, i ^ step) for i in range(size)])  7.43 us
    ppermute x3, starting transfers between devices, from_root(): got = lax.ppermute(value, axis, [(0, k)])  6 us
    unnamed x10, local copies, waits for them, and re-layouts  2.8 us
    dot_general x8, matrix products, apply_left(): return jnp.dot(square, right_side, precision=HIGHEST_PRECISION)  2.57 us
    dot_general x6, matrix products, inner_rows(): lax.dot_general(left, right, (((1,), (1,)), ((), ())), precision=HIGHEST_...  2.52 us
    ppermute x1, waiting for transfers between devices, spread_pair(): lax.ppermute(have, axis, [(i, i + dist) for i in range(size) if i % (2 *...  2.18 us
  transfers between devices with their start and end apart: 17, of which 10 were waited for; matrix products, arithmetic and copies ran while one was open for 5% of the time, Pallas kernels for 28%

profile of v11, /device:TPU:0, one launch (start us, length us, event | category | flops | bytes accessed | tf_op | source)
XLA Modules:
  0.0 72.9 jit_solution(6564854835870571259)
XLA Ops:
  0.0 0.9 %copy-done = f32[1,64,768]{2,1,0:T(8,128)S(1)} copy-done((f32[1,64,768]{2,1,0:T(8,128)S(1)}, f32[1,64,768]{2,1,0:T(8,128)}, u32[]{:S(2)}) %copy-start) | copy-done | bytes 196632
  1.5 2.4 %collective-permute-start = (f32[64,128]{1,0:T(8,128)S(1)}, f32[64,128]{1,0:T(8,128)S(1)}, u32[]{:S(2)}, u32[]{:S(2)}) collective-permute-start(f32[64,128]{1,0:T(8,128)S(1)} %convolution_bitcast_fusion), channel_id=1, source_target_pairs={{0,1},{4,5},{8,9},{12,13},{16,17},{20,21},{24,25},{28,29}} | collective-permute-start | bytes 98312 | tf_op jit(solution)/shard_map/ppermute | solution.py:88
  3.8 0.8 %collective-permute-done = f32[64,128]{1,0:T(8,128)S(1)} collective-permute-done((f32[64,128]{1,0:T(8,128)S(1)}, f32[64,128]{1,0:T(8,128)S(1)}, u32[]{:S(2)}, u32[]{:S(2)}) %collective-permute-start) | collective-permute-done | bytes 32800 | tf_op jit(solution)/shard_map/ppermute | solution.py:88
  4.7 2.4 %collective-permute-start.1 = (f32[64,128]{1,0:T(8,128)S(1)}, f32[64,128]{1,0:T(8,128)S(1)}, u32[]{:S(2)}, u32[]{:S(2)}) collective-permute-start(f32[64,128]{1,0:T(8,128)S(1)} %broadcast_select_fusion.5), channel_id=1, source_target_pairs={{0,2},{4,6},{8,10},{12,14},{16,18},{20,22},{24,26},{28,30}} | collective-permute-start | bytes 98312 | tf_op jit(solution)/shard_map/ppermute | solution.py:88
  7.0 1.3 %collective-permute-start.6 = (f32[64,768]{1,0:T(8,128)S(1)}, f32[64,768]{1,0:T(8,128)S(1)}, u32[]{:S(2)}, u32[]{:S(2)}) collective-permute-start(f32[64,768]{1,0:T(8,128)S(1)} %bitcast.28), channel_id=1, source_target_pairs={{0,2},{1,3},{4,6},{5,7},{8,10},{9,11},{12,14},{13,15},{16,18},{17,... | collective-permute-start | bytes 589832 | tf_op jit(solution)/shard_map/ppermute | solution.py:75
  8.7 1.3 %collective-permute-start.2 = (f32[64,128]{1,0:T(8,128)S(1)}, f32[64,128]{1,0:T(8,128)S(1)}, u32[]{:S(2)}, u32[]{:S(2)}) collective-permute-start(f32[64,128]{1,0:T(8,128)S(1)} %broadcast_select_fusion.6), channel_id=1, source_target_pairs={{0,3},{4,7},{8,11},{12,15},{16,19},{20,23},{24,27},{28,31}} | collective-permute-start | bytes 98312 | tf_op jit(solution)/shard_map/ppermute | solution.py:88
  10.0 2.2 %collective-permute-done.6 = f32[64,768]{1,0:T(8,128)S(1)} collective-permute-done((f32[64,768]{1,0:T(8,128)S(1)}, f32[64,768]{1,0:T(8,128)S(1)}, u32[]{:S(2)}, u32[]{:S(2)}) %collective-permute-start.6) | collective-permute-done | bytes 196640 | tf_op jit(solution)/shard_map/ppermute | solution.py:75
  12.6 2.0 %collective-permute-start.3 = (f32[64,128]{1,0:T(8,128)S(1)}, f32[64,128]{1,0:T(8,128)S(1)}, u32[]{:S(2)}, u32[]{:S(2)}) collective-permute-start(f32[64,128]{1,0:T(8,128)S(1)} %broadcast_select_fusion.7), channel_id=1, source_target_pairs={{0,4},{4,0},{8,12},{12,8},{16,20},{20,16},{24,28},{28,24},{1,5},{5... | collective-permute-start | bytes 98312 | tf_op jit(solution)/shard_map/ppermute | solution.py:29
  14.5 2.0 %collective-permute-done.3 = f32[64,128]{1,0:T(8,128)S(1)} collective-permute-done((f32[64,128]{1,0:T(8,128)S(1)}, f32[64,128]{1,0:T(8,128)S(1)}, u32[]{:S(2)}, u32[]{:S(2)}) %collective-permute-start.3) | collective-permute-done | bytes 32800 | tf_op jit(solution)/shard_map/ppermute | solution.py:29
  16.5 2.0 %collective-permute-start.4 = (f32[64,128]{1,0:T(8,128)S(1)}, f32[64,128]{1,0:T(8,128)S(1)}, u32[]{:S(2)}, u32[]{:S(2)}) collective-permute-start(f32[64,128]{1,0:T(8,128)S(1)} %add.66), channel_id=1, source_target_pairs={{0,8},{4,12},{8,0},{12,4},{16,24},{20,28},{24,16},{28,20},{1,9},{5... | collective-permute-start | bytes 98312 | tf_op jit(solution)/shard_map/ppermute | solution.py:29
  19.5 1.6 %collective-permute-start.8 = (f32[64,256]{1,0:T(8,128)S(1)}, f32[64,256]{1,0:T(8,128)S(1)}, u32[]{:S(2)}, u32[]{:S(2)}) collective-permute-start(f32[64,256]{1,0:T(8,128)S(1)} %pad_maximum_fusion.5), channel_id=1, source_target_pairs={{0,4},{4,0},{8,12},{12,8},{16,20},{20,16},{24,28},{28,24},{1,5},{5... | collective-permute-start | bytes 196616 | tf_op jit(solution)/shard_map/ppermute | solution.py:29
  21.1 2.7 %collective-permute-start.5 = (f32[64,128]{1,0:T(8,128)S(1)}, f32[64,128]{1,0:T(8,128)S(1)}, u32[]{:S(2)}, u32[]{:S(2)}) collective-permute-start(f32[64,128]{1,0:T(8,128)S(1)} %add.67), channel_id=1, source_target_pairs={{0,16},{4,20},{8,24},{12,28},{16,0},{20,4},{24,8},{28,12},{1,17},{... | collective-permute-start | bytes 98312 | tf_op jit(solution)/shard_map/ppermute | solution.py:29
  23.8 1.3 %collective-permute-start.9 = (f32[64,256]{1,0:T(8,128)S(1)}, f32[64,256]{1,0:T(8,128)S(1)}, u32[]{:S(2)}, u32[]{:S(2)}) collective-permute-start(f32[64,256]{1,0:T(8,128)S(1)} %fusion.29), channel_id=1, source_target_pairs={{0,8},{4,12},{8,0},{12,4},{16,24},{20,28},{24,16},{28,20},{1,9},{5... | collective-permute-start | bytes 196616 | tf_op jit(solution)/shard_map/ppermute | solution.py:29
  25.1 0.8 %collective-permute-done.5 = f32[64,128]{1,0:T(8,128)S(1)} collective-permute-done((f32[64,128]{1,0:T(8,128)S(1)}, f32[64,128]{1,0:T(8,128)S(1)}, u32[]{:S(2)}, u32[]{:S(2)}) %collective-permute-start.5) | collective-permute-done | bytes 32800 | tf_op jit(solution)/shard_map/ppermute | solution.py:29
  25.9 0.6 add.68.head_ref
  26.6 10.2 %shard_map.17 = (f32[64,64]{1,0:T(8,128)}, f32[64,64]{1,0:T(8,128)}) custom-call(f32[64,128]{1,0:T(8,128)} %add.68.head_ref), custom_call_target="tpu_custom_call" | custom-call | tf_op jit(solution)/shard_map/pallas_call | solution.py:67
  36.8 2.8 %collective-permute-start.10 = (f32[64,256]{1,0:T(8,128)S(1)}, f32[64,256]{1,0:T(8,128)S(1)}, u32[]{:S(2)}, u32[]{:S(2)}) collective-permute-start(f32[64,256]{1,0:T(8,128)S(1)} %add.72), channel_id=1, source_target_pairs={{0,16},{4,20},{8,24},{12,28},{16,0},{20,4},{24,8},{28,12},{1,17},{... | collective-permute-start | bytes 196616 | tf_op jit(solution)/shard_map/ppermute | solution.py:29
  39.9 2.1 %collective-permute-done.10 = f32[64,256]{1,0:T(8,128)S(1)} collective-permute-done((f32[64,256]{1,0:T(8,128)S(1)}, f32[64,256]{1,0:T(8,128)S(1)}, u32[]{:S(2)}, u32[]{:S(2)}) %collective-permute-start.10) | collective-permute-done | bytes 65568 | tf_op jit(solution)/shard_map/ppermute | solution.py:29
  45.3 1.3 %collective-permute-start.11 = (f32[64,128]{1,0:T(8,128)S(1)}, f32[64,128]{1,0:T(8,128)S(1)}, u32[]{:S(2)}, u32[]{:S(2)}) collective-permute-start(f32[64,128]{1,0:T(8,128)S(1)} %fusion.3), channel_id=1, source_target_pairs={{0,4},{4,0},{8,12},{12,8},{16,20},{20,16},{24,28},{28,24},{1,5},{5... | collective-permute-start | bytes 98312 | tf_op jit(solution)/shard_map/ppermute | solution.py:29
  46.7 0.8 %collective-permute-start.14 = (f32[64,128]{1,0:T(8,128)S(1)}, f32[64,128]{1,0:T(8,128)S(1)}, u32[]{:S(2)}, u32[]{:S(2)}) collective-permute-start(f32[64,128]{1,0:T(8,128)S(1)} %pad_maximum_fusion.6), channel_id=1, source_target_pairs={{0,4},{4,0},{8,12},{12,8},{16,20},{20,16},{24,28},{28,24},{1,5},{5... | collective-permute-start | bytes 98312 | tf_op jit(solution)/shard_map/ppermute | solution.py:29
  47.5 1.8 %collective-permute-done.11 = f32[64,128]{1,0:T(8,128)S(1)} collective-permute-done((f32[64,128]{1,0:T(8,128)S(1)}, f32[64,128]{1,0:T(8,128)S(1)}, u32[]{:S(2)}, u32[]{:S(2)}) %collective-permute-start.11) | collective-permute-done | bytes 32800 | tf_op jit(solution)/shard_map/ppermute | solution.py:29
  49.3 1.7 %collective-permute-start.12 = (f32[64,128]{1,0:T(8,128)S(1)}, f32[64,128]{1,0:T(8,128)S(1)}, u32[]{:S(2)}, u32[]{:S(2)}) collective-permute-start(f32[64,128]{1,0:T(8,128)S(1)} %add.74), channel_id=1, source_target_pairs={{0,8},{4,12},{8,0},{12,4},{16,24},{20,28},{24,16},{28,20},{1,9},{5... | collective-permute-start | bytes 98312 | tf_op jit(solution)/shard_map/ppermute | solution.py:29
  51.1 1.6 %collective-permute-start.15 = (f32[64,128]{1,0:T(8,128)S(1)}, f32[64,128]{1,0:T(8,128)S(1)}, u32[]{:S(2)}, u32[]{:S(2)}) collective-permute-start(f32[64,128]{1,0:T(8,128)S(1)} %fusion.51), channel_id=1, source_target_pairs={{0,8},{4,12},{8,0},{12,4},{16,24},{20,28},{24,16},{28,20},{1,9},{5... | collective-permute-start | bytes 98312 | tf_op jit(solution)/shard_map/ppermute | solution.py:29
  52.6 0.6 collective-permute-done.12
  53.3 2.8 %collective-permute-start.13 = (f32[64,128]{1,0:T(8,128)S(1)}, f32[64,128]{1,0:T(8,128)S(1)}, u32[]{:S(2)}, u32[]{:S(2)}) collective-permute-start(f32[64,128]{1,0:T(8,128)S(1)} %add.75), channel_id=1, source_target_pairs={{0,16},{4,20},{8,24},{12,28},{16,0},{20,4},{24,8},{28,12},{1,17},{... | collective-permute-start | bytes 98312 | tf_op jit(solution)/shard_map/ppermute | solution.py:29
  56.1 2.1 %collective-permute-start.16 = (f32[64,128]{1,0:T(8,128)S(1)}, f32[64,128]{1,0:T(8,128)S(1)}, u32[]{:S(2)}, u32[]{:S(2)}) collective-permute-start(f32[64,128]{1,0:T(8,128)S(1)} %add.78), channel_id=1, source_target_pairs={{0,16},{4,20},{8,24},{12,28},{16,0},{20,4},{24,8},{28,12},{1,17},{... | collective-permute-start | bytes 98312 | tf_op jit(solution)/shard_map/ppermute | solution.py:29
  58.2 0.6 add.76.head_ref
  58.8 10.2 %shard_map.18 = (f32[64,64]{1,0:T(8,128)}, f32[64,64]{1,0:T(8,128)}) custom-call(f32[64,128]{1,0:T(8,128)} %add.76.head_ref), custom_call_target="tpu_custom_call" | custom-call | tf_op jit(solution)/shard_map/pallas_call | solution.py:67
  69.0 1.1 %convolution_subtract_fusion.1 = f32[64,768]{1,0:T(8,128)S(1)} fusion(f32[64,64]{1,0:T(8,128)} %get-tuple-element.18, f32[64,768]{1,0:T(8,128)S(1)} %fusion.1, s32[768]{0:T(1024)S(1)} %fusion.23), kind=kOutput, calls=%fused_computation.2 | convolution fusion | flops 37896192 | bytes 412672 | tf_op jit(solution)/shard_map/dot_general | solution.py:15
  70.1 0.7 copy-done.3
  71.0 0.6 copy-done.4
  71.9 1.1 %fusion = f32[1,64,768]{2,1,0:T(8,128)} fusion(f32[64,768]{1,0:T(8,128)S(1)} %convolution_subtract_fusion.3, f32[64,64]{1,0:T(8,128)S(1)} %fusion.16, f32[64,768]{1,0:T(8,128)S(1)} %convolution_subtract_fusion.1), kind=kOutput, calls=%fused_computation.1 | convolution fusion | flops 37797888 | bytes 606208 | tf_op jit(solution)/shard_map/dot_general | solution.py:143
  (55 shorter events, 6.5 us)
Async XLA Ops:
  0.0 0.9 %copy-start = (f32[1,64,768]{2,1,0:T(8,128)S(1)}, f32[1,64,768]{2,1,0:T(8,128)}, u32[]{:S(2)}) copy-start(f32[1,64,768]{2,1,0:T(8,128)} %param.1) | copy-start | bytes 589828
  1.5 3.2 %collective-permute-start = (f32[64,128]{1,0:T(8,128)S(1)}, f32[64,128]{1,0:T(8,128)S(1)}, u32[]{:S(2)}, u32[]{:S(2)}) collective-permute-start(f32[64,128]{1,0:T(8,128)S(1)} %convolution_bitcast_fusion), channel_id=1, source_target_pairs={{0,1},{4,5},{8,9},{12,13},{16,17},{20,21},{24,25},{28,29}} | collective-permute-start | bytes 98312 | tf_op jit(solution)/shard_map/ppermute | solution.py:88
  4.7 4.1 %collective-permute-start.1 = (f32[64,128]{1,0:T(8,128)S(1)}, f32[64,128]{1,0:T(8,128)S(1)}, u32[]{:S(2)}, u32[]{:S(2)}) collective-permute-start(f32[64,128]{1,0:T(8,128)S(1)} %broadcast_select_fusion.5), channel_id=1, source_target_pairs={{0,2},{4,6},{8,10},{12,14},{16,18},{20,22},{24,26},{28,30}} | collective-permute-start | bytes 98312 | tf_op jit(solution)/shard_map/ppermute | solution.py:88
  7.0 5.2 %collective-permute-start.6 = (f32[64,768]{1,0:T(8,128)S(1)}, f32[64,768]{1,0:T(8,128)S(1)}, u32[]{:S(2)}, u32[]{:S(2)}) collective-permute-start(f32[64,768]{1,0:T(8,128)S(1)} %bitcast.28), channel_id=1, source_target_pairs={{0,2},{1,3},{4,6},{5,7},{8,10},{9,11},{12,14},{13,15},{16,18},{17,... | collective-permute-start | bytes 589832 | tf_op jit(solution)/shard_map/ppermute | solution.py:75
  8.7 3.8 %collective-permute-start.2 = (f32[64,128]{1,0:T(8,128)S(1)}, f32[64,128]{1,0:T(8,128)S(1)}, u32[]{:S(2)}, u32[]{:S(2)}) collective-permute-start(f32[64,128]{1,0:T(8,128)S(1)} %broadcast_select_fusion.6), channel_id=1, source_target_pairs={{0,3},{4,7},{8,11},{12,15},{16,19},{20,23},{24,27},{28,31}} | collective-permute-start | bytes 98312 | tf_op jit(solution)/shard_map/ppermute | solution.py:88
  12.2 6.3 %collective-permute-start.7 = (f32[64,768]{1,0:T(8,128)S(1)}, f32[64,768]{1,0:T(8,128)S(1)}, u32[]{:S(2)}, u32[]{:S(2)}) collective-permute-start(f32[64,768]{1,0:T(8,128)S(1)} %broadcast_select_fusion), channel_id=1, source_target_pairs={{0,1},{1,0},{2,3},{3,2},{4,5},{5,4},{6,7},{7,6},{8,9},{9,8},{10,11... | collective-permute-start | bytes 589832 | tf_op jit(solution)/shard_map/ppermute | solution.py:80
  12.6 3.9 %collective-permute-start.3 = (f32[64,128]{1,0:T(8,128)S(1)}, f32[64,128]{1,0:T(8,128)S(1)}, u32[]{:S(2)}, u32[]{:S(2)}) collective-permute-start(f32[64,128]{1,0:T(8,128)S(1)} %broadcast_select_fusion.7), channel_id=1, source_target_pairs={{0,4},{4,0},{8,12},{12,8},{16,20},{20,16},{24,28},{28,24},{1,5},{5... | collective-permute-start | bytes 98312 | tf_op jit(solution)/shard_map/ppermute | solution.py:29
  16.5 4.6 %collective-permute-start.4 = (f32[64,128]{1,0:T(8,128)S(1)}, f32[64,128]{1,0:T(8,128)S(1)}, u32[]{:S(2)}, u32[]{:S(2)}) collective-permute-start(f32[64,128]{1,0:T(8,128)S(1)} %add.66), channel_id=1, source_target_pairs={{0,8},{4,12},{8,0},{12,4},{16,24},{20,28},{24,16},{28,20},{1,9},{5... | collective-permute-start | bytes 98312 | tf_op jit(solution)/shard_map/ppermute | solution.py:29
  19.5 4.3 %collective-permute-start.8 = (f32[64,256]{1,0:T(8,128)S(1)}, f32[64,256]{1,0:T(8,128)S(1)}, u32[]{:S(2)}, u32[]{:S(2)}) collective-permute-start(f32[64,256]{1,0:T(8,128)S(1)} %pad_maximum_fusion.5), channel_id=1, source_target_pairs={{0,4},{4,0},{8,12},{12,8},{16,20},{20,16},{24,28},{28,24},{1,5},{5... | collective-permute-start | bytes 196616 | tf_op jit(solution)/shard_map/ppermute | solution.py:29
  21.1 4.9 %collective-permute-start.5 = (f32[64,128]{1,0:T(8,128)S(1)}, f32[64,128]{1,0:T(8,128)S(1)}, u32[]{:S(2)}, u32[]{:S(2)}) collective-permute-start(f32[64,128]{1,0:T(8,128)S(1)} %add.67), channel_id=1, source_target_pairs={{0,16},{4,20},{8,24},{12,28},{16,0},{20,4},{24,8},{28,12},{1,17},{... | collective-permute-start | bytes 98312 | tf_op jit(solution)/shard_map/ppermute | solution.py:29
  23.8 13.0 %collective-permute-start.9 = (f32[64,256]{1,0:T(8,128)S(1)}, f32[64,256]{1,0:T(8,128)S(1)}, u32[]{:S(2)}, u32[]{:S(2)}) collective-permute-start(f32[64,256]{1,0:T(8,128)S(1)} %fusion.29), channel_id=1, source_target_pairs={{0,8},{4,12},{8,0},{12,4},{16,24},{20,28},{24,16},{28,20},{1,9},{5... | collective-permute-start | bytes 196616 | tf_op jit(solution)/shard_map/ppermute | solution.py:29
  36.8 2.8 %copy-start.1 = (f32[64,64]{1,0:T(8,128)S(1)}, f32[64,64]{1,0:T(8,128)}, u32[]{:S(2)}) copy-start(f32[64,64]{1,0:T(8,128)} %get-tuple-element.16) | copy-start | bytes 49156
  36.8 5.2 %collective-permute-start.10 = (f32[64,256]{1,0:T(8,128)S(1)}, f32[64,256]{1,0:T(8,128)S(1)}, u32[]{:S(2)}, u32[]{:S(2)}) collective-permute-start(f32[64,256]{1,0:T(8,128)S(1)} %add.72), channel_id=1, source_target_pairs={{0,16},{4,20},{8,24},{12,28},{16,0},{20,4},{24,8},{28,12},{1,17},{... | collective-permute-start | bytes 196616 | tf_op jit(solution)/shard_map/ppermute | solution.py:29
  42.3 0.8 %copy-start.2 = (f32[64,64]{1,0:T(8,128)S(1)}, f32[64,64]{1,0:T(8,128)}, u32[]{:S(2)}) copy-start(f32[64,64]{1,0:T(8,128)} %get-tuple-element.14) | copy-start | bytes 49156
  45.3 4.0 %collective-permute-start.11 = (f32[64,128]{1,0:T(8,128)S(1)}, f32[64,128]{1,0:T(8,128)S(1)}, u32[]{:S(2)}, u32[]{:S(2)}) collective-permute-start(f32[64,128]{1,0:T(8,128)S(1)} %fusion.3), channel_id=1, source_target_pairs={{0,4},{4,0},{8,12},{12,8},{16,20},{20,16},{24,28},{28,24},{1,5},{5... | collective-permute-start | bytes 98312 | tf_op jit(solution)/shard_map/ppermute | solution.py:29
  46.7 4.3 %collective-permute-start.14 = (f32[64,128]{1,0:T(8,128)S(1)}, f32[64,128]{1,0:T(8,128)S(1)}, u32[]{:S(2)}, u32[]{:S(2)}) collective-permute-start(f32[64,128]{1,0:T(8,128)S(1)} %pad_maximum_fusion.6), channel_id=1, source_target_pairs={{0,4},{4,0},{8,12},{12,8},{16,20},{20,16},{24,28},{28,24},{1,5},{5... | collective-permute-start | bytes 98312 | tf_op jit(solution)/shard_map/ppermute | solution.py:29
  49.3 3.9 %collective-permute-start.12 = (f32[64,128]{1,0:T(8,128)S(1)}, f32[64,128]{1,0:T(8,128)S(1)}, u32[]{:S(2)}, u32[]{:S(2)}) collective-permute-start(f32[64,128]{1,0:T(8,128)S(1)} %add.74), channel_id=1, source_target_pairs={{0,8},{4,12},{8,0},{12,4},{16,24},{20,28},{24,16},{28,20},{1,9},{5... | collective-permute-start | bytes 98312 | tf_op jit(solution)/shard_map/ppermute | solution.py:29
  51.1 5.0 %collective-permute-start.15 = (f32[64,128]{1,0:T(8,128)S(1)}, f32[64,128]{1,0:T(8,128)S(1)}, u32[]{:S(2)}, u32[]{:S(2)}) collective-permute-start(f32[64,128]{1,0:T(8,128)S(1)} %fusion.51), channel_id=1, source_target_pairs={{0,8},{4,12},{8,0},{12,4},{16,24},{20,28},{24,16},{28,20},{1,9},{5... | collective-permute-start | bytes 98312 | tf_op jit(solution)/shard_map/ppermute | solution.py:29
  53.3 4.9 %collective-permute-start.13 = (f32[64,128]{1,0:T(8,128)S(1)}, f32[64,128]{1,0:T(8,128)S(1)}, u32[]{:S(2)}, u32[]{:S(2)}) collective-permute-start(f32[64,128]{1,0:T(8,128)S(1)} %add.75), channel_id=1, source_target_pairs={{0,16},{4,20},{8,24},{12,28},{16,0},{20,4},{24,8},{28,12},{1,17},{... | collective-permute-start | bytes 98312 | tf_op jit(solution)/shard_map/ppermute | solution.py:29
  56.1 14.0 %collective-permute-start.16 = (f32[64,128]{1,0:T(8,128)S(1)}, f32[64,128]{1,0:T(8,128)S(1)}, u32[]{:S(2)}, u32[]{:S(2)}) collective-permute-start(f32[64,128]{1,0:T(8,128)S(1)} %add.78), channel_id=1, source_target_pairs={{0,16},{4,20},{8,24},{12,28},{16,0},{20,4},{24,8},{28,12},{1,17},{... | collective-permute-start | bytes 98312 | tf_op jit(solution)/shard_map/ppermute | solution.py:29
  70.1 0.8 %copy-start.3 = (f32[64,64]{1,0:T(8,128)S(1)}, f32[64,64]{1,0:T(8,128)}, u32[]{:S(2)}) copy-start(f32[64,64]{1,0:T(8,128)} %get-tuple-element.18) | copy-start | bytes 49156
  70.9 0.8 %copy-start.4 = (f32[64,64]{1,0:T(8,128)S(1)}, f32[64,64]{1,0:T(8,128)}, u32[]{:S(2)}) copy-start(f32[64,64]{1,0:T(8,128)} %get-tuple-element.17) | copy-start | bytes 49156

commit v12 on v9

--- a/solution.py
+++ b/solution.py
@@ -33,7 +33,7 @@
 def invert_near_identity(square):
     identity = jnp.eye(square.shape[0], dtype=jnp.float32)
     approx = square.T * (2.0 / 4.25)
-    for _ in range(8):
+    for _ in range(7):
         approx = apply_left(approx, 2.0 * identity - apply_left(square, approx))
     return approx
 
@@ -79,7 +79,7 @@
     return jnp.where(even, have, other), jnp.where(even, other, have)
 
 
-def spread_root(value, axis, size):
+def from_root(value, axis, size):
     index = lax.axis_index(axis)
     dist = size // 2
     while dist >= 1:
@@ -110,11 +110,9 @@
                 inner_rows(panel_0, jnp.concatenate([panel_0, units[0]])), "rows", rows_size
             )
         else:
-            head = butterfly_sum(
-                inner_rows(current, jnp.concatenate([current, units[0]])), "rows", rows_size
-            )
+            head = inner_rows(current, jnp.concatenate([current, units[0]]))
+            head = butterfly_sum(from_root(head, "cols", cols_size), "rows", rows_size)
             panel_0, second = spread_pair(current, "cols", cols_size)
-            head = spread_root(head, "cols", cols_size)
 
         both = jnp.concatenate([current, second])
         tail = jnp.concatenate([inner_rows(panel_0, both), inner_rows(units[0], both)], axis=1)

time: 70.6 us -> 67.7 us (0.959)
  waiting for transfers between devices: 14.5 us -> 9.22 us
  starting transfers between devices: 26.1 us -> 28.2 us
  local copies, waits for them, and re-layouts: 0.02 us -> 0.91 us
    ppermute x12, waiting for transfers between devices: 14.5 us -> 6.68 us  [butterfly_sum(): x = x + lax.ppermute(x, axis, [(i, i ^ step) for i in range(size)])]
    ppermute x1, starting transfers between devices: 5 us -> 1.3 us  [spread_pair(): lax.ppermute(have, axis, [(i, i + dist) for i in range(size) if i % (2 *...]
    ppermute x2, starting transfers between devices: 2.62 us -> 6.15 us  [from_root(): lax.ppermute(value, axis, [(i, i + dist) for i in range(size) if i % (2 *...]
    ppermute x12, starting transfers between devices: 18.5 us -> 20.7 us  [butterfly_sum(): x = x + lax.ppermute(x, axis, [(i, i ^ step) for i in range(size)])]
    ppermute x1, waiting for transfers between devices: 0.01 us -> 2.18 us  [spread_pair(): lax.ppermute(have, axis, [(i, i + dist) for i in range(size) if i % (2 *...]
    unnamed x10, local copies, waits for them, and re-layouts: 0.02 us -> 0.91 us
    dot_general x42 -> x38, matrix products: 8.63 us -> 7.99 us  [apply_left(): return jnp.dot(square, right_side, precision=HIGHEST_PRECISION)]
  transfers between devices with their start and end apart: 16 -> 16, of which waited for: 8 -> 8; matrix products, arithmetic and copies ran while one was open for 11% -> 10% of each run, Pallas kernels for 21% -> 22%
where the time goes in v12:
time: 67.7 us; the launch traced here: 67.2 us
  starting transfers between devices  28.2 us (42%)
  Pallas kernels  14.5 us (21%)
  matrix products  12.3 us (18%)
  waiting for transfers between devices  9.22 us (14%)
  other arithmetic  1.57 us (2%)
  local copies, waits for them, and re-layouts  0.91 us (1%)
    ppermute x12, starting transfers between devices, butterfly_sum(): x = x + lax.ppermute(x, axis, [(i, i ^ step) for i in range(size)])  20.7 us
    pallas_call x2, Pallas kernels, lower_inverse(): pl.pallas_call(_eliminate_kernel, out_shape=jax.ShapeDtypeStruct((size, s...  14.5 us
    dot_general x38, matrix products, apply_left(): return jnp.dot(square, right_side, precision=HIGHEST_PRECISION)  7.99 us
    ppermute x12, waiting for transfers between devices, butterfly_sum(): x = x + lax.ppermute(x, axis, [(i, i ^ step) for i in range(size)])  6.68 us
    ppermute x2, starting transfers between devices, from_root(): lax.ppermute(value, axis, [(i, i + dist) for i in range(size) if i % (2 *...  6.15 us
    dot_general x6, matrix products, inner_rows(): lax.dot_general(left, right, (((1,), (1,)), ((), ())), precision=HIGHEST_...  2.52 us
    ppermute x1, waiting for transfers between devices, spread_pair(): lax.ppermute(have, axis, [(i, i + dist) for i in range(size) if i % (2 *...  2.18 us
    dot_general x2, matrix products, local(): current = current - jnp.dot(mixed.T, reflect, precision=HIGHEST_PRECISION)  1.43 us
  transfers between devices with their start and end apart: 16, of which 8 were waited for; matrix products, arithmetic and copies ran while one was open for 10% of the time, Pallas kernels for 22%

profile of v12, /device:TPU:0, one launch (start us, length us, event | category | flops | bytes accessed | tf_op | source)
XLA Modules:
  0.0 67.2 jit_solution(7281156012374852703)
XLA Ops:
  0.0 0.9 %copy-done = f32[1,64,768]{2,1,0:T(8,128)S(1)} copy-done((f32[1,64,768]{2,1,0:T(8,128)S(1)}, f32[1,64,768]{2,1,0:T(8,128)}, u32[]{:S(2)}) %copy-start) | copy-done | bytes 196632
  0.9 0.5 convolution_bitcast_fusion
  1.5 4.9 %collective-permute-start = (f32[64,128]{1,0:T(8,128)S(1)}, f32[64,128]{1,0:T(8,128)S(1)}, u32[]{:S(2)}, u32[]{:S(2)}) collective-permute-start(f32[64,128]{1,0:T(8,128)S(1)} %convolution_bitcast_fusion), channel_id=1, source_target_pairs={{0,2},{4,6},{8,10},{12,14},{16,18},{20,22},{24,26},{28,30}} | collective-permute-start | bytes 98312 | tf_op jit(solution)/shard_map/ppermute | solution.py:86
  6.3 1.3 %collective-permute-start.5 = (f32[64,768]{1,0:T(8,128)S(1)}, f32[64,768]{1,0:T(8,128)S(1)}, u32[]{:S(2)}, u32[]{:S(2)}) collective-permute-start(f32[64,768]{1,0:T(8,128)S(1)} %bitcast.76), channel_id=1, source_target_pairs={{0,2},{1,3},{4,6},{5,7},{8,10},{9,11},{12,14},{13,15},{16,18},{17,... | collective-permute-start | bytes 589832 | tf_op jit(solution)/shard_map/ppermute | solution.py:72
  8.0 1.3 %collective-permute-start.1 = (f32[64,128]{1,0:T(8,128)S(1)}, f32[64,128]{1,0:T(8,128)S(1)}, u32[]{:S(2)}, u32[]{:S(2)}) collective-permute-start(f32[64,128]{1,0:T(8,128)S(1)} %broadcast_select_fusion.5), channel_id=1, source_target_pairs={{0,1},{2,3},{4,5},{6,7},{8,9},{10,11},{12,13},{14,15},{16,17},{18,... | collective-permute-start | bytes 98312 | tf_op jit(solution)/shard_map/ppermute | solution.py:86
  9.3 2.2 %collective-permute-done.5 = f32[64,768]{1,0:T(8,128)S(1)} collective-permute-done((f32[64,768]{1,0:T(8,128)S(1)}, f32[64,768]{1,0:T(8,128)S(1)}, u32[]{:S(2)}, u32[]{:S(2)}) %collective-permute-start.5) | collective-permute-done | bytes 196640 | tf_op jit(solution)/shard_map/ppermute | solution.py:72
  11.6 1.6 %collective-permute-start.2 = (f32[64,128]{1,0:T(8,128)S(1)}, f32[64,128]{1,0:T(8,128)S(1)}, u32[]{:S(2)}, u32[]{:S(2)}) collective-permute-start(f32[64,128]{1,0:T(8,128)S(1)} %broadcast_select_fusion.6), channel_id=1, source_target_pairs={{0,4},{4,0},{8,12},{12,8},{16,20},{20,16},{24,28},{28,24},{1,5},{5... | collective-permute-start | bytes 98312 | tf_op jit(solution)/shard_map/ppermute | solution.py:29
  13.2 2.4 %collective-permute-done.2 = f32[64,128]{1,0:T(8,128)S(1)} collective-permute-done((f32[64,128]{1,0:T(8,128)S(1)}, f32[64,128]{1,0:T(8,128)S(1)}, u32[]{:S(2)}, u32[]{:S(2)}) %collective-permute-start.2) | collective-permute-done | bytes 32800 | tf_op jit(solution)/shard_map/ppermute | solution.py:29
  15.6 1.6 %collective-permute-start.3 = (f32[64,128]{1,0:T(8,128)S(1)}, f32[64,128]{1,0:T(8,128)S(1)}, u32[]{:S(2)}, u32[]{:S(2)}) collective-permute-start(f32[64,128]{1,0:T(8,128)S(1)} %add.70), channel_id=1, source_target_pairs={{0,8},{4,12},{8,0},{12,4},{16,24},{20,28},{24,16},{28,20},{1,9},{5... | collective-permute-start | bytes 98312 | tf_op jit(solution)/shard_map/ppermute | solution.py:29
  17.6 0.5 fusion.8
  18.1 1.6 %collective-permute-start.7 = (f32[64,256]{1,0:T(8,128)S(1)}, f32[64,256]{1,0:T(8,128)S(1)}, u32[]{:S(2)}, u32[]{:S(2)}) collective-permute-start(f32[64,256]{1,0:T(8,128)S(1)} %pad_maximum_fusion.5), channel_id=1, source_target_pairs={{0,4},{4,0},{8,12},{12,8},{16,20},{20,16},{24,28},{28,24},{1,5},{5... | collective-permute-start | bytes 196616 | tf_op jit(solution)/shard_map/ppermute | solution.py:29
  19.7 2.7 %collective-permute-start.4 = (f32[64,128]{1,0:T(8,128)S(1)}, f32[64,128]{1,0:T(8,128)S(1)}, u32[]{:S(2)}, u32[]{:S(2)}) collective-permute-start(f32[64,128]{1,0:T(8,128)S(1)} %add.71), channel_id=1, source_target_pairs={{0,16},{4,20},{8,24},{12,28},{16,0},{20,4},{24,8},{28,12},{1,17},{... | collective-permute-start | bytes 98312 | tf_op jit(solution)/shard_map/ppermute | solution.py:29
  22.5 1.3 %collective-permute-start.8 = (f32[64,256]{1,0:T(8,128)S(1)}, f32[64,256]{1,0:T(8,128)S(1)}, u32[]{:S(2)}, u32[]{:S(2)}) collective-permute-start(f32[64,256]{1,0:T(8,128)S(1)} %fusion.49), channel_id=1, source_target_pairs={{0,8},{4,12},{8,0},{12,4},{16,24},{20,28},{24,16},{28,20},{1,9},{5... | collective-permute-start | bytes 196616 | tf_op jit(solution)/shard_map/ppermute | solution.py:29
  23.8 0.8 %collective-permute-done.4 = f32[64,128]{1,0:T(8,128)S(1)} collective-permute-done((f32[64,128]{1,0:T(8,128)S(1)}, f32[64,128]{1,0:T(8,128)S(1)}, u32[]{:S(2)}, u32[]{:S(2)}) %collective-permute-start.4) | collective-permute-done | bytes 32800 | tf_op jit(solution)/shard_map/ppermute | solution.py:29
  24.6 0.6 add.72.head_ref
  25.2 7.2 %shard_map.17 = f32[64,64]{1,0:T(8,128)} custom-call(f32[64,128]{1,0:T(8,128)} %add.72.head_ref), custom_call_target="tpu_custom_call" | custom-call | tf_op jit(solution)/shard_map/pallas_call | solution.py:62
  32.5 2.8 %collective-permute-start.9 = (f32[64,256]{1,0:T(8,128)S(1)}, f32[64,256]{1,0:T(8,128)S(1)}, u32[]{:S(2)}, u32[]{:S(2)}) collective-permute-start(f32[64,256]{1,0:T(8,128)S(1)} %add.74), channel_id=1, source_target_pairs={{0,16},{4,20},{8,24},{12,28},{16,0},{20,4},{24,8},{28,12},{1,17},{... | collective-permute-start | bytes 196616 | tf_op jit(solution)/shard_map/ppermute | solution.py:29
  39.9 0.4 fusion.1
  40.6 0.5 fusion.3
  41.1 1.2 %collective-permute-start.10 = (f32[64,128]{1,0:T(8,128)S(1)}, f32[64,128]{1,0:T(8,128)S(1)}, u32[]{:S(2)}, u32[]{:S(2)}) collective-permute-start(f32[64,128]{1,0:T(8,128)S(1)} %fusion.3), channel_id=1, source_target_pairs={{0,4},{4,0},{8,12},{12,8},{16,20},{20,16},{24,28},{28,24},{1,5},{5... | collective-permute-start | bytes 98312 | tf_op jit(solution)/shard_map/ppermute | solution.py:29
  42.4 0.9 %collective-permute-start.13 = (f32[64,128]{1,0:T(8,128)S(1)}, f32[64,128]{1,0:T(8,128)S(1)}, u32[]{:S(2)}, u32[]{:S(2)}) collective-permute-start(f32[64,128]{1,0:T(8,128)S(1)} %pad_maximum_fusion.6), channel_id=1, source_target_pairs={{0,4},{4,0},{8,12},{12,8},{16,20},{20,16},{24,28},{28,24},{1,5},{5... | collective-permute-start | bytes 98312 | tf_op jit(solution)/shard_map/ppermute | solution.py:29
  43.3 1.8 %collective-permute-done.10 = f32[64,128]{1,0:T(8,128)S(1)} collective-permute-done((f32[64,128]{1,0:T(8,128)S(1)}, f32[64,128]{1,0:T(8,128)S(1)}, u32[]{:S(2)}, u32[]{:S(2)}) %collective-permute-start.10) | collective-permute-done | bytes 32800 | tf_op jit(solution)/shard_map/ppermute | solution.py:29
  45.1 1.6 %collective-permute-start.11 = (f32[64,128]{1,0:T(8,128)S(1)}, f32[64,128]{1,0:T(8,128)S(1)}, u32[]{:S(2)}, u32[]{:S(2)}) collective-permute-start(f32[64,128]{1,0:T(8,128)S(1)} %add.76), channel_id=1, source_target_pairs={{0,8},{4,12},{8,0},{12,4},{16,24},{20,28},{24,16},{28,20},{1,9},{5... | collective-permute-start | bytes 98312 | tf_op jit(solution)/shard_map/ppermute | solution.py:29
  46.7 1.5 %collective-permute-start.14 = (f32[64,128]{1,0:T(8,128)S(1)}, f32[64,128]{1,0:T(8,128)S(1)}, u32[]{:S(2)}, u32[]{:S(2)}) collective-permute-start(f32[64,128]{1,0:T(8,128)S(1)} %fusion.123), channel_id=1, source_target_pairs={{0,8},{4,12},{8,0},{12,4},{16,24},{20,28},{24,16},{28,20},{1,9},{5... | collective-permute-start | bytes 98312 | tf_op jit(solution)/shard_map/ppermute | solution.py:29
  48.2 0.9 %collective-permute-done.11 = f32[64,128]{1,0:T(8,128)S(1)} collective-permute-done((f32[64,128]{1,0:T(8,128)S(1)}, f32[64,128]{1,0:T(8,128)S(1)}, u32[]{:S(2)}, u32[]{:S(2)}) %collective-permute-start.11) | collective-permute-done | bytes 32800 | tf_op jit(solution)/shard_map/ppermute | solution.py:29
  49.1 2.1 %collective-permute-start.12 = (f32[64,128]{1,0:T(8,128)S(1)}, f32[64,128]{1,0:T(8,128)S(1)}, u32[]{:S(2)}, u32[]{:S(2)}) collective-permute-start(f32[64,128]{1,0:T(8,128)S(1)} %add.77), channel_id=1, source_target_pairs={{0,16},{4,20},{8,24},{12,28},{16,0},{20,4},{24,8},{28,12},{1,17},{... | collective-permute-start | bytes 98312 | tf_op jit(solution)/shard_map/ppermute | solution.py:29
  51.2 2.1 %collective-permute-start.15 = (f32[64,128]{1,0:T(8,128)S(1)}, f32[64,128]{1,0:T(8,128)S(1)}, u32[]{:S(2)}, u32[]{:S(2)}) collective-permute-start(f32[64,128]{1,0:T(8,128)S(1)} %add.80), channel_id=1, source_target_pairs={{0,16},{4,20},{8,24},{12,28},{16,0},{20,4},{24,8},{28,12},{1,17},{... | collective-permute-start | bytes 98312 | tf_op jit(solution)/shard_map/ppermute | solution.py:29
  53.3 0.6 collective-permute-done.12
  53.9 0.6 add.78.head_ref
  54.5 7.2 %shard_map.18 = f32[64,64]{1,0:T(8,128)} custom-call(f32[64,128]{1,0:T(8,128)} %add.78.head_ref), custom_call_target="tpu_custom_call" | custom-call | tf_op jit(solution)/shard_map/pallas_call | solution.py:62
  61.8 1.1 %convolution_subtract_fusion.1 = f32[64,768]{1,0:T(8,128)S(1)} fusion(f32[64,64]{1,0:T(8,128)} %shard_map.18, f32[64,768]{1,0:T(8,128)S(1)} %fusion.1, s32[768]{0:T(1024)S(1)} %fusion.39), kind=kOutput, calls=%fused_computation.2 | convolution fusion | flops 37896192 | bytes 412672 | tf_op jit(solution)/shard_map/dot_general | solution.py:15
  66.2 1.1 %fusion = f32[1,64,768]{2,1,0:T(8,128)} fusion(f32[64,768]{1,0:T(8,128)S(1)} %convolution_subtract_fusion.3, f32[64,64]{1,0:T(8,128)S(1)} %fusion.18, f32[64,768]{1,0:T(8,128)S(1)} %convolution_subtract_fusion.1), kind=kOutput, calls=%fused_computation.1 | convolution fusion | flops 37797888 | bytes 606208 | tf_op jit(solution)/shard_map/dot_general | solution.py:151
  (82 shorter events, 9.0 us)
Async XLA Ops:
  0.0 0.9 %copy-start = (f32[1,64,768]{2,1,0:T(8,128)S(1)}, f32[1,64,768]{2,1,0:T(8,128)}, u32[]{:S(2)}) copy-start(f32[1,64,768]{2,1,0:T(8,128)} %param.1) | copy-start | bytes 589828
  1.5 6.6 %collective-permute-start = (f32[64,128]{1,0:T(8,128)S(1)}, f32[64,128]{1,0:T(8,128)S(1)}, u32[]{:S(2)}, u32[]{:S(2)}) collective-permute-start(f32[64,128]{1,0:T(8,128)S(1)} %convolution_bitcast_fusion), channel_id=1, source_target_pairs={{0,2},{4,6},{8,10},{12,14},{16,18},{20,22},{24,26},{28,30}} | collective-permute-start | bytes 98312 | tf_op jit(solution)/shard_map/ppermute | solution.py:86
  6.3 5.2 %collective-permute-start.5 = (f32[64,768]{1,0:T(8,128)S(1)}, f32[64,768]{1,0:T(8,128)S(1)}, u32[]{:S(2)}, u32[]{:S(2)}) collective-permute-start(f32[64,768]{1,0:T(8,128)S(1)} %bitcast.76), channel_id=1, source_target_pairs={{0,2},{1,3},{4,6},{5,7},{8,10},{9,11},{12,14},{13,15},{16,18},{17,... | collective-permute-start | bytes 589832 | tf_op jit(solution)/shard_map/ppermute | solution.py:72
  8.0 3.6 %collective-permute-start.1 = (f32[64,128]{1,0:T(8,128)S(1)}, f32[64,128]{1,0:T(8,128)S(1)}, u32[]{:S(2)}, u32[]{:S(2)}) collective-permute-start(f32[64,128]{1,0:T(8,128)S(1)} %broadcast_select_fusion.5), channel_id=1, source_target_pairs={{0,1},{2,3},{4,5},{6,7},{8,9},{10,11},{12,13},{14,15},{16,17},{18,... | collective-permute-start | bytes 98312 | tf_op jit(solution)/shard_map/ppermute | solution.py:86
  11.5 5.7 %collective-permute-start.6 = (f32[64,768]{1,0:T(8,128)S(1)}, f32[64,768]{1,0:T(8,128)S(1)}, u32[]{:S(2)}, u32[]{:S(2)}) collective-permute-start(f32[64,768]{1,0:T(8,128)S(1)} %broadcast_select_fusion), channel_id=1, source_target_pairs={{0,1},{1,0},{2,3},{3,2},{4,5},{5,4},{6,7},{7,6},{8,9},{9,8},{10,11... | collective-permute-start | bytes 589832 | tf_op jit(solution)/shard_map/ppermute | solution.py:77
  11.6 4.0 %collective-permute-start.2 = (f32[64,128]{1,0:T(8,128)S(1)}, f32[64,128]{1,0:T(8,128)S(1)}, u32[]{:S(2)}, u32[]{:S(2)}) collective-permute-start(f32[64,128]{1,0:T(8,128)S(1)} %broadcast_select_fusion.6), channel_id=1, source_target_pairs={{0,4},{4,0},{8,12},{12,8},{16,20},{20,16},{24,28},{28,24},{1,5},{5... | collective-permute-start | bytes 98312 | tf_op jit(solution)/shard_map/ppermute | solution.py:29
  15.6 4.1 %collective-permute-start.3 = (f32[64,128]{1,0:T(8,128)S(1)}, f32[64,128]{1,0:T(8,128)S(1)}, u32[]{:S(2)}, u32[]{:S(2)}) collective-permute-start(f32[64,128]{1,0:T(8,128)S(1)} %add.70), channel_id=1, source_target_pairs={{0,8},{4,12},{8,0},{12,4},{16,24},{20,28},{24,16},{28,20},{1,9},{5... | collective-permute-start | bytes 98312 | tf_op jit(solution)/shard_map/ppermute | solution.py:29
  18.1 4.3 %collective-permute-start.7 = (f32[64,256]{1,0:T(8,128)S(1)}, f32[64,256]{1,0:T(8,128)S(1)}, u32[]{:S(2)}, u32[]{:S(2)}) collective-permute-start(f32[64,256]{1,0:T(8,128)S(1)} %pad_maximum_fusion.5), channel_id=1, source_target_pairs={{0,4},{4,0},{8,12},{12,8},{16,20},{20,16},{24,28},{28,24},{1,5},{5... | collective-permute-start | bytes 196616 | tf_op jit(solution)/shard_map/ppermute | solution.py:29
  19.7 4.9 %collective-permute-start.4 = (f32[64,128]{1,0:T(8,128)S(1)}, f32[64,128]{1,0:T(8,128)S(1)}, u32[]{:S(2)}, u32[]{:S(2)}) collective-permute-start(f32[64,128]{1,0:T(8,128)S(1)} %add.71), channel_id=1, source_target_pairs={{0,16},{4,20},{8,24},{12,28},{16,0},{20,4},{24,8},{28,12},{1,17},{... | collective-permute-start | bytes 98312 | tf_op jit(solution)/shard_map/ppermute | solution.py:29
  22.5 10.0 %collective-permute-start.8 = (f32[64,256]{1,0:T(8,128)S(1)}, f32[64,256]{1,0:T(8,128)S(1)}, u32[]{:S(2)}, u32[]{:S(2)}) collective-permute-start(f32[64,256]{1,0:T(8,128)S(1)} %fusion.49), channel_id=1, source_target_pairs={{0,8},{4,12},{8,0},{12,4},{16,24},{20,28},{24,16},{28,20},{1,9},{5... | collective-permute-start | bytes 196616 | tf_op jit(solution)/shard_map/ppermute | solution.py:29
  32.5 2.8 %copy-start.1 = (f32[64,64]{1,0:T(8,128)S(1)}, f32[64,64]{1,0:T(8,128)}, u32[]{:S(2)}) copy-start(f32[64,64]{1,0:T(8,128)} %shard_map.17) | copy-start | bytes 49156
  32.5 2.8 %copy-start.3 = (f32[64,128]{1,0:T(8,128)S(1)}, f32[64,128]{1,0:T(8,128)}, u32[]{:S(2)}) copy-start(f32[64,128]{1,0:T(8,128)} %add.72.head_ref) | copy-start | bytes 98308
  32.5 5.9 %collective-permute-start.9 = (f32[64,256]{1,0:T(8,128)S(1)}, f32[64,256]{1,0:T(8,128)S(1)}, u32[]{:S(2)}, u32[]{:S(2)}) collective-permute-start(f32[64,256]{1,0:T(8,128)S(1)} %add.74), channel_id=1, source_target_pairs={{0,16},{4,20},{8,24},{12,28},{16,0},{20,4},{24,8},{28,12},{1,17},{... | collective-permute-start | bytes 196616 | tf_op jit(solution)/shard_map/ppermute | solution.py:29
  41.1 4.0 %collective-permute-start.10 = (f32[64,128]{1,0:T(8,128)S(1)}, f32[64,128]{1,0:T(8,128)S(1)}, u32[]{:S(2)}, u32[]{:S(2)}) collective-permute-start(f32[64,128]{1,0:T(8,128)S(1)} %fusion.3), channel_id=1, source_target_pairs={{0,4},{4,0},{8,12},{12,8},{16,20},{20,16},{24,28},{28,24},{1,5},{5... | collective-permute-start | bytes 98312 | tf_op jit(solution)/shard_map/ppermute | solution.py:29
  42.4 4.3 %collective-permute-start.13 = (f32[64,128]{1,0:T(8,128)S(1)}, f32[64,128]{1,0:T(8,128)S(1)}, u32[]{:S(2)}, u32[]{:S(2)}) collective-permute-start(f32[64,128]{1,0:T(8,128)S(1)} %pad_maximum_fusion.6), channel_id=1, source_target_pairs={{0,4},{4,0},{8,12},{12,8},{16,20},{20,16},{24,28},{28,24},{1,5},{5... | collective-permute-start | bytes 98312 | tf_op jit(solution)/shard_map/ppermute | solution.py:29
  45.1 4.0 %collective-permute-start.11 = (f32[64,128]{1,0:T(8,128)S(1)}, f32[64,128]{1,0:T(8,128)S(1)}, u32[]{:S(2)}, u32[]{:S(2)}) collective-permute-start(f32[64,128]{1,0:T(8,128)S(1)} %add.76), channel_id=1, source_target_pairs={{0,8},{4,12},{8,0},{12,4},{16,24},{20,28},{24,16},{28,20},{1,9},{5... | collective-permute-start | bytes 98312 | tf_op jit(solution)/shard_map/ppermute | solution.py:29
  46.7 4.5 %collective-permute-start.14 = (f32[64,128]{1,0:T(8,128)S(1)}, f32[64,128]{1,0:T(8,128)S(1)}, u32[]{:S(2)}, u32[]{:S(2)}) collective-permute-start(f32[64,128]{1,0:T(8,128)S(1)} %fusion.123), channel_id=1, source_target_pairs={{0,8},{4,12},{8,0},{12,4},{16,24},{20,28},{24,16},{28,20},{1,9},{5... | collective-permute-start | bytes 98312 | tf_op jit(solution)/shard_map/ppermute | solution.py:29
  49.1 4.8 %collective-permute-start.12 = (f32[64,128]{1,0:T(8,128)S(1)}, f32[64,128]{1,0:T(8,128)S(1)}, u32[]{:S(2)}, u32[]{:S(2)}) collective-permute-start(f32[64,128]{1,0:T(8,128)S(1)} %add.77), channel_id=1, source_target_pairs={{0,16},{4,20},{8,24},{12,28},{16,0},{20,4},{24,8},{28,12},{1,17},{... | collective-permute-start | bytes 98312 | tf_op jit(solution)/shard_map/ppermute | solution.py:29
  51.2 12.1 %collective-permute-start.15 = (f32[64,128]{1,0:T(8,128)S(1)}, f32[64,128]{1,0:T(8,128)S(1)}, u32[]{:S(2)}, u32[]{:S(2)}) collective-permute-start(f32[64,128]{1,0:T(8,128)S(1)} %add.80), channel_id=1, source_target_pairs={{0,16},{4,20},{8,24},{12,28},{16,0},{20,4},{24,8},{28,12},{1,17},{... | collective-permute-start | bytes 98312 | tf_op jit(solution)/shard_map/ppermute | solution.py:29
  61.8 1.1 %copy-start.2 = (f32[64,64]{1,0:T(8,128)S(1)}, f32[64,64]{1,0:T(8,128)}, u32[]{:S(2)}) copy-start(f32[64,64]{1,0:T(8,128)} %shard_map.18) | copy-start | bytes 49156
  61.8 1.2 %copy-start.4 = (f32[64,128]{1,0:T(8,128)S(1)}, f32[64,128]{1,0:T(8,128)}, u32[]{:S(2)}) copy-start(f32[64,128]{1,0:T(8,128)} %add.78.head_ref) | copy-start | bytes 98308

commit v13 on v12

--- a/solution.py
+++ b/solution.py
@@ -133,17 +133,18 @@
         second = second - jnp.dot(mixed_sec.T, reflect, precision=HIGHEST_PRECISION)
 
         panel_1 = jnp.where((global_rows >= width)[None, :], second, jnp.zeros_like(second))
-        head = butterfly_sum(
-            inner_rows(panel_1, jnp.concatenate([panel_1, units[1]])), "rows", rows_size
-        )
-        tail = butterfly_sum(
-            jnp.concatenate([inner_rows(panel_1, current), inner_rows(units[1], current)], axis=1),
+        sums = butterfly_sum(
+            jnp.concatenate(
+                [inner_rows(panel_1, jnp.concatenate([panel_1, units[1]])),
+                 inner_rows(panel_1, current), inner_rows(units[1], current)],
+                axis=1,
+            ),
             "rows",
             rows_size,
         )
-        top_rows = head[:, width:]
-        basis_cur, unit_cur = tail[:, :width], tail[:, width:]
-        lower_inv = lower_inverse(head)
+        top_rows = sums[:, width:2 * width]
+        basis_cur, unit_cur = sums[:, 2 * width:3 * width], sums[:, 3 * width:]
+        lower_inv = lower_inverse(sums)
         top_block = apply_left(lower_inv, top_rows)
         inverse = invert_near_identity(identity - top_block.T)
         reflect = units[1] - apply_left(lower_inv, panel_1)

time: 67.7 us -> 70.2 us (1.037)
  waiting for transfers between devices: 9.22 us -> 16.7 us
  starting transfers between devices: 28.2 us -> 23.2 us
    ppermute x12 -> x9, waiting for transfers between devices: 6.68 us -> 14.2 us  [butterfly_sum(): x = x + lax.ppermute(x, axis, [(i, i ^ step) for i in range(size)])]
    ppermute x12 -> x9, starting transfers between devices: 20.7 us -> 15.7 us  [butterfly_sum(): x = x + lax.ppermute(x, axis, [(i, i ^ step) for i in range(size)])]
  transfers between devices with their start and end apart: 16 -> 13, of which waited for: 8 -> 8; matrix products, arithmetic and copies ran while one was open for 10% -> 7% of each run, Pallas kernels for 22% -> 10%
where the time goes in v13:
time: 70.2 us; the launch traced here: 69.8 us
  starting transfers between devices  23.2 us (33%)
  waiting for transfers between devices  16.7 us (24%)
  Pallas kernels  14.6 us (21%)
  matrix products  12.3 us (18%)
  other arithmetic  1.59 us (2%)
  local copies, waits for them, and re-layouts  0.91 us (1%)
    ppermute x9, starting transfers between devices, butterfly_sum(): x = x + lax.ppermute(x, axis, [(i, i ^ step) for i in range(size)])  15.7 us
    pallas_call x2, Pallas kernels, lower_inverse(): pl.pallas_call(_eliminate_kernel, out_shape=jax.ShapeDtypeStruct((size, s...  14.6 us
    ppermute x9, waiting for transfers between devices, butterfly_sum(): x = x + lax.ppermute(x, axis, [(i, i ^ step) for i in range(size)])  14.2 us
    dot_general x38, matrix products, apply_left(): return jnp.dot(square, right_side, precision=HIGHEST_PRECISION)  7.98 us
    ppermute x2, starting transfers between devices, from_root(): lax.ppermute(value, axis, [(i, i + dist) for i in range(size) if i % (2 *...  6.15 us
    dot_general x6, matrix products, inner_rows(): lax.dot_general(left, right, (((1,), (1,)), ((), ())), precision=HIGHEST_...  2.51 us
    ppermute x1, waiting for transfers between devices, spread_pair(): lax.ppermute(have, axis, [(i, i + dist) for i in range(size) if i % (2 *...  2.18 us
    dot_general x2, matrix products, local(): current = current - jnp.dot(mixed.T, reflect, precision=HIGHEST_PRECISION)  1.43 us
  transfers between devices with their start and end apart: 13, of which 8 were waited for; matrix products, arithmetic and copies ran while one was open for 7% of the time, Pallas kernels for 10%

profile of v13, /device:TPU:0, one launch (start us, length us, event | category | flops | bytes accessed | tf_op | source)
XLA Modules:
  0.0 69.8 jit_solution(10181730768236454958)
XLA Ops:
  0.0 0.9 %copy-done = f32[1,64,768]{2,1,0:T(8,128)S(1)} copy-done((f32[1,64,768]{2,1,0:T(8,128)S(1)}, f32[1,64,768]{2,1,0:T(8,128)}, u32[]{:S(2)}) %copy-start) | copy-done | bytes 196632
  0.9 0.5 convolution_bitcast_fusion
  1.5 4.9 %collective-permute-start = (f32[64,128]{1,0:T(8,128)S(1)}, f32[64,128]{1,0:T(8,128)S(1)}, u32[]{:S(2)}, u32[]{:S(2)}) collective-permute-start(f32[64,128]{1,0:T(8,128)S(1)} %convolution_bitcast_fusion), channel_id=1, source_target_pairs={{0,2},{4,6},{8,10},{12,14},{16,18},{20,22},{24,26},{28,30}} | collective-permute-start | bytes 98312 | tf_op jit(solution)/shard_map/ppermute | solution.py:86
  6.3 1.3 %collective-permute-start.5 = (f32[64,768]{1,0:T(8,128)S(1)}, f32[64,768]{1,0:T(8,128)S(1)}, u32[]{:S(2)}, u32[]{:S(2)}) collective-permute-start(f32[64,768]{1,0:T(8,128)S(1)} %bitcast.76), channel_id=1, source_target_pairs={{0,2},{1,3},{4,6},{5,7},{8,10},{9,11},{12,14},{13,15},{16,18},{17,... | collective-permute-start | bytes 589832 | tf_op jit(solution)/shard_map/ppermute | solution.py:72
  7.7 0.3 collective-permute-done
  8.0 1.3 %collective-permute-start.1 = (f32[64,128]{1,0:T(8,128)S(1)}, f32[64,128]{1,0:T(8,128)S(1)}, u32[]{:S(2)}, u32[]{:S(2)}) collective-permute-start(f32[64,128]{1,0:T(8,128)S(1)} %broadcast_select_fusion.5), channel_id=1, source_target_pairs={{0,1},{2,3},{4,5},{6,7},{8,9},{10,11},{12,13},{14,15},{16,17},{18,... | collective-permute-start | bytes 98312 | tf_op jit(solution)/shard_map/ppermute | solution.py:86
  9.3 2.2 %collective-permute-done.5 = f32[64,768]{1,0:T(8,128)S(1)} collective-permute-done((f32[64,768]{1,0:T(8,128)S(1)}, f32[64,768]{1,0:T(8,128)S(1)}, u32[]{:S(2)}, u32[]{:S(2)}) %collective-permute-start.5) | collective-permute-done | bytes 196640 | tf_op jit(solution)/shard_map/ppermute | solution.py:72
  11.6 1.6 %collective-permute-start.2 = (f32[64,128]{1,0:T(8,128)S(1)}, f32[64,128]{1,0:T(8,128)S(1)}, u32[]{:S(2)}, u32[]{:S(2)}) collective-permute-start(f32[64,128]{1,0:T(8,128)S(1)} %broadcast_select_fusion.6), channel_id=1, source_target_pairs={{0,4},{4,0},{8,12},{12,8},{16,20},{20,16},{24,28},{28,24},{1,5},{5... | collective-permute-start | bytes 98312 | tf_op jit(solution)/shard_map/ppermute | solution.py:29
  13.2 2.4 %collective-permute-done.2 = f32[64,128]{1,0:T(8,128)S(1)} collective-permute-done((f32[64,128]{1,0:T(8,128)S(1)}, f32[64,128]{1,0:T(8,128)S(1)}, u32[]{:S(2)}, u32[]{:S(2)}) %collective-permute-start.2) | collective-permute-done | bytes 32800 | tf_op jit(solution)/shard_map/ppermute | solution.py:29
  15.6 1.6 %collective-permute-start.3 = (f32[64,128]{1,0:T(8,128)S(1)}, f32[64,128]{1,0:T(8,128)S(1)}, u32[]{:S(2)}, u32[]{:S(2)}) collective-permute-start(f32[64,128]{1,0:T(8,128)S(1)} %add.61), channel_id=1, source_target_pairs={{0,8},{4,12},{8,0},{12,4},{16,24},{20,28},{24,16},{28,20},{1,9},{5... | collective-permute-start | bytes 98312 | tf_op jit(solution)/shard_map/ppermute | solution.py:29
  17.2 0.4 fusion.7
  17.6 0.5 fusion.8
  18.1 1.6 %collective-permute-start.7 = (f32[64,256]{1,0:T(8,128)S(1)}, f32[64,256]{1,0:T(8,128)S(1)}, u32[]{:S(2)}, u32[]{:S(2)}) collective-permute-start(f32[64,256]{1,0:T(8,128)S(1)} %pad_maximum_fusion.5), channel_id=1, source_target_pairs={{0,4},{4,0},{8,12},{12,8},{16,20},{20,16},{24,28},{28,24},{1,5},{5... | collective-permute-start | bytes 196616 | tf_op jit(solution)/shard_map/ppermute | solution.py:29
  19.7 2.7 %collective-permute-start.4 = (f32[64,128]{1,0:T(8,128)S(1)}, f32[64,128]{1,0:T(8,128)S(1)}, u32[]{:S(2)}, u32[]{:S(2)}) collective-permute-start(f32[64,128]{1,0:T(8,128)S(1)} %add.62), channel_id=1, source_target_pairs={{0,16},{4,20},{8,24},{12,28},{16,0},{20,4},{24,8},{28,12},{1,17},{... | collective-permute-start | bytes 98312 | tf_op jit(solution)/shard_map/ppermute | solution.py:29
  22.5 1.3 %collective-permute-start.8 = (f32[64,256]{1,0:T(8,128)S(1)}, f32[64,256]{1,0:T(8,128)S(1)}, u32[]{:S(2)}, u32[]{:S(2)}) collective-permute-start(f32[64,256]{1,0:T(8,128)S(1)} %fusion.49), channel_id=1, source_target_pairs={{0,8},{4,12},{8,0},{12,4},{16,24},{20,28},{24,16},{28,20},{1,9},{5... | collective-permute-start | bytes 196616 | tf_op jit(solution)/shard_map/ppermute | solution.py:29
  23.8 0.8 %collective-permute-done.4 = f32[64,128]{1,0:T(8,128)S(1)} collective-permute-done((f32[64,128]{1,0:T(8,128)S(1)}, f32[64,128]{1,0:T(8,128)S(1)}, u32[]{:S(2)}, u32[]{:S(2)}) %collective-permute-start.4) | collective-permute-done | bytes 32800 | tf_op jit(solution)/shard_map/ppermute | solution.py:29
  24.6 0.6 add.63.head_ref
  25.2 7.2 %shard_map.17 = f32[64,64]{1,0:T(8,128)} custom-call(f32[64,128]{1,0:T(8,128)} %add.63.head_ref), custom_call_target="tpu_custom_call" | custom-call | tf_op jit(solution)/shard_map/pallas_call | solution.py:62
  32.5 2.8 %collective-permute-start.9 = (f32[64,256]{1,0:T(8,128)S(1)}, f32[64,256]{1,0:T(8,128)S(1)}, u32[]{:S(2)}, u32[]{:S(2)}) collective-permute-start(f32[64,256]{1,0:T(8,128)S(1)} %add.65), channel_id=1, source_target_pairs={{0,16},{4,20},{8,24},{12,28},{16,0},{20,4},{24,8},{28,12},{1,17},{... | collective-permute-start | bytes 196616 | tf_op jit(solution)/shard_map/ppermute | solution.py:29
  39.2 0.4 convolution_subtract_fusion.3
  39.9 0.4 fusion.1
  40.6 0.5 fusion.3
  41.2 1.2 %collective-permute-start.10 = (f32[64,256]{1,0:T(8,128)S(1)}, f32[64,256]{1,0:T(8,128)S(1)}, u32[]{:S(2)}, u32[]{:S(2)}) collective-permute-start(f32[64,256]{1,0:T(8,128)S(1)} %pad_maximum_fusion.6), channel_id=1, source_target_pairs={{0,4},{4,0},{8,12},{12,8},{16,20},{20,16},{24,28},{28,24},{1,5},{5... | collective-permute-start | bytes 196616 | tf_op jit(solution)/shard_map/ppermute | solution.py:29
  42.3 3.1 %collective-permute-done.10 = f32[64,256]{1,0:T(8,128)S(1)} collective-permute-done((f32[64,256]{1,0:T(8,128)S(1)}, f32[64,256]{1,0:T(8,128)S(1)}, u32[]{:S(2)}, u32[]{:S(2)}) %collective-permute-start.10) | collective-permute-done | bytes 65568 | tf_op jit(solution)/shard_map/ppermute | solution.py:29
  45.5 1.6 %collective-permute-start.11 = (f32[64,256]{1,0:T(8,128)S(1)}, f32[64,256]{1,0:T(8,128)S(1)}, u32[]{:S(2)}, u32[]{:S(2)}) collective-permute-start(f32[64,256]{1,0:T(8,128)S(1)} %fusion.123), channel_id=1, source_target_pairs={{0,8},{4,12},{8,0},{12,4},{16,24},{20,28},{24,16},{28,20},{1,9},{5... | collective-permute-start | bytes 196616 | tf_op jit(solution)/shard_map/ppermute | solution.py:29
  47.1 3.4 %collective-permute-done.11 = f32[64,256]{1,0:T(8,128)S(1)} collective-permute-done((f32[64,256]{1,0:T(8,128)S(1)}, f32[64,256]{1,0:T(8,128)S(1)}, u32[]{:S(2)}, u32[]{:S(2)}) %collective-permute-start.11) | collective-permute-done | bytes 65568 | tf_op jit(solution)/shard_map/ppermute | solution.py:29
  50.5 1.6 %collective-permute-start.12 = (f32[64,256]{1,0:T(8,128)S(1)}, f32[64,256]{1,0:T(8,128)S(1)}, u32[]{:S(2)}, u32[]{:S(2)}) collective-permute-start(f32[64,256]{1,0:T(8,128)S(1)} %add.68), channel_id=1, source_target_pairs={{0,16},{4,20},{8,24},{12,28},{16,0},{20,4},{24,8},{28,12},{1,17},{... | collective-permute-start | bytes 196616 | tf_op jit(solution)/shard_map/ppermute | solution.py:29
  52.1 4.4 %collective-permute-done.12 = f32[64,256]{1,0:T(8,128)S(1)} collective-permute-done((f32[64,256]{1,0:T(8,128)S(1)}, f32[64,256]{1,0:T(8,128)S(1)}, u32[]{:S(2)}, u32[]{:S(2)}) %collective-permute-start.12) | collective-permute-done | bytes 65568 | tf_op jit(solution)/shard_map/ppermute | solution.py:29
  56.4 0.6 add.69.head_ref
  57.1 7.3 %shard_map.18 = f32[64,64]{1,0:T(8,128)} custom-call(f32[64,256]{1,0:T(8,128)} %add.69.head_ref), custom_call_target="tpu_custom_call" | custom-call | tf_op jit(solution)/shard_map/pallas_call | solution.py:62
  64.4 1.1 %convolution_subtract_fusion.1 = f32[64,768]{1,0:T(8,128)S(1)} fusion(f32[64,64]{1,0:T(8,128)} %shard_map.18, f32[64,768]{1,0:T(8,128)S(1)} %fusion.1, s32[768]{0:T(1024)S(1)} %fusion.39), kind=kOutput, calls=%fused_computation.2 | convolution fusion | flops 37896192 | bytes 412672 | tf_op jit(solution)/shard_map/dot_general | solution.py:15
  68.7 1.1 %fusion = f32[1,64,768]{2,1,0:T(8,128)} fusion(f32[64,768]{1,0:T(8,128)S(1)} %convolution_subtract_fusion.3, f32[64,64]{1,0:T(8,128)S(1)} %fusion.18, f32[64,768]{1,0:T(8,128)S(1)} %convolution_subtract_fusion.1), kind=kOutput, calls=%fused_computation.1 | convolution fusion | flops 37797888 | bytes 606208 | tf_op jit(solution)/shard_map/dot_general | solution.py:152
  (73 shorter events, 7.9 us)
Async XLA Ops:
  0.0 0.9 %copy-start = (f32[1,64,768]{2,1,0:T(8,128)S(1)}, f32[1,64,768]{2,1,0:T(8,128)}, u32[]{:S(2)}) copy-start(f32[1,64,768]{2,1,0:T(8,128)} %param.1) | copy-start | bytes 589828
  1.5 6.6 %collective-permute-start = (f32[64,128]{1,0:T(8,128)S(1)}, f32[64,128]{1,0:T(8,128)S(1)}, u32[]{:S(2)}, u32[]{:S(2)}) collective-permute-start(f32[64,128]{1,0:T(8,128)S(1)} %convolution_bitcast_fusion), channel_id=1, source_target_pairs={{0,2},{4,6},{8,10},{12,14},{16,18},{20,22},{24,26},{28,30}} | collective-permute-start | bytes 98312 | tf_op jit(solution)/shard_map/ppermute | solution.py:86
  6.3 5.2 %collective-permute-start.5 = (f32[64,768]{1,0:T(8,128)S(1)}, f32[64,768]{1,0:T(8,128)S(1)}, u32[]{:S(2)}, u32[]{:S(2)}) collective-permute-start(f32[64,768]{1,0:T(8,128)S(1)} %bitcast.76), channel_id=1, source_target_pairs={{0,2},{1,3},{4,6},{5,7},{8,10},{9,11},{12,14},{13,15},{16,18},{17,... | collective-permute-start | bytes 589832 | tf_op jit(solution)/shard_map/ppermute | solution.py:72
  8.0 3.6 %collective-permute-start.1 = (f32[64,128]{1,0:T(8,128)S(1)}, f32[64,128]{1,0:T(8,128)S(1)}, u32[]{:S(2)}, u32[]{:S(2)}) collective-permute-start(f32[64,128]{1,0:T(8,128)S(1)} %broadcast_select_fusion.5), channel_id=1, source_target_pairs={{0,1},{2,3},{4,5},{6,7},{8,9},{10,11},{12,13},{14,15},{16,17},{18,... | collective-permute-start | bytes 98312 | tf_op jit(solution)/shard_map/ppermute | solution.py:86
  11.5 5.7 %collective-permute-start.6 = (f32[64,768]{1,0:T(8,128)S(1)}, f32[64,768]{1,0:T(8,128)S(1)}, u32[]{:S(2)}, u32[]{:S(2)}) collective-permute-start(f32[64,768]{1,0:T(8,128)S(1)} %broadcast_select_fusion), channel_id=1, source_target_pairs={{0,1},{1,0},{2,3},{3,2},{4,5},{5,4},{6,7},{7,6},{8,9},{9,8},{10,11... | collective-permute-start | bytes 589832 | tf_op jit(solution)/shard_map/ppermute | solution.py:77
  11.6 4.0 %collective-permute-start.2 = (f32[64,128]{1,0:T(8,128)S(1)}, f32[64,128]{1,0:T(8,128)S(1)}, u32[]{:S(2)}, u32[]{:S(2)}) collective-permute-start(f32[64,128]{1,0:T(8,128)S(1)} %broadcast_select_fusion.6), channel_id=1, source_target_pairs={{0,4},{4,0},{8,12},{12,8},{16,20},{20,16},{24,28},{28,24},{1,5},{5... | collective-permute-start | bytes 98312 | tf_op jit(solution)/shard_map/ppermute | solution.py:29
  15.6 4.1 %collective-permute-start.3 = (f32[64,128]{1,0:T(8,128)S(1)}, f32[64,128]{1,0:T(8,128)S(1)}, u32[]{:S(2)}, u32[]{:S(2)}) collective-permute-start(f32[64,128]{1,0:T(8,128)S(1)} %add.61), channel_id=1, source_target_pairs={{0,8},{4,12},{8,0},{12,4},{16,24},{20,28},{24,16},{28,20},{1,9},{5... | collective-permute-start | bytes 98312 | tf_op jit(solution)/shard_map/ppermute | solution.py:29
  18.1 4.3 %collective-permute-start.7 = (f32[64,256]{1,0:T(8,128)S(1)}, f32[64,256]{1,0:T(8,128)S(1)}, u32[]{:S(2)}, u32[]{:S(2)}) collective-permute-start(f32[64,256]{1,0:T(8,128)S(1)} %pad_maximum_fusion.5), channel_id=1, source_target_pairs={{0,4},{4,0},{8,12},{12,8},{16,20},{20,16},{24,28},{28,24},{1,5},{5... | collective-permute-start | bytes 196616 | tf_op jit(solution)/shard_map/ppermute | solution.py:29
  19.7 4.9 %collective-permute-start.4 = (f32[64,128]{1,0:T(8,128)S(1)}, f32[64,128]{1,0:T(8,128)S(1)}, u32[]{:S(2)}, u32[]{:S(2)}) collective-permute-start(f32[64,128]{1,0:T(8,128)S(1)} %add.62), channel_id=1, source_target_pairs={{0,16},{4,20},{8,24},{12,28},{16,0},{20,4},{24,8},{28,12},{1,17},{... | collective-permute-start | bytes 98312 | tf_op jit(solution)/shard_map/ppermute | solution.py:29
  22.5 10.0 %collective-permute-start.8 = (f32[64,256]{1,0:T(8,128)S(1)}, f32[64,256]{1,0:T(8,128)S(1)}, u32[]{:S(2)}, u32[]{:S(2)}) collective-permute-start(f32[64,256]{1,0:T(8,128)S(1)} %fusion.49), channel_id=1, source_target_pairs={{0,8},{4,12},{8,0},{12,4},{16,24},{20,28},{24,16},{28,20},{1,9},{5... | collective-permute-start | bytes 196616 | tf_op jit(solution)/shard_map/ppermute | solution.py:29
  32.5 2.8 %copy-start.1 = (f32[64,64]{1,0:T(8,128)S(1)}, f32[64,64]{1,0:T(8,128)}, u32[]{:S(2)}) copy-start(f32[64,64]{1,0:T(8,128)} %shard_map.17) | copy-start | bytes 49156
  32.5 2.8 %copy-start.4 = (f32[64,128]{1,0:T(8,128)S(1)}, f32[64,128]{1,0:T(8,128)}, u32[]{:S(2)}) copy-start(f32[64,128]{1,0:T(8,128)} %add.63.head_ref) | copy-start | bytes 98308
  32.5 5.9 %collective-permute-start.9 = (f32[64,256]{1,0:T(8,128)S(1)}, f32[64,256]{1,0:T(8,128)S(1)}, u32[]{:S(2)}, u32[]{:S(2)}) collective-permute-start(f32[64,256]{1,0:T(8,128)S(1)} %add.65), channel_id=1, source_target_pairs={{0,16},{4,20},{8,24},{12,28},{16,0},{20,4},{24,8},{28,12},{1,17},{... | collective-permute-start | bytes 196616 | tf_op jit(solution)/shard_map/ppermute | solution.py:29
  41.2 4.3 %collective-permute-start.10 = (f32[64,256]{1,0:T(8,128)S(1)}, f32[64,256]{1,0:T(8,128)S(1)}, u32[]{:S(2)}, u32[]{:S(2)}) collective-permute-start(f32[64,256]{1,0:T(8,128)S(1)} %pad_maximum_fusion.6), channel_id=1, source_target_pairs={{0,4},{4,0},{8,12},{12,8},{16,20},{20,16},{24,28},{28,24},{1,5},{5... | collective-permute-start | bytes 196616 | tf_op jit(solution)/shard_map/ppermute | solution.py:29
  45.5 4.9 %collective-permute-start.11 = (f32[64,256]{1,0:T(8,128)S(1)}, f32[64,256]{1,0:T(8,128)S(1)}, u32[]{:S(2)}, u32[]{:S(2)}) collective-permute-start(f32[64,256]{1,0:T(8,128)S(1)} %fusion.123), channel_id=1, source_target_pairs={{0,8},{4,12},{8,0},{12,4},{16,24},{20,28},{24,16},{28,20},{1,9},{5... | collective-permute-start | bytes 196616 | tf_op jit(solution)/shard_map/ppermute | solution.py:29
  50.5 5.9 %collective-permute-start.12 = (f32[64,256]{1,0:T(8,128)S(1)}, f32[64,256]{1,0:T(8,128)S(1)}, u32[]{:S(2)}, u32[]{:S(2)}) collective-permute-start(f32[64,256]{1,0:T(8,128)S(1)} %add.68), channel_id=1, source_target_pairs={{0,16},{4,20},{8,24},{12,28},{16,0},{20,4},{24,8},{28,12},{1,17},{... | collective-permute-start | bytes 196616 | tf_op jit(solution)/shard_map/ppermute | solution.py:29
  64.4 1.1 %copy-start.2 = (f32[64,256]{1,0:T(8,128)S(1)}, f32[64,256]{1,0:T(8,128)}, u32[]{:S(2)}) copy-start(f32[64,256]{1,0:T(8,128)} %add.69.head_ref) | copy-start | bytes 196612
  64.4 1.1 %copy-start.3 = (f32[64,64]{1,0:T(8,128)S(1)}, f32[64,64]{1,0:T(8,128)}, u32[]{:S(2)}) copy-start(f32[64,64]{1,0:T(8,128)} %shard_map.18) | copy-start | bytes 49156

commit v14 on v12

--- a/solution.py
+++ b/solution.py
@@ -13,6 +13,14 @@
 
 def apply_left(square, right_side):
     return jnp.dot(square, right_side, precision=HIGHEST_PRECISION)
+
+
+def reflect_update(block, mixed, lower_inv, unit_rows, panel):
+    weights = jnp.concatenate([mixed, -jnp.dot(lower_inv.T, mixed, precision=HIGHEST_PRECISION)])
+    return block - lax.dot_general(
+        weights, jnp.concatenate([unit_rows, panel]), (((0,), (0,)), ((), ())),
+        precision=HIGHEST_PRECISION,
+    )
 
 
 def butterfly_steps(size):
@@ -126,11 +134,10 @@
         )
         top_block = apply_left(lower_inv, top_rows)
         inverse = invert_near_identity(identity - top_block.T)
-        reflect = units[0] - apply_left(lower_inv, panel_0)
         mixed = apply_left(inverse, unit_cur - apply_left(lower_inv, basis_cur))
         mixed_sec = apply_left(inverse, unit_sec - apply_left(lower_inv, basis_sec))
-        current = current - jnp.dot(mixed.T, reflect, precision=HIGHEST_PRECISION)
-        second = second - jnp.dot(mixed_sec.T, reflect, precision=HIGHEST_PRECISION)
+        current = reflect_update(current, mixed, lower_inv, units[0], panel_0)
+        second = reflect_update(second, mixed_sec, lower_inv, units[0], panel_0)
 
         panel_1 = jnp.where((global_rows >= width)[None, :], second, jnp.zeros_like(second))
         head = butterfly_sum(
@@ -146,9 +153,8 @@
         lower_inv = lower_inverse(head)
         top_block = apply_left(lower_inv, top_rows)
         inverse = invert_near_identity(identity - top_block.T)
-        reflect = units[1] - apply_left(lower_inv, panel_1)
         mixed = apply_left(inverse, unit_cur - apply_left(lower_inv, basis_cur))
-        current = current - jnp.dot(mixed.T, reflect, precision=HIGHEST_PRECISION)
+        current = reflect_update(current, mixed, lower_inv, units[1], panel_1)
         return current.reshape(matrix.shape)
 
     return local

time: 67.7 us -> 68.8 us (1.016)
  local copies, waits for them, and re-layouts: 0.91 us -> 1.64 us
    unnamed x10, local copies, waits for them, and re-layouts: 0.91 us -> 1.64 us
    dot_general x38 -> x36, matrix products: 7.99 us -> 7.51 us  [apply_left(): return jnp.dot(square, right_side, precision=HIGHEST_PRECISION)]
    dot_general x3 -> x6, matrix products: 1.8 us -> 2.28 us  [the longest x3 1.79 us: reflect_update(): lax.dot_general(weights, jnp.concatenate([unit_rows, panel]), (((0,), (0,...]
  transfers between devices with their start and end apart: 16 -> 16, of which waited for: 8 -> 8; matrix products, arithmetic and copies ran while one was open for 10% -> 9% of each run, Pallas kernels for 22% -> 21%
where the time goes in v14:
time: 68.8 us; the launch traced here: 68.3 us
  starting transfers between devices  28.3 us (41%)
  Pallas kernels  14.6 us (21%)
  matrix products  12.3 us (18%)
  waiting for transfers between devices  9.4 us (14%)
  local copies, waits for them, and re-layouts  1.64 us (2%)
  other arithmetic  1.58 us (2%)
    ppermute x12, starting transfers between devices, butterfly_sum(): x = x + lax.ppermute(x, axis, [(i, i ^ step) for i in range(size)])  20.8 us
    pallas_call x2, Pallas kernels, lower_inverse(): pl.pallas_call(_eliminate_kernel, out_shape=jax.ShapeDtypeStruct((size, s...  14.6 us
    dot_general x36, matrix products, apply_left(): return jnp.dot(square, right_side, precision=HIGHEST_PRECISION)  7.51 us
    ppermute x12, waiting for transfers between devices, butterfly_sum(): x = x + lax.ppermute(x, axis, [(i, i ^ step) for i in range(size)])  6.86 us
    ppermute x2, starting transfers between devices, from_root(): lax.ppermute(value, axis, [(i, i + dist) for i in range(size) if i % (2 *...  6.15 us
    dot_general x6, matrix products, inner_rows(): lax.dot_general(left, right, (((1,), (1,)), ((), ())), precision=HIGHEST_...  2.51 us
    ppermute x1, waiting for transfers between devices, spread_pair(): lax.ppermute(have, axis, [(i, i + dist) for i in range(size) if i % (2 *...  2.18 us
    dot_general x3, matrix products, reflect_update(): lax.dot_general(weights, jnp.concatenate([unit_rows, panel]), (((0,), (0,...  1.79 us
  transfers between devices with their start and end apart: 16, of which 8 were waited for; matrix products, arithmetic and copies ran while one was open for 9% of the time, Pallas kernels for 21%

profile of v14, /device:TPU:0, one launch (start us, length us, event | category | flops | bytes accessed | tf_op | source)
XLA Modules:
  0.0 68.3 jit_solution(5956862889291448637)
XLA Ops:
  0.0 0.9 %copy-done = f32[1,64,768]{2,1,0:T(8,128)S(1)} copy-done((f32[1,64,768]{2,1,0:T(8,128)S(1)}, f32[1,64,768]{2,1,0:T(8,128)}, u32[]{:S(2)}) %copy-start) | copy-done | bytes 196632
  0.9 0.5 convolution_bitcast_fusion
  1.5 4.9 %collective-permute-start = (f32[64,128]{1,0:T(8,128)S(1)}, f32[64,128]{1,0:T(8,128)S(1)}, u32[]{:S(2)}, u32[]{:S(2)}) collective-permute-start(f32[64,128]{1,0:T(8,128)S(1)} %convolution_bitcast_fusion), channel_id=1, source_target_pairs={{0,2},{4,6},{8,10},{12,14},{16,18},{20,22},{24,26},{28,30}} | collective-permute-start | bytes 98312 | tf_op jit(solution)/shard_map/ppermute | solution.py:94
  6.3 1.3 %collective-permute-start.5 = (f32[64,768]{1,0:T(8,128)S(1)}, f32[64,768]{1,0:T(8,128)S(1)}, u32[]{:S(2)}, u32[]{:S(2)}) collective-permute-start(f32[64,768]{1,0:T(8,128)S(1)} %bitcast.73), channel_id=1, source_target_pairs={{0,2},{1,3},{4,6},{5,7},{8,10},{9,11},{12,14},{13,15},{16,18},{17,... | collective-permute-start | bytes 589832 | tf_op jit(solution)/shard_map/ppermute | solution.py:80
  8.0 1.3 %collective-permute-start.1 = (f32[64,128]{1,0:T(8,128)S(1)}, f32[64,128]{1,0:T(8,128)S(1)}, u32[]{:S(2)}, u32[]{:S(2)}) collective-permute-start(f32[64,128]{1,0:T(8,128)S(1)} %broadcast_select_fusion.4), channel_id=1, source_target_pairs={{0,1},{2,3},{4,5},{6,7},{8,9},{10,11},{12,13},{14,15},{16,17},{18,... | collective-permute-start | bytes 98312 | tf_op jit(solution)/shard_map/ppermute | solution.py:94
  9.3 2.2 %collective-permute-done.5 = f32[64,768]{1,0:T(8,128)S(1)} collective-permute-done((f32[64,768]{1,0:T(8,128)S(1)}, f32[64,768]{1,0:T(8,128)S(1)}, u32[]{:S(2)}, u32[]{:S(2)}) %collective-permute-start.5) | collective-permute-done | bytes 196640 | tf_op jit(solution)/shard_map/ppermute | solution.py:80
  11.6 1.6 %collective-permute-start.2 = (f32[64,128]{1,0:T(8,128)S(1)}, f32[64,128]{1,0:T(8,128)S(1)}, u32[]{:S(2)}, u32[]{:S(2)}) collective-permute-start(f32[64,128]{1,0:T(8,128)S(1)} %broadcast_select_fusion.5), channel_id=1, source_target_pairs={{0,4},{4,0},{8,12},{12,8},{16,20},{20,16},{24,28},{28,24},{1,5},{5... | collective-permute-start | bytes 98312 | tf_op jit(solution)/shard_map/ppermute | solution.py:37
  13.2 2.4 %collective-permute-done.2 = f32[64,128]{1,0:T(8,128)S(1)} collective-permute-done((f32[64,128]{1,0:T(8,128)S(1)}, f32[64,128]{1,0:T(8,128)S(1)}, u32[]{:S(2)}, u32[]{:S(2)}) %collective-permute-start.2) | collective-permute-done | bytes 32800 | tf_op jit(solution)/shard_map/ppermute | solution.py:37
  15.6 1.6 %collective-permute-start.3 = (f32[64,128]{1,0:T(8,128)S(1)}, f32[64,128]{1,0:T(8,128)S(1)}, u32[]{:S(2)}, u32[]{:S(2)}) collective-permute-start(f32[64,128]{1,0:T(8,128)S(1)} %add.70), channel_id=1, source_target_pairs={{0,8},{4,12},{8,0},{12,4},{16,24},{20,28},{24,16},{28,20},{1,9},{5... | collective-permute-start | bytes 98312 | tf_op jit(solution)/shard_map/ppermute | solution.py:37
  17.6 0.5 fusion.11
  18.1 1.6 %collective-permute-start.7 = (f32[64,256]{1,0:T(8,128)S(1)}, f32[64,256]{1,0:T(8,128)S(1)}, u32[]{:S(2)}, u32[]{:S(2)}) collective-permute-start(f32[64,256]{1,0:T(8,128)S(1)} %pad_maximum_fusion.8), channel_id=1, source_target_pairs={{0,4},{4,0},{8,12},{12,8},{16,20},{20,16},{24,28},{28,24},{1,5},{5... | collective-permute-start | bytes 196616 | tf_op jit(solution)/shard_map/ppermute | solution.py:37
  19.7 2.7 %collective-permute-start.4 = (f32[64,128]{1,0:T(8,128)S(1)}, f32[64,128]{1,0:T(8,128)S(1)}, u32[]{:S(2)}, u32[]{:S(2)}) collective-permute-start(f32[64,128]{1,0:T(8,128)S(1)} %add.71), channel_id=1, source_target_pairs={{0,16},{4,20},{8,24},{12,28},{16,0},{20,4},{24,8},{28,12},{1,17},{... | collective-permute-start | bytes 98312 | tf_op jit(solution)/shard_map/ppermute | solution.py:37
  22.5 1.3 %collective-permute-start.8 = (f32[64,256]{1,0:T(8,128)S(1)}, f32[64,256]{1,0:T(8,128)S(1)}, u32[]{:S(2)}, u32[]{:S(2)}) collective-permute-start(f32[64,256]{1,0:T(8,128)S(1)} %fusion.64), channel_id=1, source_target_pairs={{0,8},{4,12},{8,0},{12,4},{16,24},{20,28},{24,16},{28,20},{1,9},{5... | collective-permute-start | bytes 196616 | tf_op jit(solution)/shard_map/ppermute | solution.py:37
  23.8 0.8 %collective-permute-done.4 = f32[64,128]{1,0:T(8,128)S(1)} collective-permute-done((f32[64,128]{1,0:T(8,128)S(1)}, f32[64,128]{1,0:T(8,128)S(1)}, u32[]{:S(2)}, u32[]{:S(2)}) %collective-permute-start.4) | collective-permute-done | bytes 32800 | tf_op jit(solution)/shard_map/ppermute | solution.py:37
  24.6 0.6 add.72.head_ref
  25.2 7.2 %shard_map.17 = f32[64,64]{1,0:T(8,128)} custom-call(f32[64,128]{1,0:T(8,128)} %add.72.head_ref), custom_call_target="tpu_custom_call" | custom-call | tf_op jit(solution)/shard_map/pallas_call | solution.py:70
  32.5 2.8 %collective-permute-start.9 = (f32[64,256]{1,0:T(8,128)S(1)}, f32[64,256]{1,0:T(8,128)S(1)}, u32[]{:S(2)}, u32[]{:S(2)}) collective-permute-start(f32[64,256]{1,0:T(8,128)S(1)} %add.74), channel_id=1, source_target_pairs={{0,16},{4,20},{8,24},{12,28},{16,0},{20,4},{24,8},{28,12},{1,17},{... | collective-permute-start | bytes 196616 | tf_op jit(solution)/shard_map/ppermute | solution.py:37
  40.7 0.5 fusion.3
  41.3 1.2 %collective-permute-start.10 = (f32[64,128]{1,0:T(8,128)S(1)}, f32[64,128]{1,0:T(8,128)S(1)}, u32[]{:S(2)}, u32[]{:S(2)}) collective-permute-start(f32[64,128]{1,0:T(8,128)S(1)} %fusion.3), channel_id=1, source_target_pairs={{0,4},{4,0},{8,12},{12,8},{16,20},{20,16},{24,28},{28,24},{1,5},{5... | collective-permute-start | bytes 98312 | tf_op jit(solution)/shard_map/ppermute | solution.py:37
  42.5 0.9 %collective-permute-start.13 = (f32[64,128]{1,0:T(8,128)S(1)}, f32[64,128]{1,0:T(8,128)S(1)}, u32[]{:S(2)}, u32[]{:S(2)}) collective-permute-start(f32[64,128]{1,0:T(8,128)S(1)} %pad_maximum_fusion.9), channel_id=1, source_target_pairs={{0,4},{4,0},{8,12},{12,8},{16,20},{20,16},{24,28},{28,24},{1,5},{5... | collective-permute-start | bytes 98312 | tf_op jit(solution)/shard_map/ppermute | solution.py:37
  43.4 1.8 %collective-permute-done.10 = f32[64,128]{1,0:T(8,128)S(1)} collective-permute-done((f32[64,128]{1,0:T(8,128)S(1)}, f32[64,128]{1,0:T(8,128)S(1)}, u32[]{:S(2)}, u32[]{:S(2)}) %collective-permute-start.10) | collective-permute-done | bytes 32800 | tf_op jit(solution)/shard_map/ppermute | solution.py:37
  45.2 1.6 %collective-permute-start.11 = (f32[64,128]{1,0:T(8,128)S(1)}, f32[64,128]{1,0:T(8,128)S(1)}, u32[]{:S(2)}, u32[]{:S(2)}) collective-permute-start(f32[64,128]{1,0:T(8,128)S(1)} %add.76), channel_id=1, source_target_pairs={{0,8},{4,12},{8,0},{12,4},{16,24},{20,28},{24,16},{28,20},{1,9},{5... | collective-permute-start | bytes 98312 | tf_op jit(solution)/shard_map/ppermute | solution.py:37
  46.9 1.5 %collective-permute-start.14 = (f32[64,128]{1,0:T(8,128)S(1)}, f32[64,128]{1,0:T(8,128)S(1)}, u32[]{:S(2)}, u32[]{:S(2)}) collective-permute-start(f32[64,128]{1,0:T(8,128)S(1)} %fusion.135), channel_id=1, source_target_pairs={{0,8},{4,12},{8,0},{12,4},{16,24},{20,28},{24,16},{28,20},{1,9},{5... | collective-permute-start | bytes 98312 | tf_op jit(solution)/shard_map/ppermute | solution.py:37
  48.4 1.2 %collective-permute-done.11 = f32[64,128]{1,0:T(8,128)S(1)} collective-permute-done((f32[64,128]{1,0:T(8,128)S(1)}, f32[64,128]{1,0:T(8,128)S(1)}, u32[]{:S(2)}, u32[]{:S(2)}) %collective-permute-start.11) | collective-permute-done | bytes 32800 | tf_op jit(solution)/shard_map/ppermute | solution.py:37
  49.5 2.1 %collective-permute-start.12 = (f32[64,128]{1,0:T(8,128)S(1)}, f32[64,128]{1,0:T(8,128)S(1)}, u32[]{:S(2)}, u32[]{:S(2)}) collective-permute-start(f32[64,128]{1,0:T(8,128)S(1)} %add.77), channel_id=1, source_target_pairs={{0,16},{4,20},{8,24},{12,28},{16,0},{20,4},{24,8},{28,12},{1,17},{... | collective-permute-start | bytes 98312 | tf_op jit(solution)/shard_map/ppermute | solution.py:37
  51.7 2.1 %collective-permute-start.15 = (f32[64,128]{1,0:T(8,128)S(1)}, f32[64,128]{1,0:T(8,128)S(1)}, u32[]{:S(2)}, u32[]{:S(2)}) collective-permute-start(f32[64,128]{1,0:T(8,128)S(1)} %add.80), channel_id=1, source_target_pairs={{0,16},{4,20},{8,24},{12,28},{16,0},{20,4},{24,8},{28,12},{1,17},{... | collective-permute-start | bytes 98312 | tf_op jit(solution)/shard_map/ppermute | solution.py:37
  53.8 0.6 collective-permute-done.12
  54.3 0.6 add.78.head_ref
  55.0 7.3 %shard_map.18 = f32[64,64]{1,0:T(8,128)} custom-call(f32[64,128]{1,0:T(8,128)} %add.78.head_ref), custom_call_target="tpu_custom_call" | custom-call | tf_op jit(solution)/shard_map/pallas_call | solution.py:70
  62.3 1.1 %fusion.22 = f32[64,64]{1,0:T(8,128)S(1)} fusion(f32[64,64]{1,0:T(8,128)} %shard_map.18, f32[64,128]{1,0:T(8,128)S(1)} %copy-done.4), kind=kOutput, calls=%fused_computation.57 | convolution fusion | flops 3145728 | bytes 65536 | tf_op jit(solution)/shard_map/dot_general | solution.py:15
  63.4 0.7 %copy-done.2 = f32[64,64]{1,0:T(8,128)S(1)} copy-done((f32[64,64]{1,0:T(8,128)S(1)}, f32[64,64]{1,0:T(8,128)}, u32[]{:S(2)}) %copy-start.2) | copy-done | bytes 16408
  67.2 1.0 %fusion = f32[1,64,768]{2,1,0:T(8,128)} fusion(f32[64,768]{1,0:T(8,128)S(1)} %convolution_subtract_fusion.2, f32[64,768]{1,0:T(8,128)S(1)} %fusion.1, f32[64,768]{1,0:T(8,128)S(1)} %fusion.13, f32[64,64]{0,1:T(8,128)S(1)} %convolution_negate_fusion, f32[64,64]{0,1:T(8,128)S(1)} %fusion.21), kind=kOutput, calls=%fused_computation.1 | convolution fusion | flops 75653120 | bytes 819200 | tf_op jit(solution)/shard_map/dot_general | solution.py:20
  (83 shorter events, 9.5 us)
Async XLA Ops:
  0.0 0.9 %copy-start = (f32[1,64,768]{2,1,0:T(8,128)S(1)}, f32[1,64,768]{2,1,0:T(8,128)}, u32[]{:S(2)}) copy-start(f32[1,64,768]{2,1,0:T(8,128)} %param.1) | copy-start | bytes 589828
  1.5 6.6 %collective-permute-start = (f32[64,128]{1,0:T(8,128)S(1)}, f32[64,128]{1,0:T(8,128)S(1)}, u32[]{:S(2)}, u32[]{:S(2)}) collective-permute-start(f32[64,128]{1,0:T(8,128)S(1)} %convolution_bitcast_fusion), channel_id=1, source_target_pairs={{0,2},{4,6},{8,10},{12,14},{16,18},{20,22},{24,26},{28,30}} | collective-permute-start | bytes 98312 | tf_op jit(solution)/shard_map/ppermute | solution.py:94
  6.3 5.2 %collective-permute-start.5 = (f32[64,768]{1,0:T(8,128)S(1)}, f32[64,768]{1,0:T(8,128)S(1)}, u32[]{:S(2)}, u32[]{:S(2)}) collective-permute-start(f32[64,768]{1,0:T(8,128)S(1)} %bitcast.73), channel_id=1, source_target_pairs={{0,2},{1,3},{4,6},{5,7},{8,10},{9,11},{12,14},{13,15},{16,18},{17,... | collective-permute-start | bytes 589832 | tf_op jit(solution)/shard_map/ppermute | solution.py:80
  8.0 3.6 %collective-permute-start.1 = (f32[64,128]{1,0:T(8,128)S(1)}, f32[64,128]{1,0:T(8,128)S(1)}, u32[]{:S(2)}, u32[]{:S(2)}) collective-permute-start(f32[64,128]{1,0:T(8,128)S(1)} %broadcast_select_fusion.4), channel_id=1, source_target_pairs={{0,1},{2,3},{4,5},{6,7},{8,9},{10,11},{12,13},{14,15},{16,17},{18,... | collective-permute-start | bytes 98312 | tf_op jit(solution)/shard_map/ppermute | solution.py:94
  11.5 5.7 %collective-permute-start.6 = (f32[64,768]{1,0:T(8,128)S(1)}, f32[64,768]{1,0:T(8,128)S(1)}, u32[]{:S(2)}, u32[]{:S(2)}) collective-permute-start(f32[64,768]{1,0:T(8,128)S(1)} %broadcast_select_fusion), channel_id=1, source_target_pairs={{0,1},{1,0},{2,3},{3,2},{4,5},{5,4},{6,7},{7,6},{8,9},{9,8},{10,11... | collective-permute-start | bytes 589832 | tf_op jit(solution)/shard_map/ppermute | solution.py:85
  11.6 4.0 %collective-permute-start.2 = (f32[64,128]{1,0:T(8,128)S(1)}, f32[64,128]{1,0:T(8,128)S(1)}, u32[]{:S(2)}, u32[]{:S(2)}) collective-permute-start(f32[64,128]{1,0:T(8,128)S(1)} %broadcast_select_fusion.5), channel_id=1, source_target_pairs={{0,4},{4,0},{8,12},{12,8},{16,20},{20,16},{24,28},{28,24},{1,5},{5... | collective-permute-start | bytes 98312 | tf_op jit(solution)/shard_map/ppermute | solution.py:37
  15.6 4.1 %collective-permute-start.3 = (f32[64,128]{1,0:T(8,128)S(1)}, f32[64,128]{1,0:T(8,128)S(1)}, u32[]{:S(2)}, u32[]{:S(2)}) collective-permute-start(f32[64,128]{1,0:T(8,128)S(1)} %add.70), channel_id=1, source_target_pairs={{0,8},{4,12},{8,0},{12,4},{16,24},{20,28},{24,16},{28,20},{1,9},{5... | collective-permute-start | bytes 98312 | tf_op jit(solution)/shard_map/ppermute | solution.py:37
  18.1 4.3 %collective-permute-start.7 = (f32[64,256]{1,0:T(8,128)S(1)}, f32[64,256]{1,0:T(8,128)S(1)}, u32[]{:S(2)}, u32[]{:S(2)}) collective-permute-start(f32[64,256]{1,0:T(8,128)S(1)} %pad_maximum_fusion.8), channel_id=1, source_target_pairs={{0,4},{4,0},{8,12},{12,8},{16,20},{20,16},{24,28},{28,24},{1,5},{5... | collective-permute-start | bytes 196616 | tf_op jit(solution)/shard_map/ppermute | solution.py:37
  19.7 4.9 %collective-permute-start.4 = (f32[64,128]{1,0:T(8,128)S(1)}, f32[64,128]{1,0:T(8,128)S(1)}, u32[]{:S(2)}, u32[]{:S(2)}) collective-permute-start(f32[64,128]{1,0:T(8,128)S(1)} %add.71), channel_id=1, source_target_pairs={{0,16},{4,20},{8,24},{12,28},{16,0},{20,4},{24,8},{28,12},{1,17},{... | collective-permute-start | bytes 98312 | tf_op jit(solution)/shard_map/ppermute | solution.py:37
  22.5 10.0 %collective-permute-start.8 = (f32[64,256]{1,0:T(8,128)S(1)}, f32[64,256]{1,0:T(8,128)S(1)}, u32[]{:S(2)}, u32[]{:S(2)}) collective-permute-start(f32[64,256]{1,0:T(8,128)S(1)} %fusion.64), channel_id=1, source_target_pairs={{0,8},{4,12},{8,0},{12,4},{16,24},{20,28},{24,16},{28,20},{1,9},{5... | collective-permute-start | bytes 196616 | tf_op jit(solution)/shard_map/ppermute | solution.py:37
  32.5 2.8 %copy-start.1 = (f32[64,64]{1,0:T(8,128)S(1)}, f32[64,64]{1,0:T(8,128)}, u32[]{:S(2)}) copy-start(f32[64,64]{1,0:T(8,128)} %shard_map.17) | copy-start | bytes 49156
  32.5 2.8 %copy-start.3 = (f32[64,128]{1,0:T(8,128)S(1)}, f32[64,128]{1,0:T(8,128)}, u32[]{:S(2)}) copy-start(f32[64,128]{1,0:T(8,128)} %add.72.head_ref) | copy-start | bytes 98308
  32.5 5.6 %collective-permute-start.9 = (f32[64,256]{1,0:T(8,128)S(1)}, f32[64,256]{1,0:T(8,128)S(1)}, u32[]{:S(2)}, u32[]{:S(2)}) collective-permute-start(f32[64,256]{1,0:T(8,128)S(1)} %add.74), channel_id=1, source_target_pairs={{0,16},{4,20},{8,24},{12,28},{16,0},{20,4},{24,8},{28,12},{1,17},{... | collective-permute-start | bytes 196616 | tf_op jit(solution)/shard_map/ppermute | solution.py:37
  41.3 4.0 %collective-permute-start.10 = (f32[64,128]{1,0:T(8,128)S(1)}, f32[64,128]{1,0:T(8,128)S(1)}, u32[]{:S(2)}, u32[]{:S(2)}) collective-permute-start(f32[64,128]{1,0:T(8,128)S(1)} %fusion.3), channel_id=1, source_target_pairs={{0,4},{4,0},{8,12},{12,8},{16,20},{20,16},{24,28},{28,24},{1,5},{5... | collective-permute-start | bytes 98312 | tf_op jit(solution)/shard_map/ppermute | solution.py:37
  42.5 4.3 %collective-permute-start.13 = (f32[64,128]{1,0:T(8,128)S(1)}, f32[64,128]{1,0:T(8,128)S(1)}, u32[]{:S(2)}, u32[]{:S(2)}) collective-permute-start(f32[64,128]{1,0:T(8,128)S(1)} %pad_maximum_fusion.9), channel_id=1, source_target_pairs={{0,4},{4,0},{8,12},{12,8},{16,20},{20,16},{24,28},{28,24},{1,5},{5... | collective-permute-start | bytes 98312 | tf_op jit(solution)/shard_map/ppermute | solution.py:37
  45.2 4.3 %collective-permute-start.11 = (f32[64,128]{1,0:T(8,128)S(1)}, f32[64,128]{1,0:T(8,128)S(1)}, u32[]{:S(2)}, u32[]{:S(2)}) collective-permute-start(f32[64,128]{1,0:T(8,128)S(1)} %add.76), channel_id=1, source_target_pairs={{0,8},{4,12},{8,0},{12,4},{16,24},{20,28},{24,16},{28,20},{1,9},{5... | collective-permute-start | bytes 98312 | tf_op jit(solution)/shard_map/ppermute | solution.py:37
  46.9 4.8 %collective-permute-start.14 = (f32[64,128]{1,0:T(8,128)S(1)}, f32[64,128]{1,0:T(8,128)S(1)}, u32[]{:S(2)}, u32[]{:S(2)}) collective-permute-start(f32[64,128]{1,0:T(8,128)S(1)} %fusion.135), channel_id=1, source_target_pairs={{0,8},{4,12},{8,0},{12,4},{16,24},{20,28},{24,16},{28,20},{1,9},{5... | collective-permute-start | bytes 98312 | tf_op jit(solution)/shard_map/ppermute | solution.py:37
  49.5 4.8 %collective-permute-start.12 = (f32[64,128]{1,0:T(8,128)S(1)}, f32[64,128]{1,0:T(8,128)S(1)}, u32[]{:S(2)}, u32[]{:S(2)}) collective-permute-start(f32[64,128]{1,0:T(8,128)S(1)} %add.77), channel_id=1, source_target_pairs={{0,16},{4,20},{8,24},{12,28},{16,0},{20,4},{24,8},{28,12},{1,17},{... | collective-permute-start | bytes 98312 | tf_op jit(solution)/shard_map/ppermute | solution.py:37
  51.7 11.7 %collective-permute-start.15 = (f32[64,128]{1,0:T(8,128)S(1)}, f32[64,128]{1,0:T(8,128)S(1)}, u32[]{:S(2)}, u32[]{:S(2)}) collective-permute-start(f32[64,128]{1,0:T(8,128)S(1)} %add.80), channel_id=1, source_target_pairs={{0,16},{4,20},{8,24},{12,28},{16,0},{20,4},{24,8},{28,12},{1,17},{... | collective-permute-start | bytes 98312 | tf_op jit(solution)/shard_map/ppermute | solution.py:37
  55.0 7.3 %copy-start.4 = (f32[64,128]{1,0:T(8,128)S(1)}, f32[64,128]{1,0:T(8,128)}, u32[]{:S(2)}) copy-start(f32[64,128]{1,0:T(8,128)} %add.78.head_ref) | copy-start | bytes 98308
  63.3 0.8 %copy-start.2 = (f32[64,64]{1,0:T(8,128)S(1)}, f32[64,64]{1,0:T(8,128)}, u32[]{:S(2)}) copy-start(f32[64,64]{1,0:T(8,128)} %shard_map.18) | copy-start | bytes 49156

commit v15 on v12

--- a/solution.py
+++ b/solution.py
@@ -50,7 +50,6 @@
         row = work[j:j + 1, :]
         pivot = row[:, j:j + 1]
         scale = lax.rsqrt(pivot)
-        scale = scale * (1.5 - 0.5 * pivot * scale * scale)
         scaled = row * scale
         weight = jnp.where(row_ids > j, work[:, j:j + 1] * scale, 0.0)
         work = jnp.where(rows == j, scaled, work - weight * scaled)
@@ -118,8 +117,9 @@
         tail = jnp.concatenate([inner_rows(panel_0, both), inner_rows(units[0], both)], axis=1)
         steps = butterfly_steps(rows_size)
         tail = butterfly_sum(tail, "rows", rows_size, None if steps is None else steps[:-1])
-        lower_inv, tail = lax.optimization_barrier((lower_inverse(head), tail))
+        head, tail = lax.optimization_barrier((head, tail))
         tail = butterfly_sum(tail, "rows", rows_size, None if steps is None else steps[-1:])
+        lower_inv = lower_inverse(head)
         top_rows = head[:, width:]
         basis_cur, basis_sec, unit_cur, unit_sec = (
             tail[:, i * width:(i + 1) * width] for i in range(4)

time: 67.7 us -> 70.3 us (1.038)
  waiting for transfers between devices: 9.22 us -> 16 us
  starting transfers between devices: 28.2 us -> 23.5 us
  Pallas kernels: 14.5 us -> 13.6 us
  matrix products: 12.3 us -> 13.1 us
    ppermute x12, waiting for transfers between devices: 6.68 us -> 13.5 us  [butterfly_sum(): x = x + lax.ppermute(x, axis, [(i, i ^ step) for i in range(size)])]
    ppermute x12, starting transfers between devices: 20.7 us -> 16 us  [butterfly_sum(): x = x + lax.ppermute(x, axis, [(i, i ^ step) for i in range(size)])]
    pallas_call x2, Pallas kernels: 14.5 us -> 13.6 us  [lower_inverse(): pl.pallas_call(_eliminate_kernel, out_shape=jax.ShapeDtypeStruct((size, s...]
    dot_general x38, matrix products: 7.99 us -> 8.74 us  [apply_left(): return jnp.dot(square, right_side, precision=HIGHEST_PRECISION)]
  transfers between devices with their start and end apart: 16 -> 16, of which waited for: 8 -> 11; matrix products, arithmetic and copies ran while one was open for 10% -> 11% of each run, Pallas kernels for 22% -> 19%
where the time goes in v15:
time: 70.3 us; the launch traced here: 69.7 us
  starting transfers between devices  23.5 us (33%)
  waiting for transfers between devices  16 us (23%)
  Pallas kernels  13.6 us (19%)
  matrix products  13.1 us (19%)
  other arithmetic  1.57 us (2%)
  local copies, waits for them, and re-layouts  1.49 us (2%)
    ppermute x12, starting transfers between devices, butterfly_sum(): x = x + lax.ppermute(x, axis, [(i, i ^ step) for i in range(size)])  16 us
    pallas_call x2, Pallas kernels, lower_inverse(): pl.pallas_call(_eliminate_kernel, out_shape=jax.ShapeDtypeStruct((size, s...  13.6 us
    ppermute x12, waiting for transfers between devices, butterfly_sum(): x = x + lax.ppermute(x, axis, [(i, i ^ step) for i in range(size)])  13.5 us
    dot_general x38, matrix products, apply_left(): return jnp.dot(square, right_side, precision=HIGHEST_PRECISION)  8.74 us
    ppermute x2, starting transfers between devices, from_root(): lax.ppermute(value, axis, [(i, i + dist) for i in range(size) if i % (2 *...  6.15 us
    dot_general x6, matrix products, inner_rows(): lax.dot_general(left, right, (((1,), (1,)), ((), ())), precision=HIGHEST_...  2.52 us
    ppermute x1, waiting for transfers between devices, spread_pair(): lax.ppermute(have, axis, [(i, i + dist) for i in range(size) if i % (2 *...  2.18 us
    unnamed x10, local copies, waits for them, and re-layouts  1.49 us
  transfers between devices with their start and end apart: 16, of which 11 were waited for; matrix products, arithmetic and copies ran while one was open for 11% of the time, Pallas kernels for 19%

profile of v15, /device:TPU:0, one launch (start us, length us, event | category | flops | bytes accessed | tf_op | source)
XLA Modules:
  0.0 69.7 jit_solution(5327639702547522369)
XLA Ops:
  0.0 0.9 %copy-done = f32[1,64,768]{2,1,0:T(8,128)S(1)} copy-done((f32[1,64,768]{2,1,0:T(8,128)S(1)}, f32[1,64,768]{2,1,0:T(8,128)}, u32[]{:S(2)}) %copy-start) | copy-done | bytes 196632
  1.5 4.9 %collective-permute-start = (f32[64,128]{1,0:T(8,128)S(1)}, f32[64,128]{1,0:T(8,128)S(1)}, u32[]{:S(2)}, u32[]{:S(2)}) collective-permute-start(f32[64,128]{1,0:T(8,128)S(1)} %convolution_bitcast_fusion), channel_id=1, source_target_pairs={{0,2},{4,6},{8,10},{12,14},{16,18},{20,22},{24,26},{28,30}} | collective-permute-start | bytes 98312 | tf_op jit(solution)/shard_map/ppermute | solution.py:85
  6.3 1.3 %collective-permute-start.5 = (f32[64,768]{1,0:T(8,128)S(1)}, f32[64,768]{1,0:T(8,128)S(1)}, u32[]{:S(2)}, u32[]{:S(2)}) collective-permute-start(f32[64,768]{1,0:T(8,128)S(1)} %bitcast.76), channel_id=1, source_target_pairs={{0,2},{1,3},{4,6},{5,7},{8,10},{9,11},{12,14},{13,15},{16,18},{17,... | collective-permute-start | bytes 589832 | tf_op jit(solution)/shard_map/ppermute | solution.py:71
  8.0 1.3 %collective-permute-start.1 = (f32[64,128]{1,0:T(8,128)S(1)}, f32[64,128]{1,0:T(8,128)S(1)}, u32[]{:S(2)}, u32[]{:S(2)}) collective-permute-start(f32[64,128]{1,0:T(8,128)S(1)} %broadcast_select_fusion.5), channel_id=1, source_target_pairs={{0,1},{2,3},{4,5},{6,7},{8,9},{10,11},{12,13},{14,15},{16,17},{18,... | collective-permute-start | bytes 98312 | tf_op jit(solution)/shard_map/ppermute | solution.py:85
  9.3 2.2 %collective-permute-done.5 = f32[64,768]{1,0:T(8,128)S(1)} collective-permute-done((f32[64,768]{1,0:T(8,128)S(1)}, f32[64,768]{1,0:T(8,128)S(1)}, u32[]{:S(2)}, u32[]{:S(2)}) %collective-permute-start.5) | collective-permute-done | bytes 196640 | tf_op jit(solution)/shard_map/ppermute | solution.py:71
  11.6 1.6 %collective-permute-start.2 = (f32[64,128]{1,0:T(8,128)S(1)}, f32[64,128]{1,0:T(8,128)S(1)}, u32[]{:S(2)}, u32[]{:S(2)}) collective-permute-start(f32[64,128]{1,0:T(8,128)S(1)} %broadcast_select_fusion.6), channel_id=1, source_target_pairs={{0,4},{4,0},{8,12},{12,8},{16,20},{20,16},{24,28},{28,24},{1,5},{5... | collective-permute-start | bytes 98312 | tf_op jit(solution)/shard_map/ppermute | solution.py:29
  13.2 2.4 %collective-permute-done.2 = f32[64,128]{1,0:T(8,128)S(1)} collective-permute-done((f32[64,128]{1,0:T(8,128)S(1)}, f32[64,128]{1,0:T(8,128)S(1)}, u32[]{:S(2)}, u32[]{:S(2)}) %collective-permute-start.2) | collective-permute-done | bytes 32800 | tf_op jit(solution)/shard_map/ppermute | solution.py:29
  15.6 1.6 %collective-permute-start.3 = (f32[64,128]{1,0:T(8,128)S(1)}, f32[64,128]{1,0:T(8,128)S(1)}, u32[]{:S(2)}, u32[]{:S(2)}) collective-permute-start(f32[64,128]{1,0:T(8,128)S(1)} %add.70), channel_id=1, source_target_pairs={{0,8},{4,12},{8,0},{12,4},{16,24},{20,28},{24,16},{28,20},{1,9},{5... | collective-permute-start | bytes 98312 | tf_op jit(solution)/shard_map/ppermute | solution.py:29
  17.6 0.5 fusion.8
  18.1 1.6 %collective-permute-start.7 = (f32[64,256]{1,0:T(8,128)S(1)}, f32[64,256]{1,0:T(8,128)S(1)}, u32[]{:S(2)}, u32[]{:S(2)}) collective-permute-start(f32[64,256]{1,0:T(8,128)S(1)} %pad_maximum_fusion.5), channel_id=1, source_target_pairs={{0,4},{4,0},{8,12},{12,8},{16,20},{20,16},{24,28},{28,24},{1,5},{5... | collective-permute-start | bytes 196616 | tf_op jit(solution)/shard_map/ppermute | solution.py:29
  19.7 2.7 %collective-permute-start.4 = (f32[64,128]{1,0:T(8,128)S(1)}, f32[64,128]{1,0:T(8,128)S(1)}, u32[]{:S(2)}, u32[]{:S(2)}) collective-permute-start(f32[64,128]{1,0:T(8,128)S(1)} %add.71), channel_id=1, source_target_pairs={{0,16},{4,20},{8,24},{12,28},{16,0},{20,4},{24,8},{28,12},{1,17},{... | collective-permute-start | bytes 98312 | tf_op jit(solution)/shard_map/ppermute | solution.py:29
  22.5 1.3 %collective-permute-start.8 = (f32[64,256]{1,0:T(8,128)S(1)}, f32[64,256]{1,0:T(8,128)S(1)}, u32[]{:S(2)}, u32[]{:S(2)}) collective-permute-start(f32[64,256]{1,0:T(8,128)S(1)} %fusion.49), channel_id=1, source_target_pairs={{0,8},{4,12},{8,0},{12,4},{16,24},{20,28},{24,16},{28,20},{1,9},{5... | collective-permute-start | bytes 196616 | tf_op jit(solution)/shard_map/ppermute | solution.py:29
  23.8 0.8 %collective-permute-done.4 = f32[64,128]{1,0:T(8,128)S(1)} collective-permute-done((f32[64,128]{1,0:T(8,128)S(1)}, f32[64,128]{1,0:T(8,128)S(1)}, u32[]{:S(2)}, u32[]{:S(2)}) %collective-permute-start.4) | collective-permute-done | bytes 32800 | tf_op jit(solution)/shard_map/ppermute | solution.py:29
  24.6 0.6 add.72.head_ref
  25.2 1.6 %collective-permute-done.8 = f32[64,256]{1,0:T(8,128)S(1)} collective-permute-done((f32[64,256]{1,0:T(8,128)S(1)}, f32[64,256]{1,0:T(8,128)S(1)}, u32[]{:S(2)}, u32[]{:S(2)}) %collective-permute-start.8) | collective-permute-done | bytes 65568 | tf_op jit(solution)/shard_map/ppermute | solution.py:29
  26.8 3.0 %collective-permute-start.9 = (f32[64,256]{1,0:T(8,128)S(1)}, f32[64,256]{1,0:T(8,128)S(1)}, u32[]{:S(2)}, u32[]{:S(2)}) collective-permute-start(f32[64,256]{1,0:T(8,128)S(1)} %add.74), channel_id=1, source_target_pairs={{0,16},{4,20},{8,24},{12,28},{16,0},{20,4},{24,8},{28,12},{1,17},{... | collective-permute-start | bytes 196616 | tf_op jit(solution)/shard_map/ppermute | solution.py:29
  29.9 6.8 %shard_map.17 = f32[64,64]{1,0:T(8,128)} custom-call(f32[64,128]{1,0:T(8,128)} %add.72.head_ref), custom_call_target="tpu_custom_call" | custom-call | tf_op jit(solution)/shard_map/pallas_call | solution.py:61
  36.7 1.1 %fusion.27 = f32[64,64]{1,0:T(8,128)S(1)} fusion(f32[64,64]{1,0:T(8,128)} %shard_map.17, f32[64,128]{1,0:T(8,128)S(1)} %copy-done.3), kind=kOutput, calls=%fused_computation.64 | convolution fusion | flops 3145728 | bytes 65536 | tf_op jit(solution)/shard_map/dot_general | solution.py:15
  40.1 0.6 copy-done.1
  43.3 0.5 fusion.3
  43.9 1.6 %collective-permute-start.10 = (f32[64,128]{1,0:T(8,128)S(1)}, f32[64,128]{1,0:T(8,128)S(1)}, u32[]{:S(2)}, u32[]{:S(2)}) collective-permute-start(f32[64,128]{1,0:T(8,128)S(1)} %fusion.3), channel_id=1, source_target_pairs={{0,4},{4,0},{8,12},{12,8},{16,20},{20,16},{24,28},{28,24},{1,5},{5... | collective-permute-start | bytes 98312 | tf_op jit(solution)/shard_map/ppermute | solution.py:29
  45.5 0.5 collective-permute-start.13
  46.0 1.8 %collective-permute-done.10 = f32[64,128]{1,0:T(8,128)S(1)} collective-permute-done((f32[64,128]{1,0:T(8,128)S(1)}, f32[64,128]{1,0:T(8,128)S(1)}, u32[]{:S(2)}, u32[]{:S(2)}) %collective-permute-start.10) | collective-permute-done | bytes 32800 | tf_op jit(solution)/shard_map/ppermute | solution.py:29
  47.9 1.5 %collective-permute-done.13 = f32[64,128]{1,0:T(8,128)S(1)} collective-permute-done((f32[64,128]{1,0:T(8,128)S(1)}, f32[64,128]{1,0:T(8,128)S(1)}, u32[]{:S(2)}, u32[]{:S(2)}) %collective-permute-start.13) | collective-permute-done | bytes 32800 | tf_op jit(solution)/shard_map/ppermute | solution.py:29
  50.0 2.1 %collective-permute-done.11 = f32[64,128]{1,0:T(8,128)S(1)} collective-permute-done((f32[64,128]{1,0:T(8,128)S(1)}, f32[64,128]{1,0:T(8,128)S(1)}, u32[]{:S(2)}, u32[]{:S(2)}) %collective-permute-start.11) | collective-permute-done | bytes 32800 | tf_op jit(solution)/shard_map/ppermute | solution.py:29
  52.1 1.3 %collective-permute-done.14 = f32[64,128]{1,0:T(8,128)S(1)} collective-permute-done((f32[64,128]{1,0:T(8,128)S(1)}, f32[64,128]{1,0:T(8,128)S(1)}, u32[]{:S(2)}, u32[]{:S(2)}) %collective-permute-start.14) | collective-permute-done | bytes 32800 | tf_op jit(solution)/shard_map/ppermute | solution.py:29
  53.4 1.6 %collective-permute-start.15 = (f32[64,128]{1,0:T(8,128)S(1)}, f32[64,128]{1,0:T(8,128)S(1)}, u32[]{:S(2)}, u32[]{:S(2)}) collective-permute-start(f32[64,128]{1,0:T(8,128)S(1)} %add.80), channel_id=1, source_target_pairs={{0,16},{4,20},{8,24},{12,28},{16,0},{20,4},{24,8},{28,12},{1,17},{... | collective-permute-start | bytes 98312 | tf_op jit(solution)/shard_map/ppermute | solution.py:29
  55.1 1.8 %collective-permute-done.12 = f32[64,128]{1,0:T(8,128)S(1)} collective-permute-done((f32[64,128]{1,0:T(8,128)S(1)}, f32[64,128]{1,0:T(8,128)S(1)}, u32[]{:S(2)}, u32[]{:S(2)}) %collective-permute-start.12) | collective-permute-done | bytes 32800 | tf_op jit(solution)/shard_map/ppermute | solution.py:29
  56.9 0.6 add.78.head_ref
  57.5 6.8 %shard_map.18 = f32[64,64]{1,0:T(8,128)} custom-call(f32[64,128]{1,0:T(8,128)} %add.78.head_ref), custom_call_target="tpu_custom_call" | custom-call | tf_op jit(solution)/shard_map/pallas_call | solution.py:61
  64.3 1.1 %convolution_subtract_fusion.1 = f32[64,768]{1,0:T(8,128)S(1)} fusion(f32[64,64]{1,0:T(8,128)} %shard_map.18, f32[64,768]{1,0:T(8,128)S(1)} %fusion.1, s32[768]{0:T(1024)S(1)} %fusion.39), kind=kOutput, calls=%fused_computation.2 | convolution fusion | flops 37896192 | bytes 412672 | tf_op jit(solution)/shard_map/dot_general | solution.py:15
  68.7 1.1 %fusion = f32[1,64,768]{2,1,0:T(8,128)} fusion(f32[64,768]{1,0:T(8,128)S(1)} %convolution_subtract_fusion.3, f32[64,64]{1,0:T(8,128)S(1)} %fusion.18, f32[64,768]{1,0:T(8,128)S(1)} %convolution_subtract_fusion.1), kind=kOutput, calls=%fused_computation.1 | convolution fusion | flops 37797888 | bytes 606208 | tf_op jit(solution)/shard_map/dot_general | solution.py:151
  (82 shorter events, 10.1 us)
Async XLA Ops:
  0.0 0.9 %copy-start = (f32[1,64,768]{2,1,0:T(8,128)S(1)}, f32[1,64,768]{2,1,0:T(8,128)}, u32[]{:S(2)}) copy-start(f32[1,64,768]{2,1,0:T(8,128)} %param.1) | copy-start | bytes 589828
  1.5 6.6 %collective-permute-start = (f32[64,128]{1,0:T(8,128)S(1)}, f32[64,128]{1,0:T(8,128)S(1)}, u32[]{:S(2)}, u32[]{:S(2)}) collective-permute-start(f32[64,128]{1,0:T(8,128)S(1)} %convolution_bitcast_fusion), channel_id=1, source_target_pairs={{0,2},{4,6},{8,10},{12,14},{16,18},{20,22},{24,26},{28,30}} | collective-permute-start | bytes 98312 | tf_op jit(solution)/shard_map/ppermute | solution.py:85
  6.3 5.2 %collective-permute-start.5 = (f32[64,768]{1,0:T(8,128)S(1)}, f32[64,768]{1,0:T(8,128)S(1)}, u32[]{:S(2)}, u32[]{:S(2)}) collective-permute-start(f32[64,768]{1,0:T(8,128)S(1)} %bitcast.76), channel_id=1, source_target_pairs={{0,2},{1,3},{4,6},{5,7},{8,10},{9,11},{12,14},{13,15},{16,18},{17,... | collective-permute-start | bytes 589832 | tf_op jit(solution)/shard_map/ppermute | solution.py:71
  8.0 3.6 %collective-permute-start.1 = (f32[64,128]{1,0:T(8,128)S(1)}, f32[64,128]{1,0:T(8,128)S(1)}, u32[]{:S(2)}, u32[]{:S(2)}) collective-permute-start(f32[64,128]{1,0:T(8,128)S(1)} %broadcast_select_fusion.5), channel_id=1, source_target_pairs={{0,1},{2,3},{4,5},{6,7},{8,9},{10,11},{12,13},{14,15},{16,17},{18,... | collective-permute-start | bytes 98312 | tf_op jit(solution)/shard_map/ppermute | solution.py:85
  11.5 5.7 %collective-permute-start.6 = (f32[64,768]{1,0:T(8,128)S(1)}, f32[64,768]{1,0:T(8,128)S(1)}, u32[]{:S(2)}, u32[]{:S(2)}) collective-permute-start(f32[64,768]{1,0:T(8,128)S(1)} %broadcast_select_fusion), channel_id=1, source_target_pairs={{0,1},{1,0},{2,3},{3,2},{4,5},{5,4},{6,7},{7,6},{8,9},{9,8},{10,11... | collective-permute-start | bytes 589832 | tf_op jit(solution)/shard_map/ppermute | solution.py:76
  11.6 4.0 %collective-permute-start.2 = (f32[64,128]{1,0:T(8,128)S(1)}, f32[64,128]{1,0:T(8,128)S(1)}, u32[]{:S(2)}, u32[]{:S(2)}) collective-permute-start(f32[64,128]{1,0:T(8,128)S(1)} %broadcast_select_fusion.6), channel_id=1, source_target_pairs={{0,4},{4,0},{8,12},{12,8},{16,20},{20,16},{24,28},{28,24},{1,5},{5... | collective-permute-start | bytes 98312 | tf_op jit(solution)/shard_map/ppermute | solution.py:29
  15.6 4.1 %collective-permute-start.3 = (f32[64,128]{1,0:T(8,128)S(1)}, f32[64,128]{1,0:T(8,128)S(1)}, u32[]{:S(2)}, u32[]{:S(2)}) collective-permute-start(f32[64,128]{1,0:T(8,128)S(1)} %add.70), channel_id=1, source_target_pairs={{0,8},{4,12},{8,0},{12,4},{16,24},{20,28},{24,16},{28,20},{1,9},{5... | collective-permute-start | bytes 98312 | tf_op jit(solution)/shard_map/ppermute | solution.py:29
  18.1 4.3 %collective-permute-start.7 = (f32[64,256]{1,0:T(8,128)S(1)}, f32[64,256]{1,0:T(8,128)S(1)}, u32[]{:S(2)}, u32[]{:S(2)}) collective-permute-start(f32[64,256]{1,0:T(8,128)S(1)} %pad_maximum_fusion.5), channel_id=1, source_target_pairs={{0,4},{4,0},{8,12},{12,8},{16,20},{20,16},{24,28},{28,24},{1,5},{5... | collective-permute-start | bytes 196616 | tf_op jit(solution)/shard_map/ppermute | solution.py:29
  19.7 4.9 %collective-permute-start.4 = (f32[64,128]{1,0:T(8,128)S(1)}, f32[64,128]{1,0:T(8,128)S(1)}, u32[]{:S(2)}, u32[]{:S(2)}) collective-permute-start(f32[64,128]{1,0:T(8,128)S(1)} %add.71), channel_id=1, source_target_pairs={{0,16},{4,20},{8,24},{12,28},{16,0},{20,4},{24,8},{28,12},{1,17},{... | collective-permute-start | bytes 98312 | tf_op jit(solution)/shard_map/ppermute | solution.py:29
  22.5 4.3 %collective-permute-start.8 = (f32[64,256]{1,0:T(8,128)S(1)}, f32[64,256]{1,0:T(8,128)S(1)}, u32[]{:S(2)}, u32[]{:S(2)}) collective-permute-start(f32[64,256]{1,0:T(8,128)S(1)} %fusion.49), channel_id=1, source_target_pairs={{0,8},{4,12},{8,0},{12,4},{16,24},{20,28},{24,16},{28,20},{1,9},{5... | collective-permute-start | bytes 196616 | tf_op jit(solution)/shard_map/ppermute | solution.py:29
  26.8 9.8 %copy-start.3 = (f32[64,128]{1,0:T(8,128)S(1)}, f32[64,128]{1,0:T(8,128)}, u32[]{:S(2)}) copy-start(f32[64,128]{1,0:T(8,128)} %add.72.head_ref) | copy-start | bytes 98308
  26.8 14.3 %collective-permute-start.9 = (f32[64,256]{1,0:T(8,128)S(1)}, f32[64,256]{1,0:T(8,128)S(1)}, u32[]{:S(2)}, u32[]{:S(2)}) collective-permute-start(f32[64,256]{1,0:T(8,128)S(1)} %add.74), channel_id=1, source_target_pairs={{0,16},{4,20},{8,24},{12,28},{16,0},{20,4},{24,8},{28,12},{1,17},{... | collective-permute-start | bytes 196616 | tf_op jit(solution)/shard_map/ppermute | solution.py:29
  39.9 0.8 %copy-start.1 = (f32[64,64]{1,0:T(8,128)S(1)}, f32[64,64]{1,0:T(8,128)}, u32[]{:S(2)}) copy-start(f32[64,64]{1,0:T(8,128)} %shard_map.17) | copy-start | bytes 49156
  43.9 4.0 %collective-permute-start.10 = (f32[64,128]{1,0:T(8,128)S(1)}, f32[64,128]{1,0:T(8,128)S(1)}, u32[]{:S(2)}, u32[]{:S(2)}) collective-permute-start(f32[64,128]{1,0:T(8,128)S(1)} %fusion.3), channel_id=1, source_target_pairs={{0,4},{4,0},{8,12},{12,8},{16,20},{20,16},{24,28},{28,24},{1,5},{5... | collective-permute-start | bytes 98312 | tf_op jit(solution)/shard_map/ppermute | solution.py:29
  45.5 3.9 %collective-permute-start.13 = (f32[64,128]{1,0:T(8,128)S(1)}, f32[64,128]{1,0:T(8,128)S(1)}, u32[]{:S(2)}, u32[]{:S(2)}) collective-permute-start(f32[64,128]{1,0:T(8,128)S(1)} %pad_maximum_fusion.6), channel_id=1, source_target_pairs={{0,4},{4,0},{8,12},{12,8},{16,20},{20,16},{24,28},{28,24},{1,5},{5... | collective-permute-start | bytes 98312 | tf_op jit(solution)/shard_map/ppermute | solution.py:29
  47.9 4.2 %collective-permute-start.11 = (f32[64,128]{1,0:T(8,128)S(1)}, f32[64,128]{1,0:T(8,128)S(1)}, u32[]{:S(2)}, u32[]{:S(2)}) collective-permute-start(f32[64,128]{1,0:T(8,128)S(1)} %add.76), channel_id=1, source_target_pairs={{0,8},{4,12},{8,0},{12,4},{16,24},{20,28},{24,16},{28,20},{1,9},{5... | collective-permute-start | bytes 98312 | tf_op jit(solution)/shard_map/ppermute | solution.py:29
  49.5 3.9 %collective-permute-start.14 = (f32[64,128]{1,0:T(8,128)S(1)}, f32[64,128]{1,0:T(8,128)S(1)}, u32[]{:S(2)}, u32[]{:S(2)}) collective-permute-start(f32[64,128]{1,0:T(8,128)S(1)} %fusion.123), channel_id=1, source_target_pairs={{0,8},{4,12},{8,0},{12,4},{16,24},{20,28},{24,16},{28,20},{1,9},{5... | collective-permute-start | bytes 98312 | tf_op jit(solution)/shard_map/ppermute | solution.py:29
  52.1 4.8 %collective-permute-start.12 = (f32[64,128]{1,0:T(8,128)S(1)}, f32[64,128]{1,0:T(8,128)S(1)}, u32[]{:S(2)}, u32[]{:S(2)}) collective-permute-start(f32[64,128]{1,0:T(8,128)S(1)} %add.77), channel_id=1, source_target_pairs={{0,16},{4,20},{8,24},{12,28},{16,0},{20,4},{24,8},{28,12},{1,17},{... | collective-permute-start | bytes 98312 | tf_op jit(solution)/shard_map/ppermute | solution.py:29
  53.4 12.3 %collective-permute-start.15 = (f32[64,128]{1,0:T(8,128)S(1)}, f32[64,128]{1,0:T(8,128)S(1)}, u32[]{:S(2)}, u32[]{:S(2)}) collective-permute-start(f32[64,128]{1,0:T(8,128)S(1)} %add.80), channel_id=1, source_target_pairs={{0,16},{4,20},{8,24},{12,28},{16,0},{20,4},{24,8},{28,12},{1,17},{... | collective-permute-start | bytes 98312 | tf_op jit(solution)/shard_map/ppermute | solution.py:29
  64.3 1.1 %copy-start.2 = (f32[64,64]{1,0:T(8,128)S(1)}, f32[64,64]{1,0:T(8,128)}, u32[]{:S(2)}) copy-start(f32[64,64]{1,0:T(8,128)} %shard_map.18) | copy-start | bytes 49156
  64.3 1.2 %copy-start.4 = (f32[64,128]{1,0:T(8,128)S(1)}, f32[64,128]{1,0:T(8,128)}, u32[]{:S(2)}) copy-start(f32[64,128]{1,0:T(8,128)} %add.78.head_ref) | copy-start | bytes 98308

commit v16 on v10

--- a/solution.py
+++ b/solution.py
@@ -33,7 +33,7 @@
 def invert_near_identity(square):
     identity = jnp.eye(square.shape[0], dtype=jnp.float32)
     approx = square.T * (2.0 / 4.25)
-    for _ in range(8):
+    for _ in range(7):
         approx = apply_left(approx, 2.0 * identity - apply_left(square, approx))
     return approx
 
@@ -64,27 +64,27 @@
     )(head)
 
 
-def spread_pair(block, axis, size):
+def spread_pair(block, value, axis, size):
     index = lax.axis_index(axis)
+    length = block.shape[1]
     have = block
     dist = size // 2
     while dist >= 2:
         got = lax.ppermute(
-            have, axis, [(i, i + dist) for i in range(size) if i % (2 * dist) < 2]
+            jnp.concatenate([have, value], axis=1),
+            axis,
+            [(i, i + dist) for i in range(size) if i % (2 * dist) < 2],
         )
-        have = jnp.where(index % (2 * dist) >= dist, got, have)
+        have = jnp.where(index % (2 * dist) >= dist, got[:, :length], have)
+        value = jnp.where(index % (2 * dist) == dist, got[:, length:], value)
         dist //= 2
-    other = lax.ppermute(have, axis, [(i, i ^ 1) for i in range(size)])
+    got = lax.ppermute(
+        jnp.concatenate([have, value], axis=1), axis, [(i, i ^ 1) for i in range(size)]
+    )
     even = index % 2 == 0
-    return jnp.where(even, have, other), jnp.where(even, other, have)
-
-
-def from_root(value, axis, size):
-    index = lax.axis_index(axis)
-    for k in range(1, size):
-        got = lax.ppermute(value, axis, [(0, k)])
-        value = jnp.where(index == k, got, value)
-    return value
+    other = got[:, :length]
+    value = jnp.where(even, value, got[:, length:])
+    return jnp.where(even, have, other), jnp.where(even, other, have), value
 
 
 def make_local(rows_size, cols_size):
@@ -107,8 +107,8 @@
             )
         else:
             head = inner_rows(current, jnp.concatenate([current, units[0]]))
-            head = butterfly_sum(from_root(head, "cols", cols_size), "rows", rows_size)
-            panel_0, second = spread_pair(current, "cols", cols_size)
+            panel_0, second, head = spread_pair(current, head, "cols", cols_size)
+            head = butterfly_sum(head, "rows", rows_size)
 
         both = jnp.concatenate([current, second])
         tail = jnp.concatenate([inner_rows(panel_0, both), inner_rows(units[0], both)], axis=1)

time: 69.6 us -> 71.3 us (1.024)
  waiting for transfers between devices: 9.99 us -> 17.8 us
  starting transfers between devices: 28.7 us -> 23.3 us
    ppermute x12, waiting for transfers between devices: 6.37 us -> 11.6 us  [butterfly_sum(): x = x + lax.ppermute(x, axis, [(i, i ^ step) for i in range(size)])]
    ppermute x12, starting transfers between devices: 21.3 us -> 18.3 us  [butterfly_sum(): x = x + lax.ppermute(x, axis, [(i, i ^ step) for i in range(size)])]
    ppermute x5 -> x2, waiting for transfers between devices: 3.63 us -> 6.27 us  [the longest x1 4.81 us: spread_pair(): lax.ppermute(jnp.concatenate([have, value], axis=1), axis, [(i, i + dist)...]
    ppermute x5 -> x2, starting transfers between devices: 7.37 us -> 4.96 us  [the longest x1 4.88 us: spread_pair(): lax.ppermute(jnp.concatenate([have, value], axis=1), axis, [(i, i + dist)...]
    dot_general x42 -> x38, matrix products: 8.63 us -> 7.99 us  [apply_left(): return jnp.dot(square, right_side, precision=HIGHEST_PRECISION)]
  transfers between devices with their start and end apart: 17 -> 14, of which waited for: 10 -> 8; matrix products, arithmetic and copies ran while one was open for 10% -> 8% of each run, Pallas kernels for 21% -> 20%
where the time goes in v16:
time: 71.3 us; the launch traced here: 70.9 us
  starting transfers between devices  23.3 us (33%)
  waiting for transfers between devices  17.8 us (25%)
  Pallas kernels  14.5 us (20%)
  matrix products  12.3 us (17%)
  other arithmetic  1.6 us (2%)
  local copies, waits for them, and re-layouts  0.91 us (1%)
    ppermute x12, starting transfers between devices, butterfly_sum(): x = x + lax.ppermute(x, axis, [(i, i ^ step) for i in range(size)])  18.3 us
    pallas_call x2, Pallas kernels, lower_inverse(): pl.pallas_call(_eliminate_kernel, out_shape=jax.ShapeDtypeStruct((size, s...  14.5 us
    ppermute x12, waiting for transfers between devices, butterfly_sum(): x = x + lax.ppermute(x, axis, [(i, i ^ step) for i in range(size)])  11.6 us
    dot_general x38, matrix products, apply_left(): return jnp.dot(square, right_side, precision=HIGHEST_PRECISION)  7.99 us
    ppermute x1, starting transfers between devices, spread_pair(): lax.ppermute(jnp.concatenate([have, value], axis=1), axis, [(i, i + dist)...  4.88 us
    ppermute x1, waiting for transfers between devices, spread_pair(): lax.ppermute(jnp.concatenate([have, value], axis=1), axis, [(i, i + dist)...  4.81 us
    dot_general x6, matrix products, inner_rows(): lax.dot_general(left, right, (((1,), (1,)), ((), ())), precision=HIGHEST_...  2.52 us
    ppermute x1, waiting for transfers between devices, spread_pair(): lax.ppermute(jnp.concatenate([have, value], axis=1), axis, [(i, i ^ 1) fo...  1.45 us
  transfers between devices with their start and end apart: 14, of which 8 were waited for; matrix products, arithmetic and copies ran while one was open for 8% of the time, Pallas kernels for 20%

profile of v16, /device:TPU:0, one launch (start us, length us, event | category | flops | bytes accessed | tf_op | source)
XLA Modules:
  0.0 70.9 jit_solution(15154012806753082575)
XLA Ops:
  0.0 0.9 %copy-done = f32[1,64,768]{2,1,0:T(8,128)S(1)} copy-done((f32[1,64,768]{2,1,0:T(8,128)S(1)}, f32[1,64,768]{2,1,0:T(8,128)}, u32[]{:S(2)}) %copy-start) | copy-done | bytes 196632
  0.9 0.5 convolution_bitcast_fusion
  1.5 4.9 %collective-permute-start = (f32[64,896]{1,0:T(8,128)S(1)}, f32[64,896]{1,0:T(8,128)S(1)}, u32[]{:S(2)}, u32[]{:S(2)}) collective-permute-start(f32[64,896]{1,0:T(8,128)S(1)} %pad_maximum_fusion.5), channel_id=1, source_target_pairs={{0,2},{1,3},{4,6},{5,7},{8,10},{9,11},{12,14},{13,15},{16,18},{17,... | collective-permute-start | bytes 688136 | tf_op jit(solution)/shard_map/ppermute | solution.py:73
  6.4 4.8 %collective-permute-done = f32[64,896]{1,0:T(8,128)S(1)} collective-permute-done((f32[64,896]{1,0:T(8,128)S(1)}, f32[64,896]{1,0:T(8,128)S(1)}, u32[]{:S(2)}, u32[]{:S(2)}) %collective-permute-start) | collective-permute-done | bytes 229408 | tf_op jit(solution)/shard_map/ppermute | solution.py:73
  11.4 1.5 %collective-permute-done.1 = f32[64,896]{1,0:T(8,128)S(1)} collective-permute-done((f32[64,896]{1,0:T(8,128)S(1)}, f32[64,896]{1,0:T(8,128)S(1)}, u32[]{:S(2)}, u32[]{:S(2)}) %collective-permute-start.1) | collective-permute-done | bytes 229408 | tf_op jit(solution)/shard_map/ppermute | solution.py:81
  13.2 0.5 fusion.8
  13.8 1.6 %collective-permute-start.5 = (f32[64,256]{1,0:T(8,128)S(1)}, f32[64,256]{1,0:T(8,128)S(1)}, u32[]{:S(2)}, u32[]{:S(2)}) collective-permute-start(f32[64,256]{1,0:T(8,128)S(1)} %pad_maximum_fusion.7), channel_id=1, source_target_pairs={{0,4},{4,0},{8,12},{12,8},{16,20},{20,16},{24,28},{28,24},{1,5},{5... | collective-permute-start | bytes 196616 | tf_op jit(solution)/shard_map/ppermute | solution.py:29
  15.3 0.5 collective-permute-start.2
  15.9 3.4 %collective-permute-done.2 = f32[64,128]{1,0:T(8,128)S(1)} collective-permute-done((f32[64,128]{1,0:T(8,128)S(1)}, f32[64,128]{1,0:T(8,128)S(1)}, u32[]{:S(2)}, u32[]{:S(2)}) %collective-permute-start.2) | collective-permute-done | bytes 32800 | tf_op jit(solution)/shard_map/ppermute | solution.py:29
  19.2 1.6 %collective-permute-start.3 = (f32[64,128]{1,0:T(8,128)S(1)}, f32[64,128]{1,0:T(8,128)S(1)}, u32[]{:S(2)}, u32[]{:S(2)}) collective-permute-start(f32[64,128]{1,0:T(8,128)S(1)} %add.69), channel_id=1, source_target_pairs={{0,8},{4,12},{8,0},{12,4},{16,24},{20,28},{24,16},{28,20},{1,9},{5... | collective-permute-start | bytes 98312 | tf_op jit(solution)/shard_map/ppermute | solution.py:29
  20.8 0.5 collective-permute-start.6
  21.4 2.2 %collective-permute-done.3 = f32[64,128]{1,0:T(8,128)S(1)} collective-permute-done((f32[64,128]{1,0:T(8,128)S(1)}, f32[64,128]{1,0:T(8,128)S(1)}, u32[]{:S(2)}, u32[]{:S(2)}) %collective-permute-start.3) | collective-permute-done | bytes 32800 | tf_op jit(solution)/shard_map/ppermute | solution.py:29
  23.5 2.6 %collective-permute-start.4 = (f32[64,128]{1,0:T(8,128)S(1)}, f32[64,128]{1,0:T(8,128)S(1)}, u32[]{:S(2)}, u32[]{:S(2)}) collective-permute-start(f32[64,128]{1,0:T(8,128)S(1)} %add.70), channel_id=1, source_target_pairs={{0,16},{4,20},{8,24},{12,28},{16,0},{20,4},{24,8},{28,12},{1,17},{... | collective-permute-start | bytes 98312 | tf_op jit(solution)/shard_map/ppermute | solution.py:29
  26.1 2.2 %collective-permute-done.4 = f32[64,128]{1,0:T(8,128)S(1)} collective-permute-done((f32[64,128]{1,0:T(8,128)S(1)}, f32[64,128]{1,0:T(8,128)S(1)}, u32[]{:S(2)}, u32[]{:S(2)}) %collective-permute-start.4) | collective-permute-done | bytes 32800 | tf_op jit(solution)/shard_map/ppermute | solution.py:29
  28.3 0.6 add.71.head_ref
  29.0 7.3 %shard_map.17 = f32[64,64]{1,0:T(8,128)} custom-call(f32[64,128]{1,0:T(8,128)} %add.71.head_ref), custom_call_target="tpu_custom_call" | custom-call | tf_op jit(solution)/shard_map/pallas_call | solution.py:62
  36.2 2.8 %collective-permute-start.7 = (f32[64,256]{1,0:T(8,128)S(1)}, f32[64,256]{1,0:T(8,128)S(1)}, u32[]{:S(2)}, u32[]{:S(2)}) collective-permute-start(f32[64,256]{1,0:T(8,128)S(1)} %add.73), channel_id=1, source_target_pairs={{0,16},{4,20},{8,24},{12,28},{16,0},{20,4},{24,8},{28,12},{1,17},{... | collective-permute-start | bytes 196616 | tf_op jit(solution)/shard_map/ppermute | solution.py:29
  43.6 0.4 fusion.1
  44.3 0.5 fusion.3
  44.8 1.0 %collective-permute-start.8 = (f32[64,128]{1,0:T(8,128)S(1)}, f32[64,128]{1,0:T(8,128)S(1)}, u32[]{:S(2)}, u32[]{:S(2)}) collective-permute-start(f32[64,128]{1,0:T(8,128)S(1)} %fusion.3), channel_id=1, source_target_pairs={{0,4},{4,0},{8,12},{12,8},{16,20},{20,16},{24,28},{28,24},{1,5},{5... | collective-permute-start | bytes 98312 | tf_op jit(solution)/shard_map/ppermute | solution.py:29
  45.9 1.1 %collective-permute-start.11 = (f32[64,128]{1,0:T(8,128)S(1)}, f32[64,128]{1,0:T(8,128)S(1)}, u32[]{:S(2)}, u32[]{:S(2)}) collective-permute-start(f32[64,128]{1,0:T(8,128)S(1)} %pad_maximum_fusion.8), channel_id=1, source_target_pairs={{0,4},{4,0},{8,12},{12,8},{16,20},{20,16},{24,28},{28,24},{1,5},{5... | collective-permute-start | bytes 98312 | tf_op jit(solution)/shard_map/ppermute | solution.py:29
  47.0 1.8 %collective-permute-done.8 = f32[64,128]{1,0:T(8,128)S(1)} collective-permute-done((f32[64,128]{1,0:T(8,128)S(1)}, f32[64,128]{1,0:T(8,128)S(1)}, u32[]{:S(2)}, u32[]{:S(2)}) %collective-permute-start.8) | collective-permute-done | bytes 32800 | tf_op jit(solution)/shard_map/ppermute | solution.py:29
  48.8 1.5 %collective-permute-start.9 = (f32[64,128]{1,0:T(8,128)S(1)}, f32[64,128]{1,0:T(8,128)S(1)}, u32[]{:S(2)}, u32[]{:S(2)}) collective-permute-start(f32[64,128]{1,0:T(8,128)S(1)} %add.75), channel_id=1, source_target_pairs={{0,8},{4,12},{8,0},{12,4},{16,24},{20,28},{24,16},{28,20},{1,9},{5... | collective-permute-start | bytes 98312 | tf_op jit(solution)/shard_map/ppermute | solution.py:29
  50.4 1.0 %collective-permute-start.12 = (f32[64,128]{1,0:T(8,128)S(1)}, f32[64,128]{1,0:T(8,128)S(1)}, u32[]{:S(2)}, u32[]{:S(2)}) collective-permute-start(f32[64,128]{1,0:T(8,128)S(1)} %fusion.123), channel_id=1, source_target_pairs={{0,8},{4,12},{8,0},{12,4},{16,24},{20,28},{24,16},{28,20},{1,9},{5... | collective-permute-start | bytes 98312 | tf_op jit(solution)/shard_map/ppermute | solution.py:29
  51.4 1.4 %collective-permute-done.9 = f32[64,128]{1,0:T(8,128)S(1)} collective-permute-done((f32[64,128]{1,0:T(8,128)S(1)}, f32[64,128]{1,0:T(8,128)S(1)}, u32[]{:S(2)}, u32[]{:S(2)}) %collective-permute-start.9) | collective-permute-done | bytes 32800 | tf_op jit(solution)/shard_map/ppermute | solution.py:29
  52.8 2.1 %collective-permute-start.10 = (f32[64,128]{1,0:T(8,128)S(1)}, f32[64,128]{1,0:T(8,128)S(1)}, u32[]{:S(2)}, u32[]{:S(2)}) collective-permute-start(f32[64,128]{1,0:T(8,128)S(1)} %add.76), channel_id=1, source_target_pairs={{0,16},{4,20},{8,24},{12,28},{16,0},{20,4},{24,8},{28,12},{1,17},{... | collective-permute-start | bytes 98312 | tf_op jit(solution)/shard_map/ppermute | solution.py:29
  54.9 2.1 %collective-permute-start.13 = (f32[64,128]{1,0:T(8,128)S(1)}, f32[64,128]{1,0:T(8,128)S(1)}, u32[]{:S(2)}, u32[]{:S(2)}) collective-permute-start(f32[64,128]{1,0:T(8,128)S(1)} %add.79), channel_id=1, source_target_pairs={{0,16},{4,20},{8,24},{12,28},{16,0},{20,4},{24,8},{28,12},{1,17},{... | collective-permute-start | bytes 98312 | tf_op jit(solution)/shard_map/ppermute | solution.py:29
  57.0 0.6 collective-permute-done.10
  57.6 0.6 add.77.head_ref
  58.2 7.3 %shard_map.18 = f32[64,64]{1,0:T(8,128)} custom-call(f32[64,128]{1,0:T(8,128)} %add.77.head_ref), custom_call_target="tpu_custom_call" | custom-call | tf_op jit(solution)/shard_map/pallas_call | solution.py:62
  65.5 1.1 %convolution_subtract_fusion.1 = f32[64,768]{1,0:T(8,128)S(1)} fusion(f32[64,64]{1,0:T(8,128)} %shard_map.18, f32[64,768]{1,0:T(8,128)S(1)} %fusion.1, s32[768]{0:T(1024)S(1)} %fusion.39), kind=kOutput, calls=%fused_computation.2 | convolution fusion | flops 37896192 | bytes 412672 | tf_op jit(solution)/shard_map/dot_general | solution.py:15
  69.9 1.1 %fusion = f32[1,64,768]{2,1,0:T(8,128)} fusion(f32[64,768]{1,0:T(8,128)S(1)} %convolution_subtract_fusion.3, f32[64,64]{1,0:T(8,128)S(1)} %fusion.18, f32[64,768]{1,0:T(8,128)S(1)} %convolution_subtract_fusion.1), kind=kOutput, calls=%fused_computation.1 | convolution fusion | flops 37797888 | bytes 606208 | tf_op jit(solution)/shard_map/dot_general | solution.py:147
  (80 shorter events, 8.6 us)
Async XLA Ops:
  0.0 0.9 %copy-start = (f32[1,64,768]{2,1,0:T(8,128)S(1)}, f32[1,64,768]{2,1,0:T(8,128)}, u32[]{:S(2)}) copy-start(f32[1,64,768]{2,1,0:T(8,128)} %param.1) | copy-start | bytes 589828
  1.5 9.7 %collective-permute-start = (f32[64,896]{1,0:T(8,128)S(1)}, f32[64,896]{1,0:T(8,128)S(1)}, u32[]{:S(2)}, u32[]{:S(2)}) collective-permute-start(f32[64,896]{1,0:T(8,128)S(1)} %pad_maximum_fusion.5), channel_id=1, source_target_pairs={{0,2},{1,3},{4,6},{5,7},{8,10},{9,11},{12,14},{13,15},{16,18},{17,... | collective-permute-start | bytes 688136 | tf_op jit(solution)/shard_map/ppermute | solution.py:73
  11.3 1.6 %collective-permute-start.1 = (f32[64,896]{1,0:T(8,128)S(1)}, f32[64,896]{1,0:T(8,128)S(1)}, u32[]{:S(2)}, u32[]{:S(2)}) collective-permute-start(f32[64,896]{1,0:T(8,128)S(1)} %pad_maximum_fusion.6), channel_id=1, source_target_pairs={{0,1},{1,0},{2,3},{3,2},{4,5},{5,4},{6,7},{7,6},{8,9},{9,8},{10,11... | collective-permute-start | bytes 688136 | tf_op jit(solution)/shard_map/ppermute | solution.py:81
  13.8 7.1 %collective-permute-start.5 = (f32[64,256]{1,0:T(8,128)S(1)}, f32[64,256]{1,0:T(8,128)S(1)}, u32[]{:S(2)}, u32[]{:S(2)}) collective-permute-start(f32[64,256]{1,0:T(8,128)S(1)} %pad_maximum_fusion.7), channel_id=1, source_target_pairs={{0,4},{4,0},{8,12},{12,8},{16,20},{20,16},{24,28},{28,24},{1,5},{5... | collective-permute-start | bytes 196616 | tf_op jit(solution)/shard_map/ppermute | solution.py:29
  15.3 3.9 %collective-permute-start.2 = (f32[64,128]{1,0:T(8,128)S(1)}, f32[64,128]{1,0:T(8,128)S(1)}, u32[]{:S(2)}, u32[]{:S(2)}) collective-permute-start(f32[64,128]{1,0:T(8,128)S(1)} %slice_select_fusion.5), channel_id=1, source_target_pairs={{0,4},{4,0},{8,12},{12,8},{16,20},{20,16},{24,28},{28,24},{1,5},{5... | collective-permute-start | bytes 98312 | tf_op jit(solution)/shard_map/ppermute | solution.py:29
  19.2 4.3 %collective-permute-start.3 = (f32[64,128]{1,0:T(8,128)S(1)}, f32[64,128]{1,0:T(8,128)S(1)}, u32[]{:S(2)}, u32[]{:S(2)}) collective-permute-start(f32[64,128]{1,0:T(8,128)S(1)} %add.69), channel_id=1, source_target_pairs={{0,8},{4,12},{8,0},{12,4},{16,24},{20,28},{24,16},{28,20},{1,9},{5... | collective-permute-start | bytes 98312 | tf_op jit(solution)/shard_map/ppermute | solution.py:29
  20.8 15.4 %collective-permute-start.6 = (f32[64,256]{1,0:T(8,128)S(1)}, f32[64,256]{1,0:T(8,128)S(1)}, u32[]{:S(2)}, u32[]{:S(2)}) collective-permute-start(f32[64,256]{1,0:T(8,128)S(1)} %fusion.49), channel_id=1, source_target_pairs={{0,8},{4,12},{8,0},{12,4},{16,24},{20,28},{24,16},{28,20},{1,9},{5... | collective-permute-start | bytes 196616 | tf_op jit(solution)/shard_map/ppermute | solution.py:29
  23.5 4.8 %collective-permute-start.4 = (f32[64,128]{1,0:T(8,128)S(1)}, f32[64,128]{1,0:T(8,128)S(1)}, u32[]{:S(2)}, u32[]{:S(2)}) collective-permute-start(f32[64,128]{1,0:T(8,128)S(1)} %add.70), channel_id=1, source_target_pairs={{0,16},{4,20},{8,24},{12,28},{16,0},{20,4},{24,8},{28,12},{1,17},{... | collective-permute-start | bytes 98312 | tf_op jit(solution)/shard_map/ppermute | solution.py:29
  36.2 2.8 %copy-start.1 = (f32[64,64]{1,0:T(8,128)S(1)}, f32[64,64]{1,0:T(8,128)}, u32[]{:S(2)}) copy-start(f32[64,64]{1,0:T(8,128)} %shard_map.17) | copy-start | bytes 49156
  36.2 2.8 %copy-start.3 = (f32[64,128]{1,0:T(8,128)S(1)}, f32[64,128]{1,0:T(8,128)}, u32[]{:S(2)}) copy-start(f32[64,128]{1,0:T(8,128)} %add.71.head_ref) | copy-start | bytes 98308
  36.2 5.9 %collective-permute-start.7 = (f32[64,256]{1,0:T(8,128)S(1)}, f32[64,256]{1,0:T(8,128)S(1)}, u32[]{:S(2)}, u32[]{:S(2)}) collective-permute-start(f32[64,256]{1,0:T(8,128)S(1)} %add.73), channel_id=1, source_target_pairs={{0,16},{4,20},{8,24},{12,28},{16,0},{20,4},{24,8},{28,12},{1,17},{... | collective-permute-start | bytes 196616 | tf_op jit(solution)/shard_map/ppermute | solution.py:29
  44.8 4.0 %collective-permute-start.8 = (f32[64,128]{1,0:T(8,128)S(1)}, f32[64,128]{1,0:T(8,128)S(1)}, u32[]{:S(2)}, u32[]{:S(2)}) collective-permute-start(f32[64,128]{1,0:T(8,128)S(1)} %fusion.3), channel_id=1, source_target_pairs={{0,4},{4,0},{8,12},{12,8},{16,20},{20,16},{24,28},{28,24},{1,5},{5... | collective-permute-start | bytes 98312 | tf_op jit(solution)/shard_map/ppermute | solution.py:29
  45.9 4.4 %collective-permute-start.11 = (f32[64,128]{1,0:T(8,128)S(1)}, f32[64,128]{1,0:T(8,128)S(1)}, u32[]{:S(2)}, u32[]{:S(2)}) collective-permute-start(f32[64,128]{1,0:T(8,128)S(1)} %pad_maximum_fusion.8), channel_id=1, source_target_pairs={{0,4},{4,0},{8,12},{12,8},{16,20},{20,16},{24,28},{28,24},{1,5},{5... | collective-permute-start | bytes 98312 | tf_op jit(solution)/shard_map/ppermute | solution.py:29
  48.8 4.0 %collective-permute-start.9 = (f32[64,128]{1,0:T(8,128)S(1)}, f32[64,128]{1,0:T(8,128)S(1)}, u32[]{:S(2)}, u32[]{:S(2)}) collective-permute-start(f32[64,128]{1,0:T(8,128)S(1)} %add.75), channel_id=1, source_target_pairs={{0,8},{4,12},{8,0},{12,4},{16,24},{20,28},{24,16},{28,20},{1,9},{5... | collective-permute-start | bytes 98312 | tf_op jit(solution)/shard_map/ppermute | solution.py:29
  50.4 4.5 %collective-permute-start.12 = (f32[64,128]{1,0:T(8,128)S(1)}, f32[64,128]{1,0:T(8,128)S(1)}, u32[]{:S(2)}, u32[]{:S(2)}) collective-permute-start(f32[64,128]{1,0:T(8,128)S(1)} %fusion.123), channel_id=1, source_target_pairs={{0,8},{4,12},{8,0},{12,4},{16,24},{20,28},{24,16},{28,20},{1,9},{5... | collective-permute-start | bytes 98312 | tf_op jit(solution)/shard_map/ppermute | solution.py:29
  52.8 4.8 %collective-permute-start.10 = (f32[64,128]{1,0:T(8,128)S(1)}, f32[64,128]{1,0:T(8,128)S(1)}, u32[]{:S(2)}, u32[]{:S(2)}) collective-permute-start(f32[64,128]{1,0:T(8,128)S(1)} %add.76), channel_id=1, source_target_pairs={{0,16},{4,20},{8,24},{12,28},{16,0},{20,4},{24,8},{28,12},{1,17},{... | collective-permute-start | bytes 98312 | tf_op jit(solution)/shard_map/ppermute | solution.py:29
  54.9 12.0 %collective-permute-start.13 = (f32[64,128]{1,0:T(8,128)S(1)}, f32[64,128]{1,0:T(8,128)S(1)}, u32[]{:S(2)}, u32[]{:S(2)}) collective-permute-start(f32[64,128]{1,0:T(8,128)S(1)} %add.79), channel_id=1, source_target_pairs={{0,16},{4,20},{8,24},{12,28},{16,0},{20,4},{24,8},{28,12},{1,17},{... | collective-permute-start | bytes 98312 | tf_op jit(solution)/shard_map/ppermute | solution.py:29
  65.5 1.1 %copy-start.2 = (f32[64,64]{1,0:T(8,128)S(1)}, f32[64,64]{1,0:T(8,128)}, u32[]{:S(2)}) copy-start(f32[64,64]{1,0:T(8,128)} %shard_map.18) | copy-start | bytes 49156
  65.5 1.2 %copy-start.4 = (f32[64,128]{1,0:T(8,128)S(1)}, f32[64,128]{1,0:T(8,128)}, u32[]{:S(2)}) copy-start(f32[64,128]{1,0:T(8,128)} %add.77.head_ref) | copy-start | bytes 98308

commit v17 on v12

--- a/solution.py
+++ b/solution.py
@@ -30,6 +30,14 @@
     return x
 
 
+def butterfly_parts(x, axis, size):
+    steps = butterfly_steps(size)
+    if steps is None:
+        return lax.psum(x, axis), jnp.zeros_like(x)
+    x = butterfly_sum(x, axis, size, steps[:-1])
+    return x, lax.ppermute(x, axis, [(i, i ^ steps[-1]) for i in range(size)])
+
+
 def invert_near_identity(square):
     identity = jnp.eye(square.shape[0], dtype=jnp.float32)
     approx = square.T * (2.0 / 4.25)
@@ -38,30 +46,29 @@
     return approx
 
 
-def _eliminate_kernel(head_ref, out_ref):
+def _eliminate_kernel(part_ref, last_ref, out_ref):
     size = out_ref.shape[0]
     wide = 2 * size
     rows = lax.broadcasted_iota(jnp.int32, (size, wide), 0)
     lanes = lax.broadcasted_iota(jnp.int32, (size, wide), 1)
     row_ids = lax.broadcasted_iota(jnp.int32, (size, 1), 0)
-    work = head_ref[:, :wide]
+    work = part_ref[:, :wide] + last_ref[:, :wide]
     work = jnp.where(lanes < size, work, (lanes == rows + size).astype(jnp.float32))
     for j in range(size):
         row = work[j:j + 1, :]
         pivot = row[:, j:j + 1]
         scale = lax.rsqrt(pivot)
-        scale = scale * (1.5 - 0.5 * pivot * scale * scale)
         scaled = row * scale
         weight = jnp.where(row_ids > j, work[:, j:j + 1] * scale, 0.0)
         work = jnp.where(rows == j, scaled, work - weight * scaled)
     out_ref[...] = work[:, size:]
 
 
-def lower_inverse(head):
-    size = head.shape[0]
+def lower_inverse(parts):
+    size = parts[0].shape[0]
     return pl.pallas_call(
         _eliminate_kernel, out_shape=jax.ShapeDtypeStruct((size, size), jnp.float32)
-    )(head)
+    )(*parts)
 
 
 def spread_pair(block, axis, size):
@@ -106,12 +113,12 @@
             gathered = lax.all_gather(current, "cols")
             panel_0 = gathered[0]
             second = gathered[1]
-            head = butterfly_sum(
+            head = butterfly_parts(
                 inner_rows(panel_0, jnp.concatenate([panel_0, units[0]])), "rows", rows_size
             )
         else:
             head = inner_rows(current, jnp.concatenate([current, units[0]]))
-            head = butterfly_sum(from_root(head, "cols", cols_size), "rows", rows_size)
+            head = butterfly_parts(from_root(head, "cols", cols_size), "rows", rows_size)
             panel_0, second = spread_pair(current, "cols", cols_size)
 
         both = jnp.concatenate([current, second])
@@ -120,7 +127,7 @@
         tail = butterfly_sum(tail, "rows", rows_size, None if steps is None else steps[:-1])
         lower_inv, tail = lax.optimization_barrier((lower_inverse(head), tail))
         tail = butterfly_sum(tail, "rows", rows_size, None if steps is None else steps[-1:])
-        top_rows = head[:, width:]
+        top_rows = (head[0] + head[1])[:, width:]
         basis_cur, basis_sec, unit_cur, unit_sec = (
             tail[:, i * width:(i + 1) * width] for i in range(4)
         )
@@ -133,7 +140,7 @@
         second = second - jnp.dot(mixed_sec.T, reflect, precision=HIGHEST_PRECISION)
 
         panel_1 = jnp.where((global_rows >= width)[None, :], second, jnp.zeros_like(second))
-        head = butterfly_sum(
+        head = butterfly_parts(
             inner_rows(panel_1, jnp.concatenate([panel_1, units[1]])), "rows", rows_size
         )
         tail = butterfly_sum(
@@ -141,7 +148,7 @@
             "rows",
             rows_size,
         )
-        top_rows = head[:, width:]
+        top_rows = (head[0] + head[1])[:, width:]
         basis_cur, unit_cur = tail[:, :width], tail[:, width:]
         lower_inv = lower_inverse(head)
         top_block = apply_left(lower_inv, top_rows)

time: 67.7 us -> 68.3 us (level)
  local copies, waits for them, and re-layouts: 0.91 us -> 3.47 us
  other arithmetic: 1.57 us -> 0.33 us
  Pallas kernels: 14.5 us -> 13.6 us
    ppermute x0 -> x2, starting transfers between devices: none -> 4.69 us  [butterfly_parts(): return (x, lax.ppermute(x, axis, [(i, i ^ steps[-1]) for i in range(size)]))]
    ppermute x12 -> x10, starting transfers between devices: 20.7 us -> 16.1 us  [butterfly_sum(): x = x + lax.ppermute(x, axis, [(i, i ^ step) for i in range(size)])]
    unnamed x10 -> x22, local copies, waits for them, and re-layouts: 0.91 us -> 3.47 us
    ppermute x0 -> x2, waiting for transfers between devices: none -> 1.5 us  [butterfly_parts(): return (x, lax.ppermute(x, axis, [(i, i ^ steps[-1]) for i in range(size)]))]
    ppermute x12 -> x10, waiting for transfers between devices: 6.68 us -> 5.24 us  [butterfly_sum(): x = x + lax.ppermute(x, axis, [(i, i ^ step) for i in range(size)])]
    add x12 -> x10, other arithmetic: 1.38 us -> 0.14 us  [butterfly_sum(): x = x + lax.ppermute(x, axis, [(i, i ^ step) for i in range(size)])]
    pallas_call x2, Pallas kernels: 14.5 us -> 13.6 us  [lower_inverse(): pl.pallas_call(_eliminate_kernel, out_shape=jax.ShapeDtypeStruct((size, s...]
  transfers between devices with their start and end apart: 16 -> 16, of which waited for: 8 -> 8; matrix products, arithmetic and copies ran while one was open for 10% -> 8% of each run, Pallas kernels for 22% -> 20%
where the time goes in v17:
time: 68.3 us; the launch traced here: 67.8 us
  starting transfers between devices  28.3 us (41%)
  Pallas kernels  13.6 us (20%)
  matrix products  12.2 us (18%)
  waiting for transfers between devices  9.28 us (14%)
  local copies, waits for them, and re-layouts  3.47 us (5%)
    ppermute x10, starting transfers between devices, butterfly_sum(): x = x + lax.ppermute(x, axis, [(i, i ^ step) for i in range(size)])  16.1 us
    pallas_call x2, Pallas kernels, lower_inverse(): pl.pallas_call(_eliminate_kernel, out_shape=jax.ShapeDtypeStruct((size, s...  13.6 us
    dot_general x38, matrix products, apply_left(): return jnp.dot(square, right_side, precision=HIGHEST_PRECISION)  7.92 us
    ppermute x2, starting transfers between devices, from_root(): lax.ppermute(value, axis, [(i, i + dist) for i in range(size) if i % (2 *...  6.15 us
    ppermute x10, waiting for transfers between devices, butterfly_sum(): x = x + lax.ppermute(x, axis, [(i, i ^ step) for i in range(size)])  5.24 us
    ppermute x2, starting transfers between devices, butterfly_parts(): return (x, lax.ppermute(x, axis, [(i, i ^ steps[-1]) for i in range(size)]))  4.69 us
    unnamed x22, local copies, waits for them, and re-layouts  3.47 us
    dot_general x6, matrix products, inner_rows(): lax.dot_general(left, right, (((1,), (1,)), ((), ())), precision=HIGHEST_...  2.52 us
  transfers between devices with their start and end apart: 16, of which 8 were waited for; matrix products, arithmetic and copies ran while one was open for 8% of the time, Pallas kernels for 20%

profile of v17, /device:TPU:0, one launch (start us, length us, event | category | flops | bytes accessed | tf_op | source)
XLA Modules:
  0.0 67.8 jit_solution(12420218086435533830)
XLA Ops:
  0.0 0.9 %copy-done = f32[1,64,768]{2,1,0:T(8,128)S(1)} copy-done((f32[1,64,768]{2,1,0:T(8,128)S(1)}, f32[1,64,768]{2,1,0:T(8,128)}, u32[]{:S(2)}) %copy-start) | copy-done | bytes 196632
  1.5 4.9 %collective-permute-start = (f32[64,128]{1,0:T(8,128)S(1)}, f32[64,128]{1,0:T(8,128)S(1)}, u32[]{:S(2)}, u32[]{:S(2)}) collective-permute-start(f32[64,128]{1,0:T(8,128)S(1)} %convolution_bitcast_fusion), channel_id=1, source_target_pairs={{0,2},{4,6},{8,10},{12,14},{16,18},{20,22},{24,26},{28,30}} | collective-permute-start | bytes 98312 | tf_op jit(solution)/shard_map/ppermute | solution.py:93
  6.3 1.3 %collective-permute-start.5 = (f32[64,768]{1,0:T(8,128)S(1)}, f32[64,768]{1,0:T(8,128)S(1)}, u32[]{:S(2)}, u32[]{:S(2)}) collective-permute-start(f32[64,768]{1,0:T(8,128)S(1)} %bitcast.76), channel_id=1, source_target_pairs={{0,2},{1,3},{4,6},{5,7},{8,10},{9,11},{12,14},{13,15},{16,18},{17,... | collective-permute-start | bytes 589832 | tf_op jit(solution)/shard_map/ppermute | solution.py:79
  8.0 1.3 %collective-permute-start.1 = (f32[64,128]{1,0:T(8,128)S(1)}, f32[64,128]{1,0:T(8,128)S(1)}, u32[]{:S(2)}, u32[]{:S(2)}) collective-permute-start(f32[64,128]{1,0:T(8,128)S(1)} %broadcast_select_fusion.5), channel_id=1, source_target_pairs={{0,1},{2,3},{4,5},{6,7},{8,9},{10,11},{12,13},{14,15},{16,17},{18,... | collective-permute-start | bytes 98312 | tf_op jit(solution)/shard_map/ppermute | solution.py:93
  9.3 2.2 %collective-permute-done.5 = f32[64,768]{1,0:T(8,128)S(1)} collective-permute-done((f32[64,768]{1,0:T(8,128)S(1)}, f32[64,768]{1,0:T(8,128)S(1)}, u32[]{:S(2)}, u32[]{:S(2)}) %collective-permute-start.5) | collective-permute-done | bytes 196640 | tf_op jit(solution)/shard_map/ppermute | solution.py:79
  11.6 1.6 %collective-permute-start.2 = (f32[64,128]{1,0:T(8,128)S(1)}, f32[64,128]{1,0:T(8,128)S(1)}, u32[]{:S(2)}, u32[]{:S(2)}) collective-permute-start(f32[64,128]{1,0:T(8,128)S(1)} %broadcast_select_fusion.6), channel_id=1, source_target_pairs={{0,4},{4,0},{8,12},{12,8},{16,20},{20,16},{24,28},{28,24},{1,5},{5... | collective-permute-start | bytes 98312 | tf_op jit(solution)/shard_map/ppermute | solution.py:29
  13.2 2.4 %collective-permute-done.2 = f32[64,128]{1,0:T(8,128)S(1)} collective-permute-done((f32[64,128]{1,0:T(8,128)S(1)}, f32[64,128]{1,0:T(8,128)S(1)}, u32[]{:S(2)}, u32[]{:S(2)}) %collective-permute-start.2) | collective-permute-done | bytes 32800 | tf_op jit(solution)/shard_map/ppermute | solution.py:29
  15.6 1.6 %collective-permute-start.3 = (f32[64,128]{1,0:T(8,128)S(1)}, f32[64,128]{1,0:T(8,128)S(1)}, u32[]{:S(2)}, u32[]{:S(2)}) collective-permute-start(f32[64,128]{1,0:T(8,128)S(1)} %add.70), channel_id=1, source_target_pairs={{0,8},{4,12},{8,0},{12,4},{16,24},{20,28},{24,16},{28,20},{1,9},{5... | collective-permute-start | bytes 98312 | tf_op jit(solution)/shard_map/ppermute | solution.py:29
  17.6 0.5 fusion.8
  18.1 1.6 %collective-permute-start.7 = (f32[64,256]{1,0:T(8,128)S(1)}, f32[64,256]{1,0:T(8,128)S(1)}, u32[]{:S(2)}, u32[]{:S(2)}) collective-permute-start(f32[64,256]{1,0:T(8,128)S(1)} %pad_maximum_fusion.5), channel_id=1, source_target_pairs={{0,4},{4,0},{8,12},{12,8},{16,20},{20,16},{24,28},{28,24},{1,5},{5... | collective-permute-start | bytes 196616 | tf_op jit(solution)/shard_map/ppermute | solution.py:29
  19.7 2.7 %collective-permute-start.4 = (f32[64,128]{1,0:T(8,128)S(1)}, f32[64,128]{1,0:T(8,128)S(1)}, u32[]{:S(2)}, u32[]{:S(2)}) collective-permute-start(f32[64,128]{1,0:T(8,128)S(1)} %add.71.part_ref), channel_id=1, source_target_pairs={{0,16},{4,20},{8,24},{12,28},{16,0},{20,4},{24,8},{28,12},{1,17},{... | collective-permute-start | bytes 98312 | tf_op jit(solution)/shard_map/ppermute | solution.py:38
  22.5 1.4 %collective-permute-start.8 = (f32[64,256]{1,0:T(8,128)S(1)}, f32[64,256]{1,0:T(8,128)S(1)}, u32[]{:S(2)}, u32[]{:S(2)}) collective-permute-start(f32[64,256]{1,0:T(8,128)S(1)} %fusion.49), channel_id=1, source_target_pairs={{0,8},{4,12},{8,0},{12,4},{16,24},{20,28},{24,16},{28,20},{1,9},{5... | collective-permute-start | bytes 196616 | tf_op jit(solution)/shard_map/ppermute | solution.py:29
  23.9 0.8 %collective-permute-done.4.last_ref = f32[64,128]{1,0:T(8,128)S(1)} collective-permute-done((f32[64,128]{1,0:T(8,128)S(1)}, f32[64,128]{1,0:T(8,128)S(1)}, u32[]{:S(2)}, u32[]{:S(2)}) %collective-permute-start.4) | collective-permute-done | bytes 32800 | tf_op jit(solution)/shard_map/ppermute | solution.py:38
  24.6 0.6 copy-done.7
  25.3 6.8 %shard_map.17 = f32[64,64]{1,0:T(8,128)} custom-call(f32[64,128]{1,0:T(8,128)} %copy-done.3, f32[64,128]{1,0:T(8,128)} %copy-done.7), custom_call_target="tpu_custom_call" | custom-call | tf_op jit(solution)/shard_map/pallas_call | solution.py:69
  32.1 2.7 %collective-permute-start.9 = (f32[64,256]{1,0:T(8,128)S(1)}, f32[64,256]{1,0:T(8,128)S(1)}, u32[]{:S(2)}, u32[]{:S(2)}) collective-permute-start(f32[64,256]{1,0:T(8,128)S(1)} %add.74), channel_id=1, source_target_pairs={{0,16},{4,20},{8,24},{12,28},{16,0},{20,4},{24,8},{28,12},{1,17},{... | collective-permute-start | bytes 196616 | tf_op jit(solution)/shard_map/ppermute | solution.py:29
  40.2 0.5 fusion.3
  40.7 1.3 %collective-permute-start.10 = (f32[64,128]{1,0:T(8,128)S(1)}, f32[64,128]{1,0:T(8,128)S(1)}, u32[]{:S(2)}, u32[]{:S(2)}) collective-permute-start(f32[64,128]{1,0:T(8,128)S(1)} %fusion.3), channel_id=1, source_target_pairs={{0,4},{4,0},{8,12},{12,8},{16,20},{20,16},{24,28},{28,24},{1,5},{5... | collective-permute-start | bytes 98312 | tf_op jit(solution)/shard_map/ppermute | solution.py:29
  42.0 0.8 %collective-permute-start.13 = (f32[64,128]{1,0:T(8,128)S(1)}, f32[64,128]{1,0:T(8,128)S(1)}, u32[]{:S(2)}, u32[]{:S(2)}) collective-permute-start(f32[64,128]{1,0:T(8,128)S(1)} %pad_maximum_fusion.6), channel_id=1, source_target_pairs={{0,4},{4,0},{8,12},{12,8},{16,20},{20,16},{24,28},{28,24},{1,5},{5... | collective-permute-start | bytes 98312 | tf_op jit(solution)/shard_map/ppermute | solution.py:29
  42.9 1.8 %collective-permute-done.10 = f32[64,128]{1,0:T(8,128)S(1)} collective-permute-done((f32[64,128]{1,0:T(8,128)S(1)}, f32[64,128]{1,0:T(8,128)S(1)}, u32[]{:S(2)}, u32[]{:S(2)}) %collective-permute-start.10) | collective-permute-done | bytes 32800 | tf_op jit(solution)/shard_map/ppermute | solution.py:29
  44.7 1.6 %collective-permute-start.11 = (f32[64,128]{1,0:T(8,128)S(1)}, f32[64,128]{1,0:T(8,128)S(1)}, u32[]{:S(2)}, u32[]{:S(2)}) collective-permute-start(f32[64,128]{1,0:T(8,128)S(1)} %add.76), channel_id=1, source_target_pairs={{0,8},{4,12},{8,0},{12,4},{16,24},{20,28},{24,16},{28,20},{1,9},{5... | collective-permute-start | bytes 98312 | tf_op jit(solution)/shard_map/ppermute | solution.py:29
  46.4 1.5 %collective-permute-start.14 = (f32[64,128]{1,0:T(8,128)S(1)}, f32[64,128]{1,0:T(8,128)S(1)}, u32[]{:S(2)}, u32[]{:S(2)}) collective-permute-start(f32[64,128]{1,0:T(8,128)S(1)} %fusion.123), channel_id=1, source_target_pairs={{0,8},{4,12},{8,0},{12,4},{16,24},{20,28},{24,16},{28,20},{1,9},{5... | collective-permute-start | bytes 98312 | tf_op jit(solution)/shard_map/ppermute | solution.py:29
  47.8 0.9 %collective-permute-done.11 = f32[64,128]{1,0:T(8,128)S(1)} collective-permute-done((f32[64,128]{1,0:T(8,128)S(1)}, f32[64,128]{1,0:T(8,128)S(1)}, u32[]{:S(2)}, u32[]{:S(2)}) %collective-permute-start.11) | collective-permute-done | bytes 32800 | tf_op jit(solution)/shard_map/ppermute | solution.py:29
  48.8 2.0 %collective-permute-start.12 = (f32[64,128]{1,0:T(8,128)S(1)}, f32[64,128]{1,0:T(8,128)S(1)}, u32[]{:S(2)}, u32[]{:S(2)}) collective-permute-start(f32[64,128]{1,0:T(8,128)S(1)} %add.77.part_ref), channel_id=1, source_target_pairs={{0,16},{4,20},{8,24},{12,28},{16,0},{20,4},{24,8},{28,12},{1,17},{... | collective-permute-start | bytes 98312 | tf_op jit(solution)/shard_map/ppermute | solution.py:38
  50.8 2.1 %collective-permute-start.15 = (f32[64,128]{1,0:T(8,128)S(1)}, f32[64,128]{1,0:T(8,128)S(1)}, u32[]{:S(2)}, u32[]{:S(2)}) collective-permute-start(f32[64,128]{1,0:T(8,128)S(1)} %add.80), channel_id=1, source_target_pairs={{0,16},{4,20},{8,24},{12,28},{16,0},{20,4},{24,8},{28,12},{1,17},{... | collective-permute-start | bytes 98312 | tf_op jit(solution)/shard_map/ppermute | solution.py:29
  52.9 0.7 %collective-permute-done.12.last_ref = f32[64,128]{1,0:T(8,128)S(1)} collective-permute-done((f32[64,128]{1,0:T(8,128)S(1)}, f32[64,128]{1,0:T(8,128)S(1)}, u32[]{:S(2)}, u32[]{:S(2)}) %collective-permute-start.12) | collective-permute-done | bytes 32800 | tf_op jit(solution)/shard_map/ppermute | solution.py:38
  53.7 0.6 copy-done.9
  54.3 6.8 %shard_map.18 = f32[64,64]{1,0:T(8,128)} custom-call(f32[64,128]{1,0:T(8,128)} %copy-done.5, f32[64,128]{1,0:T(8,128)} %copy-done.9), custom_call_target="tpu_custom_call" | custom-call | tf_op jit(solution)/shard_map/pallas_call | solution.py:69
  61.1 1.1 %convolution_subtract_fusion.1 = f32[64,768]{1,0:T(8,128)S(1)} fusion(f32[64,64]{1,0:T(8,128)} %shard_map.18, f32[64,768]{1,0:T(8,128)S(1)} %fusion.1, s32[768]{0:T(1024)S(1)} %fusion.39), kind=kOutput, calls=%fused_computation.2 | convolution fusion | flops 37896192 | bytes 412672 | tf_op jit(solution)/shard_map/dot_general | solution.py:15
  62.2 0.7 %copy-done.2 = f32[64,64]{1,0:T(8,128)S(1)} copy-done((f32[64,64]{1,0:T(8,128)S(1)}, f32[64,64]{1,0:T(8,128)}, u32[]{:S(2)}) %copy-start.2) | copy-done | bytes 16408
  63.1 0.6 copy-done.6
  66.7 1.1 %fusion = f32[1,64,768]{2,1,0:T(8,128)} fusion(f32[64,768]{1,0:T(8,128)S(1)} %convolution_subtract_fusion.3, f32[64,64]{1,0:T(8,128)S(1)} %fusion.18, f32[64,768]{1,0:T(8,128)S(1)} %convolution_subtract_fusion.1), kind=kOutput, calls=%fused_computation.1 | convolution fusion | flops 37797888 | bytes 606208 | tf_op jit(solution)/shard_map/dot_general | solution.py:158
  (92 shorter events, 9.9 us)
Async XLA Ops:
  0.0 0.9 %copy-start = (f32[1,64,768]{2,1,0:T(8,128)S(1)}, f32[1,64,768]{2,1,0:T(8,128)}, u32[]{:S(2)}) copy-start(f32[1,64,768]{2,1,0:T(8,128)} %param.1) | copy-start | bytes 589828
  1.5 6.6 %collective-permute-start = (f32[64,128]{1,0:T(8,128)S(1)}, f32[64,128]{1,0:T(8,128)S(1)}, u32[]{:S(2)}, u32[]{:S(2)}) collective-permute-start(f32[64,128]{1,0:T(8,128)S(1)} %convolution_bitcast_fusion), channel_id=1, source_target_pairs={{0,2},{4,6},{8,10},{12,14},{16,18},{20,22},{24,26},{28,30}} | collective-permute-start | bytes 98312 | tf_op jit(solution)/shard_map/ppermute | solution.py:93
  6.3 5.2 %collective-permute-start.5 = (f32[64,768]{1,0:T(8,128)S(1)}, f32[64,768]{1,0:T(8,128)S(1)}, u32[]{:S(2)}, u32[]{:S(2)}) collective-permute-start(f32[64,768]{1,0:T(8,128)S(1)} %bitcast.76), channel_id=1, source_target_pairs={{0,2},{1,3},{4,6},{5,7},{8,10},{9,11},{12,14},{13,15},{16,18},{17,... | collective-permute-start | bytes 589832 | tf_op jit(solution)/shard_map/ppermute | solution.py:79
  8.0 3.6 %collective-permute-start.1 = (f32[64,128]{1,0:T(8,128)S(1)}, f32[64,128]{1,0:T(8,128)S(1)}, u32[]{:S(2)}, u32[]{:S(2)}) collective-permute-start(f32[64,128]{1,0:T(8,128)S(1)} %broadcast_select_fusion.5), channel_id=1, source_target_pairs={{0,1},{2,3},{4,5},{6,7},{8,9},{10,11},{12,13},{14,15},{16,17},{18,... | collective-permute-start | bytes 98312 | tf_op jit(solution)/shard_map/ppermute | solution.py:93
  11.5 5.7 %collective-permute-start.6 = (f32[64,768]{1,0:T(8,128)S(1)}, f32[64,768]{1,0:T(8,128)S(1)}, u32[]{:S(2)}, u32[]{:S(2)}) collective-permute-start(f32[64,768]{1,0:T(8,128)S(1)} %broadcast_select_fusion), channel_id=1, source_target_pairs={{0,1},{1,0},{2,3},{3,2},{4,5},{5,4},{6,7},{7,6},{8,9},{9,8},{10,11... | collective-permute-start | bytes 589832 | tf_op jit(solution)/shard_map/ppermute | solution.py:84
  11.6 4.0 %collective-permute-start.2 = (f32[64,128]{1,0:T(8,128)S(1)}, f32[64,128]{1,0:T(8,128)S(1)}, u32[]{:S(2)}, u32[]{:S(2)}) collective-permute-start(f32[64,128]{1,0:T(8,128)S(1)} %broadcast_select_fusion.6), channel_id=1, source_target_pairs={{0,4},{4,0},{8,12},{12,8},{16,20},{20,16},{24,28},{28,24},{1,5},{5... | collective-permute-start | bytes 98312 | tf_op jit(solution)/shard_map/ppermute | solution.py:29
  15.6 4.1 %collective-permute-start.3 = (f32[64,128]{1,0:T(8,128)S(1)}, f32[64,128]{1,0:T(8,128)S(1)}, u32[]{:S(2)}, u32[]{:S(2)}) collective-permute-start(f32[64,128]{1,0:T(8,128)S(1)} %add.70), channel_id=1, source_target_pairs={{0,8},{4,12},{8,0},{12,4},{16,24},{20,28},{24,16},{28,20},{1,9},{5... | collective-permute-start | bytes 98312 | tf_op jit(solution)/shard_map/ppermute | solution.py:29
  18.1 4.3 %collective-permute-start.7 = (f32[64,256]{1,0:T(8,128)S(1)}, f32[64,256]{1,0:T(8,128)S(1)}, u32[]{:S(2)}, u32[]{:S(2)}) collective-permute-start(f32[64,256]{1,0:T(8,128)S(1)} %pad_maximum_fusion.5), channel_id=1, source_target_pairs={{0,4},{4,0},{8,12},{12,8},{16,20},{20,16},{24,28},{28,24},{1,5},{5... | collective-permute-start | bytes 196616 | tf_op jit(solution)/shard_map/ppermute | solution.py:29
  19.7 2.7 %copy-start.3 = (f32[64,128]{1,0:T(8,128)}, f32[64,128]{1,0:T(8,128)S(1)}, u32[]{:S(2)}) copy-start(f32[64,128]{1,0:T(8,128)S(1)} %add.71.part_ref) | copy-start | bytes 98308
  19.7 4.9 %collective-permute-start.4 = (f32[64,128]{1,0:T(8,128)S(1)}, f32[64,128]{1,0:T(8,128)S(1)}, u32[]{:S(2)}, u32[]{:S(2)}) collective-permute-start(f32[64,128]{1,0:T(8,128)S(1)} %add.71.part_ref), channel_id=1, source_target_pairs={{0,16},{4,20},{8,24},{12,28},{16,0},{20,4},{24,8},{28,12},{1,17},{... | collective-permute-start | bytes 98312 | tf_op jit(solution)/shard_map/ppermute | solution.py:38
  22.5 9.6 %collective-permute-start.8 = (f32[64,256]{1,0:T(8,128)S(1)}, f32[64,256]{1,0:T(8,128)S(1)}, u32[]{:S(2)}, u32[]{:S(2)}) collective-permute-start(f32[64,256]{1,0:T(8,128)S(1)} %fusion.49), channel_id=1, source_target_pairs={{0,8},{4,12},{8,0},{12,4},{16,24},{20,28},{24,16},{28,20},{1,9},{5... | collective-permute-start | bytes 196616 | tf_op jit(solution)/shard_map/ppermute | solution.py:29
  24.6 0.6 copy-start.7
  32.1 2.8 %copy-start.1 = (f32[64,64]{1,0:T(8,128)S(1)}, f32[64,64]{1,0:T(8,128)}, u32[]{:S(2)}) copy-start(f32[64,64]{1,0:T(8,128)} %shard_map.17) | copy-start | bytes 49156
  32.1 2.8 %copy-start.4 = (f32[64,128]{1,0:T(8,128)S(1)}, f32[64,128]{1,0:T(8,128)}, u32[]{:S(2)}) copy-start(f32[64,128]{1,0:T(8,128)} %copy-done.3) | copy-start | bytes 98308
  32.1 2.8 %copy-start.8 = (f32[64,128]{1,0:T(8,128)S(1)}, f32[64,128]{1,0:T(8,128)}, u32[]{:S(2)}) copy-start(f32[64,128]{1,0:T(8,128)} %copy-done.7) | copy-start | bytes 98308
  32.1 5.9 %collective-permute-start.9 = (f32[64,256]{1,0:T(8,128)S(1)}, f32[64,256]{1,0:T(8,128)S(1)}, u32[]{:S(2)}, u32[]{:S(2)}) collective-permute-start(f32[64,256]{1,0:T(8,128)S(1)} %add.74), channel_id=1, source_target_pairs={{0,16},{4,20},{8,24},{12,28},{16,0},{20,4},{24,8},{28,12},{1,17},{... | collective-permute-start | bytes 196616 | tf_op jit(solution)/shard_map/ppermute | solution.py:29
  40.7 4.0 %collective-permute-start.10 = (f32[64,128]{1,0:T(8,128)S(1)}, f32[64,128]{1,0:T(8,128)S(1)}, u32[]{:S(2)}, u32[]{:S(2)}) collective-permute-start(f32[64,128]{1,0:T(8,128)S(1)} %fusion.3), channel_id=1, source_target_pairs={{0,4},{4,0},{8,12},{12,8},{16,20},{20,16},{24,28},{28,24},{1,5},{5... | collective-permute-start | bytes 98312 | tf_op jit(solution)/shard_map/ppermute | solution.py:29
  42.0 4.3 %collective-permute-start.13 = (f32[64,128]{1,0:T(8,128)S(1)}, f32[64,128]{1,0:T(8,128)S(1)}, u32[]{:S(2)}, u32[]{:S(2)}) collective-permute-start(f32[64,128]{1,0:T(8,128)S(1)} %pad_maximum_fusion.6), channel_id=1, source_target_pairs={{0,4},{4,0},{8,12},{12,8},{16,20},{20,16},{24,28},{28,24},{1,5},{5... | collective-permute-start | bytes 98312 | tf_op jit(solution)/shard_map/ppermute | solution.py:29
  44.7 4.1 %collective-permute-start.11 = (f32[64,128]{1,0:T(8,128)S(1)}, f32[64,128]{1,0:T(8,128)S(1)}, u32[]{:S(2)}, u32[]{:S(2)}) collective-permute-start(f32[64,128]{1,0:T(8,128)S(1)} %add.76), channel_id=1, source_target_pairs={{0,8},{4,12},{8,0},{12,4},{16,24},{20,28},{24,16},{28,20},{1,9},{5... | collective-permute-start | bytes 98312 | tf_op jit(solution)/shard_map/ppermute | solution.py:29
  46.4 4.5 %collective-permute-start.14 = (f32[64,128]{1,0:T(8,128)S(1)}, f32[64,128]{1,0:T(8,128)S(1)}, u32[]{:S(2)}, u32[]{:S(2)}) collective-permute-start(f32[64,128]{1,0:T(8,128)S(1)} %fusion.123), channel_id=1, source_target_pairs={{0,8},{4,12},{8,0},{12,4},{16,24},{20,28},{24,16},{28,20},{1,9},{5... | collective-permute-start | bytes 98312 | tf_op jit(solution)/shard_map/ppermute | solution.py:29
  48.8 2.1 %copy-start.5 = (f32[64,128]{1,0:T(8,128)}, f32[64,128]{1,0:T(8,128)S(1)}, u32[]{:S(2)}) copy-start(f32[64,128]{1,0:T(8,128)S(1)} %add.77.part_ref) | copy-start | bytes 98308
  48.8 4.9 %collective-permute-start.12 = (f32[64,128]{1,0:T(8,128)S(1)}, f32[64,128]{1,0:T(8,128)S(1)}, u32[]{:S(2)}, u32[]{:S(2)}) collective-permute-start(f32[64,128]{1,0:T(8,128)S(1)} %add.77.part_ref), channel_id=1, source_target_pairs={{0,16},{4,20},{8,24},{12,28},{16,0},{20,4},{24,8},{28,12},{1,17},{... | collective-permute-start | bytes 98312 | tf_op jit(solution)/shard_map/ppermute | solution.py:38
  50.8 11.3 %collective-permute-start.15 = (f32[64,128]{1,0:T(8,128)S(1)}, f32[64,128]{1,0:T(8,128)S(1)}, u32[]{:S(2)}, u32[]{:S(2)}) collective-permute-start(f32[64,128]{1,0:T(8,128)S(1)} %add.80), channel_id=1, source_target_pairs={{0,16},{4,20},{8,24},{12,28},{16,0},{20,4},{24,8},{28,12},{1,17},{... | collective-permute-start | bytes 98312 | tf_op jit(solution)/shard_map/ppermute | solution.py:29
  53.7 0.6 copy-start.9
  62.2 0.8 %copy-start.2 = (f32[64,64]{1,0:T(8,128)S(1)}, f32[64,64]{1,0:T(8,128)}, u32[]{:S(2)}) copy-start(f32[64,64]{1,0:T(8,128)} %shard_map.18) | copy-start | bytes 49156
  62.9 0.8 %copy-start.6 = (f32[64,128]{1,0:T(8,128)S(1)}, f32[64,128]{1,0:T(8,128)}, u32[]{:S(2)}) copy-start(f32[64,128]{1,0:T(8,128)} %copy-done.5) | copy-start | bytes 98308
  62.9 0.8 %copy-start.10 = (f32[64,128]{1,0:T(8,128)S(1)}, f32[64,128]{1,0:T(8,128)}, u32[]{:S(2)}) copy-start(f32[64,128]{1,0:T(8,128)} %copy-done.9) | copy-start | bytes 98308

commit v18 on v12

--- a/solution.py
+++ b/solution.py
@@ -32,8 +32,8 @@
 
 def invert_near_identity(square):
     identity = jnp.eye(square.shape[0], dtype=jnp.float32)
-    approx = square.T * (2.0 / 4.25)
-    for _ in range(7):
+    approx = square.T * (2.0 / (0.25 + 4.84))
+    for _ in range(8):
         approx = apply_left(approx, 2.0 * identity - apply_left(square, approx))
     return approx
 

time: 67.7 us -> 68.2 us (level)
    dot_general x38 -> x42, matrix products: 7.99 us -> 8.63 us  [apply_left(): return jnp.dot(square, right_side, precision=HIGHEST_PRECISION)]
  transfers between devices with their start and end apart: 16 -> 16, of which waited for: 8 -> 8; matrix products, arithmetic and copies ran while one was open for 10% -> 11% of each run, Pallas kernels for 22% -> 21%
where the time goes in v18:
time: 68.2 us; the launch traced here: 67.8 us
  starting transfers between devices  28 us (41%)
  Pallas kernels  14.5 us (21%)
  matrix products  12.9 us (19%)
  waiting for transfers between devices  9.37 us (14%)
  other arithmetic  1.57 us (2%)
  local copies, waits for them, and re-layouts  0.91 us (1%)
    ppermute x12, starting transfers between devices, butterfly_sum(): x = x + lax.ppermute(x, axis, [(i, i ^ step) for i in range(size)])  20.4 us
    pallas_call x2, Pallas kernels, lower_inverse(): pl.pallas_call(_eliminate_kernel, out_shape=jax.ShapeDtypeStruct((size, s...  14.5 us
    dot_general x42, matrix products, apply_left(): return jnp.dot(square, right_side, precision=HIGHEST_PRECISION)  8.63 us
    ppermute x12, waiting for transfers between devices, butterfly_sum(): x = x + lax.ppermute(x, axis, [(i, i ^ step) for i in range(size)])  6.83 us
    ppermute x2, starting transfers between devices, from_root(): lax.ppermute(value, axis, [(i, i + dist) for i in range(size) if i % (2 *...  6.15 us
    dot_general x6, matrix products, inner_rows(): lax.dot_general(left, right, (((1,), (1,)), ((), ())), precision=HIGHEST_...  2.51 us
    ppermute x1, waiting for transfers between devices, spread_pair(): lax.ppermute(have, axis, [(i, i + dist) for i in range(size) if i % (2 *...  2.18 us
    dot_general x2, matrix products, local(): current = current - jnp.dot(mixed.T, reflect, precision=HIGHEST_PRECISION)  1.43 us
  transfers between devices with their start and end apart: 16, of which 8 were waited for; matrix products, arithmetic and copies ran while one was open for 11% of the time, Pallas kernels for 21%

profile of v18, /device:TPU:0, one launch (start us, length us, event | category | flops | bytes accessed | tf_op | source)
XLA Modules:
  0.0 67.8 jit_solution(4278638709580140040)
XLA Ops:
  0.0 0.9 %copy-done = f32[1,64,768]{2,1,0:T(8,128)S(1)} copy-done((f32[1,64,768]{2,1,0:T(8,128)S(1)}, f32[1,64,768]{2,1,0:T(8,128)}, u32[]{:S(2)}) %copy-start) | copy-done | bytes 196632
  0.9 0.5 convolution_bitcast_fusion
  1.5 4.9 %collective-permute-start = (f32[64,128]{1,0:T(8,128)S(1)}, f32[64,128]{1,0:T(8,128)S(1)}, u32[]{:S(2)}, u32[]{:S(2)}) collective-permute-start(f32[64,128]{1,0:T(8,128)S(1)} %convolution_bitcast_fusion), channel_id=1, source_target_pairs={{0,2},{4,6},{8,10},{12,14},{16,18},{20,22},{24,26},{28,30}} | collective-permute-start | bytes 98312 | tf_op jit(solution)/shard_map/ppermute | solution.py:86
  6.3 1.3 %collective-permute-start.5 = (f32[64,768]{1,0:T(8,128)S(1)}, f32[64,768]{1,0:T(8,128)S(1)}, u32[]{:S(2)}, u32[]{:S(2)}) collective-permute-start(f32[64,768]{1,0:T(8,128)S(1)} %bitcast.82), channel_id=1, source_target_pairs={{0,2},{1,3},{4,6},{5,7},{8,10},{9,11},{12,14},{13,15},{16,18},{17,... | collective-permute-start | bytes 589832 | tf_op jit(solution)/shard_map/ppermute | solution.py:72
  8.0 1.3 %collective-permute-start.1 = (f32[64,128]{1,0:T(8,128)S(1)}, f32[64,128]{1,0:T(8,128)S(1)}, u32[]{:S(2)}, u32[]{:S(2)}) collective-permute-start(f32[64,128]{1,0:T(8,128)S(1)} %broadcast_select_fusion.5), channel_id=1, source_target_pairs={{0,1},{2,3},{4,5},{6,7},{8,9},{10,11},{12,13},{14,15},{16,17},{18,... | collective-permute-start | bytes 98312 | tf_op jit(solution)/shard_map/ppermute | solution.py:86
  9.3 2.2 %collective-permute-done.5 = f32[64,768]{1,0:T(8,128)S(1)} collective-permute-done((f32[64,768]{1,0:T(8,128)S(1)}, f32[64,768]{1,0:T(8,128)S(1)}, u32[]{:S(2)}, u32[]{:S(2)}) %collective-permute-start.5) | collective-permute-done | bytes 196640 | tf_op jit(solution)/shard_map/ppermute | solution.py:72
  11.6 1.6 %collective-permute-start.2 = (f32[64,128]{1,0:T(8,128)S(1)}, f32[64,128]{1,0:T(8,128)S(1)}, u32[]{:S(2)}, u32[]{:S(2)}) collective-permute-start(f32[64,128]{1,0:T(8,128)S(1)} %broadcast_select_fusion.6), channel_id=1, source_target_pairs={{0,4},{4,0},{8,12},{12,8},{16,20},{20,16},{24,28},{28,24},{1,5},{5... | collective-permute-start | bytes 98312 | tf_op jit(solution)/shard_map/ppermute | solution.py:29
  13.2 2.4 %collective-permute-done.2 = f32[64,128]{1,0:T(8,128)S(1)} collective-permute-done((f32[64,128]{1,0:T(8,128)S(1)}, f32[64,128]{1,0:T(8,128)S(1)}, u32[]{:S(2)}, u32[]{:S(2)}) %collective-permute-start.2) | collective-permute-done | bytes 32800 | tf_op jit(solution)/shard_map/ppermute | solution.py:29
  15.6 1.6 %collective-permute-start.3 = (f32[64,128]{1,0:T(8,128)S(1)}, f32[64,128]{1,0:T(8,128)S(1)}, u32[]{:S(2)}, u32[]{:S(2)}) collective-permute-start(f32[64,128]{1,0:T(8,128)S(1)} %add.70), channel_id=1, source_target_pairs={{0,8},{4,12},{8,0},{12,4},{16,24},{20,28},{24,16},{28,20},{1,9},{5... | collective-permute-start | bytes 98312 | tf_op jit(solution)/shard_map/ppermute | solution.py:29
  17.6 0.5 fusion.8
  18.1 1.6 %collective-permute-start.7 = (f32[64,256]{1,0:T(8,128)S(1)}, f32[64,256]{1,0:T(8,128)S(1)}, u32[]{:S(2)}, u32[]{:S(2)}) collective-permute-start(f32[64,256]{1,0:T(8,128)S(1)} %pad_maximum_fusion.5), channel_id=1, source_target_pairs={{0,4},{4,0},{8,12},{12,8},{16,20},{20,16},{24,28},{28,24},{1,5},{5... | collective-permute-start | bytes 196616 | tf_op jit(solution)/shard_map/ppermute | solution.py:29
  19.7 2.7 %collective-permute-start.4 = (f32[64,128]{1,0:T(8,128)S(1)}, f32[64,128]{1,0:T(8,128)S(1)}, u32[]{:S(2)}, u32[]{:S(2)}) collective-permute-start(f32[64,128]{1,0:T(8,128)S(1)} %add.71), channel_id=1, source_target_pairs={{0,16},{4,20},{8,24},{12,28},{16,0},{20,4},{24,8},{28,12},{1,17},{... | collective-permute-start | bytes 98312 | tf_op jit(solution)/shard_map/ppermute | solution.py:29
  22.5 1.3 %collective-permute-start.8 = (f32[64,256]{1,0:T(8,128)S(1)}, f32[64,256]{1,0:T(8,128)S(1)}, u32[]{:S(2)}, u32[]{:S(2)}) collective-permute-start(f32[64,256]{1,0:T(8,128)S(1)} %fusion.49), channel_id=1, source_target_pairs={{0,8},{4,12},{8,0},{12,4},{16,24},{20,28},{24,16},{28,20},{1,9},{5... | collective-permute-start | bytes 196616 | tf_op jit(solution)/shard_map/ppermute | solution.py:29
  23.8 0.8 %collective-permute-done.4 = f32[64,128]{1,0:T(8,128)S(1)} collective-permute-done((f32[64,128]{1,0:T(8,128)S(1)}, f32[64,128]{1,0:T(8,128)S(1)}, u32[]{:S(2)}, u32[]{:S(2)}) %collective-permute-start.4) | collective-permute-done | bytes 32800 | tf_op jit(solution)/shard_map/ppermute | solution.py:29
  24.6 0.6 add.72.head_ref
  25.2 7.2 %shard_map.17 = f32[64,64]{1,0:T(8,128)} custom-call(f32[64,128]{1,0:T(8,128)} %add.72.head_ref), custom_call_target="tpu_custom_call" | custom-call | tf_op jit(solution)/shard_map/pallas_call | solution.py:62
  32.5 2.8 %collective-permute-start.9 = (f32[64,256]{1,0:T(8,128)S(1)}, f32[64,256]{1,0:T(8,128)S(1)}, u32[]{:S(2)}, u32[]{:S(2)}) collective-permute-start(f32[64,256]{1,0:T(8,128)S(1)} %add.74), channel_id=1, source_target_pairs={{0,16},{4,20},{8,24},{12,28},{16,0},{20,4},{24,8},{28,12},{1,17},{... | collective-permute-start | bytes 196616 | tf_op jit(solution)/shard_map/ppermute | solution.py:29
  40.2 0.4 fusion.1
  40.9 0.5 fusion.3
  41.5 1.2 %collective-permute-start.10 = (f32[64,128]{1,0:T(8,128)S(1)}, f32[64,128]{1,0:T(8,128)S(1)}, u32[]{:S(2)}, u32[]{:S(2)}) collective-permute-start(f32[64,128]{1,0:T(8,128)S(1)} %fusion.3), channel_id=1, source_target_pairs={{0,4},{4,0},{8,12},{12,8},{16,20},{20,16},{24,28},{28,24},{1,5},{5... | collective-permute-start | bytes 98312 | tf_op jit(solution)/shard_map/ppermute | solution.py:29
  42.7 0.9 %collective-permute-start.13 = (f32[64,128]{1,0:T(8,128)S(1)}, f32[64,128]{1,0:T(8,128)S(1)}, u32[]{:S(2)}, u32[]{:S(2)}) collective-permute-start(f32[64,128]{1,0:T(8,128)S(1)} %pad_maximum_fusion.6), channel_id=1, source_target_pairs={{0,4},{4,0},{8,12},{12,8},{16,20},{20,16},{24,28},{28,24},{1,5},{5... | collective-permute-start | bytes 98312 | tf_op jit(solution)/shard_map/ppermute | solution.py:29
  43.6 1.8 %collective-permute-done.10 = f32[64,128]{1,0:T(8,128)S(1)} collective-permute-done((f32[64,128]{1,0:T(8,128)S(1)}, f32[64,128]{1,0:T(8,128)S(1)}, u32[]{:S(2)}, u32[]{:S(2)}) %collective-permute-start.10) | collective-permute-done | bytes 32800 | tf_op jit(solution)/shard_map/ppermute | solution.py:29
  45.4 1.6 %collective-permute-start.11 = (f32[64,128]{1,0:T(8,128)S(1)}, f32[64,128]{1,0:T(8,128)S(1)}, u32[]{:S(2)}, u32[]{:S(2)}) collective-permute-start(f32[64,128]{1,0:T(8,128)S(1)} %add.76), channel_id=1, source_target_pairs={{0,8},{4,12},{8,0},{12,4},{16,24},{20,28},{24,16},{28,20},{1,9},{5... | collective-permute-start | bytes 98312 | tf_op jit(solution)/shard_map/ppermute | solution.py:29
  47.1 1.5 %collective-permute-start.14 = (f32[64,128]{1,0:T(8,128)S(1)}, f32[64,128]{1,0:T(8,128)S(1)}, u32[]{:S(2)}, u32[]{:S(2)}) collective-permute-start(f32[64,128]{1,0:T(8,128)S(1)} %fusion.131), channel_id=1, source_target_pairs={{0,8},{4,12},{8,0},{12,4},{16,24},{20,28},{24,16},{28,20},{1,9},{5... | collective-permute-start | bytes 98312 | tf_op jit(solution)/shard_map/ppermute | solution.py:29
  48.5 0.8 %collective-permute-done.11 = f32[64,128]{1,0:T(8,128)S(1)} collective-permute-done((f32[64,128]{1,0:T(8,128)S(1)}, f32[64,128]{1,0:T(8,128)S(1)}, u32[]{:S(2)}, u32[]{:S(2)}) %collective-permute-start.11) | collective-permute-done | bytes 32800 | tf_op jit(solution)/shard_map/ppermute | solution.py:29
  49.4 1.8 %collective-permute-start.12 = (f32[64,128]{1,0:T(8,128)S(1)}, f32[64,128]{1,0:T(8,128)S(1)}, u32[]{:S(2)}, u32[]{:S(2)}) collective-permute-start(f32[64,128]{1,0:T(8,128)S(1)} %add.77), channel_id=1, source_target_pairs={{0,16},{4,20},{8,24},{12,28},{16,0},{20,4},{24,8},{28,12},{1,17},{... | collective-permute-start | bytes 98312 | tf_op jit(solution)/shard_map/ppermute | solution.py:29
  51.2 2.1 %collective-permute-start.15 = (f32[64,128]{1,0:T(8,128)S(1)}, f32[64,128]{1,0:T(8,128)S(1)}, u32[]{:S(2)}, u32[]{:S(2)}) collective-permute-start(f32[64,128]{1,0:T(8,128)S(1)} %add.80), channel_id=1, source_target_pairs={{0,16},{4,20},{8,24},{12,28},{16,0},{20,4},{24,8},{28,12},{1,17},{... | collective-permute-start | bytes 98312 | tf_op jit(solution)/shard_map/ppermute | solution.py:29
  53.3 0.9 %collective-permute-done.12 = f32[64,128]{1,0:T(8,128)S(1)} collective-permute-done((f32[64,128]{1,0:T(8,128)S(1)}, f32[64,128]{1,0:T(8,128)S(1)}, u32[]{:S(2)}, u32[]{:S(2)}) %collective-permute-start.12) | collective-permute-done | bytes 32800 | tf_op jit(solution)/shard_map/ppermute | solution.py:29
  54.2 0.6 add.78.head_ref
  54.8 7.2 %shard_map.18 = f32[64,64]{1,0:T(8,128)} custom-call(f32[64,128]{1,0:T(8,128)} %add.78.head_ref), custom_call_target="tpu_custom_call" | custom-call | tf_op jit(solution)/shard_map/pallas_call | solution.py:62
  62.0 1.1 %convolution_subtract_fusion.1 = f32[64,768]{1,0:T(8,128)S(1)} fusion(f32[64,64]{1,0:T(8,128)} %shard_map.18, f32[64,768]{1,0:T(8,128)S(1)} %fusion.1, s32[768]{0:T(1024)S(1)} %fusion.39), kind=kOutput, calls=%fused_computation.2 | convolution fusion | flops 37896192 | bytes 412672 | tf_op jit(solution)/shard_map/dot_general | solution.py:15
  66.8 1.1 %fusion = f32[1,64,768]{2,1,0:T(8,128)} fusion(f32[64,768]{1,0:T(8,128)S(1)} %convolution_subtract_fusion.3, f32[64,64]{1,0:T(8,128)S(1)} %fusion.18, f32[64,768]{1,0:T(8,128)S(1)} %convolution_subtract_fusion.1), kind=kOutput, calls=%fused_computation.1 | convolution fusion | flops 37797888 | bytes 606208 | tf_op jit(solution)/shard_map/dot_general | solution.py:151
  (86 shorter events, 9.7 us)
Async XLA Ops:
  0.0 0.9 %copy-start = (f32[1,64,768]{2,1,0:T(8,128)S(1)}, f32[1,64,768]{2,1,0:T(8,128)}, u32[]{:S(2)}) copy-start(f32[1,64,768]{2,1,0:T(8,128)} %param.1) | copy-start | bytes 589828
  1.5 6.6 %collective-permute-start = (f32[64,128]{1,0:T(8,128)S(1)}, f32[64,128]{1,0:T(8,128)S(1)}, u32[]{:S(2)}, u32[]{:S(2)}) collective-permute-start(f32[64,128]{1,0:T(8,128)S(1)} %convolution_bitcast_fusion), channel_id=1, source_target_pairs={{0,2},{4,6},{8,10},{12,14},{16,18},{20,22},{24,26},{28,30}} | collective-permute-start | bytes 98312 | tf_op jit(solution)/shard_map/ppermute | solution.py:86
  6.3 5.2 %collective-permute-start.5 = (f32[64,768]{1,0:T(8,128)S(1)}, f32[64,768]{1,0:T(8,128)S(1)}, u32[]{:S(2)}, u32[]{:S(2)}) collective-permute-start(f32[64,768]{1,0:T(8,128)S(1)} %bitcast.82), channel_id=1, source_target_pairs={{0,2},{1,3},{4,6},{5,7},{8,10},{9,11},{12,14},{13,15},{16,18},{17,... | collective-permute-start | bytes 589832 | tf_op jit(solution)/shard_map/ppermute | solution.py:72
  8.0 3.6 %collective-permute-start.1 = (f32[64,128]{1,0:T(8,128)S(1)}, f32[64,128]{1,0:T(8,128)S(1)}, u32[]{:S(2)}, u32[]{:S(2)}) collective-permute-start(f32[64,128]{1,0:T(8,128)S(1)} %broadcast_select_fusion.5), channel_id=1, source_target_pairs={{0,1},{2,3},{4,5},{6,7},{8,9},{10,11},{12,13},{14,15},{16,17},{18,... | collective-permute-start | bytes 98312 | tf_op jit(solution)/shard_map/ppermute | solution.py:86
  11.5 5.7 %collective-permute-start.6 = (f32[64,768]{1,0:T(8,128)S(1)}, f32[64,768]{1,0:T(8,128)S(1)}, u32[]{:S(2)}, u32[]{:S(2)}) collective-permute-start(f32[64,768]{1,0:T(8,128)S(1)} %broadcast_select_fusion), channel_id=1, source_target_pairs={{0,1},{1,0},{2,3},{3,2},{4,5},{5,4},{6,7},{7,6},{8,9},{9,8},{10,11... | collective-permute-start | bytes 589832 | tf_op jit(solution)/shard_map/ppermute | solution.py:77
  11.6 4.0 %collective-permute-start.2 = (f32[64,128]{1,0:T(8,128)S(1)}, f32[64,128]{1,0:T(8,128)S(1)}, u32[]{:S(2)}, u32[]{:S(2)}) collective-permute-start(f32[64,128]{1,0:T(8,128)S(1)} %broadcast_select_fusion.6), channel_id=1, source_target_pairs={{0,4},{4,0},{8,12},{12,8},{16,20},{20,16},{24,28},{28,24},{1,5},{5... | collective-permute-start | bytes 98312 | tf_op jit(solution)/shard_map/ppermute | solution.py:29
  15.6 4.1 %collective-permute-start.3 = (f32[64,128]{1,0:T(8,128)S(1)}, f32[64,128]{1,0:T(8,128)S(1)}, u32[]{:S(2)}, u32[]{:S(2)}) collective-permute-start(f32[64,128]{1,0:T(8,128)S(1)} %add.70), channel_id=1, source_target_pairs={{0,8},{4,12},{8,0},{12,4},{16,24},{20,28},{24,16},{28,20},{1,9},{5... | collective-permute-start | bytes 98312 | tf_op jit(solution)/shard_map/ppermute | solution.py:29
  18.1 4.3 %collective-permute-start.7 = (f32[64,256]{1,0:T(8,128)S(1)}, f32[64,256]{1,0:T(8,128)S(1)}, u32[]{:S(2)}, u32[]{:S(2)}) collective-permute-start(f32[64,256]{1,0:T(8,128)S(1)} %pad_maximum_fusion.5), channel_id=1, source_target_pairs={{0,4},{4,0},{8,12},{12,8},{16,20},{20,16},{24,28},{28,24},{1,5},{5... | collective-permute-start | bytes 196616 | tf_op jit(solution)/shard_map/ppermute | solution.py:29
  19.7 4.9 %collective-permute-start.4 = (f32[64,128]{1,0:T(8,128)S(1)}, f32[64,128]{1,0:T(8,128)S(1)}, u32[]{:S(2)}, u32[]{:S(2)}) collective-permute-start(f32[64,128]{1,0:T(8,128)S(1)} %add.71), channel_id=1, source_target_pairs={{0,16},{4,20},{8,24},{12,28},{16,0},{20,4},{24,8},{28,12},{1,17},{... | collective-permute-start | bytes 98312 | tf_op jit(solution)/shard_map/ppermute | solution.py:29
  22.5 10.0 %collective-permute-start.8 = (f32[64,256]{1,0:T(8,128)S(1)}, f32[64,256]{1,0:T(8,128)S(1)}, u32[]{:S(2)}, u32[]{:S(2)}) collective-permute-start(f32[64,256]{1,0:T(8,128)S(1)} %fusion.49), channel_id=1, source_target_pairs={{0,8},{4,12},{8,0},{12,4},{16,24},{20,28},{24,16},{28,20},{1,9},{5... | collective-permute-start | bytes 196616 | tf_op jit(solution)/shard_map/ppermute | solution.py:29
  32.5 2.8 %copy-start.1 = (f32[64,64]{1,0:T(8,128)S(1)}, f32[64,64]{1,0:T(8,128)}, u32[]{:S(2)}) copy-start(f32[64,64]{1,0:T(8,128)} %shard_map.17) | copy-start | bytes 49156
  32.5 2.8 %copy-start.3 = (f32[64,128]{1,0:T(8,128)S(1)}, f32[64,128]{1,0:T(8,128)}, u32[]{:S(2)}) copy-start(f32[64,128]{1,0:T(8,128)} %add.72.head_ref) | copy-start | bytes 98308
  32.5 6.2 %collective-permute-start.9 = (f32[64,256]{1,0:T(8,128)S(1)}, f32[64,256]{1,0:T(8,128)S(1)}, u32[]{:S(2)}, u32[]{:S(2)}) collective-permute-start(f32[64,256]{1,0:T(8,128)S(1)} %add.74), channel_id=1, source_target_pairs={{0,16},{4,20},{8,24},{12,28},{16,0},{20,4},{24,8},{28,12},{1,17},{... | collective-permute-start | bytes 196616 | tf_op jit(solution)/shard_map/ppermute | solution.py:29
  41.5 4.0 %collective-permute-start.10 = (f32[64,128]{1,0:T(8,128)S(1)}, f32[64,128]{1,0:T(8,128)S(1)}, u32[]{:S(2)}, u32[]{:S(2)}) collective-permute-start(f32[64,128]{1,0:T(8,128)S(1)} %fusion.3), channel_id=1, source_target_pairs={{0,4},{4,0},{8,12},{12,8},{16,20},{20,16},{24,28},{28,24},{1,5},{5... | collective-permute-start | bytes 98312 | tf_op jit(solution)/shard_map/ppermute | solution.py:29
  42.7 4.3 %collective-permute-start.13 = (f32[64,128]{1,0:T(8,128)S(1)}, f32[64,128]{1,0:T(8,128)S(1)}, u32[]{:S(2)}, u32[]{:S(2)}) collective-permute-start(f32[64,128]{1,0:T(8,128)S(1)} %pad_maximum_fusion.6), channel_id=1, source_target_pairs={{0,4},{4,0},{8,12},{12,8},{16,20},{20,16},{24,28},{28,24},{1,5},{5... | collective-permute-start | bytes 98312 | tf_op jit(solution)/shard_map/ppermute | solution.py:29
  45.4 3.9 %collective-permute-start.11 = (f32[64,128]{1,0:T(8,128)S(1)}, f32[64,128]{1,0:T(8,128)S(1)}, u32[]{:S(2)}, u32[]{:S(2)}) collective-permute-start(f32[64,128]{1,0:T(8,128)S(1)} %add.76), channel_id=1, source_target_pairs={{0,8},{4,12},{8,0},{12,4},{16,24},{20,28},{24,16},{28,20},{1,9},{5... | collective-permute-start | bytes 98312 | tf_op jit(solution)/shard_map/ppermute | solution.py:29
  47.1 4.1 %collective-permute-start.14 = (f32[64,128]{1,0:T(8,128)S(1)}, f32[64,128]{1,0:T(8,128)S(1)}, u32[]{:S(2)}, u32[]{:S(2)}) collective-permute-start(f32[64,128]{1,0:T(8,128)S(1)} %fusion.131), channel_id=1, source_target_pairs={{0,8},{4,12},{8,0},{12,4},{16,24},{20,28},{24,16},{28,20},{1,9},{5... | collective-permute-start | bytes 98312 | tf_op jit(solution)/shard_map/ppermute | solution.py:29
  49.4 4.8 %collective-permute-start.12 = (f32[64,128]{1,0:T(8,128)S(1)}, f32[64,128]{1,0:T(8,128)S(1)}, u32[]{:S(2)}, u32[]{:S(2)}) collective-permute-start(f32[64,128]{1,0:T(8,128)S(1)} %add.77), channel_id=1, source_target_pairs={{0,16},{4,20},{8,24},{12,28},{16,0},{20,4},{24,8},{28,12},{1,17},{... | collective-permute-start | bytes 98312 | tf_op jit(solution)/shard_map/ppermute | solution.py:29
  51.2 12.3 %collective-permute-start.15 = (f32[64,128]{1,0:T(8,128)S(1)}, f32[64,128]{1,0:T(8,128)S(1)}, u32[]{:S(2)}, u32[]{:S(2)}) collective-permute-start(f32[64,128]{1,0:T(8,128)S(1)} %add.80), channel_id=1, source_target_pairs={{0,16},{4,20},{8,24},{12,28},{16,0},{20,4},{24,8},{28,12},{1,17},{... | collective-permute-start | bytes 98312 | tf_op jit(solution)/shard_map/ppermute | solution.py:29
  62.0 1.1 %copy-start.2 = (f32[64,64]{1,0:T(8,128)S(1)}, f32[64,64]{1,0:T(8,128)}, u32[]{:S(2)}) copy-start(f32[64,64]{1,0:T(8,128)} %shard_map.18) | copy-start | bytes 49156
  62.0 1.2 %copy-start.4 = (f32[64,128]{1,0:T(8,128)S(1)}, f32[64,128]{1,0:T(8,128)}, u32[]{:S(2)}) copy-start(f32[64,128]{1,0:T(8,128)} %add.78.head_ref) | copy-start | bytes 98308

commit v19 on v18

--- a/solution.py
+++ b/solution.py
@@ -50,7 +50,6 @@
         row = work[j:j + 1, :]
         pivot = row[:, j:j + 1]
         scale = lax.rsqrt(pivot)
-        scale = scale * (1.5 - 0.5 * pivot * scale * scale)
         scaled = row * scale
         weight = jnp.where(row_ids > j, work[:, j:j + 1] * scale, 0.0)
         work = jnp.where(rows == j, scaled, work - weight * scaled)
@@ -64,7 +63,7 @@
     )(head)
 
 
-def spread_pair(block, axis, size):
+def spread_pair(block, axis, size, hold=None):
     index = lax.axis_index(axis)
     have = block
     dist = size // 2
@@ -74,9 +73,11 @@
         )
         have = jnp.where(index % (2 * dist) >= dist, got, have)
         dist //= 2
+    if hold is not None:
+        have, hold = lax.optimization_barrier((have, hold))
     other = lax.ppermute(have, axis, [(i, i ^ 1) for i in range(size)])
     even = index % 2 == 0
-    return jnp.where(even, have, other), jnp.where(even, other, have)
+    return jnp.where(even, have, other), jnp.where(even, other, have), hold
 
 
 def from_root(value, axis, size):
@@ -111,8 +112,11 @@
             )
         else:
             head = inner_rows(current, jnp.concatenate([current, units[0]]))
-            head = butterfly_sum(from_root(head, "cols", cols_size), "rows", rows_size)
-            panel_0, second = spread_pair(current, "cols", cols_size)
+            head = from_root(head, "cols", cols_size)
+            steps = butterfly_steps(rows_size)
+            head = butterfly_sum(head, "rows", rows_size, None if steps is None else steps[:1])
+            panel_0, second, head = spread_pair(current, "cols", cols_size, head)
+            head = butterfly_sum(head, "rows", rows_size, [] if steps is None else steps[1:])
 
         both = jnp.concatenate([current, second])
         tail = jnp.concatenate([inner_rows(panel_0, both), inner_rows(units[0], both)], axis=1)

time: 68.2 us -> 69.9 us (1.025)
  starting transfers between devices: 28 us -> 30.7 us
  Pallas kernels: 14.5 us -> 13.6 us
    ppermute x1, starting transfers between devices: 1.3 us -> 4.23 us  [spread_pair(): lax.ppermute(have, axis, [(i, i + dist) for i in range(size) if i % (2 *...]
    ppermute x1, waiting for transfers between devices: 2.18 us -> 0.01 us  [spread_pair(): lax.ppermute(have, axis, [(i, i + dist) for i in range(size) if i % (2 *...]
    ppermute x2, waiting for transfers between devices: 0.35 us -> 1.57 us  [from_root(): lax.ppermute(value, axis, [(i, i + dist) for i in range(size) if i % (2 *...]
    pallas_call x2, Pallas kernels: 14.5 us -> 13.6 us  [lower_inverse(): pl.pallas_call(_eliminate_kernel, out_shape=jax.ShapeDtypeStruct((size, s...]
    ppermute x12, waiting for transfers between devices: 6.83 us -> 7.67 us  [butterfly_sum(): x = x + lax.ppermute(x, axis, [(i, i ^ step) for i in range(size)])]
  transfers between devices with their start and end apart: 16 -> 16, of which waited for: 8 -> 7; matrix products, arithmetic and copies ran while one was open for 11% -> 10% of each run, Pallas kernels for 21% -> 20%
where the time goes in v19:
time: 69.9 us; the launch traced here: 69.5 us
  starting transfers between devices  30.7 us (44%)
  Pallas kernels  13.6 us (19%)
  matrix products  12.9 us (18%)
  waiting for transfers between devices  9.24 us (13%)
  other arithmetic  1.58 us (2%)
  local copies, waits for them, and re-layouts  0.91 us (1%)
    ppermute x12, starting transfers between devices, butterfly_sum(): x = x + lax.ppermute(x, axis, [(i, i ^ step) for i in range(size)])  20.2 us
    pallas_call x2, Pallas kernels, lower_inverse(): pl.pallas_call(_eliminate_kernel, out_shape=jax.ShapeDtypeStruct((size, s...  13.6 us
    dot_general x42, matrix products, apply_left(): return jnp.dot(square, right_side, precision=HIGHEST_PRECISION)  8.63 us
    ppermute x12, waiting for transfers between devices, butterfly_sum(): x = x + lax.ppermute(x, axis, [(i, i ^ step) for i in range(size)])  7.67 us
    ppermute x2, starting transfers between devices, from_root(): lax.ppermute(value, axis, [(i, i + dist) for i in range(size) if i % (2 *...  6.15 us
    ppermute x1, starting transfers between devices, spread_pair(): lax.ppermute(have, axis, [(i, i + dist) for i in range(size) if i % (2 *...  4.23 us
    dot_general x6, matrix products, inner_rows(): lax.dot_general(left, right, (((1,), (1,)), ((), ())), precision=HIGHEST_...  2.51 us
    ppermute x2, waiting for transfers between devices, from_root(): lax.ppermute(value, axis, [(i, i + dist) for i in range(size) if i % (2 *...  1.57 us
  transfers between devices with their start and end apart: 16, of which 7 were waited for; matrix products, arithmetic and copies ran while one was open for 10% of the time, Pallas kernels for 20%

profile of v19, /device:TPU:0, one launch (start us, length us, event | category | flops | bytes accessed | tf_op | source)
XLA Modules:
  0.0 69.5 jit_solution(12561367762573869334)
XLA Ops:
  0.0 0.9 %copy-done = f32[1,64,768]{2,1,0:T(8,128)S(1)} copy-done((f32[1,64,768]{2,1,0:T(8,128)S(1)}, f32[1,64,768]{2,1,0:T(8,128)}, u32[]{:S(2)}) %copy-start) | copy-done | bytes 196632
  0.9 0.5 convolution_bitcast_fusion
  1.5 4.9 %collective-permute-start.1 = (f32[64,128]{1,0:T(8,128)S(1)}, f32[64,128]{1,0:T(8,128)S(1)}, u32[]{:S(2)}, u32[]{:S(2)}) collective-permute-start(f32[64,128]{1,0:T(8,128)S(1)} %convolution_bitcast_fusion), channel_id=1, source_target_pairs={{0,2},{4,6},{8,10},{12,14},{16,18},{20,22},{24,26},{28,30}} | collective-permute-start | bytes 98312 | tf_op jit(solution)/shard_map/ppermute | solution.py:87
  6.4 1.6 %collective-permute-done.1 = f32[64,128]{1,0:T(8,128)S(1)} collective-permute-done((f32[64,128]{1,0:T(8,128)S(1)}, f32[64,128]{1,0:T(8,128)S(1)}, u32[]{:S(2)}, u32[]{:S(2)}) %collective-permute-start.1) | collective-permute-done | bytes 32800 | tf_op jit(solution)/shard_map/ppermute | solution.py:87
  7.9 1.3 %collective-permute-start.2 = (f32[64,128]{1,0:T(8,128)S(1)}, f32[64,128]{1,0:T(8,128)S(1)}, u32[]{:S(2)}, u32[]{:S(2)}) collective-permute-start(f32[64,128]{1,0:T(8,128)S(1)} %broadcast_select_fusion.5), channel_id=1, source_target_pairs={{0,1},{2,3},{4,5},{6,7},{8,9},{10,11},{12,13},{14,15},{16,17},{18,... | collective-permute-start | bytes 98312 | tf_op jit(solution)/shard_map/ppermute | solution.py:87
  9.2 4.2 %collective-permute-start = (f32[64,768]{1,0:T(8,128)S(1)}, f32[64,768]{1,0:T(8,128)S(1)}, u32[]{:S(2)}, u32[]{:S(2)}) collective-permute-start(f32[64,768]{1,0:T(8,128)S(1)} %bitcast.82), channel_id=1, source_target_pairs={{0,2},{1,3},{4,6},{5,7},{8,10},{9,11},{12,14},{13,15},{16,18},{17,... | collective-permute-start | bytes 589832 | tf_op jit(solution)/shard_map/ppermute | solution.py:71
  13.5 1.6 %collective-permute-start.3 = (f32[64,128]{1,0:T(8,128)S(1)}, f32[64,128]{1,0:T(8,128)S(1)}, u32[]{:S(2)}, u32[]{:S(2)}) collective-permute-start(f32[64,128]{1,0:T(8,128)S(1)} %broadcast_select_fusion.6), channel_id=1, source_target_pairs={{0,4},{4,0},{8,12},{12,8},{16,20},{20,16},{24,28},{28,24},{1,5},{5... | collective-permute-start | bytes 98312 | tf_op jit(solution)/shard_map/ppermute | solution.py:29
  15.0 2.4 %collective-permute-done.3 = f32[64,128]{1,0:T(8,128)S(1)} collective-permute-done((f32[64,128]{1,0:T(8,128)S(1)}, f32[64,128]{1,0:T(8,128)S(1)}, u32[]{:S(2)}, u32[]{:S(2)}) %collective-permute-start.3) | collective-permute-done | bytes 32800 | tf_op jit(solution)/shard_map/ppermute | solution.py:29
  17.6 1.6 %collective-permute-start.4 = (f32[64,128]{1,0:T(8,128)S(1)}, f32[64,128]{1,0:T(8,128)S(1)}, u32[]{:S(2)}, u32[]{:S(2)}) collective-permute-start(f32[64,128]{1,0:T(8,128)S(1)} %add.70), channel_id=1, source_target_pairs={{0,8},{4,12},{8,0},{12,4},{16,24},{20,28},{24,16},{28,20},{1,9},{5... | collective-permute-start | bytes 98312 | tf_op jit(solution)/shard_map/ppermute | solution.py:29
  19.6 0.5 fusion.8
  20.2 1.6 %collective-permute-start.7 = (f32[64,256]{1,0:T(8,128)S(1)}, f32[64,256]{1,0:T(8,128)S(1)}, u32[]{:S(2)}, u32[]{:S(2)}) collective-permute-start(f32[64,256]{1,0:T(8,128)S(1)} %pad_maximum_fusion.5), channel_id=1, source_target_pairs={{0,4},{4,0},{8,12},{12,8},{16,20},{20,16},{24,28},{28,24},{1,5},{5... | collective-permute-start | bytes 196616 | tf_op jit(solution)/shard_map/ppermute | solution.py:29
  21.8 2.6 %collective-permute-start.5 = (f32[64,128]{1,0:T(8,128)S(1)}, f32[64,128]{1,0:T(8,128)S(1)}, u32[]{:S(2)}, u32[]{:S(2)}) collective-permute-start(f32[64,128]{1,0:T(8,128)S(1)} %add.71), channel_id=1, source_target_pairs={{0,16},{4,20},{8,24},{12,28},{16,0},{20,4},{24,8},{28,12},{1,17},{... | collective-permute-start | bytes 98312 | tf_op jit(solution)/shard_map/ppermute | solution.py:29
  24.5 1.4 %collective-permute-start.8 = (f32[64,256]{1,0:T(8,128)S(1)}, f32[64,256]{1,0:T(8,128)S(1)}, u32[]{:S(2)}, u32[]{:S(2)}) collective-permute-start(f32[64,256]{1,0:T(8,128)S(1)} %fusion.49), channel_id=1, source_target_pairs={{0,8},{4,12},{8,0},{12,4},{16,24},{20,28},{24,16},{28,20},{1,9},{5... | collective-permute-start | bytes 196616 | tf_op jit(solution)/shard_map/ppermute | solution.py:29
  25.9 0.7 %collective-permute-done.5 = f32[64,128]{1,0:T(8,128)S(1)} collective-permute-done((f32[64,128]{1,0:T(8,128)S(1)}, f32[64,128]{1,0:T(8,128)S(1)}, u32[]{:S(2)}, u32[]{:S(2)}) %collective-permute-start.5) | collective-permute-done | bytes 32800 | tf_op jit(solution)/shard_map/ppermute | solution.py:29
  26.7 0.6 add.72.head_ref
  27.3 6.8 %shard_map.17 = f32[64,64]{1,0:T(8,128)} custom-call(f32[64,128]{1,0:T(8,128)} %add.72.head_ref), custom_call_target="tpu_custom_call" | custom-call | tf_op jit(solution)/shard_map/pallas_call | solution.py:61
  34.1 2.9 %collective-permute-start.9 = (f32[64,256]{1,0:T(8,128)S(1)}, f32[64,256]{1,0:T(8,128)S(1)}, u32[]{:S(2)}, u32[]{:S(2)}) collective-permute-start(f32[64,256]{1,0:T(8,128)S(1)} %add.74), channel_id=1, source_target_pairs={{0,16},{4,20},{8,24},{12,28},{16,0},{20,4},{24,8},{28,12},{1,17},{... | collective-permute-start | bytes 196616 | tf_op jit(solution)/shard_map/ppermute | solution.py:29
  42.0 0.4 fusion.1
  42.7 0.5 fusion.3
  43.3 1.3 %collective-permute-start.10 = (f32[64,128]{1,0:T(8,128)S(1)}, f32[64,128]{1,0:T(8,128)S(1)}, u32[]{:S(2)}, u32[]{:S(2)}) collective-permute-start(f32[64,128]{1,0:T(8,128)S(1)} %fusion.3), channel_id=1, source_target_pairs={{0,4},{4,0},{8,12},{12,8},{16,20},{20,16},{24,28},{28,24},{1,5},{5... | collective-permute-start | bytes 98312 | tf_op jit(solution)/shard_map/ppermute | solution.py:29
  44.7 0.8 %collective-permute-start.13 = (f32[64,128]{1,0:T(8,128)S(1)}, f32[64,128]{1,0:T(8,128)S(1)}, u32[]{:S(2)}, u32[]{:S(2)}) collective-permute-start(f32[64,128]{1,0:T(8,128)S(1)} %pad_maximum_fusion.6), channel_id=1, source_target_pairs={{0,4},{4,0},{8,12},{12,8},{16,20},{20,16},{24,28},{28,24},{1,5},{5... | collective-permute-start | bytes 98312 | tf_op jit(solution)/shard_map/ppermute | solution.py:29
  45.4 1.8 %collective-permute-done.10 = f32[64,128]{1,0:T(8,128)S(1)} collective-permute-done((f32[64,128]{1,0:T(8,128)S(1)}, f32[64,128]{1,0:T(8,128)S(1)}, u32[]{:S(2)}, u32[]{:S(2)}) %collective-permute-start.10) | collective-permute-done | bytes 32800 | tf_op jit(solution)/shard_map/ppermute | solution.py:29
  47.2 1.3 %collective-permute-start.11 = (f32[64,128]{1,0:T(8,128)S(1)}, f32[64,128]{1,0:T(8,128)S(1)}, u32[]{:S(2)}, u32[]{:S(2)}) collective-permute-start(f32[64,128]{1,0:T(8,128)S(1)} %add.76), channel_id=1, source_target_pairs={{0,8},{4,12},{8,0},{12,4},{16,24},{20,28},{24,16},{28,20},{1,9},{5... | collective-permute-start | bytes 98312 | tf_op jit(solution)/shard_map/ppermute | solution.py:29
  48.7 1.6 %collective-permute-start.14 = (f32[64,128]{1,0:T(8,128)S(1)}, f32[64,128]{1,0:T(8,128)S(1)}, u32[]{:S(2)}, u32[]{:S(2)}) collective-permute-start(f32[64,128]{1,0:T(8,128)S(1)} %fusion.131), channel_id=1, source_target_pairs={{0,8},{4,12},{8,0},{12,4},{16,24},{20,28},{24,16},{28,20},{1,9},{5... | collective-permute-start | bytes 98312 | tf_op jit(solution)/shard_map/ppermute | solution.py:29
  50.3 1.2 %collective-permute-done.11 = f32[64,128]{1,0:T(8,128)S(1)} collective-permute-done((f32[64,128]{1,0:T(8,128)S(1)}, f32[64,128]{1,0:T(8,128)S(1)}, u32[]{:S(2)}, u32[]{:S(2)}) %collective-permute-start.11) | collective-permute-done | bytes 32800 | tf_op jit(solution)/shard_map/ppermute | solution.py:29
  51.5 1.4 %collective-permute-start.12 = (f32[64,128]{1,0:T(8,128)S(1)}, f32[64,128]{1,0:T(8,128)S(1)}, u32[]{:S(2)}, u32[]{:S(2)}) collective-permute-start(f32[64,128]{1,0:T(8,128)S(1)} %add.77), channel_id=1, source_target_pairs={{0,16},{4,20},{8,24},{12,28},{16,0},{20,4},{24,8},{28,12},{1,17},{... | collective-permute-start | bytes 98312 | tf_op jit(solution)/shard_map/ppermute | solution.py:29
  53.0 2.0 %collective-permute-start.15 = (f32[64,128]{1,0:T(8,128)S(1)}, f32[64,128]{1,0:T(8,128)S(1)}, u32[]{:S(2)}, u32[]{:S(2)}) collective-permute-start(f32[64,128]{1,0:T(8,128)S(1)} %add.80), channel_id=1, source_target_pairs={{0,16},{4,20},{8,24},{12,28},{16,0},{20,4},{24,8},{28,12},{1,17},{... | collective-permute-start | bytes 98312 | tf_op jit(solution)/shard_map/ppermute | solution.py:29
  55.0 1.4 %collective-permute-done.12 = f32[64,128]{1,0:T(8,128)S(1)} collective-permute-done((f32[64,128]{1,0:T(8,128)S(1)}, f32[64,128]{1,0:T(8,128)S(1)}, u32[]{:S(2)}, u32[]{:S(2)}) %collective-permute-start.12) | collective-permute-done | bytes 32800 | tf_op jit(solution)/shard_map/ppermute | solution.py:29
  56.3 0.6 add.78.head_ref
  56.9 6.8 %shard_map.18 = f32[64,64]{1,0:T(8,128)} custom-call(f32[64,128]{1,0:T(8,128)} %add.78.head_ref), custom_call_target="tpu_custom_call" | custom-call | tf_op jit(solution)/shard_map/pallas_call | solution.py:61
  63.7 1.1 %convolution_subtract_fusion.1 = f32[64,768]{1,0:T(8,128)S(1)} fusion(f32[64,64]{1,0:T(8,128)} %shard_map.18, f32[64,768]{1,0:T(8,128)S(1)} %fusion.1, s32[768]{0:T(1024)S(1)} %fusion.39), kind=kOutput, calls=%fused_computation.2 | convolution fusion | flops 37896192 | bytes 412672 | tf_op jit(solution)/shard_map/dot_general | solution.py:15
  68.5 1.1 %fusion = f32[1,64,768]{2,1,0:T(8,128)} fusion(f32[64,768]{1,0:T(8,128)S(1)} %convolution_subtract_fusion.3, f32[64,64]{1,0:T(8,128)S(1)} %fusion.18, f32[64,768]{1,0:T(8,128)S(1)} %convolution_subtract_fusion.1), kind=kOutput, calls=%fused_computation.1 | convolution fusion | flops 37797888 | bytes 606208 | tf_op jit(solution)/shard_map/dot_general | solution.py:155
  (86 shorter events, 9.3 us)
Async XLA Ops:
  0.0 0.9 %copy-start = (f32[1,64,768]{2,1,0:T(8,128)S(1)}, f32[1,64,768]{2,1,0:T(8,128)}, u32[]{:S(2)}) copy-start(f32[1,64,768]{2,1,0:T(8,128)} %param.1) | copy-start | bytes 589828
  1.5 6.5 %collective-permute-start.1 = (f32[64,128]{1,0:T(8,128)S(1)}, f32[64,128]{1,0:T(8,128)S(1)}, u32[]{:S(2)}, u32[]{:S(2)}) collective-permute-start(f32[64,128]{1,0:T(8,128)S(1)} %convolution_bitcast_fusion), channel_id=1, source_target_pairs={{0,2},{4,6},{8,10},{12,14},{16,18},{20,22},{24,26},{28,30}} | collective-permute-start | bytes 98312 | tf_op jit(solution)/shard_map/ppermute | solution.py:87
  7.9 5.5 %collective-permute-start.2 = (f32[64,128]{1,0:T(8,128)S(1)}, f32[64,128]{1,0:T(8,128)S(1)}, u32[]{:S(2)}, u32[]{:S(2)}) collective-permute-start(f32[64,128]{1,0:T(8,128)S(1)} %broadcast_select_fusion.5), channel_id=1, source_target_pairs={{0,1},{2,3},{4,5},{6,7},{8,9},{10,11},{12,13},{14,15},{16,17},{18,... | collective-permute-start | bytes 98312 | tf_op jit(solution)/shard_map/ppermute | solution.py:87
  9.2 8.3 %collective-permute-start = (f32[64,768]{1,0:T(8,128)S(1)}, f32[64,768]{1,0:T(8,128)S(1)}, u32[]{:S(2)}, u32[]{:S(2)}) collective-permute-start(f32[64,768]{1,0:T(8,128)S(1)} %bitcast.82), channel_id=1, source_target_pairs={{0,2},{1,3},{4,6},{5,7},{8,10},{9,11},{12,14},{13,15},{16,18},{17,... | collective-permute-start | bytes 589832 | tf_op jit(solution)/shard_map/ppermute | solution.py:71
  13.5 4.0 %collective-permute-start.3 = (f32[64,128]{1,0:T(8,128)S(1)}, f32[64,128]{1,0:T(8,128)S(1)}, u32[]{:S(2)}, u32[]{:S(2)}) collective-permute-start(f32[64,128]{1,0:T(8,128)S(1)} %broadcast_select_fusion.6), channel_id=1, source_target_pairs={{0,4},{4,0},{8,12},{12,8},{16,20},{20,16},{24,28},{28,24},{1,5},{5... | collective-permute-start | bytes 98312 | tf_op jit(solution)/shard_map/ppermute | solution.py:29
  17.5 1.7 %collective-permute-start.6 = (f32[64,768]{1,0:T(8,128)S(1)}, f32[64,768]{1,0:T(8,128)S(1)}, u32[]{:S(2)}, u32[]{:S(2)}) collective-permute-start(f32[64,768]{1,0:T(8,128)S(1)} %broadcast_select_fusion.2), channel_id=1, source_target_pairs={{0,1},{1,0},{2,3},{3,2},{4,5},{5,4},{6,7},{7,6},{8,9},{9,8},{10,11... | collective-permute-start | bytes 589832 | tf_op jit(solution)/shard_map/ppermute | solution.py:78
  17.6 4.2 %collective-permute-start.4 = (f32[64,128]{1,0:T(8,128)S(1)}, f32[64,128]{1,0:T(8,128)S(1)}, u32[]{:S(2)}, u32[]{:S(2)}) collective-permute-start(f32[64,128]{1,0:T(8,128)S(1)} %add.70), channel_id=1, source_target_pairs={{0,8},{4,12},{8,0},{12,4},{16,24},{20,28},{24,16},{28,20},{1,9},{5... | collective-permute-start | bytes 98312 | tf_op jit(solution)/shard_map/ppermute | solution.py:29
  20.2 4.3 %collective-permute-start.7 = (f32[64,256]{1,0:T(8,128)S(1)}, f32[64,256]{1,0:T(8,128)S(1)}, u32[]{:S(2)}, u32[]{:S(2)}) collective-permute-start(f32[64,256]{1,0:T(8,128)S(1)} %pad_maximum_fusion.5), channel_id=1, source_target_pairs={{0,4},{4,0},{8,12},{12,8},{16,20},{20,16},{24,28},{28,24},{1,5},{5... | collective-permute-start | bytes 196616 | tf_op jit(solution)/shard_map/ppermute | solution.py:29
  21.8 4.9 %collective-permute-start.5 = (f32[64,128]{1,0:T(8,128)S(1)}, f32[64,128]{1,0:T(8,128)S(1)}, u32[]{:S(2)}, u32[]{:S(2)}) collective-permute-start(f32[64,128]{1,0:T(8,128)S(1)} %add.71), channel_id=1, source_target_pairs={{0,16},{4,20},{8,24},{12,28},{16,0},{20,4},{24,8},{28,12},{1,17},{... | collective-permute-start | bytes 98312 | tf_op jit(solution)/shard_map/ppermute | solution.py:29
  24.5 9.6 %collective-permute-start.8 = (f32[64,256]{1,0:T(8,128)S(1)}, f32[64,256]{1,0:T(8,128)S(1)}, u32[]{:S(2)}, u32[]{:S(2)}) collective-permute-start(f32[64,256]{1,0:T(8,128)S(1)} %fusion.49), channel_id=1, source_target_pairs={{0,8},{4,12},{8,0},{12,4},{16,24},{20,28},{24,16},{28,20},{1,9},{5... | collective-permute-start | bytes 196616 | tf_op jit(solution)/shard_map/ppermute | solution.py:29
  34.1 3.0 %copy-start.1 = (f32[64,64]{1,0:T(8,128)S(1)}, f32[64,64]{1,0:T(8,128)}, u32[]{:S(2)}) copy-start(f32[64,64]{1,0:T(8,128)} %shard_map.17) | copy-start | bytes 49156
  34.1 3.0 %copy-start.3 = (f32[64,128]{1,0:T(8,128)S(1)}, f32[64,128]{1,0:T(8,128)}, u32[]{:S(2)}) copy-start(f32[64,128]{1,0:T(8,128)} %add.72.head_ref) | copy-start | bytes 98308
  34.1 6.4 %collective-permute-start.9 = (f32[64,256]{1,0:T(8,128)S(1)}, f32[64,256]{1,0:T(8,128)S(1)}, u32[]{:S(2)}, u32[]{:S(2)}) collective-permute-start(f32[64,256]{1,0:T(8,128)S(1)} %add.74), channel_id=1, source_target_pairs={{0,16},{4,20},{8,24},{12,28},{16,0},{20,4},{24,8},{28,12},{1,17},{... | collective-permute-start | bytes 196616 | tf_op jit(solution)/shard_map/ppermute | solution.py:29
  43.3 4.0 %collective-permute-start.10 = (f32[64,128]{1,0:T(8,128)S(1)}, f32[64,128]{1,0:T(8,128)S(1)}, u32[]{:S(2)}, u32[]{:S(2)}) collective-permute-start(f32[64,128]{1,0:T(8,128)S(1)} %fusion.3), channel_id=1, source_target_pairs={{0,4},{4,0},{8,12},{12,8},{16,20},{20,16},{24,28},{28,24},{1,5},{5... | collective-permute-start | bytes 98312 | tf_op jit(solution)/shard_map/ppermute | solution.py:29
  44.7 3.9 %collective-permute-start.13 = (f32[64,128]{1,0:T(8,128)S(1)}, f32[64,128]{1,0:T(8,128)S(1)}, u32[]{:S(2)}, u32[]{:S(2)}) collective-permute-start(f32[64,128]{1,0:T(8,128)S(1)} %pad_maximum_fusion.6), channel_id=1, source_target_pairs={{0,4},{4,0},{8,12},{12,8},{16,20},{20,16},{24,28},{28,24},{1,5},{5... | collective-permute-start | bytes 98312 | tf_op jit(solution)/shard_map/ppermute | solution.py:29
  47.2 4.3 %collective-permute-start.11 = (f32[64,128]{1,0:T(8,128)S(1)}, f32[64,128]{1,0:T(8,128)S(1)}, u32[]{:S(2)}, u32[]{:S(2)}) collective-permute-start(f32[64,128]{1,0:T(8,128)S(1)} %add.76), channel_id=1, source_target_pairs={{0,8},{4,12},{8,0},{12,4},{16,24},{20,28},{24,16},{28,20},{1,9},{5... | collective-permute-start | bytes 98312 | tf_op jit(solution)/shard_map/ppermute | solution.py:29
  48.7 4.3 %collective-permute-start.14 = (f32[64,128]{1,0:T(8,128)S(1)}, f32[64,128]{1,0:T(8,128)S(1)}, u32[]{:S(2)}, u32[]{:S(2)}) collective-permute-start(f32[64,128]{1,0:T(8,128)S(1)} %fusion.131), channel_id=1, source_target_pairs={{0,8},{4,12},{8,0},{12,4},{16,24},{20,28},{24,16},{28,20},{1,9},{5... | collective-permute-start | bytes 98312 | tf_op jit(solution)/shard_map/ppermute | solution.py:29
  51.5 4.8 %collective-permute-start.12 = (f32[64,128]{1,0:T(8,128)S(1)}, f32[64,128]{1,0:T(8,128)S(1)}, u32[]{:S(2)}, u32[]{:S(2)}) collective-permute-start(f32[64,128]{1,0:T(8,128)S(1)} %add.77), channel_id=1, source_target_pairs={{0,16},{4,20},{8,24},{12,28},{16,0},{20,4},{24,8},{28,12},{1,17},{... | collective-permute-start | bytes 98312 | tf_op jit(solution)/shard_map/ppermute | solution.py:29
  53.0 12.3 %collective-permute-start.15 = (f32[64,128]{1,0:T(8,128)S(1)}, f32[64,128]{1,0:T(8,128)S(1)}, u32[]{:S(2)}, u32[]{:S(2)}) collective-permute-start(f32[64,128]{1,0:T(8,128)S(1)} %add.80), channel_id=1, source_target_pairs={{0,16},{4,20},{8,24},{12,28},{16,0},{20,4},{24,8},{28,12},{1,17},{... | collective-permute-start | bytes 98312 | tf_op jit(solution)/shard_map/ppermute | solution.py:29
  63.7 1.1 %copy-start.2 = (f32[64,64]{1,0:T(8,128)S(1)}, f32[64,64]{1,0:T(8,128)}, u32[]{:S(2)}) copy-start(f32[64,64]{1,0:T(8,128)} %shard_map.18) | copy-start | bytes 49156
  63.7 1.2 %copy-start.4 = (f32[64,128]{1,0:T(8,128)S(1)}, f32[64,128]{1,0:T(8,128)}, u32[]{:S(2)}) copy-start(f32[64,128]{1,0:T(8,128)} %add.78.head_ref) | copy-start | bytes 98308

commit v20 on v18

--- a/solution.py
+++ b/solution.py
@@ -50,7 +50,6 @@
         row = work[j:j + 1, :]
         pivot = row[:, j:j + 1]
         scale = lax.rsqrt(pivot)
-        scale = scale * (1.5 - 0.5 * pivot * scale * scale)
         scaled = row * scale
         weight = jnp.where(row_ids > j, work[:, j:j + 1] * scale, 0.0)
         work = jnp.where(rows == j, scaled, work - weight * scaled)

time: 68.2 us -> 67.3 us (0.987)
  Pallas kernels: 14.5 us -> 13.6 us
    pallas_call x2, Pallas kernels: 14.5 us -> 13.6 us  [lower_inverse(): pl.pallas_call(_eliminate_kernel, out_shape=jax.ShapeDtypeStruct((size, s...]
  transfers between devices with their start and end apart: 16 -> 16, of which waited for: 8 -> 8; matrix products, arithmetic and copies ran while one was open for 11% -> 11% of each run, Pallas kernels for 21% -> 20%
where the time goes in v20:
time: 67.3 us; the launch traced here: 66.9 us
  starting transfers between devices  28 us (42%)
  Pallas kernels  13.6 us (20%)
  matrix products  12.9 us (19%)
  waiting for transfers between devices  9.37 us (14%)
  other arithmetic  1.57 us (2%)
  local copies, waits for them, and re-layouts  0.91 us (1%)
    ppermute x12, starting transfers between devices, butterfly_sum(): x = x + lax.ppermute(x, axis, [(i, i ^ step) for i in range(size)])  20.4 us
    pallas_call x2, Pallas kernels, lower_inverse(): pl.pallas_call(_eliminate_kernel, out_shape=jax.ShapeDtypeStruct((size, s...  13.6 us
    dot_general x42, matrix products, apply_left(): return jnp.dot(square, right_side, precision=HIGHEST_PRECISION)  8.63 us
    ppermute x12, waiting for transfers between devices, butterfly_sum(): x = x + lax.ppermute(x, axis, [(i, i ^ step) for i in range(size)])  6.83 us
    ppermute x2, starting transfers between devices, from_root(): lax.ppermute(value, axis, [(i, i + dist) for i in range(size) if i % (2 *...  6.15 us
    dot_general x6, matrix products, inner_rows(): lax.dot_general(left, right, (((1,), (1,)), ((), ())), precision=HIGHEST_...  2.51 us
    ppermute x1, waiting for transfers between devices, spread_pair(): lax.ppermute(have, axis, [(i, i + dist) for i in range(size) if i % (2 *...  2.18 us
    dot_general x2, matrix products, local(): current = current - jnp.dot(mixed.T, reflect, precision=HIGHEST_PRECISION)  1.42 us
  transfers between devices with their start and end apart: 16, of which 8 were waited for; matrix products, arithmetic and copies ran while one was open for 11% of the time, Pallas kernels for 20%

profile of v20, /device:TPU:0, one launch (start us, length us, event | category | flops | bytes accessed | tf_op | source)
XLA Modules:
  0.0 66.9 jit_solution(11271690311470199781)
XLA Ops:
  0.0 0.9 %copy-done = f32[1,64,768]{2,1,0:T(8,128)S(1)} copy-done((f32[1,64,768]{2,1,0:T(8,128)S(1)}, f32[1,64,768]{2,1,0:T(8,128)}, u32[]{:S(2)}) %copy-start) | copy-done | bytes 196632
  0.9 0.5 convolution_bitcast_fusion
  1.5 4.9 %collective-permute-start = (f32[64,128]{1,0:T(8,128)S(1)}, f32[64,128]{1,0:T(8,128)S(1)}, u32[]{:S(2)}, u32[]{:S(2)}) collective-permute-start(f32[64,128]{1,0:T(8,128)S(1)} %convolution_bitcast_fusion), channel_id=1, source_target_pairs={{0,2},{4,6},{8,10},{12,14},{16,18},{20,22},{24,26},{28,30}} | collective-permute-start | bytes 98312 | tf_op jit(solution)/shard_map/ppermute | solution.py:85
  6.3 1.3 %collective-permute-start.5 = (f32[64,768]{1,0:T(8,128)S(1)}, f32[64,768]{1,0:T(8,128)S(1)}, u32[]{:S(2)}, u32[]{:S(2)}) collective-permute-start(f32[64,768]{1,0:T(8,128)S(1)} %bitcast.82), channel_id=1, source_target_pairs={{0,2},{1,3},{4,6},{5,7},{8,10},{9,11},{12,14},{13,15},{16,18},{17,... | collective-permute-start | bytes 589832 | tf_op jit(solution)/shard_map/ppermute | solution.py:71
  8.0 1.3 %collective-permute-start.1 = (f32[64,128]{1,0:T(8,128)S(1)}, f32[64,128]{1,0:T(8,128)S(1)}, u32[]{:S(2)}, u32[]{:S(2)}) collective-permute-start(f32[64,128]{1,0:T(8,128)S(1)} %broadcast_select_fusion.5), channel_id=1, source_target_pairs={{0,1},{2,3},{4,5},{6,7},{8,9},{10,11},{12,13},{14,15},{16,17},{18,... | collective-permute-start | bytes 98312 | tf_op jit(solution)/shard_map/ppermute | solution.py:85
  9.3 2.2 %collective-permute-done.5 = f32[64,768]{1,0:T(8,128)S(1)} collective-permute-done((f32[64,768]{1,0:T(8,128)S(1)}, f32[64,768]{1,0:T(8,128)S(1)}, u32[]{:S(2)}, u32[]{:S(2)}) %collective-permute-start.5) | collective-permute-done | bytes 196640 | tf_op jit(solution)/shard_map/ppermute | solution.py:71
  11.6 1.6 %collective-permute-start.2 = (f32[64,128]{1,0:T(8,128)S(1)}, f32[64,128]{1,0:T(8,128)S(1)}, u32[]{:S(2)}, u32[]{:S(2)}) collective-permute-start(f32[64,128]{1,0:T(8,128)S(1)} %broadcast_select_fusion.6), channel_id=1, source_target_pairs={{0,4},{4,0},{8,12},{12,8},{16,20},{20,16},{24,28},{28,24},{1,5},{5... | collective-permute-start | bytes 98312 | tf_op jit(solution)/shard_map/ppermute | solution.py:29
  13.2 2.4 %collective-permute-done.2 = f32[64,128]{1,0:T(8,128)S(1)} collective-permute-done((f32[64,128]{1,0:T(8,128)S(1)}, f32[64,128]{1,0:T(8,128)S(1)}, u32[]{:S(2)}, u32[]{:S(2)}) %collective-permute-start.2) | collective-permute-done | bytes 32800 | tf_op jit(solution)/shard_map/ppermute | solution.py:29
  15.6 1.6 %collective-permute-start.3 = (f32[64,128]{1,0:T(8,128)S(1)}, f32[64,128]{1,0:T(8,128)S(1)}, u32[]{:S(2)}, u32[]{:S(2)}) collective-permute-start(f32[64,128]{1,0:T(8,128)S(1)} %add.70), channel_id=1, source_target_pairs={{0,8},{4,12},{8,0},{12,4},{16,24},{20,28},{24,16},{28,20},{1,9},{5... | collective-permute-start | bytes 98312 | tf_op jit(solution)/shard_map/ppermute | solution.py:29
  17.6 0.5 fusion.8
  18.1 1.6 %collective-permute-start.7 = (f32[64,256]{1,0:T(8,128)S(1)}, f32[64,256]{1,0:T(8,128)S(1)}, u32[]{:S(2)}, u32[]{:S(2)}) collective-permute-start(f32[64,256]{1,0:T(8,128)S(1)} %pad_maximum_fusion.5), channel_id=1, source_target_pairs={{0,4},{4,0},{8,12},{12,8},{16,20},{20,16},{24,28},{28,24},{1,5},{5... | collective-permute-start | bytes 196616 | tf_op jit(solution)/shard_map/ppermute | solution.py:29
  19.7 2.7 %collective-permute-start.4 = (f32[64,128]{1,0:T(8,128)S(1)}, f32[64,128]{1,0:T(8,128)S(1)}, u32[]{:S(2)}, u32[]{:S(2)}) collective-permute-start(f32[64,128]{1,0:T(8,128)S(1)} %add.71), channel_id=1, source_target_pairs={{0,16},{4,20},{8,24},{12,28},{16,0},{20,4},{24,8},{28,12},{1,17},{... | collective-permute-start | bytes 98312 | tf_op jit(solution)/shard_map/ppermute | solution.py:29
  22.5 1.3 %collective-permute-start.8 = (f32[64,256]{1,0:T(8,128)S(1)}, f32[64,256]{1,0:T(8,128)S(1)}, u32[]{:S(2)}, u32[]{:S(2)}) collective-permute-start(f32[64,256]{1,0:T(8,128)S(1)} %fusion.49), channel_id=1, source_target_pairs={{0,8},{4,12},{8,0},{12,4},{16,24},{20,28},{24,16},{28,20},{1,9},{5... | collective-permute-start | bytes 196616 | tf_op jit(solution)/shard_map/ppermute | solution.py:29
  23.8 0.8 %collective-permute-done.4 = f32[64,128]{1,0:T(8,128)S(1)} collective-permute-done((f32[64,128]{1,0:T(8,128)S(1)}, f32[64,128]{1,0:T(8,128)S(1)}, u32[]{:S(2)}, u32[]{:S(2)}) %collective-permute-start.4) | collective-permute-done | bytes 32800 | tf_op jit(solution)/shard_map/ppermute | solution.py:29
  24.6 0.6 add.72.head_ref
  25.2 6.8 %shard_map.17 = f32[64,64]{1,0:T(8,128)} custom-call(f32[64,128]{1,0:T(8,128)} %add.72.head_ref), custom_call_target="tpu_custom_call" | custom-call | tf_op jit(solution)/shard_map/pallas_call | solution.py:61
  32.0 2.8 %collective-permute-start.9 = (f32[64,256]{1,0:T(8,128)S(1)}, f32[64,256]{1,0:T(8,128)S(1)}, u32[]{:S(2)}, u32[]{:S(2)}) collective-permute-start(f32[64,256]{1,0:T(8,128)S(1)} %add.74), channel_id=1, source_target_pairs={{0,16},{4,20},{8,24},{12,28},{16,0},{20,4},{24,8},{28,12},{1,17},{... | collective-permute-start | bytes 196616 | tf_op jit(solution)/shard_map/ppermute | solution.py:29
  39.8 0.4 fusion.1
  40.5 0.5 fusion.3
  41.0 1.2 %collective-permute-start.10 = (f32[64,128]{1,0:T(8,128)S(1)}, f32[64,128]{1,0:T(8,128)S(1)}, u32[]{:S(2)}, u32[]{:S(2)}) collective-permute-start(f32[64,128]{1,0:T(8,128)S(1)} %fusion.3), channel_id=1, source_target_pairs={{0,4},{4,0},{8,12},{12,8},{16,20},{20,16},{24,28},{28,24},{1,5},{5... | collective-permute-start | bytes 98312 | tf_op jit(solution)/shard_map/ppermute | solution.py:29
  42.3 0.9 %collective-permute-start.13 = (f32[64,128]{1,0:T(8,128)S(1)}, f32[64,128]{1,0:T(8,128)S(1)}, u32[]{:S(2)}, u32[]{:S(2)}) collective-permute-start(f32[64,128]{1,0:T(8,128)S(1)} %pad_maximum_fusion.6), channel_id=1, source_target_pairs={{0,4},{4,0},{8,12},{12,8},{16,20},{20,16},{24,28},{28,24},{1,5},{5... | collective-permute-start | bytes 98312 | tf_op jit(solution)/shard_map/ppermute | solution.py:29
  43.2 1.8 %collective-permute-done.10 = f32[64,128]{1,0:T(8,128)S(1)} collective-permute-done((f32[64,128]{1,0:T(8,128)S(1)}, f32[64,128]{1,0:T(8,128)S(1)}, u32[]{:S(2)}, u32[]{:S(2)}) %collective-permute-start.10) | collective-permute-done | bytes 32800 | tf_op jit(solution)/shard_map/ppermute | solution.py:29
  45.0 1.6 %collective-permute-start.11 = (f32[64,128]{1,0:T(8,128)S(1)}, f32[64,128]{1,0:T(8,128)S(1)}, u32[]{:S(2)}, u32[]{:S(2)}) collective-permute-start(f32[64,128]{1,0:T(8,128)S(1)} %add.76), channel_id=1, source_target_pairs={{0,8},{4,12},{8,0},{12,4},{16,24},{20,28},{24,16},{28,20},{1,9},{5... | collective-permute-start | bytes 98312 | tf_op jit(solution)/shard_map/ppermute | solution.py:29
  46.6 1.5 %collective-permute-start.14 = (f32[64,128]{1,0:T(8,128)S(1)}, f32[64,128]{1,0:T(8,128)S(1)}, u32[]{:S(2)}, u32[]{:S(2)}) collective-permute-start(f32[64,128]{1,0:T(8,128)S(1)} %fusion.131), channel_id=1, source_target_pairs={{0,8},{4,12},{8,0},{12,4},{16,24},{20,28},{24,16},{28,20},{1,9},{5... | collective-permute-start | bytes 98312 | tf_op jit(solution)/shard_map/ppermute | solution.py:29
  48.1 0.8 %collective-permute-done.11 = f32[64,128]{1,0:T(8,128)S(1)} collective-permute-done((f32[64,128]{1,0:T(8,128)S(1)}, f32[64,128]{1,0:T(8,128)S(1)}, u32[]{:S(2)}, u32[]{:S(2)}) %collective-permute-start.11) | collective-permute-done | bytes 32800 | tf_op jit(solution)/shard_map/ppermute | solution.py:29
  48.9 1.8 %collective-permute-start.12 = (f32[64,128]{1,0:T(8,128)S(1)}, f32[64,128]{1,0:T(8,128)S(1)}, u32[]{:S(2)}, u32[]{:S(2)}) collective-permute-start(f32[64,128]{1,0:T(8,128)S(1)} %add.77), channel_id=1, source_target_pairs={{0,16},{4,20},{8,24},{12,28},{16,0},{20,4},{24,8},{28,12},{1,17},{... | collective-permute-start | bytes 98312 | tf_op jit(solution)/shard_map/ppermute | solution.py:29
  50.7 2.1 %collective-permute-start.15 = (f32[64,128]{1,0:T(8,128)S(1)}, f32[64,128]{1,0:T(8,128)S(1)}, u32[]{:S(2)}, u32[]{:S(2)}) collective-permute-start(f32[64,128]{1,0:T(8,128)S(1)} %add.80), channel_id=1, source_target_pairs={{0,16},{4,20},{8,24},{12,28},{16,0},{20,4},{24,8},{28,12},{1,17},{... | collective-permute-start | bytes 98312 | tf_op jit(solution)/shard_map/ppermute | solution.py:29
  52.8 0.9 %collective-permute-done.12 = f32[64,128]{1,0:T(8,128)S(1)} collective-permute-done((f32[64,128]{1,0:T(8,128)S(1)}, f32[64,128]{1,0:T(8,128)S(1)}, u32[]{:S(2)}, u32[]{:S(2)}) %collective-permute-start.12) | collective-permute-done | bytes 32800 | tf_op jit(solution)/shard_map/ppermute | solution.py:29
  53.7 0.6 add.78.head_ref
  54.3 6.8 %shard_map.18 = f32[64,64]{1,0:T(8,128)} custom-call(f32[64,128]{1,0:T(8,128)} %add.78.head_ref), custom_call_target="tpu_custom_call" | custom-call | tf_op jit(solution)/shard_map/pallas_call | solution.py:61
  61.1 1.1 %convolution_subtract_fusion.1 = f32[64,768]{1,0:T(8,128)S(1)} fusion(f32[64,64]{1,0:T(8,128)} %shard_map.18, f32[64,768]{1,0:T(8,128)S(1)} %fusion.1, s32[768]{0:T(1024)S(1)} %fusion.39), kind=kOutput, calls=%fused_computation.2 | convolution fusion | flops 37896192 | bytes 412672 | tf_op jit(solution)/shard_map/dot_general | solution.py:15
  65.8 1.1 %fusion = f32[1,64,768]{2,1,0:T(8,128)} fusion(f32[64,768]{1,0:T(8,128)S(1)} %convolution_subtract_fusion.3, f32[64,64]{1,0:T(8,128)S(1)} %fusion.18, f32[64,768]{1,0:T(8,128)S(1)} %convolution_subtract_fusion.1), kind=kOutput, calls=%fused_computation.1 | convolution fusion | flops 37797888 | bytes 606208 | tf_op jit(solution)/shard_map/dot_general | solution.py:150
  (86 shorter events, 9.7 us)
Async XLA Ops:
  0.0 0.9 %copy-start = (f32[1,64,768]{2,1,0:T(8,128)S(1)}, f32[1,64,768]{2,1,0:T(8,128)}, u32[]{:S(2)}) copy-start(f32[1,64,768]{2,1,0:T(8,128)} %param.1) | copy-start | bytes 589828
  1.5 6.6 %collective-permute-start = (f32[64,128]{1,0:T(8,128)S(1)}, f32[64,128]{1,0:T(8,128)S(1)}, u32[]{:S(2)}, u32[]{:S(2)}) collective-permute-start(f32[64,128]{1,0:T(8,128)S(1)} %convolution_bitcast_fusion), channel_id=1, source_target_pairs={{0,2},{4,6},{8,10},{12,14},{16,18},{20,22},{24,26},{28,30}} | collective-permute-start | bytes 98312 | tf_op jit(solution)/shard_map/ppermute | solution.py:85
  6.3 5.2 %collective-permute-start.5 = (f32[64,768]{1,0:T(8,128)S(1)}, f32[64,768]{1,0:T(8,128)S(1)}, u32[]{:S(2)}, u32[]{:S(2)}) collective-permute-start(f32[64,768]{1,0:T(8,128)S(1)} %bitcast.82), channel_id=1, source_target_pairs={{0,2},{1,3},{4,6},{5,7},{8,10},{9,11},{12,14},{13,15},{16,18},{17,... | collective-permute-start | bytes 589832 | tf_op jit(solution)/shard_map/ppermute | solution.py:71
  8.0 3.6 %collective-permute-start.1 = (f32[64,128]{1,0:T(8,128)S(1)}, f32[64,128]{1,0:T(8,128)S(1)}, u32[]{:S(2)}, u32[]{:S(2)}) collective-permute-start(f32[64,128]{1,0:T(8,128)S(1)} %broadcast_select_fusion.5), channel_id=1, source_target_pairs={{0,1},{2,3},{4,5},{6,7},{8,9},{10,11},{12,13},{14,15},{16,17},{18,... | collective-permute-start | bytes 98312 | tf_op jit(solution)/shard_map/ppermute | solution.py:85
  11.5 5.7 %collective-permute-start.6 = (f32[64,768]{1,0:T(8,128)S(1)}, f32[64,768]{1,0:T(8,128)S(1)}, u32[]{:S(2)}, u32[]{:S(2)}) collective-permute-start(f32[64,768]{1,0:T(8,128)S(1)} %broadcast_select_fusion), channel_id=1, source_target_pairs={{0,1},{1,0},{2,3},{3,2},{4,5},{5,4},{6,7},{7,6},{8,9},{9,8},{10,11... | collective-permute-start | bytes 589832 | tf_op jit(solution)/shard_map/ppermute | solution.py:76
  11.6 4.0 %collective-permute-start.2 = (f32[64,128]{1,0:T(8,128)S(1)}, f32[64,128]{1,0:T(8,128)S(1)}, u32[]{:S(2)}, u32[]{:S(2)}) collective-permute-start(f32[64,128]{1,0:T(8,128)S(1)} %broadcast_select_fusion.6), channel_id=1, source_target_pairs={{0,4},{4,0},{8,12},{12,8},{16,20},{20,16},{24,28},{28,24},{1,5},{5... | collective-permute-start | bytes 98312 | tf_op jit(solution)/shard_map/ppermute | solution.py:29
  15.6 4.1 %collective-permute-start.3 = (f32[64,128]{1,0:T(8,128)S(1)}, f32[64,128]{1,0:T(8,128)S(1)}, u32[]{:S(2)}, u32[]{:S(2)}) collective-permute-start(f32[64,128]{1,0:T(8,128)S(1)} %add.70), channel_id=1, source_target_pairs={{0,8},{4,12},{8,0},{12,4},{16,24},{20,28},{24,16},{28,20},{1,9},{5... | collective-permute-start | bytes 98312 | tf_op jit(solution)/shard_map/ppermute | solution.py:29
  18.1 4.3 %collective-permute-start.7 = (f32[64,256]{1,0:T(8,128)S(1)}, f32[64,256]{1,0:T(8,128)S(1)}, u32[]{:S(2)}, u32[]{:S(2)}) collective-permute-start(f32[64,256]{1,0:T(8,128)S(1)} %pad_maximum_fusion.5), channel_id=1, source_target_pairs={{0,4},{4,0},{8,12},{12,8},{16,20},{20,16},{24,28},{28,24},{1,5},{5... | collective-permute-start | bytes 196616 | tf_op jit(solution)/shard_map/ppermute | solution.py:29
  19.7 4.9 %collective-permute-start.4 = (f32[64,128]{1,0:T(8,128)S(1)}, f32[64,128]{1,0:T(8,128)S(1)}, u32[]{:S(2)}, u32[]{:S(2)}) collective-permute-start(f32[64,128]{1,0:T(8,128)S(1)} %add.71), channel_id=1, source_target_pairs={{0,16},{4,20},{8,24},{12,28},{16,0},{20,4},{24,8},{28,12},{1,17},{... | collective-permute-start | bytes 98312 | tf_op jit(solution)/shard_map/ppermute | solution.py:29
  22.5 9.6 %collective-permute-start.8 = (f32[64,256]{1,0:T(8,128)S(1)}, f32[64,256]{1,0:T(8,128)S(1)}, u32[]{:S(2)}, u32[]{:S(2)}) collective-permute-start(f32[64,256]{1,0:T(8,128)S(1)} %fusion.49), channel_id=1, source_target_pairs={{0,8},{4,12},{8,0},{12,4},{16,24},{20,28},{24,16},{28,20},{1,9},{5... | collective-permute-start | bytes 196616 | tf_op jit(solution)/shard_map/ppermute | solution.py:29
  32.0 2.8 %copy-start.1 = (f32[64,64]{1,0:T(8,128)S(1)}, f32[64,64]{1,0:T(8,128)}, u32[]{:S(2)}) copy-start(f32[64,64]{1,0:T(8,128)} %shard_map.17) | copy-start | bytes 49156
  32.0 2.8 %copy-start.3 = (f32[64,128]{1,0:T(8,128)S(1)}, f32[64,128]{1,0:T(8,128)}, u32[]{:S(2)}) copy-start(f32[64,128]{1,0:T(8,128)} %add.72.head_ref) | copy-start | bytes 98308
  32.0 6.2 %collective-permute-start.9 = (f32[64,256]{1,0:T(8,128)S(1)}, f32[64,256]{1,0:T(8,128)S(1)}, u32[]{:S(2)}, u32[]{:S(2)}) collective-permute-start(f32[64,256]{1,0:T(8,128)S(1)} %add.74), channel_id=1, source_target_pairs={{0,16},{4,20},{8,24},{12,28},{16,0},{20,4},{24,8},{28,12},{1,17},{... | collective-permute-start | bytes 196616 | tf_op jit(solution)/shard_map/ppermute | solution.py:29
  41.0 4.0 %collective-permute-start.10 = (f32[64,128]{1,0:T(8,128)S(1)}, f32[64,128]{1,0:T(8,128)S(1)}, u32[]{:S(2)}, u32[]{:S(2)}) collective-permute-start(f32[64,128]{1,0:T(8,128)S(1)} %fusion.3), channel_id=1, source_target_pairs={{0,4},{4,0},{8,12},{12,8},{16,20},{20,16},{24,28},{28,24},{1,5},{5... | collective-permute-start | bytes 98312 | tf_op jit(solution)/shard_map/ppermute | solution.py:29
  42.3 4.3 %collective-permute-start.13 = (f32[64,128]{1,0:T(8,128)S(1)}, f32[64,128]{1,0:T(8,128)S(1)}, u32[]{:S(2)}, u32[]{:S(2)}) collective-permute-start(f32[64,128]{1,0:T(8,128)S(1)} %pad_maximum_fusion.6), channel_id=1, source_target_pairs={{0,4},{4,0},{8,12},{12,8},{16,20},{20,16},{24,28},{28,24},{1,5},{5... | collective-permute-start | bytes 98312 | tf_op jit(solution)/shard_map/ppermute | solution.py:29
  45.0 3.9 %collective-permute-start.11 = (f32[64,128]{1,0:T(8,128)S(1)}, f32[64,128]{1,0:T(8,128)S(1)}, u32[]{:S(2)}, u32[]{:S(2)}) collective-permute-start(f32[64,128]{1,0:T(8,128)S(1)} %add.76), channel_id=1, source_target_pairs={{0,8},{4,12},{8,0},{12,4},{16,24},{20,28},{24,16},{28,20},{1,9},{5... | collective-permute-start | bytes 98312 | tf_op jit(solution)/shard_map/ppermute | solution.py:29
  46.6 4.1 %collective-permute-start.14 = (f32[64,128]{1,0:T(8,128)S(1)}, f32[64,128]{1,0:T(8,128)S(1)}, u32[]{:S(2)}, u32[]{:S(2)}) collective-permute-start(f32[64,128]{1,0:T(8,128)S(1)} %fusion.131), channel_id=1, source_target_pairs={{0,8},{4,12},{8,0},{12,4},{16,24},{20,28},{24,16},{28,20},{1,9},{5... | collective-permute-start | bytes 98312 | tf_op jit(solution)/shard_map/ppermute | solution.py:29
  48.9 4.8 %collective-permute-start.12 = (f32[64,128]{1,0:T(8,128)S(1)}, f32[64,128]{1,0:T(8,128)S(1)}, u32[]{:S(2)}, u32[]{:S(2)}) collective-permute-start(f32[64,128]{1,0:T(8,128)S(1)} %add.77), channel_id=1, source_target_pairs={{0,16},{4,20},{8,24},{12,28},{16,0},{20,4},{24,8},{28,12},{1,17},{... | collective-permute-start | bytes 98312 | tf_op jit(solution)/shard_map/ppermute | solution.py:29
  50.7 11.9 %collective-permute-start.15 = (f32[64,128]{1,0:T(8,128)S(1)}, f32[64,128]{1,0:T(8,128)S(1)}, u32[]{:S(2)}, u32[]{:S(2)}) collective-permute-start(f32[64,128]{1,0:T(8,128)S(1)} %add.80), channel_id=1, source_target_pairs={{0,16},{4,20},{8,24},{12,28},{16,0},{20,4},{24,8},{28,12},{1,17},{... | collective-permute-start | bytes 98312 | tf_op jit(solution)/shard_map/ppermute | solution.py:29
  61.1 1.1 %copy-start.2 = (f32[64,64]{1,0:T(8,128)S(1)}, f32[64,64]{1,0:T(8,128)}, u32[]{:S(2)}) copy-start(f32[64,64]{1,0:T(8,128)} %shard_map.18) | copy-start | bytes 49156
  61.1 1.2 %copy-start.4 = (f32[64,128]{1,0:T(8,128)S(1)}, f32[64,128]{1,0:T(8,128)}, u32[]{:S(2)}) copy-start(f32[64,128]{1,0:T(8,128)} %add.78.head_ref) | copy-start | bytes 98308

commit v21 on v20

--- a/solution.py
+++ b/solution.py
@@ -33,7 +33,7 @@
 def invert_near_identity(square):
     identity = jnp.eye(square.shape[0], dtype=jnp.float32)
     approx = square.T * (2.0 / (0.25 + 4.84))
-    for _ in range(8):
+    for _ in range(7):
         approx = apply_left(approx, 2.0 * identity - apply_left(square, approx))
     return approx
 

time: 67.3 us -> 66.7 us (level)
    dot_general x42 -> x38, matrix products: 8.63 us -> 7.99 us  [apply_left(): return jnp.dot(square, right_side, precision=HIGHEST_PRECISION)]
  transfers between devices with their start and end apart: 16 -> 16, of which waited for: 8 -> 8; matrix products, arithmetic and copies ran while one was open for 11% -> 10% of each run, Pallas kernels for 20% -> 20%
where the time goes in v21:
time: 66.7 us; the launch traced here: 66.3 us
  starting transfers between devices  28.2 us (42%)
  Pallas kernels  13.6 us (20%)
  matrix products  12.3 us (18%)
  waiting for transfers between devices  9.21 us (14%)
  other arithmetic  1.57 us (2%)
  local copies, waits for them, and re-layouts  0.91 us (1%)
    ppermute x12, starting transfers between devices, butterfly_sum(): x = x + lax.ppermute(x, axis, [(i, i ^ step) for i in range(size)])  20.7 us
    pallas_call x2, Pallas kernels, lower_inverse(): pl.pallas_call(_eliminate_kernel, out_shape=jax.ShapeDtypeStruct((size, s...  13.6 us
    dot_general x38, matrix products, apply_left(): return jnp.dot(square, right_side, precision=HIGHEST_PRECISION)  7.99 us
    ppermute x12, waiting for transfers between devices, butterfly_sum(): x = x + lax.ppermute(x, axis, [(i, i ^ step) for i in range(size)])  6.67 us
    ppermute x2, starting transfers between devices, from_root(): lax.ppermute(value, axis, [(i, i + dist) for i in range(size) if i % (2 *...  6.15 us
    dot_general x6, matrix products, inner_rows(): lax.dot_general(left, right, (((1,), (1,)), ((), ())), precision=HIGHEST_...  2.52 us
    ppermute x1, waiting for transfers between devices, spread_pair(): lax.ppermute(have, axis, [(i, i + dist) for i in range(size) if i % (2 *...  2.18 us
    dot_general x2, matrix products, local(): current = current - jnp.dot(mixed.T, reflect, precision=HIGHEST_PRECISION)  1.43 us
  transfers between devices with their start and end apart: 16, of which 8 were waited for; matrix products, arithmetic and copies ran while one was open for 10% of the time, Pallas kernels for 20%

profile of v21, /device:TPU:0, one launch (start us, length us, event | category | flops | bytes accessed | tf_op | source)
XLA Modules:
  0.0 66.3 jit_solution(1602500105107989351)
XLA Ops:
  0.0 0.9 %copy-done = f32[1,64,768]{2,1,0:T(8,128)S(1)} copy-done((f32[1,64,768]{2,1,0:T(8,128)S(1)}, f32[1,64,768]{2,1,0:T(8,128)}, u32[]{:S(2)}) %copy-start) | copy-done | bytes 196632
  0.9 0.5 convolution_bitcast_fusion
  1.5 4.9 %collective-permute-start = (f32[64,128]{1,0:T(8,128)S(1)}, f32[64,128]{1,0:T(8,128)S(1)}, u32[]{:S(2)}, u32[]{:S(2)}) collective-permute-start(f32[64,128]{1,0:T(8,128)S(1)} %convolution_bitcast_fusion), channel_id=1, source_target_pairs={{0,2},{4,6},{8,10},{12,14},{16,18},{20,22},{24,26},{28,30}} | collective-permute-start | bytes 98312 | tf_op jit(solution)/shard_map/ppermute | solution.py:85
  6.3 1.3 %collective-permute-start.5 = (f32[64,768]{1,0:T(8,128)S(1)}, f32[64,768]{1,0:T(8,128)S(1)}, u32[]{:S(2)}, u32[]{:S(2)}) collective-permute-start(f32[64,768]{1,0:T(8,128)S(1)} %bitcast.76), channel_id=1, source_target_pairs={{0,2},{1,3},{4,6},{5,7},{8,10},{9,11},{12,14},{13,15},{16,18},{17,... | collective-permute-start | bytes 589832 | tf_op jit(solution)/shard_map/ppermute | solution.py:71
  8.0 1.3 %collective-permute-start.1 = (f32[64,128]{1,0:T(8,128)S(1)}, f32[64,128]{1,0:T(8,128)S(1)}, u32[]{:S(2)}, u32[]{:S(2)}) collective-permute-start(f32[64,128]{1,0:T(8,128)S(1)} %broadcast_select_fusion.5), channel_id=1, source_target_pairs={{0,1},{2,3},{4,5},{6,7},{8,9},{10,11},{12,13},{14,15},{16,17},{18,... | collective-permute-start | bytes 98312 | tf_op jit(solution)/shard_map/ppermute | solution.py:85
  9.3 2.2 %collective-permute-done.5 = f32[64,768]{1,0:T(8,128)S(1)} collective-permute-done((f32[64,768]{1,0:T(8,128)S(1)}, f32[64,768]{1,0:T(8,128)S(1)}, u32[]{:S(2)}, u32[]{:S(2)}) %collective-permute-start.5) | collective-permute-done | bytes 196640 | tf_op jit(solution)/shard_map/ppermute | solution.py:71
  11.6 1.6 %collective-permute-start.2 = (f32[64,128]{1,0:T(8,128)S(1)}, f32[64,128]{1,0:T(8,128)S(1)}, u32[]{:S(2)}, u32[]{:S(2)}) collective-permute-start(f32[64,128]{1,0:T(8,128)S(1)} %broadcast_select_fusion.6), channel_id=1, source_target_pairs={{0,4},{4,0},{8,12},{12,8},{16,20},{20,16},{24,28},{28,24},{1,5},{5... | collective-permute-start | bytes 98312 | tf_op jit(solution)/shard_map/ppermute | solution.py:29
  13.2 2.4 %collective-permute-done.2 = f32[64,128]{1,0:T(8,128)S(1)} collective-permute-done((f32[64,128]{1,0:T(8,128)S(1)}, f32[64,128]{1,0:T(8,128)S(1)}, u32[]{:S(2)}, u32[]{:S(2)}) %collective-permute-start.2) | collective-permute-done | bytes 32800 | tf_op jit(solution)/shard_map/ppermute | solution.py:29
  15.6 1.6 %collective-permute-start.3 = (f32[64,128]{1,0:T(8,128)S(1)}, f32[64,128]{1,0:T(8,128)S(1)}, u32[]{:S(2)}, u32[]{:S(2)}) collective-permute-start(f32[64,128]{1,0:T(8,128)S(1)} %add.70), channel_id=1, source_target_pairs={{0,8},{4,12},{8,0},{12,4},{16,24},{20,28},{24,16},{28,20},{1,9},{5... | collective-permute-start | bytes 98312 | tf_op jit(solution)/shard_map/ppermute | solution.py:29
  17.6 0.5 fusion.8
  18.1 1.6 %collective-permute-start.7 = (f32[64,256]{1,0:T(8,128)S(1)}, f32[64,256]{1,0:T(8,128)S(1)}, u32[]{:S(2)}, u32[]{:S(2)}) collective-permute-start(f32[64,256]{1,0:T(8,128)S(1)} %pad_maximum_fusion.5), channel_id=1, source_target_pairs={{0,4},{4,0},{8,12},{12,8},{16,20},{20,16},{24,28},{28,24},{1,5},{5... | collective-permute-start | bytes 196616 | tf_op jit(solution)/shard_map/ppermute | solution.py:29
  19.7 2.7 %collective-permute-start.4 = (f32[64,128]{1,0:T(8,128)S(1)}, f32[64,128]{1,0:T(8,128)S(1)}, u32[]{:S(2)}, u32[]{:S(2)}) collective-permute-start(f32[64,128]{1,0:T(8,128)S(1)} %add.71), channel_id=1, source_target_pairs={{0,16},{4,20},{8,24},{12,28},{16,0},{20,4},{24,8},{28,12},{1,17},{... | collective-permute-start | bytes 98312 | tf_op jit(solution)/shard_map/ppermute | solution.py:29
  22.5 1.3 %collective-permute-start.8 = (f32[64,256]{1,0:T(8,128)S(1)}, f32[64,256]{1,0:T(8,128)S(1)}, u32[]{:S(2)}, u32[]{:S(2)}) collective-permute-start(f32[64,256]{1,0:T(8,128)S(1)} %fusion.49), channel_id=1, source_target_pairs={{0,8},{4,12},{8,0},{12,4},{16,24},{20,28},{24,16},{28,20},{1,9},{5... | collective-permute-start | bytes 196616 | tf_op jit(solution)/shard_map/ppermute | solution.py:29
  23.8 0.8 %collective-permute-done.4 = f32[64,128]{1,0:T(8,128)S(1)} collective-permute-done((f32[64,128]{1,0:T(8,128)S(1)}, f32[64,128]{1,0:T(8,128)S(1)}, u32[]{:S(2)}, u32[]{:S(2)}) %collective-permute-start.4) | collective-permute-done | bytes 32800 | tf_op jit(solution)/shard_map/ppermute | solution.py:29
  24.6 0.6 add.72.head_ref
  25.2 6.8 %shard_map.17 = f32[64,64]{1,0:T(8,128)} custom-call(f32[64,128]{1,0:T(8,128)} %add.72.head_ref), custom_call_target="tpu_custom_call" | custom-call | tf_op jit(solution)/shard_map/pallas_call | solution.py:61
  32.0 2.8 %collective-permute-start.9 = (f32[64,256]{1,0:T(8,128)S(1)}, f32[64,256]{1,0:T(8,128)S(1)}, u32[]{:S(2)}, u32[]{:S(2)}) collective-permute-start(f32[64,256]{1,0:T(8,128)S(1)} %add.74), channel_id=1, source_target_pairs={{0,16},{4,20},{8,24},{12,28},{16,0},{20,4},{24,8},{28,12},{1,17},{... | collective-permute-start | bytes 196616 | tf_op jit(solution)/shard_map/ppermute | solution.py:29
  39.4 0.4 fusion.1
  40.1 0.5 fusion.3
  40.7 1.2 %collective-permute-start.10 = (f32[64,128]{1,0:T(8,128)S(1)}, f32[64,128]{1,0:T(8,128)S(1)}, u32[]{:S(2)}, u32[]{:S(2)}) collective-permute-start(f32[64,128]{1,0:T(8,128)S(1)} %fusion.3), channel_id=1, source_target_pairs={{0,4},{4,0},{8,12},{12,8},{16,20},{20,16},{24,28},{28,24},{1,5},{5... | collective-permute-start | bytes 98312 | tf_op jit(solution)/shard_map/ppermute | solution.py:29
  41.9 0.9 %collective-permute-start.13 = (f32[64,128]{1,0:T(8,128)S(1)}, f32[64,128]{1,0:T(8,128)S(1)}, u32[]{:S(2)}, u32[]{:S(2)}) collective-permute-start(f32[64,128]{1,0:T(8,128)S(1)} %pad_maximum_fusion.6), channel_id=1, source_target_pairs={{0,4},{4,0},{8,12},{12,8},{16,20},{20,16},{24,28},{28,24},{1,5},{5... | collective-permute-start | bytes 98312 | tf_op jit(solution)/shard_map/ppermute | solution.py:29
  42.8 1.8 %collective-permute-done.10 = f32[64,128]{1,0:T(8,128)S(1)} collective-permute-done((f32[64,128]{1,0:T(8,128)S(1)}, f32[64,128]{1,0:T(8,128)S(1)}, u32[]{:S(2)}, u32[]{:S(2)}) %collective-permute-start.10) | collective-permute-done | bytes 32800 | tf_op jit(solution)/shard_map/ppermute | solution.py:29
  44.6 1.6 %collective-permute-start.11 = (f32[64,128]{1,0:T(8,128)S(1)}, f32[64,128]{1,0:T(8,128)S(1)}, u32[]{:S(2)}, u32[]{:S(2)}) collective-permute-start(f32[64,128]{1,0:T(8,128)S(1)} %add.76), channel_id=1, source_target_pairs={{0,8},{4,12},{8,0},{12,4},{16,24},{20,28},{24,16},{28,20},{1,9},{5... | collective-permute-start | bytes 98312 | tf_op jit(solution)/shard_map/ppermute | solution.py:29
  46.3 1.5 %collective-permute-start.14 = (f32[64,128]{1,0:T(8,128)S(1)}, f32[64,128]{1,0:T(8,128)S(1)}, u32[]{:S(2)}, u32[]{:S(2)}) collective-permute-start(f32[64,128]{1,0:T(8,128)S(1)} %fusion.123), channel_id=1, source_target_pairs={{0,8},{4,12},{8,0},{12,4},{16,24},{20,28},{24,16},{28,20},{1,9},{5... | collective-permute-start | bytes 98312 | tf_op jit(solution)/shard_map/ppermute | solution.py:29
  47.7 0.9 %collective-permute-done.11 = f32[64,128]{1,0:T(8,128)S(1)} collective-permute-done((f32[64,128]{1,0:T(8,128)S(1)}, f32[64,128]{1,0:T(8,128)S(1)}, u32[]{:S(2)}, u32[]{:S(2)}) %collective-permute-start.11) | collective-permute-done | bytes 32800 | tf_op jit(solution)/shard_map/ppermute | solution.py:29
  48.7 2.1 %collective-permute-start.12 = (f32[64,128]{1,0:T(8,128)S(1)}, f32[64,128]{1,0:T(8,128)S(1)}, u32[]{:S(2)}, u32[]{:S(2)}) collective-permute-start(f32[64,128]{1,0:T(8,128)S(1)} %add.77), channel_id=1, source_target_pairs={{0,16},{4,20},{8,24},{12,28},{16,0},{20,4},{24,8},{28,12},{1,17},{... | collective-permute-start | bytes 98312 | tf_op jit(solution)/shard_map/ppermute | solution.py:29
  50.7 2.1 %collective-permute-start.15 = (f32[64,128]{1,0:T(8,128)S(1)}, f32[64,128]{1,0:T(8,128)S(1)}, u32[]{:S(2)}, u32[]{:S(2)}) collective-permute-start(f32[64,128]{1,0:T(8,128)S(1)} %add.80), channel_id=1, source_target_pairs={{0,16},{4,20},{8,24},{12,28},{16,0},{20,4},{24,8},{28,12},{1,17},{... | collective-permute-start | bytes 98312 | tf_op jit(solution)/shard_map/ppermute | solution.py:29
  52.8 0.6 collective-permute-done.12
  53.5 0.6 add.78.head_ref
  54.1 6.8 %shard_map.18 = f32[64,64]{1,0:T(8,128)} custom-call(f32[64,128]{1,0:T(8,128)} %add.78.head_ref), custom_call_target="tpu_custom_call" | custom-call | tf_op jit(solution)/shard_map/pallas_call | solution.py:61
  60.9 1.1 %convolution_subtract_fusion.1 = f32[64,768]{1,0:T(8,128)S(1)} fusion(f32[64,64]{1,0:T(8,128)} %shard_map.18, f32[64,768]{1,0:T(8,128)S(1)} %fusion.1, s32[768]{0:T(1024)S(1)} %fusion.39), kind=kOutput, calls=%fused_computation.2 | convolution fusion | flops 37896192 | bytes 412672 | tf_op jit(solution)/shard_map/dot_general | solution.py:15
  65.3 1.1 %fusion = f32[1,64,768]{2,1,0:T(8,128)} fusion(f32[64,768]{1,0:T(8,128)S(1)} %convolution_subtract_fusion.3, f32[64,64]{1,0:T(8,128)S(1)} %fusion.18, f32[64,768]{1,0:T(8,128)S(1)} %convolution_subtract_fusion.1), kind=kOutput, calls=%fused_computation.1 | convolution fusion | flops 37797888 | bytes 606208 | tf_op jit(solution)/shard_map/dot_general | solution.py:150
  (82 shorter events, 9.0 us)
Async XLA Ops:
  0.0 0.9 %copy-start = (f32[1,64,768]{2,1,0:T(8,128)S(1)}, f32[1,64,768]{2,1,0:T(8,128)}, u32[]{:S(2)}) copy-start(f32[1,64,768]{2,1,0:T(8,128)} %param.1) | copy-start | bytes 589828
  1.5 6.6 %collective-permute-start = (f32[64,128]{1,0:T(8,128)S(1)}, f32[64,128]{1,0:T(8,128)S(1)}, u32[]{:S(2)}, u32[]{:S(2)}) collective-permute-start(f32[64,128]{1,0:T(8,128)S(1)} %convolution_bitcast_fusion), channel_id=1, source_target_pairs={{0,2},{4,6},{8,10},{12,14},{16,18},{20,22},{24,26},{28,30}} | collective-permute-start | bytes 98312 | tf_op jit(solution)/shard_map/ppermute | solution.py:85
  6.3 5.2 %collective-permute-start.5 = (f32[64,768]{1,0:T(8,128)S(1)}, f32[64,768]{1,0:T(8,128)S(1)}, u32[]{:S(2)}, u32[]{:S(2)}) collective-permute-start(f32[64,768]{1,0:T(8,128)S(1)} %bitcast.76), channel_id=1, source_target_pairs={{0,2},{1,3},{4,6},{5,7},{8,10},{9,11},{12,14},{13,15},{16,18},{17,... | collective-permute-start | bytes 589832 | tf_op jit(solution)/shard_map/ppermute | solution.py:71
  8.0 3.6 %collective-permute-start.1 = (f32[64,128]{1,0:T(8,128)S(1)}, f32[64,128]{1,0:T(8,128)S(1)}, u32[]{:S(2)}, u32[]{:S(2)}) collective-permute-start(f32[64,128]{1,0:T(8,128)S(1)} %broadcast_select_fusion.5), channel_id=1, source_target_pairs={{0,1},{2,3},{4,5},{6,7},{8,9},{10,11},{12,13},{14,15},{16,17},{18,... | collective-permute-start | bytes 98312 | tf_op jit(solution)/shard_map/ppermute | solution.py:85
  11.5 5.7 %collective-permute-start.6 = (f32[64,768]{1,0:T(8,128)S(1)}, f32[64,768]{1,0:T(8,128)S(1)}, u32[]{:S(2)}, u32[]{:S(2)}) collective-permute-start(f32[64,768]{1,0:T(8,128)S(1)} %broadcast_select_fusion), channel_id=1, source_target_pairs={{0,1},{1,0},{2,3},{3,2},{4,5},{5,4},{6,7},{7,6},{8,9},{9,8},{10,11... | collective-permute-start | bytes 589832 | tf_op jit(solution)/shard_map/ppermute | solution.py:76
  11.6 4.0 %collective-permute-start.2 = (f32[64,128]{1,0:T(8,128)S(1)}, f32[64,128]{1,0:T(8,128)S(1)}, u32[]{:S(2)}, u32[]{:S(2)}) collective-permute-start(f32[64,128]{1,0:T(8,128)S(1)} %broadcast_select_fusion.6), channel_id=1, source_target_pairs={{0,4},{4,0},{8,12},{12,8},{16,20},{20,16},{24,28},{28,24},{1,5},{5... | collective-permute-start | bytes 98312 | tf_op jit(solution)/shard_map/ppermute | solution.py:29
  15.6 4.1 %collective-permute-start.3 = (f32[64,128]{1,0:T(8,128)S(1)}, f32[64,128]{1,0:T(8,128)S(1)}, u32[]{:S(2)}, u32[]{:S(2)}) collective-permute-start(f32[64,128]{1,0:T(8,128)S(1)} %add.70), channel_id=1, source_target_pairs={{0,8},{4,12},{8,0},{12,4},{16,24},{20,28},{24,16},{28,20},{1,9},{5... | collective-permute-start | bytes 98312 | tf_op jit(solution)/shard_map/ppermute | solution.py:29
  18.1 4.3 %collective-permute-start.7 = (f32[64,256]{1,0:T(8,128)S(1)}, f32[64,256]{1,0:T(8,128)S(1)}, u32[]{:S(2)}, u32[]{:S(2)}) collective-permute-start(f32[64,256]{1,0:T(8,128)S(1)} %pad_maximum_fusion.5), channel_id=1, source_target_pairs={{0,4},{4,0},{8,12},{12,8},{16,20},{20,16},{24,28},{28,24},{1,5},{5... | collective-permute-start | bytes 196616 | tf_op jit(solution)/shard_map/ppermute | solution.py:29
  19.7 4.9 %collective-permute-start.4 = (f32[64,128]{1,0:T(8,128)S(1)}, f32[64,128]{1,0:T(8,128)S(1)}, u32[]{:S(2)}, u32[]{:S(2)}) collective-permute-start(f32[64,128]{1,0:T(8,128)S(1)} %add.71), channel_id=1, source_target_pairs={{0,16},{4,20},{8,24},{12,28},{16,0},{20,4},{24,8},{28,12},{1,17},{... | collective-permute-start | bytes 98312 | tf_op jit(solution)/shard_map/ppermute | solution.py:29
  22.5 9.6 %collective-permute-start.8 = (f32[64,256]{1,0:T(8,128)S(1)}, f32[64,256]{1,0:T(8,128)S(1)}, u32[]{:S(2)}, u32[]{:S(2)}) collective-permute-start(f32[64,256]{1,0:T(8,128)S(1)} %fusion.49), channel_id=1, source_target_pairs={{0,8},{4,12},{8,0},{12,4},{16,24},{20,28},{24,16},{28,20},{1,9},{5... | collective-permute-start | bytes 196616 | tf_op jit(solution)/shard_map/ppermute | solution.py:29
  32.0 2.8 %copy-start.1 = (f32[64,64]{1,0:T(8,128)S(1)}, f32[64,64]{1,0:T(8,128)}, u32[]{:S(2)}) copy-start(f32[64,64]{1,0:T(8,128)} %shard_map.17) | copy-start | bytes 49156
  32.0 2.8 %copy-start.3 = (f32[64,128]{1,0:T(8,128)S(1)}, f32[64,128]{1,0:T(8,128)}, u32[]{:S(2)}) copy-start(f32[64,128]{1,0:T(8,128)} %add.72.head_ref) | copy-start | bytes 98308
  32.0 5.9 %collective-permute-start.9 = (f32[64,256]{1,0:T(8,128)S(1)}, f32[64,256]{1,0:T(8,128)S(1)}, u32[]{:S(2)}, u32[]{:S(2)}) collective-permute-start(f32[64,256]{1,0:T(8,128)S(1)} %add.74), channel_id=1, source_target_pairs={{0,16},{4,20},{8,24},{12,28},{16,0},{20,4},{24,8},{28,12},{1,17},{... | collective-permute-start | bytes 196616 | tf_op jit(solution)/shard_map/ppermute | solution.py:29
  40.7 4.0 %collective-permute-start.10 = (f32[64,128]{1,0:T(8,128)S(1)}, f32[64,128]{1,0:T(8,128)S(1)}, u32[]{:S(2)}, u32[]{:S(2)}) collective-permute-start(f32[64,128]{1,0:T(8,128)S(1)} %fusion.3), channel_id=1, source_target_pairs={{0,4},{4,0},{8,12},{12,8},{16,20},{20,16},{24,28},{28,24},{1,5},{5... | collective-permute-start | bytes 98312 | tf_op jit(solution)/shard_map/ppermute | solution.py:29
  41.9 4.3 %collective-permute-start.13 = (f32[64,128]{1,0:T(8,128)S(1)}, f32[64,128]{1,0:T(8,128)S(1)}, u32[]{:S(2)}, u32[]{:S(2)}) collective-permute-start(f32[64,128]{1,0:T(8,128)S(1)} %pad_maximum_fusion.6), channel_id=1, source_target_pairs={{0,4},{4,0},{8,12},{12,8},{16,20},{20,16},{24,28},{28,24},{1,5},{5... | collective-permute-start | bytes 98312 | tf_op jit(solution)/shard_map/ppermute | solution.py:29
  44.6 4.0 %collective-permute-start.11 = (f32[64,128]{1,0:T(8,128)S(1)}, f32[64,128]{1,0:T(8,128)S(1)}, u32[]{:S(2)}, u32[]{:S(2)}) collective-permute-start(f32[64,128]{1,0:T(8,128)S(1)} %add.76), channel_id=1, source_target_pairs={{0,8},{4,12},{8,0},{12,4},{16,24},{20,28},{24,16},{28,20},{1,9},{5... | collective-permute-start | bytes 98312 | tf_op jit(solution)/shard_map/ppermute | solution.py:29
  46.3 4.5 %collective-permute-start.14 = (f32[64,128]{1,0:T(8,128)S(1)}, f32[64,128]{1,0:T(8,128)S(1)}, u32[]{:S(2)}, u32[]{:S(2)}) collective-permute-start(f32[64,128]{1,0:T(8,128)S(1)} %fusion.123), channel_id=1, source_target_pairs={{0,8},{4,12},{8,0},{12,4},{16,24},{20,28},{24,16},{28,20},{1,9},{5... | collective-permute-start | bytes 98312 | tf_op jit(solution)/shard_map/ppermute | solution.py:29
  48.7 4.8 %collective-permute-start.12 = (f32[64,128]{1,0:T(8,128)S(1)}, f32[64,128]{1,0:T(8,128)S(1)}, u32[]{:S(2)}, u32[]{:S(2)}) collective-permute-start(f32[64,128]{1,0:T(8,128)S(1)} %add.77), channel_id=1, source_target_pairs={{0,16},{4,20},{8,24},{12,28},{16,0},{20,4},{24,8},{28,12},{1,17},{... | collective-permute-start | bytes 98312 | tf_op jit(solution)/shard_map/ppermute | solution.py:29
  50.7 11.6 %collective-permute-start.15 = (f32[64,128]{1,0:T(8,128)S(1)}, f32[64,128]{1,0:T(8,128)S(1)}, u32[]{:S(2)}, u32[]{:S(2)}) collective-permute-start(f32[64,128]{1,0:T(8,128)S(1)} %add.80), channel_id=1, source_target_pairs={{0,16},{4,20},{8,24},{12,28},{16,0},{20,4},{24,8},{28,12},{1,17},{... | collective-permute-start | bytes 98312 | tf_op jit(solution)/shard_map/ppermute | solution.py:29
  60.9 1.1 %copy-start.2 = (f32[64,64]{1,0:T(8,128)S(1)}, f32[64,64]{1,0:T(8,128)}, u32[]{:S(2)}) copy-start(f32[64,64]{1,0:T(8,128)} %shard_map.18) | copy-start | bytes 49156
  60.9 1.2 %copy-start.4 = (f32[64,128]{1,0:T(8,128)S(1)}, f32[64,128]{1,0:T(8,128)}, u32[]{:S(2)}) copy-start(f32[64,128]{1,0:T(8,128)} %add.78.head_ref) | copy-start | bytes 98308

commit v22 on v21

--- a/solution.py
+++ b/solution.py
@@ -145,9 +145,12 @@
         lower_inv = lower_inverse(head)
         top_block = apply_left(lower_inv, top_rows)
         inverse = invert_near_identity(identity - top_block.T)
-        reflect = units[1] - apply_left(lower_inv, panel_1)
         mixed = apply_left(inverse, unit_cur - apply_left(lower_inv, basis_cur))
-        current = current - jnp.dot(mixed.T, reflect, precision=HIGHEST_PRECISION)
+        weights = jnp.concatenate([mixed, -jnp.dot(lower_inv.T, mixed, precision=HIGHEST_PRECISION)])
+        current = current - lax.dot_general(
+            weights, jnp.concatenate([units[1], panel_1]), (((0,), (0,)), ((), ())),
+            precision=HIGHEST_PRECISION,
+        )
         return current.reshape(matrix.shape)
 
     return local

time: 66.7 us -> 67.4 us (1.010)
  local copies, waits for them, and re-layouts: 0.91 us -> 1.64 us
    dot_general x0 -> x2, matrix products: none -> 1.21 us  [the longest x1 1.05 us: local(): lax.dot_general(weights, jnp.concatenate([units[1], panel_1]), (((0,), (0...]
    dot_general x2 -> x1, matrix products: 1.43 us -> 0.37 us  [local(): current = current - jnp.dot(mixed.T, reflect, precision=HIGHEST_PRECISION)]
    unnamed x10, local copies, waits for them, and re-layouts: 0.91 us -> 1.64 us
    dot_general x38 -> x37, matrix products: 7.99 us -> 7.68 us  [apply_left(): return jnp.dot(square, right_side, precision=HIGHEST_PRECISION)]
where the time goes in v22:
time: 67.4 us; the launch traced here: 67 us
  starting transfers between devices  28.2 us (42%)
  Pallas kernels  13.6 us (20%)
  matrix products  12.1 us (18%)
  waiting for transfers between devices  9.21 us (14%)
  local copies, waits for them, and re-layouts  1.64 us (2%)
  other arithmetic  1.57 us (2%)
    ppermute x12, starting transfers between devices, butterfly_sum(): x = x + lax.ppermute(x, axis, [(i, i ^ step) for i in range(size)])  20.7 us
    pallas_call x2, Pallas kernels, lower_inverse(): pl.pallas_call(_eliminate_kernel, out_shape=jax.ShapeDtypeStruct((size, s...  13.6 us
    dot_general x37, matrix products, apply_left(): return jnp.dot(square, right_side, precision=HIGHEST_PRECISION)  7.68 us
    ppermute x12, waiting for transfers between devices, butterfly_sum(): x = x + lax.ppermute(x, axis, [(i, i ^ step) for i in range(size)])  6.67 us
    ppermute x2, starting transfers between devices, from_root(): lax.ppermute(value, axis, [(i, i + dist) for i in range(size) if i % (2 *...  6.15 us
    dot_general x6, matrix products, inner_rows(): lax.dot_general(left, right, (((1,), (1,)), ((), ())), precision=HIGHEST_...  2.51 us
    ppermute x1, waiting for transfers between devices, spread_pair(): lax.ppermute(have, axis, [(i, i + dist) for i in range(size) if i % (2 *...  2.18 us
    unnamed x10, local copies, waits for them, and re-layouts  1.64 us
  transfers between devices with their start and end apart: 16, of which 8 were waited for; matrix products, arithmetic and copies ran while one was open for 10% of the time, Pallas kernels for 20%

profile of v22, /device:TPU:0, one launch (start us, length us, event | category | flops | bytes accessed | tf_op | source)
XLA Modules:
  0.0 67.0 jit_solution(3923107499104728339)
XLA Ops:
  0.0 0.9 %copy-done = f32[1,64,768]{2,1,0:T(8,128)S(1)} copy-done((f32[1,64,768]{2,1,0:T(8,128)S(1)}, f32[1,64,768]{2,1,0:T(8,128)}, u32[]{:S(2)}) %copy-start) | copy-done | bytes 196632
  0.9 0.5 convolution_bitcast_fusion
  1.5 4.9 %collective-permute-start = (f32[64,128]{1,0:T(8,128)S(1)}, f32[64,128]{1,0:T(8,128)S(1)}, u32[]{:S(2)}, u32[]{:S(2)}) collective-permute-start(f32[64,128]{1,0:T(8,128)S(1)} %convolution_bitcast_fusion), channel_id=1, source_target_pairs={{0,2},{4,6},{8,10},{12,14},{16,18},{20,22},{24,26},{28,30}} | collective-permute-start | bytes 98312 | tf_op jit(solution)/shard_map/ppermute | solution.py:85
  6.3 1.3 %collective-permute-start.5 = (f32[64,768]{1,0:T(8,128)S(1)}, f32[64,768]{1,0:T(8,128)S(1)}, u32[]{:S(2)}, u32[]{:S(2)}) collective-permute-start(f32[64,768]{1,0:T(8,128)S(1)} %bitcast.74), channel_id=1, source_target_pairs={{0,2},{1,3},{4,6},{5,7},{8,10},{9,11},{12,14},{13,15},{16,18},{17,... | collective-permute-start | bytes 589832 | tf_op jit(solution)/shard_map/ppermute | solution.py:71
  8.0 1.3 %collective-permute-start.1 = (f32[64,128]{1,0:T(8,128)S(1)}, f32[64,128]{1,0:T(8,128)S(1)}, u32[]{:S(2)}, u32[]{:S(2)}) collective-permute-start(f32[64,128]{1,0:T(8,128)S(1)} %broadcast_select_fusion.5), channel_id=1, source_target_pairs={{0,1},{2,3},{4,5},{6,7},{8,9},{10,11},{12,13},{14,15},{16,17},{18,... | collective-permute-start | bytes 98312 | tf_op jit(solution)/shard_map/ppermute | solution.py:85
  9.3 2.2 %collective-permute-done.5 = f32[64,768]{1,0:T(8,128)S(1)} collective-permute-done((f32[64,768]{1,0:T(8,128)S(1)}, f32[64,768]{1,0:T(8,128)S(1)}, u32[]{:S(2)}, u32[]{:S(2)}) %collective-permute-start.5) | collective-permute-done | bytes 196640 | tf_op jit(solution)/shard_map/ppermute | solution.py:71
  11.6 1.6 %collective-permute-start.2 = (f32[64,128]{1,0:T(8,128)S(1)}, f32[64,128]{1,0:T(8,128)S(1)}, u32[]{:S(2)}, u32[]{:S(2)}) collective-permute-start(f32[64,128]{1,0:T(8,128)S(1)} %broadcast_select_fusion.6), channel_id=1, source_target_pairs={{0,4},{4,0},{8,12},{12,8},{16,20},{20,16},{24,28},{28,24},{1,5},{5... | collective-permute-start | bytes 98312 | tf_op jit(solution)/shard_map/ppermute | solution.py:29
  13.2 2.4 %collective-permute-done.2 = f32[64,128]{1,0:T(8,128)S(1)} collective-permute-done((f32[64,128]{1,0:T(8,128)S(1)}, f32[64,128]{1,0:T(8,128)S(1)}, u32[]{:S(2)}, u32[]{:S(2)}) %collective-permute-start.2) | collective-permute-done | bytes 32800 | tf_op jit(solution)/shard_map/ppermute | solution.py:29
  15.6 1.6 %collective-permute-start.3 = (f32[64,128]{1,0:T(8,128)S(1)}, f32[64,128]{1,0:T(8,128)S(1)}, u32[]{:S(2)}, u32[]{:S(2)}) collective-permute-start(f32[64,128]{1,0:T(8,128)S(1)} %add.70), channel_id=1, source_target_pairs={{0,8},{4,12},{8,0},{12,4},{16,24},{20,28},{24,16},{28,20},{1,9},{5... | collective-permute-start | bytes 98312 | tf_op jit(solution)/shard_map/ppermute | solution.py:29
  17.6 0.5 fusion.11
  18.1 1.6 %collective-permute-start.7 = (f32[64,256]{1,0:T(8,128)S(1)}, f32[64,256]{1,0:T(8,128)S(1)}, u32[]{:S(2)}, u32[]{:S(2)}) collective-permute-start(f32[64,256]{1,0:T(8,128)S(1)} %pad_maximum_fusion.5), channel_id=1, source_target_pairs={{0,4},{4,0},{8,12},{12,8},{16,20},{20,16},{24,28},{28,24},{1,5},{5... | collective-permute-start | bytes 196616 | tf_op jit(solution)/shard_map/ppermute | solution.py:29
  19.7 2.7 %collective-permute-start.4 = (f32[64,128]{1,0:T(8,128)S(1)}, f32[64,128]{1,0:T(8,128)S(1)}, u32[]{:S(2)}, u32[]{:S(2)}) collective-permute-start(f32[64,128]{1,0:T(8,128)S(1)} %add.71), channel_id=1, source_target_pairs={{0,16},{4,20},{8,24},{12,28},{16,0},{20,4},{24,8},{28,12},{1,17},{... | collective-permute-start | bytes 98312 | tf_op jit(solution)/shard_map/ppermute | solution.py:29
  22.5 1.3 %collective-permute-start.8 = (f32[64,256]{1,0:T(8,128)S(1)}, f32[64,256]{1,0:T(8,128)S(1)}, u32[]{:S(2)}, u32[]{:S(2)}) collective-permute-start(f32[64,256]{1,0:T(8,128)S(1)} %fusion.56), channel_id=1, source_target_pairs={{0,8},{4,12},{8,0},{12,4},{16,24},{20,28},{24,16},{28,20},{1,9},{5... | collective-permute-start | bytes 196616 | tf_op jit(solution)/shard_map/ppermute | solution.py:29
  23.8 0.8 %collective-permute-done.4 = f32[64,128]{1,0:T(8,128)S(1)} collective-permute-done((f32[64,128]{1,0:T(8,128)S(1)}, f32[64,128]{1,0:T(8,128)S(1)}, u32[]{:S(2)}, u32[]{:S(2)}) %collective-permute-start.4) | collective-permute-done | bytes 32800 | tf_op jit(solution)/shard_map/ppermute | solution.py:29
  24.6 0.6 add.72.head_ref
  25.2 6.8 %shard_map.17 = f32[64,64]{1,0:T(8,128)} custom-call(f32[64,128]{1,0:T(8,128)} %add.72.head_ref), custom_call_target="tpu_custom_call" | custom-call | tf_op jit(solution)/shard_map/pallas_call | solution.py:61
  32.0 2.8 %collective-permute-start.9 = (f32[64,256]{1,0:T(8,128)S(1)}, f32[64,256]{1,0:T(8,128)S(1)}, u32[]{:S(2)}, u32[]{:S(2)}) collective-permute-start(f32[64,256]{1,0:T(8,128)S(1)} %add.74), channel_id=1, source_target_pairs={{0,16},{4,20},{8,24},{12,28},{16,0},{20,4},{24,8},{28,12},{1,17},{... | collective-permute-start | bytes 196616 | tf_op jit(solution)/shard_map/ppermute | solution.py:29
  40.1 0.5 fusion.3
  40.6 1.2 %collective-permute-start.10 = (f32[64,128]{1,0:T(8,128)S(1)}, f32[64,128]{1,0:T(8,128)S(1)}, u32[]{:S(2)}, u32[]{:S(2)}) collective-permute-start(f32[64,128]{1,0:T(8,128)S(1)} %fusion.3), channel_id=1, source_target_pairs={{0,4},{4,0},{8,12},{12,8},{16,20},{20,16},{24,28},{28,24},{1,5},{5... | collective-permute-start | bytes 98312 | tf_op jit(solution)/shard_map/ppermute | solution.py:29
  41.9 0.9 %collective-permute-start.13 = (f32[64,128]{1,0:T(8,128)S(1)}, f32[64,128]{1,0:T(8,128)S(1)}, u32[]{:S(2)}, u32[]{:S(2)}) collective-permute-start(f32[64,128]{1,0:T(8,128)S(1)} %pad_maximum_fusion.6), channel_id=1, source_target_pairs={{0,4},{4,0},{8,12},{12,8},{16,20},{20,16},{24,28},{28,24},{1,5},{5... | collective-permute-start | bytes 98312 | tf_op jit(solution)/shard_map/ppermute | solution.py:29
  42.8 1.8 %collective-permute-done.10 = f32[64,128]{1,0:T(8,128)S(1)} collective-permute-done((f32[64,128]{1,0:T(8,128)S(1)}, f32[64,128]{1,0:T(8,128)S(1)}, u32[]{:S(2)}, u32[]{:S(2)}) %collective-permute-start.10) | collective-permute-done | bytes 32800 | tf_op jit(solution)/shard_map/ppermute | solution.py:29
  44.6 1.6 %collective-permute-start.11 = (f32[64,128]{1,0:T(8,128)S(1)}, f32[64,128]{1,0:T(8,128)S(1)}, u32[]{:S(2)}, u32[]{:S(2)}) collective-permute-start(f32[64,128]{1,0:T(8,128)S(1)} %add.76), channel_id=1, source_target_pairs={{0,8},{4,12},{8,0},{12,4},{16,24},{20,28},{24,16},{28,20},{1,9},{5... | collective-permute-start | bytes 98312 | tf_op jit(solution)/shard_map/ppermute | solution.py:29
  46.3 1.5 %collective-permute-start.14 = (f32[64,128]{1,0:T(8,128)S(1)}, f32[64,128]{1,0:T(8,128)S(1)}, u32[]{:S(2)}, u32[]{:S(2)}) collective-permute-start(f32[64,128]{1,0:T(8,128)S(1)} %fusion.128), channel_id=1, source_target_pairs={{0,8},{4,12},{8,0},{12,4},{16,24},{20,28},{24,16},{28,20},{1,9},{5... | collective-permute-start | bytes 98312 | tf_op jit(solution)/shard_map/ppermute | solution.py:29
  47.7 0.9 %collective-permute-done.11 = f32[64,128]{1,0:T(8,128)S(1)} collective-permute-done((f32[64,128]{1,0:T(8,128)S(1)}, f32[64,128]{1,0:T(8,128)S(1)}, u32[]{:S(2)}, u32[]{:S(2)}) %collective-permute-start.11) | collective-permute-done | bytes 32800 | tf_op jit(solution)/shard_map/ppermute | solution.py:29
  48.6 2.1 %collective-permute-start.12 = (f32[64,128]{1,0:T(8,128)S(1)}, f32[64,128]{1,0:T(8,128)S(1)}, u32[]{:S(2)}, u32[]{:S(2)}) collective-permute-start(f32[64,128]{1,0:T(8,128)S(1)} %add.77), channel_id=1, source_target_pairs={{0,16},{4,20},{8,24},{12,28},{16,0},{20,4},{24,8},{28,12},{1,17},{... | collective-permute-start | bytes 98312 | tf_op jit(solution)/shard_map/ppermute | solution.py:29
  50.7 2.1 %collective-permute-start.15 = (f32[64,128]{1,0:T(8,128)S(1)}, f32[64,128]{1,0:T(8,128)S(1)}, u32[]{:S(2)}, u32[]{:S(2)}) collective-permute-start(f32[64,128]{1,0:T(8,128)S(1)} %add.80), channel_id=1, source_target_pairs={{0,16},{4,20},{8,24},{12,28},{16,0},{20,4},{24,8},{28,12},{1,17},{... | collective-permute-start | bytes 98312 | tf_op jit(solution)/shard_map/ppermute | solution.py:29
  52.8 0.6 collective-permute-done.12
  53.5 0.6 add.78.head_ref
  54.1 6.9 %shard_map.18 = f32[64,64]{1,0:T(8,128)} custom-call(f32[64,128]{1,0:T(8,128)} %add.78.head_ref), custom_call_target="tpu_custom_call" | custom-call | tf_op jit(solution)/shard_map/pallas_call | solution.py:61
  60.9 1.1 %fusion.22 = f32[64,64]{1,0:T(8,128)S(1)} fusion(f32[64,64]{1,0:T(8,128)} %shard_map.18, f32[64,128]{1,0:T(8,128)S(1)} %copy-done.4), kind=kOutput, calls=%fused_computation.55 | convolution fusion | flops 3145728 | bytes 65536 | tf_op jit(solution)/shard_map/dot_general | solution.py:15
  62.0 0.7 %copy-done.2 = f32[64,64]{1,0:T(8,128)S(1)} copy-done((f32[64,64]{1,0:T(8,128)S(1)}, f32[64,64]{1,0:T(8,128)}, u32[]{:S(2)}) %copy-start.2) | copy-done | bytes 16408
  65.9 1.0 %fusion = f32[1,64,768]{2,1,0:T(8,128)} fusion(f32[64,768]{1,0:T(8,128)S(1)} %convolution_subtract_fusion.2, f32[64,768]{1,0:T(8,128)S(1)} %fusion.1, f32[64,768]{1,0:T(8,128)S(1)} %fusion.13, f32[64,64]{0,1:T(8,128)S(1)} %convolution_negate_fusion, f32[64,64]{0,1:T(8,128)S(1)} %fusion.21), kind=kOutput, calls=%fused_computation.1 | convolution fusion | flops 75653120 | bytes 819200 | tf_op jit(solution)/shard_map/dot_general | solution.py:150
  (82 shorter events, 9.3 us)
Async XLA Ops:
  0.0 0.9 %copy-start = (f32[1,64,768]{2,1,0:T(8,128)S(1)}, f32[1,64,768]{2,1,0:T(8,128)}, u32[]{:S(2)}) copy-start(f32[1,64,768]{2,1,0:T(8,128)} %param.1) | copy-start | bytes 589828
  1.5 6.6 %collective-permute-start = (f32[64,128]{1,0:T(8,128)S(1)}, f32[64,128]{1,0:T(8,128)S(1)}, u32[]{:S(2)}, u32[]{:S(2)}) collective-permute-start(f32[64,128]{1,0:T(8,128)S(1)} %convolution_bitcast_fusion), channel_id=1, source_target_pairs={{0,2},{4,6},{8,10},{12,14},{16,18},{20,22},{24,26},{28,30}} | collective-permute-start | bytes 98312 | tf_op jit(solution)/shard_map/ppermute | solution.py:85
  6.3 5.2 %collective-permute-start.5 = (f32[64,768]{1,0:T(8,128)S(1)}, f32[64,768]{1,0:T(8,128)S(1)}, u32[]{:S(2)}, u32[]{:S(2)}) collective-permute-start(f32[64,768]{1,0:T(8,128)S(1)} %bitcast.74), channel_id=1, source_target_pairs={{0,2},{1,3},{4,6},{5,7},{8,10},{9,11},{12,14},{13,15},{16,18},{17,... | collective-permute-start | bytes 589832 | tf_op jit(solution)/shard_map/ppermute | solution.py:71
  8.0 3.6 %collective-permute-start.1 = (f32[64,128]{1,0:T(8,128)S(1)}, f32[64,128]{1,0:T(8,128)S(1)}, u32[]{:S(2)}, u32[]{:S(2)}) collective-permute-start(f32[64,128]{1,0:T(8,128)S(1)} %broadcast_select_fusion.5), channel_id=1, source_target_pairs={{0,1},{2,3},{4,5},{6,7},{8,9},{10,11},{12,13},{14,15},{16,17},{18,... | collective-permute-start | bytes 98312 | tf_op jit(solution)/shard_map/ppermute | solution.py:85
  11.5 5.7 %collective-permute-start.6 = (f32[64,768]{1,0:T(8,128)S(1)}, f32[64,768]{1,0:T(8,128)S(1)}, u32[]{:S(2)}, u32[]{:S(2)}) collective-permute-start(f32[64,768]{1,0:T(8,128)S(1)} %broadcast_select_fusion), channel_id=1, source_target_pairs={{0,1},{1,0},{2,3},{3,2},{4,5},{5,4},{6,7},{7,6},{8,9},{9,8},{10,11... | collective-permute-start | bytes 589832 | tf_op jit(solution)/shard_map/ppermute | solution.py:76
  11.6 4.0 %collective-permute-start.2 = (f32[64,128]{1,0:T(8,128)S(1)}, f32[64,128]{1,0:T(8,128)S(1)}, u32[]{:S(2)}, u32[]{:S(2)}) collective-permute-start(f32[64,128]{1,0:T(8,128)S(1)} %broadcast_select_fusion.6), channel_id=1, source_target_pairs={{0,4},{4,0},{8,12},{12,8},{16,20},{20,16},{24,28},{28,24},{1,5},{5... | collective-permute-start | bytes 98312 | tf_op jit(solution)/shard_map/ppermute | solution.py:29
  15.6 4.1 %collective-permute-start.3 = (f32[64,128]{1,0:T(8,128)S(1)}, f32[64,128]{1,0:T(8,128)S(1)}, u32[]{:S(2)}, u32[]{:S(2)}) collective-permute-start(f32[64,128]{1,0:T(8,128)S(1)} %add.70), channel_id=1, source_target_pairs={{0,8},{4,12},{8,0},{12,4},{16,24},{20,28},{24,16},{28,20},{1,9},{5... | collective-permute-start | bytes 98312 | tf_op jit(solution)/shard_map/ppermute | solution.py:29
  18.1 4.3 %collective-permute-start.7 = (f32[64,256]{1,0:T(8,128)S(1)}, f32[64,256]{1,0:T(8,128)S(1)}, u32[]{:S(2)}, u32[]{:S(2)}) collective-permute-start(f32[64,256]{1,0:T(8,128)S(1)} %pad_maximum_fusion.5), channel_id=1, source_target_pairs={{0,4},{4,0},{8,12},{12,8},{16,20},{20,16},{24,28},{28,24},{1,5},{5... | collective-permute-start | bytes 196616 | tf_op jit(solution)/shard_map/ppermute | solution.py:29
  19.7 4.9 %collective-permute-start.4 = (f32[64,128]{1,0:T(8,128)S(1)}, f32[64,128]{1,0:T(8,128)S(1)}, u32[]{:S(2)}, u32[]{:S(2)}) collective-permute-start(f32[64,128]{1,0:T(8,128)S(1)} %add.71), channel_id=1, source_target_pairs={{0,16},{4,20},{8,24},{12,28},{16,0},{20,4},{24,8},{28,12},{1,17},{... | collective-permute-start | bytes 98312 | tf_op jit(solution)/shard_map/ppermute | solution.py:29
  22.5 9.6 %collective-permute-start.8 = (f32[64,256]{1,0:T(8,128)S(1)}, f32[64,256]{1,0:T(8,128)S(1)}, u32[]{:S(2)}, u32[]{:S(2)}) collective-permute-start(f32[64,256]{1,0:T(8,128)S(1)} %fusion.56), channel_id=1, source_target_pairs={{0,8},{4,12},{8,0},{12,4},{16,24},{20,28},{24,16},{28,20},{1,9},{5... | collective-permute-start | bytes 196616 | tf_op jit(solution)/shard_map/ppermute | solution.py:29
  32.0 2.8 %copy-start.1 = (f32[64,64]{1,0:T(8,128)S(1)}, f32[64,64]{1,0:T(8,128)}, u32[]{:S(2)}) copy-start(f32[64,64]{1,0:T(8,128)} %shard_map.17) | copy-start | bytes 49156
  32.0 2.8 %copy-start.3 = (f32[64,128]{1,0:T(8,128)S(1)}, f32[64,128]{1,0:T(8,128)}, u32[]{:S(2)}) copy-start(f32[64,128]{1,0:T(8,128)} %add.72.head_ref) | copy-start | bytes 98308
  32.0 5.9 %collective-permute-start.9 = (f32[64,256]{1,0:T(8,128)S(1)}, f32[64,256]{1,0:T(8,128)S(1)}, u32[]{:S(2)}, u32[]{:S(2)}) collective-permute-start(f32[64,256]{1,0:T(8,128)S(1)} %add.74), channel_id=1, source_target_pairs={{0,16},{4,20},{8,24},{12,28},{16,0},{20,4},{24,8},{28,12},{1,17},{... | collective-permute-start | bytes 196616 | tf_op jit(solution)/shard_map/ppermute | solution.py:29
  40.6 4.0 %collective-permute-start.10 = (f32[64,128]{1,0:T(8,128)S(1)}, f32[64,128]{1,0:T(8,128)S(1)}, u32[]{:S(2)}, u32[]{:S(2)}) collective-permute-start(f32[64,128]{1,0:T(8,128)S(1)} %fusion.3), channel_id=1, source_target_pairs={{0,4},{4,0},{8,12},{12,8},{16,20},{20,16},{24,28},{28,24},{1,5},{5... | collective-permute-start | bytes 98312 | tf_op jit(solution)/shard_map/ppermute | solution.py:29
  41.9 4.3 %collective-permute-start.13 = (f32[64,128]{1,0:T(8,128)S(1)}, f32[64,128]{1,0:T(8,128)S(1)}, u32[]{:S(2)}, u32[]{:S(2)}) collective-permute-start(f32[64,128]{1,0:T(8,128)S(1)} %pad_maximum_fusion.6), channel_id=1, source_target_pairs={{0,4},{4,0},{8,12},{12,8},{16,20},{20,16},{24,28},{28,24},{1,5},{5... | collective-permute-start | bytes 98312 | tf_op jit(solution)/shard_map/ppermute | solution.py:29
  44.6 4.0 %collective-permute-start.11 = (f32[64,128]{1,0:T(8,128)S(1)}, f32[64,128]{1,0:T(8,128)S(1)}, u32[]{:S(2)}, u32[]{:S(2)}) collective-permute-start(f32[64,128]{1,0:T(8,128)S(1)} %add.76), channel_id=1, source_target_pairs={{0,8},{4,12},{8,0},{12,4},{16,24},{20,28},{24,16},{28,20},{1,9},{5... | collective-permute-start | bytes 98312 | tf_op jit(solution)/shard_map/ppermute | solution.py:29
  46.3 4.4 %collective-permute-start.14 = (f32[64,128]{1,0:T(8,128)S(1)}, f32[64,128]{1,0:T(8,128)S(1)}, u32[]{:S(2)}, u32[]{:S(2)}) collective-permute-start(f32[64,128]{1,0:T(8,128)S(1)} %fusion.128), channel_id=1, source_target_pairs={{0,8},{4,12},{8,0},{12,4},{16,24},{20,28},{24,16},{28,20},{1,9},{5... | collective-permute-start | bytes 98312 | tf_op jit(solution)/shard_map/ppermute | solution.py:29
  48.6 4.8 %collective-permute-start.12 = (f32[64,128]{1,0:T(8,128)S(1)}, f32[64,128]{1,0:T(8,128)S(1)}, u32[]{:S(2)}, u32[]{:S(2)}) collective-permute-start(f32[64,128]{1,0:T(8,128)S(1)} %add.77), channel_id=1, source_target_pairs={{0,16},{4,20},{8,24},{12,28},{16,0},{20,4},{24,8},{28,12},{1,17},{... | collective-permute-start | bytes 98312 | tf_op jit(solution)/shard_map/ppermute | solution.py:29
  50.7 11.3 %collective-permute-start.15 = (f32[64,128]{1,0:T(8,128)S(1)}, f32[64,128]{1,0:T(8,128)S(1)}, u32[]{:S(2)}, u32[]{:S(2)}) collective-permute-start(f32[64,128]{1,0:T(8,128)S(1)} %add.80), channel_id=1, source_target_pairs={{0,16},{4,20},{8,24},{12,28},{16,0},{20,4},{24,8},{28,12},{1,17},{... | collective-permute-start | bytes 98312 | tf_op jit(solution)/shard_map/ppermute | solution.py:29
  54.1 6.9 %copy-start.4 = (f32[64,128]{1,0:T(8,128)S(1)}, f32[64,128]{1,0:T(8,128)}, u32[]{:S(2)}) copy-start(f32[64,128]{1,0:T(8,128)} %add.78.head_ref) | copy-start | bytes 98308
  62.0 0.8 %copy-start.2 = (f32[64,64]{1,0:T(8,128)S(1)}, f32[64,64]{1,0:T(8,128)}, u32[]{:S(2)}) copy-start(f32[64,64]{1,0:T(8,128)} %shard_map.18) | copy-start | bytes 49156

commit v23 on v21

--- a/solution.py
+++ b/solution.py
@@ -145,9 +145,9 @@
         lower_inv = lower_inverse(head)
         top_block = apply_left(lower_inv, top_rows)
         inverse = invert_near_identity(identity - top_block.T)
-        reflect = units[1] - apply_left(lower_inv, panel_1)
+        reflect = units[1] - jnp.dot(lower_inv, panel_1, precision=lax.Precision.HIGH)
         mixed = apply_left(inverse, unit_cur - apply_left(lower_inv, basis_cur))
-        current = current - jnp.dot(mixed.T, reflect, precision=HIGHEST_PRECISION)
+        current = current - jnp.dot(mixed.T, reflect, precision=lax.Precision.HIGH)
         return current.reshape(matrix.shape)
 
     return local

time: 66.7 us -> 66.6 us (level)
    dot_general x0 -> x2, matrix products: none -> 2.02 us  [the longest x1 1.05 us: local(): jnp.dot(lower_inv, panel_1, precision=lax.Precision.HIGH)]
    dot_general x38 -> x37, matrix products: 7.99 us -> 6.86 us  [apply_left(): return jnp.dot(square, right_side, precision=HIGHEST_PRECISION)]
    dot_general x2 -> x1, matrix products: 1.43 us -> 0.37 us  [local(): current = current - jnp.dot(mixed.T, reflect, precision=HIGHEST_PRECISION)]
  transfers between devices with their start and end apart: 16 -> 16, of which waited for: 8 -> 8; matrix products, arithmetic and copies ran while one was open for 10% -> 10% of each run, Pallas kernels for 20% -> 21%
where the time goes in v23:
time: 66.6 us; the launch traced here: 66.2 us
  starting transfers between devices  28.2 us (42%)
  Pallas kernels  13.6 us (20%)
  matrix products  12.1 us (18%)
  waiting for transfers between devices  9.21 us (14%)
  other arithmetic  1.57 us (2%)
  local copies, waits for them, and re-layouts  0.91 us (1%)
    ppermute x12, starting transfers between devices, butterfly_sum(): x = x + lax.ppermute(x, axis, [(i, i ^ step) for i in range(size)])  20.7 us
    pallas_call x2, Pallas kernels, lower_inverse(): pl.pallas_call(_eliminate_kernel, out_shape=jax.ShapeDtypeStruct((size, s...  13.6 us
    dot_general x37, matrix products, apply_left(): return jnp.dot(square, right_side, precision=HIGHEST_PRECISION)  6.86 us
    ppermute x12, waiting for transfers between devices, butterfly_sum(): x = x + lax.ppermute(x, axis, [(i, i ^ step) for i in range(size)])  6.67 us
    ppermute x2, starting transfers between devices, from_root(): lax.ppermute(value, axis, [(i, i + dist) for i in range(size) if i % (2 *...  6.15 us
    dot_general x6, matrix products, inner_rows(): lax.dot_general(left, right, (((1,), (1,)), ((), ())), precision=HIGHEST_...  2.52 us
    ppermute x1, waiting for transfers between devices, spread_pair(): lax.ppermute(have, axis, [(i, i + dist) for i in range(size) if i % (2 *...  2.18 us
    add x12, other arithmetic, butterfly_sum(): x = x + lax.ppermute(x, axis, [(i, i ^ step) for i in range(size)])  1.38 us
  transfers between devices with their start and end apart: 16, of which 8 were waited for; matrix products, arithmetic and copies ran while one was open for 10% of the time, Pallas kernels for 21%

profile of v23, /device:TPU:0, one launch (start us, length us, event | category | flops | bytes accessed | tf_op | source)
XLA Modules:
  0.0 66.2 jit_solution(12247903914062322518)
XLA Ops:
  0.0 0.9 %copy-done = f32[1,64,768]{2,1,0:T(8,128)S(1)} copy-done((f32[1,64,768]{2,1,0:T(8,128)S(1)}, f32[1,64,768]{2,1,0:T(8,128)}, u32[]{:S(2)}) %copy-start) | copy-done | bytes 196632
  0.9 0.5 convolution_bitcast_fusion
  1.5 4.9 %collective-permute-start = (f32[64,128]{1,0:T(8,128)S(1)}, f32[64,128]{1,0:T(8,128)S(1)}, u32[]{:S(2)}, u32[]{:S(2)}) collective-permute-start(f32[64,128]{1,0:T(8,128)S(1)} %convolution_bitcast_fusion), channel_id=1, source_target_pairs={{0,2},{4,6},{8,10},{12,14},{16,18},{20,22},{24,26},{28,30}} | collective-permute-start | bytes 98312 | tf_op jit(solution)/shard_map/ppermute | solution.py:85
  6.3 1.3 %collective-permute-start.5 = (f32[64,768]{1,0:T(8,128)S(1)}, f32[64,768]{1,0:T(8,128)S(1)}, u32[]{:S(2)}, u32[]{:S(2)}) collective-permute-start(f32[64,768]{1,0:T(8,128)S(1)} %bitcast.76), channel_id=1, source_target_pairs={{0,2},{1,3},{4,6},{5,7},{8,10},{9,11},{12,14},{13,15},{16,18},{17,... | collective-permute-start | bytes 589832 | tf_op jit(solution)/shard_map/ppermute | solution.py:71
  8.0 1.3 %collective-permute-start.1 = (f32[64,128]{1,0:T(8,128)S(1)}, f32[64,128]{1,0:T(8,128)S(1)}, u32[]{:S(2)}, u32[]{:S(2)}) collective-permute-start(f32[64,128]{1,0:T(8,128)S(1)} %broadcast_select_fusion.5), channel_id=1, source_target_pairs={{0,1},{2,3},{4,5},{6,7},{8,9},{10,11},{12,13},{14,15},{16,17},{18,... | collective-permute-start | bytes 98312 | tf_op jit(solution)/shard_map/ppermute | solution.py:85
  9.3 2.2 %collective-permute-done.5 = f32[64,768]{1,0:T(8,128)S(1)} collective-permute-done((f32[64,768]{1,0:T(8,128)S(1)}, f32[64,768]{1,0:T(8,128)S(1)}, u32[]{:S(2)}, u32[]{:S(2)}) %collective-permute-start.5) | collective-permute-done | bytes 196640 | tf_op jit(solution)/shard_map/ppermute | solution.py:71
  11.6 1.6 %collective-permute-start.2 = (f32[64,128]{1,0:T(8,128)S(1)}, f32[64,128]{1,0:T(8,128)S(1)}, u32[]{:S(2)}, u32[]{:S(2)}) collective-permute-start(f32[64,128]{1,0:T(8,128)S(1)} %broadcast_select_fusion.6), channel_id=1, source_target_pairs={{0,4},{4,0},{8,12},{12,8},{16,20},{20,16},{24,28},{28,24},{1,5},{5... | collective-permute-start | bytes 98312 | tf_op jit(solution)/shard_map/ppermute | solution.py:29
  13.2 2.4 %collective-permute-done.2 = f32[64,128]{1,0:T(8,128)S(1)} collective-permute-done((f32[64,128]{1,0:T(8,128)S(1)}, f32[64,128]{1,0:T(8,128)S(1)}, u32[]{:S(2)}, u32[]{:S(2)}) %collective-permute-start.2) | collective-permute-done | bytes 32800 | tf_op jit(solution)/shard_map/ppermute | solution.py:29
  15.6 1.6 %collective-permute-start.3 = (f32[64,128]{1,0:T(8,128)S(1)}, f32[64,128]{1,0:T(8,128)S(1)}, u32[]{:S(2)}, u32[]{:S(2)}) collective-permute-start(f32[64,128]{1,0:T(8,128)S(1)} %add.70), channel_id=1, source_target_pairs={{0,8},{4,12},{8,0},{12,4},{16,24},{20,28},{24,16},{28,20},{1,9},{5... | collective-permute-start | bytes 98312 | tf_op jit(solution)/shard_map/ppermute | solution.py:29
  17.6 0.5 fusion.8
  18.1 1.6 %collective-permute-start.7 = (f32[64,256]{1,0:T(8,128)S(1)}, f32[64,256]{1,0:T(8,128)S(1)}, u32[]{:S(2)}, u32[]{:S(2)}) collective-permute-start(f32[64,256]{1,0:T(8,128)S(1)} %pad_maximum_fusion.5), channel_id=1, source_target_pairs={{0,4},{4,0},{8,12},{12,8},{16,20},{20,16},{24,28},{28,24},{1,5},{5... | collective-permute-start | bytes 196616 | tf_op jit(solution)/shard_map/ppermute | solution.py:29
  19.7 2.7 %collective-permute-start.4 = (f32[64,128]{1,0:T(8,128)S(1)}, f32[64,128]{1,0:T(8,128)S(1)}, u32[]{:S(2)}, u32[]{:S(2)}) collective-permute-start(f32[64,128]{1,0:T(8,128)S(1)} %add.71), channel_id=1, source_target_pairs={{0,16},{4,20},{8,24},{12,28},{16,0},{20,4},{24,8},{28,12},{1,17},{... | collective-permute-start | bytes 98312 | tf_op jit(solution)/shard_map/ppermute | solution.py:29
  22.5 1.3 %collective-permute-start.8 = (f32[64,256]{1,0:T(8,128)S(1)}, f32[64,256]{1,0:T(8,128)S(1)}, u32[]{:S(2)}, u32[]{:S(2)}) collective-permute-start(f32[64,256]{1,0:T(8,128)S(1)} %fusion.49), channel_id=1, source_target_pairs={{0,8},{4,12},{8,0},{12,4},{16,24},{20,28},{24,16},{28,20},{1,9},{5... | collective-permute-start | bytes 196616 | tf_op jit(solution)/shard_map/ppermute | solution.py:29
  23.8 0.8 %collective-permute-done.4 = f32[64,128]{1,0:T(8,128)S(1)} collective-permute-done((f32[64,128]{1,0:T(8,128)S(1)}, f32[64,128]{1,0:T(8,128)S(1)}, u32[]{:S(2)}, u32[]{:S(2)}) %collective-permute-start.4) | collective-permute-done | bytes 32800 | tf_op jit(solution)/shard_map/ppermute | solution.py:29
  24.6 0.6 add.72.head_ref
  25.2 6.8 %shard_map.17 = f32[64,64]{1,0:T(8,128)} custom-call(f32[64,128]{1,0:T(8,128)} %add.72.head_ref), custom_call_target="tpu_custom_call" | custom-call | tf_op jit(solution)/shard_map/pallas_call | solution.py:61
  32.0 2.8 %collective-permute-start.9 = (f32[64,256]{1,0:T(8,128)S(1)}, f32[64,256]{1,0:T(8,128)S(1)}, u32[]{:S(2)}, u32[]{:S(2)}) collective-permute-start(f32[64,256]{1,0:T(8,128)S(1)} %add.74), channel_id=1, source_target_pairs={{0,16},{4,20},{8,24},{12,28},{16,0},{20,4},{24,8},{28,12},{1,17},{... | collective-permute-start | bytes 196616 | tf_op jit(solution)/shard_map/ppermute | solution.py:29
  39.4 0.4 fusion.1
  40.1 0.5 fusion.3
  40.7 1.2 %collective-permute-start.10 = (f32[64,128]{1,0:T(8,128)S(1)}, f32[64,128]{1,0:T(8,128)S(1)}, u32[]{:S(2)}, u32[]{:S(2)}) collective-permute-start(f32[64,128]{1,0:T(8,128)S(1)} %fusion.3), channel_id=1, source_target_pairs={{0,4},{4,0},{8,12},{12,8},{16,20},{20,16},{24,28},{28,24},{1,5},{5... | collective-permute-start | bytes 98312 | tf_op jit(solution)/shard_map/ppermute | solution.py:29
  41.9 0.9 %collective-permute-start.13 = (f32[64,128]{1,0:T(8,128)S(1)}, f32[64,128]{1,0:T(8,128)S(1)}, u32[]{:S(2)}, u32[]{:S(2)}) collective-permute-start(f32[64,128]{1,0:T(8,128)S(1)} %pad_maximum_fusion.6), channel_id=1, source_target_pairs={{0,4},{4,0},{8,12},{12,8},{16,20},{20,16},{24,28},{28,24},{1,5},{5... | collective-permute-start | bytes 98312 | tf_op jit(solution)/shard_map/ppermute | solution.py:29
  42.8 1.8 %collective-permute-done.10 = f32[64,128]{1,0:T(8,128)S(1)} collective-permute-done((f32[64,128]{1,0:T(8,128)S(1)}, f32[64,128]{1,0:T(8,128)S(1)}, u32[]{:S(2)}, u32[]{:S(2)}) %collective-permute-start.10) | collective-permute-done | bytes 32800 | tf_op jit(solution)/shard_map/ppermute | solution.py:29
  44.6 1.6 %collective-permute-start.11 = (f32[64,128]{1,0:T(8,128)S(1)}, f32[64,128]{1,0:T(8,128)S(1)}, u32[]{:S(2)}, u32[]{:S(2)}) collective-permute-start(f32[64,128]{1,0:T(8,128)S(1)} %add.76), channel_id=1, source_target_pairs={{0,8},{4,12},{8,0},{12,4},{16,24},{20,28},{24,16},{28,20},{1,9},{5... | collective-permute-start | bytes 98312 | tf_op jit(solution)/shard_map/ppermute | solution.py:29
  46.3 1.5 %collective-permute-start.14 = (f32[64,128]{1,0:T(8,128)S(1)}, f32[64,128]{1,0:T(8,128)S(1)}, u32[]{:S(2)}, u32[]{:S(2)}) collective-permute-start(f32[64,128]{1,0:T(8,128)S(1)} %fusion.123), channel_id=1, source_target_pairs={{0,8},{4,12},{8,0},{12,4},{16,24},{20,28},{24,16},{28,20},{1,9},{5... | collective-permute-start | bytes 98312 | tf_op jit(solution)/shard_map/ppermute | solution.py:29
  47.7 0.9 %collective-permute-done.11 = f32[64,128]{1,0:T(8,128)S(1)} collective-permute-done((f32[64,128]{1,0:T(8,128)S(1)}, f32[64,128]{1,0:T(8,128)S(1)}, u32[]{:S(2)}, u32[]{:S(2)}) %collective-permute-start.11) | collective-permute-done | bytes 32800 | tf_op jit(solution)/shard_map/ppermute | solution.py:29
  48.7 2.1 %collective-permute-start.12 = (f32[64,128]{1,0:T(8,128)S(1)}, f32[64,128]{1,0:T(8,128)S(1)}, u32[]{:S(2)}, u32[]{:S(2)}) collective-permute-start(f32[64,128]{1,0:T(8,128)S(1)} %add.77), channel_id=1, source_target_pairs={{0,16},{4,20},{8,24},{12,28},{16,0},{20,4},{24,8},{28,12},{1,17},{... | collective-permute-start | bytes 98312 | tf_op jit(solution)/shard_map/ppermute | solution.py:29
  50.7 2.1 %collective-permute-start.15 = (f32[64,128]{1,0:T(8,128)S(1)}, f32[64,128]{1,0:T(8,128)S(1)}, u32[]{:S(2)}, u32[]{:S(2)}) collective-permute-start(f32[64,128]{1,0:T(8,128)S(1)} %add.80), channel_id=1, source_target_pairs={{0,16},{4,20},{8,24},{12,28},{16,0},{20,4},{24,8},{28,12},{1,17},{... | collective-permute-start | bytes 98312 | tf_op jit(solution)/shard_map/ppermute | solution.py:29
  52.8 0.6 collective-permute-done.12
  53.5 0.6 add.78.head_ref
  54.1 6.8 %shard_map.18 = f32[64,64]{1,0:T(8,128)} custom-call(f32[64,128]{1,0:T(8,128)} %add.78.head_ref), custom_call_target="tpu_custom_call" | custom-call | tf_op jit(solution)/shard_map/pallas_call | solution.py:61
  60.9 1.0 %convolution_subtract_fusion.1 = f32[64,768]{1,0:T(8,128)S(1)} fusion(f32[64,64]{1,0:T(8,128)} %shard_map.18, f32[64,768]{1,0:T(8,128)S(1)} %fusion.1, s32[768]{0:T(1024)S(1)} %fusion.39), kind=kOutput, calls=%fused_computation.2 | convolution fusion | flops 19021824 | bytes 412672 | tf_op jit(solution)/shard_map/dot_general | solution.py:148
  65.2 1.0 %fusion = f32[1,64,768]{2,1,0:T(8,128)} fusion(f32[64,768]{1,0:T(8,128)S(1)} %convolution_subtract_fusion.3, f32[64,64]{1,0:T(8,128)S(1)} %fusion.18, f32[64,768]{1,0:T(8,128)S(1)} %convolution_subtract_fusion.1), kind=kOutput, calls=%fused_computation.1 | convolution fusion | flops 18923520 | bytes 606208 | tf_op jit(solution)/shard_map/dot_general | solution.py:150
  (82 shorter events, 9.0 us)
Async XLA Ops:
  0.0 0.9 %copy-start = (f32[1,64,768]{2,1,0:T(8,128)S(1)}, f32[1,64,768]{2,1,0:T(8,128)}, u32[]{:S(2)}) copy-start(f32[1,64,768]{2,1,0:T(8,128)} %param.1) | copy-start | bytes 589828
  1.5 6.6 %collective-permute-start = (f32[64,128]{1,0:T(8,128)S(1)}, f32[64,128]{1,0:T(8,128)S(1)}, u32[]{:S(2)}, u32[]{:S(2)}) collective-permute-start(f32[64,128]{1,0:T(8,128)S(1)} %convolution_bitcast_fusion), channel_id=1, source_target_pairs={{0,2},{4,6},{8,10},{12,14},{16,18},{20,22},{24,26},{28,30}} | collective-permute-start | bytes 98312 | tf_op jit(solution)/shard_map/ppermute | solution.py:85
  6.3 5.2 %collective-permute-start.5 = (f32[64,768]{1,0:T(8,128)S(1)}, f32[64,768]{1,0:T(8,128)S(1)}, u32[]{:S(2)}, u32[]{:S(2)}) collective-permute-start(f32[64,768]{1,0:T(8,128)S(1)} %bitcast.76), channel_id=1, source_target_pairs={{0,2},{1,3},{4,6},{5,7},{8,10},{9,11},{12,14},{13,15},{16,18},{17,... | collective-permute-start | bytes 589832 | tf_op jit(solution)/shard_map/ppermute | solution.py:71
  8.0 3.6 %collective-permute-start.1 = (f32[64,128]{1,0:T(8,128)S(1)}, f32[64,128]{1,0:T(8,128)S(1)}, u32[]{:S(2)}, u32[]{:S(2)}) collective-permute-start(f32[64,128]{1,0:T(8,128)S(1)} %broadcast_select_fusion.5), channel_id=1, source_target_pairs={{0,1},{2,3},{4,5},{6,7},{8,9},{10,11},{12,13},{14,15},{16,17},{18,... | collective-permute-start | bytes 98312 | tf_op jit(solution)/shard_map/ppermute | solution.py:85
  11.5 5.7 %collective-permute-start.6 = (f32[64,768]{1,0:T(8,128)S(1)}, f32[64,768]{1,0:T(8,128)S(1)}, u32[]{:S(2)}, u32[]{:S(2)}) collective-permute-start(f32[64,768]{1,0:T(8,128)S(1)} %broadcast_select_fusion), channel_id=1, source_target_pairs={{0,1},{1,0},{2,3},{3,2},{4,5},{5,4},{6,7},{7,6},{8,9},{9,8},{10,11... | collective-permute-start | bytes 589832 | tf_op jit(solution)/shard_map/ppermute | solution.py:76
  11.6 4.0 %collective-permute-start.2 = (f32[64,128]{1,0:T(8,128)S(1)}, f32[64,128]{1,0:T(8,128)S(1)}, u32[]{:S(2)}, u32[]{:S(2)}) collective-permute-start(f32[64,128]{1,0:T(8,128)S(1)} %broadcast_select_fusion.6), channel_id=1, source_target_pairs={{0,4},{4,0},{8,12},{12,8},{16,20},{20,16},{24,28},{28,24},{1,5},{5... | collective-permute-start | bytes 98312 | tf_op jit(solution)/shard_map/ppermute | solution.py:29
  15.6 4.1 %collective-permute-start.3 = (f32[64,128]{1,0:T(8,128)S(1)}, f32[64,128]{1,0:T(8,128)S(1)}, u32[]{:S(2)}, u32[]{:S(2)}) collective-permute-start(f32[64,128]{1,0:T(8,128)S(1)} %add.70), channel_id=1, source_target_pairs={{0,8},{4,12},{8,0},{12,4},{16,24},{20,28},{24,16},{28,20},{1,9},{5... | collective-permute-start | bytes 98312 | tf_op jit(solution)/shard_map/ppermute | solution.py:29
  18.1 4.3 %collective-permute-start.7 = (f32[64,256]{1,0:T(8,128)S(1)}, f32[64,256]{1,0:T(8,128)S(1)}, u32[]{:S(2)}, u32[]{:S(2)}) collective-permute-start(f32[64,256]{1,0:T(8,128)S(1)} %pad_maximum_fusion.5), channel_id=1, source_target_pairs={{0,4},{4,0},{8,12},{12,8},{16,20},{20,16},{24,28},{28,24},{1,5},{5... | collective-permute-start | bytes 196616 | tf_op jit(solution)/shard_map/ppermute | solution.py:29
  19.7 4.9 %collective-permute-start.4 = (f32[64,128]{1,0:T(8,128)S(1)}, f32[64,128]{1,0:T(8,128)S(1)}, u32[]{:S(2)}, u32[]{:S(2)}) collective-permute-start(f32[64,128]{1,0:T(8,128)S(1)} %add.71), channel_id=1, source_target_pairs={{0,16},{4,20},{8,24},{12,28},{16,0},{20,4},{24,8},{28,12},{1,17},{... | collective-permute-start | bytes 98312 | tf_op jit(solution)/shard_map/ppermute | solution.py:29
  22.5 9.6 %collective-permute-start.8 = (f32[64,256]{1,0:T(8,128)S(1)}, f32[64,256]{1,0:T(8,128)S(1)}, u32[]{:S(2)}, u32[]{:S(2)}) collective-permute-start(f32[64,256]{1,0:T(8,128)S(1)} %fusion.49), channel_id=1, source_target_pairs={{0,8},{4,12},{8,0},{12,4},{16,24},{20,28},{24,16},{28,20},{1,9},{5... | collective-permute-start | bytes 196616 | tf_op jit(solution)/shard_map/ppermute | solution.py:29
  32.0 2.8 %copy-start.1 = (f32[64,64]{1,0:T(8,128)S(1)}, f32[64,64]{1,0:T(8,128)}, u32[]{:S(2)}) copy-start(f32[64,64]{1,0:T(8,128)} %shard_map.17) | copy-start | bytes 49156
  32.0 2.8 %copy-start.3 = (f32[64,128]{1,0:T(8,128)S(1)}, f32[64,128]{1,0:T(8,128)}, u32[]{:S(2)}) copy-start(f32[64,128]{1,0:T(8,128)} %add.72.head_ref) | copy-start | bytes 98308
  32.0 5.9 %collective-permute-start.9 = (f32[64,256]{1,0:T(8,128)S(1)}, f32[64,256]{1,0:T(8,128)S(1)}, u32[]{:S(2)}, u32[]{:S(2)}) collective-permute-start(f32[64,256]{1,0:T(8,128)S(1)} %add.74), channel_id=1, source_target_pairs={{0,16},{4,20},{8,24},{12,28},{16,0},{20,4},{24,8},{28,12},{1,17},{... | collective-permute-start | bytes 196616 | tf_op jit(solution)/shard_map/ppermute | solution.py:29
  40.7 4.0 %collective-permute-start.10 = (f32[64,128]{1,0:T(8,128)S(1)}, f32[64,128]{1,0:T(8,128)S(1)}, u32[]{:S(2)}, u32[]{:S(2)}) collective-permute-start(f32[64,128]{1,0:T(8,128)S(1)} %fusion.3), channel_id=1, source_target_pairs={{0,4},{4,0},{8,12},{12,8},{16,20},{20,16},{24,28},{28,24},{1,5},{5... | collective-permute-start | bytes 98312 | tf_op jit(solution)/shard_map/ppermute | solution.py:29
  41.9 4.3 %collective-permute-start.13 = (f32[64,128]{1,0:T(8,128)S(1)}, f32[64,128]{1,0:T(8,128)S(1)}, u32[]{:S(2)}, u32[]{:S(2)}) collective-permute-start(f32[64,128]{1,0:T(8,128)S(1)} %pad_maximum_fusion.6), channel_id=1, source_target_pairs={{0,4},{4,0},{8,12},{12,8},{16,20},{20,16},{24,28},{28,24},{1,5},{5... | collective-permute-start | bytes 98312 | tf_op jit(solution)/shard_map/ppermute | solution.py:29
  44.6 4.0 %collective-permute-start.11 = (f32[64,128]{1,0:T(8,128)S(1)}, f32[64,128]{1,0:T(8,128)S(1)}, u32[]{:S(2)}, u32[]{:S(2)}) collective-permute-start(f32[64,128]{1,0:T(8,128)S(1)} %add.76), channel_id=1, source_target_pairs={{0,8},{4,12},{8,0},{12,4},{16,24},{20,28},{24,16},{28,20},{1,9},{5... | collective-permute-start | bytes 98312 | tf_op jit(solution)/shard_map/ppermute | solution.py:29
  46.3 4.5 %collective-permute-start.14 = (f32[64,128]{1,0:T(8,128)S(1)}, f32[64,128]{1,0:T(8,128)S(1)}, u32[]{:S(2)}, u32[]{:S(2)}) collective-permute-start(f32[64,128]{1,0:T(8,128)S(1)} %fusion.123), channel_id=1, source_target_pairs={{0,8},{4,12},{8,0},{12,4},{16,24},{20,28},{24,16},{28,20},{1,9},{5... | collective-permute-start | bytes 98312 | tf_op jit(solution)/shard_map/ppermute | solution.py:29
  48.7 4.8 %collective-permute-start.12 = (f32[64,128]{1,0:T(8,128)S(1)}, f32[64,128]{1,0:T(8,128)S(1)}, u32[]{:S(2)}, u32[]{:S(2)}) collective-permute-start(f32[64,128]{1,0:T(8,128)S(1)} %add.77), channel_id=1, source_target_pairs={{0,16},{4,20},{8,24},{12,28},{16,0},{20,4},{24,8},{28,12},{1,17},{... | collective-permute-start | bytes 98312 | tf_op jit(solution)/shard_map/ppermute | solution.py:29
  50.7 11.5 %collective-permute-start.15 = (f32[64,128]{1,0:T(8,128)S(1)}, f32[64,128]{1,0:T(8,128)S(1)}, u32[]{:S(2)}, u32[]{:S(2)}) collective-permute-start(f32[64,128]{1,0:T(8,128)S(1)} %add.80), channel_id=1, source_target_pairs={{0,16},{4,20},{8,24},{12,28},{16,0},{20,4},{24,8},{28,12},{1,17},{... | collective-permute-start | bytes 98312 | tf_op jit(solution)/shard_map/ppermute | solution.py:29
  60.9 1.1 %copy-start.2 = (f32[64,64]{1,0:T(8,128)S(1)}, f32[64,64]{1,0:T(8,128)}, u32[]{:S(2)}) copy-start(f32[64,64]{1,0:T(8,128)} %shard_map.18) | copy-start | bytes 49156
  60.9 1.1 %copy-start.4 = (f32[64,128]{1,0:T(8,128)S(1)}, f32[64,128]{1,0:T(8,128)}, u32[]{:S(2)}) copy-start(f32[64,128]{1,0:T(8,128)} %add.78.head_ref) | copy-start | bytes 98308

commit v24 on v21

--- a/solution.py
+++ b/solution.py
@@ -117,14 +117,13 @@
         tail = jnp.concatenate([inner_rows(panel_0, both), inner_rows(units[0], both)], axis=1)
         steps = butterfly_steps(rows_size)
         tail = butterfly_sum(tail, "rows", rows_size, None if steps is None else steps[:-1])
-        lower_inv, tail = lax.optimization_barrier((lower_inverse(head), tail))
+        lower_inv = lower_inverse(head)
+        inverse = invert_near_identity(identity - apply_left(lower_inv, head[:, width:]).T)
+        lower_inv, inverse, tail = lax.optimization_barrier((lower_inv, inverse, tail))
         tail = butterfly_sum(tail, "rows", rows_size, None if steps is None else steps[-1:])
-        top_rows = head[:, width:]
         basis_cur, basis_sec, unit_cur, unit_sec = (
             tail[:, i * width:(i + 1) * width] for i in range(4)
         )
-        top_block = apply_left(lower_inv, top_rows)
-        inverse = invert_near_identity(identity - top_block.T)
         reflect = units[0] - apply_left(lower_inv, panel_0)
         mixed = apply_left(inverse, unit_cur - apply_left(lower_inv, basis_cur))
         mixed_sec = apply_left(inverse, unit_sec - apply_left(lower_inv, basis_sec))

time: 66.7 us -> 82 us (1.23)
  waiting for transfers between devices: 9.21 us -> 19.6 us
  starting transfers between devices: 28.2 us -> 32.2 us
    ppermute x12, waiting for transfers between devices: 6.67 us -> 16.8 us  [butterfly_sum(): x = x + lax.ppermute(x, axis, [(i, i ^ step) for i in range(size)])]
    ppermute x1, starting transfers between devices: 1.3 us -> 4.23 us  [spread_pair(): lax.ppermute(have, axis, [(i, i + dist) for i in range(size) if i % (2 *...]
    ppermute x1, waiting for transfers between devices: 2.18 us -> 0.01 us  [spread_pair(): lax.ppermute(have, axis, [(i, i + dist) for i in range(size) if i % (2 *...]
    ppermute x1, waiting for transfers between devices: 0.01 us -> 1.26 us  [spread_pair(): other = lax.ppermute(have, axis, [(i, i ^ 1) for i in range(size)])]
    ppermute x2, waiting for transfers between devices: 0.35 us -> 1.57 us  [from_root(): lax.ppermute(value, axis, [(i, i + dist) for i in range(size) if i % (2 *...]
    ppermute x12, starting transfers between devices: 20.7 us -> 21.7 us  [butterfly_sum(): x = x + lax.ppermute(x, axis, [(i, i ^ step) for i in range(size)])]
  transfers between devices with their start and end apart: 16 -> 16, of which waited for: 8 -> 10; matrix products, arithmetic and copies ran while one was open for 10% -> 8% of each run, Pallas kernels for 20% -> 17%
where the time goes in v24:
time: 82 us; the launch traced here: 81.5 us
  starting transfers between devices  32.2 us (39%)
  waiting for transfers between devices  19.6 us (24%)
  Pallas kernels  13.6 us (17%)
  matrix products  13 us (16%)
  other arithmetic  1.57 us (2%)
  local copies, waits for them, and re-layouts  0.91 us (1%)
    ppermute x12, starting transfers between devices, butterfly_sum(): x = x + lax.ppermute(x, axis, [(i, i ^ step) for i in range(size)])  21.7 us
    ppermute x12, waiting for transfers between devices, butterfly_sum(): x = x + lax.ppermute(x, axis, [(i, i ^ step) for i in range(size)])  16.8 us
    pallas_call x2, Pallas kernels, lower_inverse(): pl.pallas_call(_eliminate_kernel, out_shape=jax.ShapeDtypeStruct((size, s...  13.6 us
    dot_general x38, matrix products, apply_left(): return jnp.dot(square, right_side, precision=HIGHEST_PRECISION)  8.73 us
    ppermute x2, starting transfers between devices, from_root(): lax.ppermute(value, axis, [(i, i + dist) for i in range(size) if i % (2 *...  6.15 us
    ppermute x1, starting transfers between devices, spread_pair(): lax.ppermute(have, axis, [(i, i + dist) for i in range(size) if i % (2 *...  4.23 us
    dot_general x6, matrix products, inner_rows(): lax.dot_general(left, right, (((1,), (1,)), ((), ())), precision=HIGHEST_...  2.51 us
  transfers between devices with their start and end apart: 16, of which 10 were waited for; matrix products, arithmetic and copies ran while one was open for 8% of the time, Pallas kernels for 17%

profile of v24, /device:TPU:0, one launch (start us, length us, event | category | flops | bytes accessed | tf_op | source)
XLA Modules:
  0.0 81.5 jit_solution(1266740382068615032)
XLA Ops:
  0.0 0.9 %copy-done = f32[1,64,768]{2,1,0:T(8,128)S(1)} copy-done((f32[1,64,768]{2,1,0:T(8,128)S(1)}, f32[1,64,768]{2,1,0:T(8,128)}, u32[]{:S(2)}) %copy-start) | copy-done | bytes 196632
  1.5 4.9 %collective-permute-start = (f32[64,128]{1,0:T(8,128)S(1)}, f32[64,128]{1,0:T(8,128)S(1)}, u32[]{:S(2)}, u32[]{:S(2)}) collective-permute-start(f32[64,128]{1,0:T(8,128)S(1)} %convolution_bitcast_fusion), channel_id=1, source_target_pairs={{0,2},{4,6},{8,10},{12,14},{16,18},{20,22},{24,26},{28,30}} | collective-permute-start | bytes 98312 | tf_op jit(solution)/shard_map/ppermute | solution.py:85
  6.4 1.6 %collective-permute-done = f32[64,128]{1,0:T(8,128)S(1)} collective-permute-done((f32[64,128]{1,0:T(8,128)S(1)}, f32[64,128]{1,0:T(8,128)S(1)}, u32[]{:S(2)}, u32[]{:S(2)}) %collective-permute-start) | collective-permute-done | bytes 32800 | tf_op jit(solution)/shard_map/ppermute | solution.py:85
  7.9 1.3 %collective-permute-start.1 = (f32[64,128]{1,0:T(8,128)S(1)}, f32[64,128]{1,0:T(8,128)S(1)}, u32[]{:S(2)}, u32[]{:S(2)}) collective-permute-start(f32[64,128]{1,0:T(8,128)S(1)} %broadcast_select_fusion.5), channel_id=1, source_target_pairs={{0,1},{2,3},{4,5},{6,7},{8,9},{10,11},{12,13},{14,15},{16,17},{18,... | collective-permute-start | bytes 98312 | tf_op jit(solution)/shard_map/ppermute | solution.py:85
  9.2 4.2 %collective-permute-start.5 = (f32[64,768]{1,0:T(8,128)S(1)}, f32[64,768]{1,0:T(8,128)S(1)}, u32[]{:S(2)}, u32[]{:S(2)}) collective-permute-start(f32[64,768]{1,0:T(8,128)S(1)} %bitcast.76), channel_id=1, source_target_pairs={{0,2},{1,3},{4,6},{5,7},{8,10},{9,11},{12,14},{13,15},{16,18},{17,... | collective-permute-start | bytes 589832 | tf_op jit(solution)/shard_map/ppermute | solution.py:71
  13.5 1.6 %collective-permute-start.2 = (f32[64,128]{1,0:T(8,128)S(1)}, f32[64,128]{1,0:T(8,128)S(1)}, u32[]{:S(2)}, u32[]{:S(2)}) collective-permute-start(f32[64,128]{1,0:T(8,128)S(1)} %broadcast_select_fusion.6), channel_id=1, source_target_pairs={{0,4},{4,0},{8,12},{12,8},{16,20},{20,16},{24,28},{28,24},{1,5},{5... | collective-permute-start | bytes 98312 | tf_op jit(solution)/shard_map/ppermute | solution.py:29
  15.0 2.4 %collective-permute-done.2 = f32[64,128]{1,0:T(8,128)S(1)} collective-permute-done((f32[64,128]{1,0:T(8,128)S(1)}, f32[64,128]{1,0:T(8,128)S(1)}, u32[]{:S(2)}, u32[]{:S(2)}) %collective-permute-start.2) | collective-permute-done | bytes 32800 | tf_op jit(solution)/shard_map/ppermute | solution.py:29
  17.5 1.6 %collective-permute-start.3 = (f32[64,128]{1,0:T(8,128)S(1)}, f32[64,128]{1,0:T(8,128)S(1)}, u32[]{:S(2)}, u32[]{:S(2)}) collective-permute-start(f32[64,128]{1,0:T(8,128)S(1)} %add.70), channel_id=1, source_target_pairs={{0,8},{4,12},{8,0},{12,4},{16,24},{20,28},{24,16},{28,20},{1,9},{5... | collective-permute-start | bytes 98312 | tf_op jit(solution)/shard_map/ppermute | solution.py:29
  19.1 2.3 %collective-permute-done.3 = f32[64,128]{1,0:T(8,128)S(1)} collective-permute-done((f32[64,128]{1,0:T(8,128)S(1)}, f32[64,128]{1,0:T(8,128)S(1)}, u32[]{:S(2)}, u32[]{:S(2)}) %collective-permute-start.3) | collective-permute-done | bytes 32800 | tf_op jit(solution)/shard_map/ppermute | solution.py:29
  21.4 2.6 %collective-permute-start.4 = (f32[64,128]{1,0:T(8,128)S(1)}, f32[64,128]{1,0:T(8,128)S(1)}, u32[]{:S(2)}, u32[]{:S(2)}) collective-permute-start(f32[64,128]{1,0:T(8,128)S(1)} %add.71), channel_id=1, source_target_pairs={{0,16},{4,20},{8,24},{12,28},{16,0},{20,4},{24,8},{28,12},{1,17},{... | collective-permute-start | bytes 98312 | tf_op jit(solution)/shard_map/ppermute | solution.py:29
  24.0 2.2 %collective-permute-done.4 = f32[64,128]{1,0:T(8,128)S(1)} collective-permute-done((f32[64,128]{1,0:T(8,128)S(1)}, f32[64,128]{1,0:T(8,128)S(1)}, u32[]{:S(2)}, u32[]{:S(2)}) %collective-permute-start.4) | collective-permute-done | bytes 32800 | tf_op jit(solution)/shard_map/ppermute | solution.py:29
  26.2 0.6 add.72.head_ref
  26.8 6.9 %shard_map.17 = f32[64,64]{1,0:T(8,128)} custom-call(f32[64,128]{1,0:T(8,128)} %add.72.head_ref), custom_call_target="tpu_custom_call" | custom-call | tf_op jit(solution)/shard_map/pallas_call | solution.py:61
  33.7 1.1 %fusion.27 = f32[64,64]{1,0:T(8,128)S(1)} fusion(f32[64,64]{1,0:T(8,128)} %shard_map.17, f32[64,128]{1,0:T(8,128)S(1)} %copy-done.4), kind=kOutput, calls=%fused_computation.62 | convolution fusion | flops 3145728 | bytes 65536 | tf_op jit(solution)/shard_map/dot_general | solution.py:15
  37.0 1.3 %collective-permute-done.6 = f32[64,768]{1,0:T(8,128)S(1)} collective-permute-done((f32[64,768]{1,0:T(8,128)S(1)}, f32[64,768]{1,0:T(8,128)S(1)}, u32[]{:S(2)}, u32[]{:S(2)}) %collective-permute-start.6) | collective-permute-done | bytes 196640 | tf_op jit(solution)/shard_map/ppermute | solution.py:76
  39.2 1.6 %collective-permute-start.7 = (f32[64,256]{1,0:T(8,128)S(1)}, f32[64,256]{1,0:T(8,128)S(1)}, u32[]{:S(2)}, u32[]{:S(2)}) collective-permute-start(f32[64,256]{1,0:T(8,128)S(1)} %pad_maximum_fusion.5), channel_id=1, source_target_pairs={{0,4},{4,0},{8,12},{12,8},{16,20},{20,16},{24,28},{28,24},{1,5},{5... | collective-permute-start | bytes 196616 | tf_op jit(solution)/shard_map/ppermute | solution.py:29
  40.9 2.6 %collective-permute-done.7 = f32[64,256]{1,0:T(8,128)S(1)} collective-permute-done((f32[64,256]{1,0:T(8,128)S(1)}, f32[64,256]{1,0:T(8,128)S(1)}, u32[]{:S(2)}, u32[]{:S(2)}) %collective-permute-start.7) | collective-permute-done | bytes 65568 | tf_op jit(solution)/shard_map/ppermute | solution.py:29
  43.6 1.6 %collective-permute-start.8 = (f32[64,256]{1,0:T(8,128)S(1)}, f32[64,256]{1,0:T(8,128)S(1)}, u32[]{:S(2)}, u32[]{:S(2)}) collective-permute-start(f32[64,256]{1,0:T(8,128)S(1)} %fusion.49), channel_id=1, source_target_pairs={{0,8},{4,12},{8,0},{12,4},{16,24},{20,28},{24,16},{28,20},{1,9},{5... | collective-permute-start | bytes 196616 | tf_op jit(solution)/shard_map/ppermute | solution.py:29
  45.4 2.5 %collective-permute-done.8 = f32[64,256]{1,0:T(8,128)S(1)} collective-permute-done((f32[64,256]{1,0:T(8,128)S(1)}, f32[64,256]{1,0:T(8,128)S(1)}, u32[]{:S(2)}, u32[]{:S(2)}) %collective-permute-start.8) | collective-permute-done | bytes 65568 | tf_op jit(solution)/shard_map/ppermute | solution.py:29
  47.9 2.7 %collective-permute-start.9 = (f32[64,256]{1,0:T(8,128)S(1)}, f32[64,256]{1,0:T(8,128)S(1)}, u32[]{:S(2)}, u32[]{:S(2)}) collective-permute-start(f32[64,256]{1,0:T(8,128)S(1)} %add.74), channel_id=1, source_target_pairs={{0,16},{4,20},{8,24},{12,28},{16,0},{20,4},{24,8},{28,12},{1,17},{... | collective-permute-start | bytes 196616 | tf_op jit(solution)/shard_map/ppermute | solution.py:29
  50.9 2.2 %collective-permute-done.9 = f32[64,256]{1,0:T(8,128)S(1)} collective-permute-done((f32[64,256]{1,0:T(8,128)S(1)}, f32[64,256]{1,0:T(8,128)S(1)}, u32[]{:S(2)}, u32[]{:S(2)}) %collective-permute-start.9) | collective-permute-done | bytes 65568 | tf_op jit(solution)/shard_map/ppermute | solution.py:29
  55.8 1.6 %collective-permute-start.10 = (f32[64,128]{1,0:T(8,128)S(1)}, f32[64,128]{1,0:T(8,128)S(1)}, u32[]{:S(2)}, u32[]{:S(2)}) collective-permute-start(f32[64,128]{1,0:T(8,128)S(1)} %fusion.3), channel_id=1, source_target_pairs={{0,4},{4,0},{8,12},{12,8},{16,20},{20,16},{24,28},{28,24},{1,5},{5... | collective-permute-start | bytes 98312 | tf_op jit(solution)/shard_map/ppermute | solution.py:29
  58.0 1.8 %collective-permute-done.10 = f32[64,128]{1,0:T(8,128)S(1)} collective-permute-done((f32[64,128]{1,0:T(8,128)S(1)}, f32[64,128]{1,0:T(8,128)S(1)}, u32[]{:S(2)}, u32[]{:S(2)}) %collective-permute-start.10) | collective-permute-done | bytes 32800 | tf_op jit(solution)/shard_map/ppermute | solution.py:29
  59.8 1.6 %collective-permute-start.11 = (f32[64,128]{1,0:T(8,128)S(1)}, f32[64,128]{1,0:T(8,128)S(1)}, u32[]{:S(2)}, u32[]{:S(2)}) collective-permute-start(f32[64,128]{1,0:T(8,128)S(1)} %add.76), channel_id=1, source_target_pairs={{0,8},{4,12},{8,0},{12,4},{16,24},{20,28},{24,16},{28,20},{1,9},{5... | collective-permute-start | bytes 98312 | tf_op jit(solution)/shard_map/ppermute | solution.py:29
  61.5 1.6 %collective-permute-start.14 = (f32[64,128]{1,0:T(8,128)S(1)}, f32[64,128]{1,0:T(8,128)S(1)}, u32[]{:S(2)}, u32[]{:S(2)}) collective-permute-start(f32[64,128]{1,0:T(8,128)S(1)} %fusion.123), channel_id=1, source_target_pairs={{0,8},{4,12},{8,0},{12,4},{16,24},{20,28},{24,16},{28,20},{1,9},{5... | collective-permute-start | bytes 98312 | tf_op jit(solution)/shard_map/ppermute | solution.py:29
  63.1 0.7 collective-permute-done.11
  63.7 3.0 %collective-permute-start.12 = (f32[64,128]{1,0:T(8,128)S(1)}, f32[64,128]{1,0:T(8,128)S(1)}, u32[]{:S(2)}, u32[]{:S(2)}) collective-permute-start(f32[64,128]{1,0:T(8,128)S(1)} %add.77), channel_id=1, source_target_pairs={{0,16},{4,20},{8,24},{12,28},{16,0},{20,4},{24,8},{28,12},{1,17},{... | collective-permute-start | bytes 98312 | tf_op jit(solution)/shard_map/ppermute | solution.py:29
  66.8 1.9 %collective-permute-start.15 = (f32[64,128]{1,0:T(8,128)S(1)}, f32[64,128]{1,0:T(8,128)S(1)}, u32[]{:S(2)}, u32[]{:S(2)}) collective-permute-start(f32[64,128]{1,0:T(8,128)S(1)} %add.80), channel_id=1, source_target_pairs={{0,16},{4,20},{8,24},{12,28},{16,0},{20,4},{24,8},{28,12},{1,17},{... | collective-permute-start | bytes 98312 | tf_op jit(solution)/shard_map/ppermute | solution.py:29
  68.6 0.6 add.78.head_ref
  69.3 6.8 %shard_map.18 = f32[64,64]{1,0:T(8,128)} custom-call(f32[64,128]{1,0:T(8,128)} %add.78.head_ref), custom_call_target="tpu_custom_call" | custom-call | tf_op jit(solution)/shard_map/pallas_call | solution.py:61
  76.1 1.1 %convolution_subtract_fusion.1 = f32[64,768]{1,0:T(8,128)S(1)} fusion(f32[64,64]{1,0:T(8,128)} %shard_map.18, f32[64,768]{1,0:T(8,128)S(1)} %fusion.1, s32[768]{0:T(1024)S(1)} %fusion.39), kind=kOutput, calls=%fused_computation.2 | convolution fusion | flops 37896192 | bytes 412672 | tf_op jit(solution)/shard_map/dot_general | solution.py:15
  80.4 1.1 %fusion = f32[1,64,768]{2,1,0:T(8,128)} fusion(f32[64,768]{1,0:T(8,128)S(1)} %convolution_subtract_fusion.3, f32[64,64]{1,0:T(8,128)S(1)} %fusion.18, f32[64,768]{1,0:T(8,128)S(1)} %convolution_subtract_fusion.1), kind=kOutput, calls=%fused_computation.1 | convolution fusion | flops 37797888 | bytes 606208 | tf_op jit(solution)/shard_map/dot_general | solution.py:149
  (82 shorter events, 10.8 us)
Async XLA Ops:
  0.0 0.9 %copy-start = (f32[1,64,768]{2,1,0:T(8,128)S(1)}, f32[1,64,768]{2,1,0:T(8,128)}, u32[]{:S(2)}) copy-start(f32[1,64,768]{2,1,0:T(8,128)} %param.1) | copy-start | bytes 589828
  1.5 6.5 %collective-permute-start = (f32[64,128]{1,0:T(8,128)S(1)}, f32[64,128]{1,0:T(8,128)S(1)}, u32[]{:S(2)}, u32[]{:S(2)}) collective-permute-start(f32[64,128]{1,0:T(8,128)S(1)} %convolution_bitcast_fusion), channel_id=1, source_target_pairs={{0,2},{4,6},{8,10},{12,14},{16,18},{20,22},{24,26},{28,30}} | collective-permute-start | bytes 98312 | tf_op jit(solution)/shard_map/ppermute | solution.py:85
  7.9 5.5 %collective-permute-start.1 = (f32[64,128]{1,0:T(8,128)S(1)}, f32[64,128]{1,0:T(8,128)S(1)}, u32[]{:S(2)}, u32[]{:S(2)}) collective-permute-start(f32[64,128]{1,0:T(8,128)S(1)} %broadcast_select_fusion.5), channel_id=1, source_target_pairs={{0,1},{2,3},{4,5},{6,7},{8,9},{10,11},{12,13},{14,15},{16,17},{18,... | collective-permute-start | bytes 98312 | tf_op jit(solution)/shard_map/ppermute | solution.py:85
  9.2 27.5 %collective-permute-start.5 = (f32[64,768]{1,0:T(8,128)S(1)}, f32[64,768]{1,0:T(8,128)S(1)}, u32[]{:S(2)}, u32[]{:S(2)}) collective-permute-start(f32[64,768]{1,0:T(8,128)S(1)} %bitcast.76), channel_id=1, source_target_pairs={{0,2},{1,3},{4,6},{5,7},{8,10},{9,11},{12,14},{13,15},{16,18},{17,... | collective-permute-start | bytes 589832 | tf_op jit(solution)/shard_map/ppermute | solution.py:71
  13.5 4.0 %collective-permute-start.2 = (f32[64,128]{1,0:T(8,128)S(1)}, f32[64,128]{1,0:T(8,128)S(1)}, u32[]{:S(2)}, u32[]{:S(2)}) collective-permute-start(f32[64,128]{1,0:T(8,128)S(1)} %broadcast_select_fusion.6), channel_id=1, source_target_pairs={{0,4},{4,0},{8,12},{12,8},{16,20},{20,16},{24,28},{28,24},{1,5},{5... | collective-permute-start | bytes 98312 | tf_op jit(solution)/shard_map/ppermute | solution.py:29
  17.5 3.9 %collective-permute-start.3 = (f32[64,128]{1,0:T(8,128)S(1)}, f32[64,128]{1,0:T(8,128)S(1)}, u32[]{:S(2)}, u32[]{:S(2)}) collective-permute-start(f32[64,128]{1,0:T(8,128)S(1)} %add.70), channel_id=1, source_target_pairs={{0,8},{4,12},{8,0},{12,4},{16,24},{20,28},{24,16},{28,20},{1,9},{5... | collective-permute-start | bytes 98312 | tf_op jit(solution)/shard_map/ppermute | solution.py:29
  21.4 4.8 %collective-permute-start.4 = (f32[64,128]{1,0:T(8,128)S(1)}, f32[64,128]{1,0:T(8,128)S(1)}, u32[]{:S(2)}, u32[]{:S(2)}) collective-permute-start(f32[64,128]{1,0:T(8,128)S(1)} %add.71), channel_id=1, source_target_pairs={{0,16},{4,20},{8,24},{12,28},{16,0},{20,4},{24,8},{28,12},{1,17},{... | collective-permute-start | bytes 98312 | tf_op jit(solution)/shard_map/ppermute | solution.py:29
  26.8 6.9 %copy-start.4 = (f32[64,128]{1,0:T(8,128)S(1)}, f32[64,128]{1,0:T(8,128)}, u32[]{:S(2)}) copy-start(f32[64,128]{1,0:T(8,128)} %add.72.head_ref) | copy-start | bytes 98308
  36.8 1.5 %collective-permute-start.6 = (f32[64,768]{1,0:T(8,128)S(1)}, f32[64,768]{1,0:T(8,128)S(1)}, u32[]{:S(2)}, u32[]{:S(2)}) collective-permute-start(f32[64,768]{1,0:T(8,128)S(1)} %broadcast_select_fusion), channel_id=1, source_target_pairs={{0,1},{1,0},{2,3},{3,2},{4,5},{5,4},{6,7},{7,6},{8,9},{9,8},{10,11... | collective-permute-start | bytes 589832 | tf_op jit(solution)/shard_map/ppermute | solution.py:76
  39.2 4.3 %collective-permute-start.7 = (f32[64,256]{1,0:T(8,128)S(1)}, f32[64,256]{1,0:T(8,128)S(1)}, u32[]{:S(2)}, u32[]{:S(2)}) collective-permute-start(f32[64,256]{1,0:T(8,128)S(1)} %pad_maximum_fusion.5), channel_id=1, source_target_pairs={{0,4},{4,0},{8,12},{12,8},{16,20},{20,16},{24,28},{28,24},{1,5},{5... | collective-permute-start | bytes 196616 | tf_op jit(solution)/shard_map/ppermute | solution.py:29
  43.6 4.3 %collective-permute-start.8 = (f32[64,256]{1,0:T(8,128)S(1)}, f32[64,256]{1,0:T(8,128)S(1)}, u32[]{:S(2)}, u32[]{:S(2)}) collective-permute-start(f32[64,256]{1,0:T(8,128)S(1)} %fusion.49), channel_id=1, source_target_pairs={{0,8},{4,12},{8,0},{12,4},{16,24},{20,28},{24,16},{28,20},{1,9},{5... | collective-permute-start | bytes 196616 | tf_op jit(solution)/shard_map/ppermute | solution.py:29
  45.4 5.2 %copy-start.1 = (f32[64,64]{1,0:T(8,128)S(1)}, f32[64,64]{1,0:T(8,128)}, u32[]{:S(2)}) copy-start(f32[64,64]{1,0:T(8,128)} %shard_map.17) | copy-start | bytes 49156
  47.9 5.2 %collective-permute-start.9 = (f32[64,256]{1,0:T(8,128)S(1)}, f32[64,256]{1,0:T(8,128)S(1)}, u32[]{:S(2)}, u32[]{:S(2)}) collective-permute-start(f32[64,256]{1,0:T(8,128)S(1)} %add.74), channel_id=1, source_target_pairs={{0,16},{4,20},{8,24},{12,28},{16,0},{20,4},{24,8},{28,12},{1,17},{... | collective-permute-start | bytes 196616 | tf_op jit(solution)/shard_map/ppermute | solution.py:29
  55.8 4.0 %collective-permute-start.10 = (f32[64,128]{1,0:T(8,128)S(1)}, f32[64,128]{1,0:T(8,128)S(1)}, u32[]{:S(2)}, u32[]{:S(2)}) collective-permute-start(f32[64,128]{1,0:T(8,128)S(1)} %fusion.3), channel_id=1, source_target_pairs={{0,4},{4,0},{8,12},{12,8},{16,20},{20,16},{24,28},{28,24},{1,5},{5... | collective-permute-start | bytes 98312 | tf_op jit(solution)/shard_map/ppermute | solution.py:29
  57.5 3.9 %collective-permute-start.13 = (f32[64,128]{1,0:T(8,128)S(1)}, f32[64,128]{1,0:T(8,128)S(1)}, u32[]{:S(2)}, u32[]{:S(2)}) collective-permute-start(f32[64,128]{1,0:T(8,128)S(1)} %pad_maximum_fusion.6), channel_id=1, source_target_pairs={{0,4},{4,0},{8,12},{12,8},{16,20},{20,16},{24,28},{28,24},{1,5},{5... | collective-permute-start | bytes 98312 | tf_op jit(solution)/shard_map/ppermute | solution.py:29
  59.8 3.9 %collective-permute-start.11 = (f32[64,128]{1,0:T(8,128)S(1)}, f32[64,128]{1,0:T(8,128)S(1)}, u32[]{:S(2)}, u32[]{:S(2)}) collective-permute-start(f32[64,128]{1,0:T(8,128)S(1)} %add.76), channel_id=1, source_target_pairs={{0,8},{4,12},{8,0},{12,4},{16,24},{20,28},{24,16},{28,20},{1,9},{5... | collective-permute-start | bytes 98312 | tf_op jit(solution)/shard_map/ppermute | solution.py:29
  61.5 5.3 %collective-permute-start.14 = (f32[64,128]{1,0:T(8,128)S(1)}, f32[64,128]{1,0:T(8,128)S(1)}, u32[]{:S(2)}, u32[]{:S(2)}) collective-permute-start(f32[64,128]{1,0:T(8,128)S(1)} %fusion.123), channel_id=1, source_target_pairs={{0,8},{4,12},{8,0},{12,4},{16,24},{20,28},{24,16},{28,20},{1,9},{5... | collective-permute-start | bytes 98312 | tf_op jit(solution)/shard_map/ppermute | solution.py:29
  63.7 4.9 %collective-permute-start.12 = (f32[64,128]{1,0:T(8,128)S(1)}, f32[64,128]{1,0:T(8,128)S(1)}, u32[]{:S(2)}, u32[]{:S(2)}) collective-permute-start(f32[64,128]{1,0:T(8,128)S(1)} %add.77), channel_id=1, source_target_pairs={{0,16},{4,20},{8,24},{12,28},{16,0},{20,4},{24,8},{28,12},{1,17},{... | collective-permute-start | bytes 98312 | tf_op jit(solution)/shard_map/ppermute | solution.py:29
  66.8 10.8 %collective-permute-start.15 = (f32[64,128]{1,0:T(8,128)S(1)}, f32[64,128]{1,0:T(8,128)S(1)}, u32[]{:S(2)}, u32[]{:S(2)}) collective-permute-start(f32[64,128]{1,0:T(8,128)S(1)} %add.80), channel_id=1, source_target_pairs={{0,16},{4,20},{8,24},{12,28},{16,0},{20,4},{24,8},{28,12},{1,17},{... | collective-permute-start | bytes 98312 | tf_op jit(solution)/shard_map/ppermute | solution.py:29
  76.0 1.1 %copy-start.2 = (f32[64,64]{1,0:T(8,128)S(1)}, f32[64,64]{1,0:T(8,128)}, u32[]{:S(2)}) copy-start(f32[64,64]{1,0:T(8,128)} %shard_map.18) | copy-start | bytes 49156
  76.0 1.2 %copy-start.3 = (f32[64,128]{1,0:T(8,128)S(1)}, f32[64,128]{1,0:T(8,128)}, u32[]{:S(2)}) copy-start(f32[64,128]{1,0:T(8,128)} %add.78.head_ref) | copy-start | bytes 98308

commit v25 on v21

--- a/solution.py
+++ b/solution.py
@@ -135,10 +135,12 @@
         head = butterfly_sum(
             inner_rows(panel_1, jnp.concatenate([panel_1, units[1]])), "rows", rows_size
         )
+        steps = butterfly_steps(rows_size)
         tail = butterfly_sum(
             jnp.concatenate([inner_rows(panel_1, current), inner_rows(units[1], current)], axis=1),
             "rows",
             rows_size,
+            None if steps is None else steps[::-1],
         )
         top_rows = head[:, width:]
         basis_cur, unit_cur = tail[:, :width], tail[:, width:]

time: 66.7 us -> 66.8 us (level)
  starting transfers between devices: 28.2 us -> 29.3 us
  waiting for transfers between devices: 9.21 us -> 8.27 us
    ppermute x12, starting transfers between devices: 20.7 us -> 21.7 us  [butterfly_sum(): x = x + lax.ppermute(x, axis, [(i, i ^ step) for i in range(size)])]
    ppermute x12, waiting for transfers between devices: 6.67 us -> 5.73 us  [butterfly_sum(): x = x + lax.ppermute(x, axis, [(i, i ^ step) for i in range(size)])]
where the time goes in v25:
time: 66.8 us; the launch traced here: 66.4 us
  starting transfers between devices  29.3 us (44%)
  Pallas kernels  13.6 us (20%)
  matrix products  12.3 us (18%)
  waiting for transfers between devices  8.27 us (12%)
  other arithmetic  1.57 us (2%)
  local copies, waits for them, and re-layouts  0.91 us (1%)
    ppermute x12, starting transfers between devices, butterfly_sum(): x = x + lax.ppermute(x, axis, [(i, i ^ step) for i in range(size)])  21.7 us
    pallas_call x2, Pallas kernels, lower_inverse(): pl.pallas_call(_eliminate_kernel, out_shape=jax.ShapeDtypeStruct((size, s...  13.6 us
    dot_general x38, matrix products, apply_left(): return jnp.dot(square, right_side, precision=HIGHEST_PRECISION)  7.99 us
    ppermute x2, starting transfers between devices, from_root(): lax.ppermute(value, axis, [(i, i + dist) for i in range(size) if i % (2 *...  6.15 us
    ppermute x12, waiting for transfers between devices, butterfly_sum(): x = x + lax.ppermute(x, axis, [(i, i ^ step) for i in range(size)])  5.73 us
    dot_general x6, matrix products, inner_rows(): lax.dot_general(left, right, (((1,), (1,)), ((), ())), precision=HIGHEST_...  2.52 us
    ppermute x1, waiting for transfers between devices, spread_pair(): lax.ppermute(have, axis, [(i, i + dist) for i in range(size) if i % (2 *...  2.18 us
    dot_general x2, matrix products, local(): current = current - jnp.dot(mixed.T, reflect, precision=HIGHEST_PRECISION)  1.43 us
  transfers between devices with their start and end apart: 16, of which 8 were waited for; matrix products, arithmetic and copies ran while one was open for 10% of the time, Pallas kernels for 20%

profile of v25, /device:TPU:0, one launch (start us, length us, event | category | flops | bytes accessed | tf_op | source)
XLA Modules:
  0.0 66.4 jit_solution(5188985990157845155)
XLA Ops:
  0.0 0.9 %copy-done = f32[1,64,768]{2,1,0:T(8,128)S(1)} copy-done((f32[1,64,768]{2,1,0:T(8,128)S(1)}, f32[1,64,768]{2,1,0:T(8,128)}, u32[]{:S(2)}) %copy-start) | copy-done | bytes 196632
  0.9 0.5 convolution_bitcast_fusion
  1.5 4.9 %collective-permute-start = (f32[64,128]{1,0:T(8,128)S(1)}, f32[64,128]{1,0:T(8,128)S(1)}, u32[]{:S(2)}, u32[]{:S(2)}) collective-permute-start(f32[64,128]{1,0:T(8,128)S(1)} %convolution_bitcast_fusion), channel_id=1, source_target_pairs={{0,2},{4,6},{8,10},{12,14},{16,18},{20,22},{24,26},{28,30}} | collective-permute-start | bytes 98312 | tf_op jit(solution)/shard_map/ppermute | solution.py:85
  6.3 1.3 %collective-permute-start.5 = (f32[64,768]{1,0:T(8,128)S(1)}, f32[64,768]{1,0:T(8,128)S(1)}, u32[]{:S(2)}, u32[]{:S(2)}) collective-permute-start(f32[64,768]{1,0:T(8,128)S(1)} %bitcast.76), channel_id=1, source_target_pairs={{0,2},{1,3},{4,6},{5,7},{8,10},{9,11},{12,14},{13,15},{16,18},{17,... | collective-permute-start | bytes 589832 | tf_op jit(solution)/shard_map/ppermute | solution.py:71
  8.0 1.3 %collective-permute-start.1 = (f32[64,128]{1,0:T(8,128)S(1)}, f32[64,128]{1,0:T(8,128)S(1)}, u32[]{:S(2)}, u32[]{:S(2)}) collective-permute-start(f32[64,128]{1,0:T(8,128)S(1)} %broadcast_select_fusion.5), channel_id=1, source_target_pairs={{0,1},{2,3},{4,5},{6,7},{8,9},{10,11},{12,13},{14,15},{16,17},{18,... | collective-permute-start | bytes 98312 | tf_op jit(solution)/shard_map/ppermute | solution.py:85
  9.3 2.2 %collective-permute-done.5 = f32[64,768]{1,0:T(8,128)S(1)} collective-permute-done((f32[64,768]{1,0:T(8,128)S(1)}, f32[64,768]{1,0:T(8,128)S(1)}, u32[]{:S(2)}, u32[]{:S(2)}) %collective-permute-start.5) | collective-permute-done | bytes 196640 | tf_op jit(solution)/shard_map/ppermute | solution.py:71
  11.6 1.6 %collective-permute-start.2 = (f32[64,128]{1,0:T(8,128)S(1)}, f32[64,128]{1,0:T(8,128)S(1)}, u32[]{:S(2)}, u32[]{:S(2)}) collective-permute-start(f32[64,128]{1,0:T(8,128)S(1)} %broadcast_select_fusion.6), channel_id=1, source_target_pairs={{0,4},{4,0},{8,12},{12,8},{16,20},{20,16},{24,28},{28,24},{1,5},{5... | collective-permute-start | bytes 98312 | tf_op jit(solution)/shard_map/ppermute | solution.py:29
  13.2 2.4 %collective-permute-done.2 = f32[64,128]{1,0:T(8,128)S(1)} collective-permute-done((f32[64,128]{1,0:T(8,128)S(1)}, f32[64,128]{1,0:T(8,128)S(1)}, u32[]{:S(2)}, u32[]{:S(2)}) %collective-permute-start.2) | collective-permute-done | bytes 32800 | tf_op jit(solution)/shard_map/ppermute | solution.py:29
  15.6 1.6 %collective-permute-start.3 = (f32[64,128]{1,0:T(8,128)S(1)}, f32[64,128]{1,0:T(8,128)S(1)}, u32[]{:S(2)}, u32[]{:S(2)}) collective-permute-start(f32[64,128]{1,0:T(8,128)S(1)} %add.70), channel_id=1, source_target_pairs={{0,8},{4,12},{8,0},{12,4},{16,24},{20,28},{24,16},{28,20},{1,9},{5... | collective-permute-start | bytes 98312 | tf_op jit(solution)/shard_map/ppermute | solution.py:29
  17.6 0.5 fusion.8
  18.1 1.6 %collective-permute-start.7 = (f32[64,256]{1,0:T(8,128)S(1)}, f32[64,256]{1,0:T(8,128)S(1)}, u32[]{:S(2)}, u32[]{:S(2)}) collective-permute-start(f32[64,256]{1,0:T(8,128)S(1)} %pad_maximum_fusion.5), channel_id=1, source_target_pairs={{0,4},{4,0},{8,12},{12,8},{16,20},{20,16},{24,28},{28,24},{1,5},{5... | collective-permute-start | bytes 196616 | tf_op jit(solution)/shard_map/ppermute | solution.py:29
  19.7 2.7 %collective-permute-start.4 = (f32[64,128]{1,0:T(8,128)S(1)}, f32[64,128]{1,0:T(8,128)S(1)}, u32[]{:S(2)}, u32[]{:S(2)}) collective-permute-start(f32[64,128]{1,0:T(8,128)S(1)} %add.71), channel_id=1, source_target_pairs={{0,16},{4,20},{8,24},{12,28},{16,0},{20,4},{24,8},{28,12},{1,17},{... | collective-permute-start | bytes 98312 | tf_op jit(solution)/shard_map/ppermute | solution.py:29
  22.5 1.3 %collective-permute-start.8 = (f32[64,256]{1,0:T(8,128)S(1)}, f32[64,256]{1,0:T(8,128)S(1)}, u32[]{:S(2)}, u32[]{:S(2)}) collective-permute-start(f32[64,256]{1,0:T(8,128)S(1)} %fusion.49), channel_id=1, source_target_pairs={{0,8},{4,12},{8,0},{12,4},{16,24},{20,28},{24,16},{28,20},{1,9},{5... | collective-permute-start | bytes 196616 | tf_op jit(solution)/shard_map/ppermute | solution.py:29
  23.8 0.8 %collective-permute-done.4 = f32[64,128]{1,0:T(8,128)S(1)} collective-permute-done((f32[64,128]{1,0:T(8,128)S(1)}, f32[64,128]{1,0:T(8,128)S(1)}, u32[]{:S(2)}, u32[]{:S(2)}) %collective-permute-start.4) | collective-permute-done | bytes 32800 | tf_op jit(solution)/shard_map/ppermute | solution.py:29
  24.6 0.6 add.72.head_ref
  25.2 6.8 %shard_map.17 = f32[64,64]{1,0:T(8,128)} custom-call(f32[64,128]{1,0:T(8,128)} %add.72.head_ref), custom_call_target="tpu_custom_call" | custom-call | tf_op jit(solution)/shard_map/pallas_call | solution.py:61
  32.0 2.8 %collective-permute-start.9 = (f32[64,256]{1,0:T(8,128)S(1)}, f32[64,256]{1,0:T(8,128)S(1)}, u32[]{:S(2)}, u32[]{:S(2)}) collective-permute-start(f32[64,256]{1,0:T(8,128)S(1)} %add.74), channel_id=1, source_target_pairs={{0,16},{4,20},{8,24},{12,28},{16,0},{20,4},{24,8},{28,12},{1,17},{... | collective-permute-start | bytes 196616 | tf_op jit(solution)/shard_map/ppermute | solution.py:29
  39.4 0.4 fusion.1
  40.1 0.5 fusion.3
  40.7 1.2 %collective-permute-start.10 = (f32[64,128]{1,0:T(8,128)S(1)}, f32[64,128]{1,0:T(8,128)S(1)}, u32[]{:S(2)}, u32[]{:S(2)}) collective-permute-start(f32[64,128]{1,0:T(8,128)S(1)} %fusion.3), channel_id=1, source_target_pairs={{0,4},{4,0},{8,12},{12,8},{16,20},{20,16},{24,28},{28,24},{1,5},{5... | collective-permute-start | bytes 98312 | tf_op jit(solution)/shard_map/ppermute | solution.py:29
  41.9 2.1 %collective-permute-start.13 = (f32[64,128]{1,0:T(8,128)S(1)}, f32[64,128]{1,0:T(8,128)S(1)}, u32[]{:S(2)}, u32[]{:S(2)}) collective-permute-start(f32[64,128]{1,0:T(8,128)S(1)} %pad_maximum_fusion.6), channel_id=1, source_target_pairs={{0,16},{4,20},{8,24},{12,28},{16,0},{20,4},{24,8},{28,12},{1,17},{... | collective-permute-start | bytes 98312 | tf_op jit(solution)/shard_map/ppermute | solution.py:29
  44.0 0.6 collective-permute-done.10
  44.6 1.6 %collective-permute-start.11 = (f32[64,128]{1,0:T(8,128)S(1)}, f32[64,128]{1,0:T(8,128)S(1)}, u32[]{:S(2)}, u32[]{:S(2)}) collective-permute-start(f32[64,128]{1,0:T(8,128)S(1)} %add.76), channel_id=1, source_target_pairs={{0,8},{4,12},{8,0},{12,4},{16,24},{20,28},{24,16},{28,20},{1,9},{5... | collective-permute-start | bytes 98312 | tf_op jit(solution)/shard_map/ppermute | solution.py:29
  46.2 0.5 collective-permute-done.13
  46.8 1.8 %collective-permute-start.14 = (f32[64,128]{1,0:T(8,128)S(1)}, f32[64,128]{1,0:T(8,128)S(1)}, u32[]{:S(2)}, u32[]{:S(2)}) collective-permute-start(f32[64,128]{1,0:T(8,128)S(1)} %fusion.123), channel_id=1, source_target_pairs={{0,8},{4,12},{8,0},{12,4},{16,24},{20,28},{24,16},{28,20},{1,9},{5... | collective-permute-start | bytes 98312 | tf_op jit(solution)/shard_map/ppermute | solution.py:29
  48.7 2.5 %collective-permute-start.12 = (f32[64,128]{1,0:T(8,128)S(1)}, f32[64,128]{1,0:T(8,128)S(1)}, u32[]{:S(2)}, u32[]{:S(2)}) collective-permute-start(f32[64,128]{1,0:T(8,128)S(1)} %add.77), channel_id=1, source_target_pairs={{0,16},{4,20},{8,24},{12,28},{16,0},{20,4},{24,8},{28,12},{1,17},{... | collective-permute-start | bytes 98312 | tf_op jit(solution)/shard_map/ppermute | solution.py:29
  51.2 1.2 %collective-permute-start.15 = (f32[64,128]{1,0:T(8,128)S(1)}, f32[64,128]{1,0:T(8,128)S(1)}, u32[]{:S(2)}, u32[]{:S(2)}) collective-permute-start(f32[64,128]{1,0:T(8,128)S(1)} %add.80), channel_id=1, source_target_pairs={{0,4},{4,0},{8,12},{12,8},{16,20},{20,16},{24,28},{28,24},{1,5},{5... | collective-permute-start | bytes 98312 | tf_op jit(solution)/shard_map/ppermute | solution.py:29
  52.3 1.2 %collective-permute-done.12 = f32[64,128]{1,0:T(8,128)S(1)} collective-permute-done((f32[64,128]{1,0:T(8,128)S(1)}, f32[64,128]{1,0:T(8,128)S(1)}, u32[]{:S(2)}, u32[]{:S(2)}) %collective-permute-start.12) | collective-permute-done | bytes 32800 | tf_op jit(solution)/shard_map/ppermute | solution.py:29
  53.6 0.6 add.78.head_ref
  54.2 6.8 %shard_map.18 = f32[64,64]{1,0:T(8,128)} custom-call(f32[64,128]{1,0:T(8,128)} %add.78.head_ref), custom_call_target="tpu_custom_call" | custom-call | tf_op jit(solution)/shard_map/pallas_call | solution.py:61
  61.0 1.1 %convolution_subtract_fusion.1 = f32[64,768]{1,0:T(8,128)S(1)} fusion(f32[64,64]{1,0:T(8,128)} %shard_map.18, f32[64,768]{1,0:T(8,128)S(1)} %fusion.1, s32[768]{0:T(1024)S(1)} %fusion.39), kind=kOutput, calls=%fused_computation.2 | convolution fusion | flops 37896192 | bytes 412672 | tf_op jit(solution)/shard_map/dot_general | solution.py:15
  65.4 1.1 %fusion = f32[1,64,768]{2,1,0:T(8,128)} fusion(f32[64,768]{1,0:T(8,128)S(1)} %convolution_subtract_fusion.3, f32[64,64]{1,0:T(8,128)S(1)} %fusion.18, f32[64,768]{1,0:T(8,128)S(1)} %convolution_subtract_fusion.1), kind=kOutput, calls=%fused_computation.1 | convolution fusion | flops 37797888 | bytes 606208 | tf_op jit(solution)/shard_map/dot_general | solution.py:152
  (82 shorter events, 9.0 us)
Async XLA Ops:
  0.0 0.9 %copy-start = (f32[1,64,768]{2,1,0:T(8,128)S(1)}, f32[1,64,768]{2,1,0:T(8,128)}, u32[]{:S(2)}) copy-start(f32[1,64,768]{2,1,0:T(8,128)} %param.1) | copy-start | bytes 589828
  1.5 6.6 %collective-permute-start = (f32[64,128]{1,0:T(8,128)S(1)}, f32[64,128]{1,0:T(8,128)S(1)}, u32[]{:S(2)}, u32[]{:S(2)}) collective-permute-start(f32[64,128]{1,0:T(8,128)S(1)} %convolution_bitcast_fusion), channel_id=1, source_target_pairs={{0,2},{4,6},{8,10},{12,14},{16,18},{20,22},{24,26},{28,30}} | collective-permute-start | bytes 98312 | tf_op jit(solution)/shard_map/ppermute | solution.py:85
  6.3 5.2 %collective-permute-start.5 = (f32[64,768]{1,0:T(8,128)S(1)}, f32[64,768]{1,0:T(8,128)S(1)}, u32[]{:S(2)}, u32[]{:S(2)}) collective-permute-start(f32[64,768]{1,0:T(8,128)S(1)} %bitcast.76), channel_id=1, source_target_pairs={{0,2},{1,3},{4,6},{5,7},{8,10},{9,11},{12,14},{13,15},{16,18},{17,... | collective-permute-start | bytes 589832 | tf_op jit(solution)/shard_map/ppermute | solution.py:71
  8.0 3.6 %collective-permute-start.1 = (f32[64,128]{1,0:T(8,128)S(1)}, f32[64,128]{1,0:T(8,128)S(1)}, u32[]{:S(2)}, u32[]{:S(2)}) collective-permute-start(f32[64,128]{1,0:T(8,128)S(1)} %broadcast_select_fusion.5), channel_id=1, source_target_pairs={{0,1},{2,3},{4,5},{6,7},{8,9},{10,11},{12,13},{14,15},{16,17},{18,... | collective-permute-start | bytes 98312 | tf_op jit(solution)/shard_map/ppermute | solution.py:85
  11.5 5.7 %collective-permute-start.6 = (f32[64,768]{1,0:T(8,128)S(1)}, f32[64,768]{1,0:T(8,128)S(1)}, u32[]{:S(2)}, u32[]{:S(2)}) collective-permute-start(f32[64,768]{1,0:T(8,128)S(1)} %broadcast_select_fusion), channel_id=1, source_target_pairs={{0,1},{1,0},{2,3},{3,2},{4,5},{5,4},{6,7},{7,6},{8,9},{9,8},{10,11... | collective-permute-start | bytes 589832 | tf_op jit(solution)/shard_map/ppermute | solution.py:76
  11.6 4.0 %collective-permute-start.2 = (f32[64,128]{1,0:T(8,128)S(1)}, f32[64,128]{1,0:T(8,128)S(1)}, u32[]{:S(2)}, u32[]{:S(2)}) collective-permute-start(f32[64,128]{1,0:T(8,128)S(1)} %broadcast_select_fusion.6), channel_id=1, source_target_pairs={{0,4},{4,0},{8,12},{12,8},{16,20},{20,16},{24,28},{28,24},{1,5},{5... | collective-permute-start | bytes 98312 | tf_op jit(solution)/shard_map/ppermute | solution.py:29
  15.6 4.1 %collective-permute-start.3 = (f32[64,128]{1,0:T(8,128)S(1)}, f32[64,128]{1,0:T(8,128)S(1)}, u32[]{:S(2)}, u32[]{:S(2)}) collective-permute-start(f32[64,128]{1,0:T(8,128)S(1)} %add.70), channel_id=1, source_target_pairs={{0,8},{4,12},{8,0},{12,4},{16,24},{20,28},{24,16},{28,20},{1,9},{5... | collective-permute-start | bytes 98312 | tf_op jit(solution)/shard_map/ppermute | solution.py:29
  18.1 4.3 %collective-permute-start.7 = (f32[64,256]{1,0:T(8,128)S(1)}, f32[64,256]{1,0:T(8,128)S(1)}, u32[]{:S(2)}, u32[]{:S(2)}) collective-permute-start(f32[64,256]{1,0:T(8,128)S(1)} %pad_maximum_fusion.5), channel_id=1, source_target_pairs={{0,4},{4,0},{8,12},{12,8},{16,20},{20,16},{24,28},{28,24},{1,5},{5... | collective-permute-start | bytes 196616 | tf_op jit(solution)/shard_map/ppermute | solution.py:29
  19.7 4.9 %collective-permute-start.4 = (f32[64,128]{1,0:T(8,128)S(1)}, f32[64,128]{1,0:T(8,128)S(1)}, u32[]{:S(2)}, u32[]{:S(2)}) collective-permute-start(f32[64,128]{1,0:T(8,128)S(1)} %add.71), channel_id=1, source_target_pairs={{0,16},{4,20},{8,24},{12,28},{16,0},{20,4},{24,8},{28,12},{1,17},{... | collective-permute-start | bytes 98312 | tf_op jit(solution)/shard_map/ppermute | solution.py:29
  22.5 9.6 %collective-permute-start.8 = (f32[64,256]{1,0:T(8,128)S(1)}, f32[64,256]{1,0:T(8,128)S(1)}, u32[]{:S(2)}, u32[]{:S(2)}) collective-permute-start(f32[64,256]{1,0:T(8,128)S(1)} %fusion.49), channel_id=1, source_target_pairs={{0,8},{4,12},{8,0},{12,4},{16,24},{20,28},{24,16},{28,20},{1,9},{5... | collective-permute-start | bytes 196616 | tf_op jit(solution)/shard_map/ppermute | solution.py:29
  32.0 2.8 %copy-start.1 = (f32[64,64]{1,0:T(8,128)S(1)}, f32[64,64]{1,0:T(8,128)}, u32[]{:S(2)}) copy-start(f32[64,64]{1,0:T(8,128)} %shard_map.17) | copy-start | bytes 49156
  32.0 2.8 %copy-start.3 = (f32[64,128]{1,0:T(8,128)S(1)}, f32[64,128]{1,0:T(8,128)}, u32[]{:S(2)}) copy-start(f32[64,128]{1,0:T(8,128)} %add.72.head_ref) | copy-start | bytes 98308
  32.0 5.9 %collective-permute-start.9 = (f32[64,256]{1,0:T(8,128)S(1)}, f32[64,256]{1,0:T(8,128)S(1)}, u32[]{:S(2)}, u32[]{:S(2)}) collective-permute-start(f32[64,256]{1,0:T(8,128)S(1)} %add.74), channel_id=1, source_target_pairs={{0,16},{4,20},{8,24},{12,28},{16,0},{20,4},{24,8},{28,12},{1,17},{... | collective-permute-start | bytes 196616 | tf_op jit(solution)/shard_map/ppermute | solution.py:29
  40.7 4.0 %collective-permute-start.10 = (f32[64,128]{1,0:T(8,128)S(1)}, f32[64,128]{1,0:T(8,128)S(1)}, u32[]{:S(2)}, u32[]{:S(2)}) collective-permute-start(f32[64,128]{1,0:T(8,128)S(1)} %fusion.3), channel_id=1, source_target_pairs={{0,4},{4,0},{8,12},{12,8},{16,20},{20,16},{24,28},{28,24},{1,5},{5... | collective-permute-start | bytes 98312 | tf_op jit(solution)/shard_map/ppermute | solution.py:29
  41.9 4.8 %collective-permute-start.13 = (f32[64,128]{1,0:T(8,128)S(1)}, f32[64,128]{1,0:T(8,128)S(1)}, u32[]{:S(2)}, u32[]{:S(2)}) collective-permute-start(f32[64,128]{1,0:T(8,128)S(1)} %pad_maximum_fusion.6), channel_id=1, source_target_pairs={{0,16},{4,20},{8,24},{12,28},{16,0},{20,4},{24,8},{28,12},{1,17},{... | collective-permute-start | bytes 98312 | tf_op jit(solution)/shard_map/ppermute | solution.py:29
  44.6 4.0 %collective-permute-start.11 = (f32[64,128]{1,0:T(8,128)S(1)}, f32[64,128]{1,0:T(8,128)S(1)}, u32[]{:S(2)}, u32[]{:S(2)}) collective-permute-start(f32[64,128]{1,0:T(8,128)S(1)} %add.76), channel_id=1, source_target_pairs={{0,8},{4,12},{8,0},{12,4},{16,24},{20,28},{24,16},{28,20},{1,9},{5... | collective-permute-start | bytes 98312 | tf_op jit(solution)/shard_map/ppermute | solution.py:29
  46.8 4.3 %collective-permute-start.14 = (f32[64,128]{1,0:T(8,128)S(1)}, f32[64,128]{1,0:T(8,128)S(1)}, u32[]{:S(2)}, u32[]{:S(2)}) collective-permute-start(f32[64,128]{1,0:T(8,128)S(1)} %fusion.123), channel_id=1, source_target_pairs={{0,8},{4,12},{8,0},{12,4},{16,24},{20,28},{24,16},{28,20},{1,9},{5... | collective-permute-start | bytes 98312 | tf_op jit(solution)/shard_map/ppermute | solution.py:29
  48.7 4.9 %collective-permute-start.12 = (f32[64,128]{1,0:T(8,128)S(1)}, f32[64,128]{1,0:T(8,128)S(1)}, u32[]{:S(2)}, u32[]{:S(2)}) collective-permute-start(f32[64,128]{1,0:T(8,128)S(1)} %add.77), channel_id=1, source_target_pairs={{0,16},{4,20},{8,24},{12,28},{16,0},{20,4},{24,8},{28,12},{1,17},{... | collective-permute-start | bytes 98312 | tf_op jit(solution)/shard_map/ppermute | solution.py:29
  51.2 11.3 %collective-permute-start.15 = (f32[64,128]{1,0:T(8,128)S(1)}, f32[64,128]{1,0:T(8,128)S(1)}, u32[]{:S(2)}, u32[]{:S(2)}) collective-permute-start(f32[64,128]{1,0:T(8,128)S(1)} %add.80), channel_id=1, source_target_pairs={{0,4},{4,0},{8,12},{12,8},{16,20},{20,16},{24,28},{28,24},{1,5},{5... | collective-permute-start | bytes 98312 | tf_op jit(solution)/shard_map/ppermute | solution.py:29
  61.0 1.1 %copy-start.2 = (f32[64,64]{1,0:T(8,128)S(1)}, f32[64,64]{1,0:T(8,128)}, u32[]{:S(2)}) copy-start(f32[64,64]{1,0:T(8,128)} %shard_map.18) | copy-start | bytes 49156
  61.0 1.2 %copy-start.4 = (f32[64,128]{1,0:T(8,128)S(1)}, f32[64,128]{1,0:T(8,128)}, u32[]{:S(2)}) copy-start(f32[64,128]{1,0:T(8,128)} %add.78.head_ref) | copy-start | bytes 98308

commit v26 on v21

--- a/solution.py
+++ b/solution.py
@@ -101,6 +101,13 @@
             (lanes == (global_rows - k * width)[None, :]).astype(jnp.float32) for k in range(2)
         ]
 
+        def top_of(block, k):
+            if local_rows < 2 * width:
+                return inner_rows(block, units[k])
+            first = lax.axis_index("rows") == 0
+            piece = block[:, k * width:(k + 1) * width]
+            return jnp.where(first, piece, jnp.zeros_like(piece))
+
         if butterfly_steps(cols_size) is None:
             gathered = lax.all_gather(current, "cols")
             panel_0 = gathered[0]
@@ -109,12 +116,12 @@
                 inner_rows(panel_0, jnp.concatenate([panel_0, units[0]])), "rows", rows_size
             )
         else:
-            head = inner_rows(current, jnp.concatenate([current, units[0]]))
+            head = jnp.concatenate([inner_rows(current, current), top_of(current, 0)], axis=1)
             head = butterfly_sum(from_root(head, "cols", cols_size), "rows", rows_size)
             panel_0, second = spread_pair(current, "cols", cols_size)
 
         both = jnp.concatenate([current, second])
-        tail = jnp.concatenate([inner_rows(panel_0, both), inner_rows(units[0], both)], axis=1)
+        tail = jnp.concatenate([inner_rows(panel_0, both), top_of(both, 0).T], axis=1)
         steps = butterfly_steps(rows_size)
         tail = butterfly_sum(tail, "rows", rows_size, None if steps is None else steps[:-1])
         lower_inv, tail = lax.optimization_barrier((lower_inverse(head), tail))
@@ -133,10 +140,12 @@
 
         panel_1 = jnp.where((global_rows >= width)[None, :], second, jnp.zeros_like(second))
         head = butterfly_sum(
-            inner_rows(panel_1, jnp.concatenate([panel_1, units[1]])), "rows", rows_size
+            jnp.concatenate([inner_rows(panel_1, panel_1), top_of(panel_1, 1)], axis=1),
+            "rows",
+            rows_size,
         )
         tail = butterfly_sum(
-            jnp.concatenate([inner_rows(panel_1, current), inner_rows(units[1], current)], axis=1),
+            jnp.concatenate([inner_rows(panel_1, current), top_of(current, 1).T], axis=1),
             "rows",
             rows_size,
         )

time: 66.7 us -> 68.2 us (1.022)
  waiting for transfers between devices: 9.21 us -> 14.1 us
  starting transfers between devices: 28.2 us -> 25.6 us
  local copies, waits for them, and re-layouts: 0.91 us -> 0.02 us
    ppermute x12, waiting for transfers between devices: 6.67 us -> 11.6 us  [butterfly_sum(): x = x + lax.ppermute(x, axis, [(i, i ^ step) for i in range(size)])]
    ppermute x12, starting transfers between devices: 20.7 us -> 18 us  [butterfly_sum(): x = x + lax.ppermute(x, axis, [(i, i ^ step) for i in range(size)])]
    unnamed x10, local copies, waits for them, and re-layouts: 0.91 us -> 0.02 us
    dot_general x6 -> x4, matrix products: 2.52 us -> 2.47 us  [inner_rows(): lax.dot_general(left, right, (((1,), (1,)), ((), ())), precision=HIGHEST_...]
  transfers between devices with their start and end apart: 16 -> 16, of which waited for: 8 -> 11; matrix products, arithmetic and copies ran while one was open for 10% -> 9% of each run, Pallas kernels for 20% -> 20%
where the time goes in v26:
time: 68.2 us; the launch traced here: 67.8 us
  starting transfers between devices  25.6 us (38%)
  waiting for transfers between devices  14.1 us (21%)
  Pallas kernels  13.6 us (20%)
  matrix products  12.2 us (18%)
  other arithmetic  1.89 us (3%)
    ppermute x12, starting transfers between devices, butterfly_sum(): x = x + lax.ppermute(x, axis, [(i, i ^ step) for i in range(size)])  18 us
    pallas_call x2, Pallas kernels, lower_inverse(): pl.pallas_call(_eliminate_kernel, out_shape=jax.ShapeDtypeStruct((size, s...  13.6 us
    ppermute x12, waiting for transfers between devices, butterfly_sum(): x = x + lax.ppermute(x, axis, [(i, i ^ step) for i in range(size)])  11.6 us
    dot_general x38, matrix products, apply_left(): return jnp.dot(square, right_side, precision=HIGHEST_PRECISION)  7.91 us
    ppermute x2, starting transfers between devices, from_root(): lax.ppermute(value, axis, [(i, i + dist) for i in range(size) if i % (2 *...  6.15 us
    dot_general x4, matrix products, inner_rows(): lax.dot_general(left, right, (((1,), (1,)), ((), ())), precision=HIGHEST_...  2.47 us
    ppermute x1, waiting for transfers between devices, spread_pair(): lax.ppermute(have, axis, [(i, i + dist) for i in range(size) if i % (2 *...  2.11 us
    dot_general x2, matrix products, local(): current = current - jnp.dot(mixed.T, reflect, precision=HIGHEST_PRECISION)  1.43 us
  transfers between devices with their start and end apart: 16, of which 11 were waited for; matrix products, arithmetic and copies ran while one was open for 9% of the time, Pallas kernels for 20%

profile of v26, /device:TPU:0, one launch (start us, length us, event | category | flops | bytes accessed | tf_op | source)
XLA Modules:
  0.0 67.8 jit_solution(8662454329001226376)
XLA Ops:
  0.0 1.4 %fusion.36 = f32[64,64]{1,0:T(8,128)S(1)} fusion(f32[1,64,768]{2,1,0:T(8,128)} %param.1), kind=kOutput, calls=%fused_computation.76 | convolution fusion | flops 37748736 | bytes 212992 | tf_op jit(solution)/shard_map/dot_general | solution.py:11
  1.5 4.9 %collective-permute-start = (f32[64,128]{1,0:T(8,128)S(1)}, f32[64,128]{1,0:T(8,128)S(1)}, u32[]{:S(2)}, u32[]{:S(2)}) collective-permute-start(f32[64,128]{1,0:T(8,128)S(1)} %pad_maximum_fusion.2), channel_id=1, source_target_pairs={{0,2},{4,6},{8,10},{12,14},{16,18},{20,22},{24,26},{28,30}} | collective-permute-start | bytes 98312 | tf_op jit(solution)/shard_map/ppermute | solution.py:85
  6.4 1.3 %collective-permute-start.5 = (f32[64,768]{1,0:T(8,128)S(1)}, f32[64,768]{1,0:T(8,128)S(1)}, u32[]{:S(2)}, u32[]{:S(2)}) collective-permute-start(f32[64,768]{1,0:T(8,128)S(1)} %bitcast.79), channel_id=1, source_target_pairs={{0,2},{1,3},{4,6},{5,7},{8,10},{9,11},{12,14},{13,15},{16,18},{17,... | collective-permute-start | bytes 589832 | tf_op jit(solution)/shard_map/ppermute | solution.py:71
  8.1 1.3 %collective-permute-start.1 = (f32[64,128]{1,0:T(8,128)S(1)}, f32[64,128]{1,0:T(8,128)S(1)}, u32[]{:S(2)}, u32[]{:S(2)}) collective-permute-start(f32[64,128]{1,0:T(8,128)S(1)} %broadcast_select_fusion.5), channel_id=1, source_target_pairs={{0,1},{2,3},{4,5},{6,7},{8,9},{10,11},{12,13},{14,15},{16,17},{18,... | collective-permute-start | bytes 98312 | tf_op jit(solution)/shard_map/ppermute | solution.py:85
  9.4 2.1 %collective-permute-done.5 = f32[64,768]{1,0:T(8,128)S(1)} collective-permute-done((f32[64,768]{1,0:T(8,128)S(1)}, f32[64,768]{1,0:T(8,128)S(1)}, u32[]{:S(2)}, u32[]{:S(2)}) %collective-permute-start.5) | collective-permute-done | bytes 196640 | tf_op jit(solution)/shard_map/ppermute | solution.py:71
  11.7 1.6 %collective-permute-start.2 = (f32[64,128]{1,0:T(8,128)S(1)}, f32[64,128]{1,0:T(8,128)S(1)}, u32[]{:S(2)}, u32[]{:S(2)}) collective-permute-start(f32[64,128]{1,0:T(8,128)S(1)} %broadcast_select_fusion.6), channel_id=1, source_target_pairs={{0,4},{4,0},{8,12},{12,8},{16,20},{20,16},{24,28},{28,24},{1,5},{5... | collective-permute-start | bytes 98312 | tf_op jit(solution)/shard_map/ppermute | solution.py:29
  13.2 2.4 %collective-permute-done.2 = f32[64,128]{1,0:T(8,128)S(1)} collective-permute-done((f32[64,128]{1,0:T(8,128)S(1)}, f32[64,128]{1,0:T(8,128)S(1)}, u32[]{:S(2)}, u32[]{:S(2)}) %collective-permute-start.2) | collective-permute-done | bytes 32800 | tf_op jit(solution)/shard_map/ppermute | solution.py:29
  15.6 1.6 %collective-permute-start.3 = (f32[64,128]{1,0:T(8,128)S(1)}, f32[64,128]{1,0:T(8,128)S(1)}, u32[]{:S(2)}, u32[]{:S(2)}) collective-permute-start(f32[64,128]{1,0:T(8,128)S(1)} %add.68), channel_id=1, source_target_pairs={{0,8},{4,12},{8,0},{12,4},{16,24},{20,28},{24,16},{28,20},{1,9},{5... | collective-permute-start | bytes 98312 | tf_op jit(solution)/shard_map/ppermute | solution.py:29
  17.3 0.5 fusion.2
  17.8 1.6 %collective-permute-start.7 = (f32[64,256]{0,1:T(8,128)S(1)}, f32[64,256]{0,1:T(8,128)S(1)}, u32[]{:S(2)}, u32[]{:S(2)}) collective-permute-start(f32[64,256]{0,1:T(8,128)S(1)} %pad_maximum_fusion), channel_id=1, source_target_pairs={{0,4},{4,0},{8,12},{12,8},{16,20},{20,16},{24,28},{28,24},{1,5},{5... | collective-permute-start | bytes 196616 | tf_op jit(solution)/shard_map/ppermute | solution.py:29
  19.6 2.6 %collective-permute-start.4 = (f32[64,128]{1,0:T(8,128)S(1)}, f32[64,128]{1,0:T(8,128)S(1)}, u32[]{:S(2)}, u32[]{:S(2)}) collective-permute-start(f32[64,128]{1,0:T(8,128)S(1)} %add.69), channel_id=1, source_target_pairs={{0,16},{4,20},{8,24},{12,28},{16,0},{20,4},{24,8},{28,12},{1,17},{... | collective-permute-start | bytes 98312 | tf_op jit(solution)/shard_map/ppermute | solution.py:29
  22.2 0.6 collective-permute-done.7
  22.8 1.0 %collective-permute-start.8 = (f32[64,256]{0,1:T(8,128)S(1)}, f32[64,256]{0,1:T(8,128)S(1)}, u32[]{:S(2)}, u32[]{:S(2)}) collective-permute-start(f32[64,256]{0,1:T(8,128)S(1)} %fusion.43), channel_id=1, source_target_pairs={{0,8},{4,12},{8,0},{12,4},{16,24},{20,28},{24,16},{28,20},{1,9},{5... | collective-permute-start | bytes 196616 | tf_op jit(solution)/shard_map/ppermute | solution.py:29
  23.8 0.7 collective-permute-done.4
  24.5 0.6 add.70.head_ref
  25.1 6.8 %shard_map.17 = f32[64,64]{1,0:T(8,128)} custom-call(f32[64,128]{1,0:T(8,128)} %add.70.head_ref), custom_call_target="tpu_custom_call" | custom-call | tf_op jit(solution)/shard_map/pallas_call | solution.py:61
  31.9 2.6 %collective-permute-start.9 = (f32[64,256]{0,1:T(8,128)S(1)}, f32[64,256]{0,1:T(8,128)S(1)}, u32[]{:S(2)}, u32[]{:S(2)}) collective-permute-start(f32[64,256]{0,1:T(8,128)S(1)} %add.72), channel_id=1, source_target_pairs={{0,16},{4,20},{8,24},{12,28},{16,0},{20,4},{24,8},{28,12},{1,17},{... | collective-permute-start | bytes 196616 | tf_op jit(solution)/shard_map/ppermute | solution.py:29
  37.6 1.6 %collective-permute-done.9 = f32[64,256]{0,1:T(8,128)S(1)} collective-permute-done((f32[64,256]{0,1:T(8,128)S(1)}, f32[64,256]{0,1:T(8,128)S(1)}, u32[]{:S(2)}, u32[]{:S(2)}) %collective-permute-start.9) | collective-permute-done | bytes 65568 | tf_op jit(solution)/shard_map/ppermute | solution.py:29
  41.7 1.5 %collective-permute-start.10 = (f32[64,128]{1,0:T(8,128)S(1)}, f32[64,128]{1,0:T(8,128)S(1)}, u32[]{:S(2)}, u32[]{:S(2)}) collective-permute-start(f32[64,128]{1,0:T(8,128)S(1)} %pad_maximum_fusion.3), channel_id=1, source_target_pairs={{0,4},{4,0},{8,12},{12,8},{16,20},{20,16},{24,28},{28,24},{1,5},{5... | collective-permute-start | bytes 98312 | tf_op jit(solution)/shard_map/ppermute | solution.py:29
  43.2 0.6 collective-permute-start.13
  43.8 1.8 %collective-permute-done.10 = f32[64,128]{1,0:T(8,128)S(1)} collective-permute-done((f32[64,128]{1,0:T(8,128)S(1)}, f32[64,128]{1,0:T(8,128)S(1)}, u32[]{:S(2)}, u32[]{:S(2)}) %collective-permute-start.10) | collective-permute-done | bytes 32800 | tf_op jit(solution)/shard_map/ppermute | solution.py:29
  45.7 0.6 collective-permute-start.11
  46.3 1.2 %collective-permute-done.13 = f32[64,128]{0,1:T(8,128)S(1)} collective-permute-done((f32[64,128]{0,1:T(8,128)S(1)}, f32[64,128]{0,1:T(8,128)S(1)}, u32[]{:S(2)}, u32[]{:S(2)}) %collective-permute-start.13) | collective-permute-done | bytes 32800 | tf_op jit(solution)/shard_map/ppermute | solution.py:29
  47.5 0.7 collective-permute-start.14
  48.2 2.0 %collective-permute-done.11 = f32[64,128]{1,0:T(8,128)S(1)} collective-permute-done((f32[64,128]{1,0:T(8,128)S(1)}, f32[64,128]{1,0:T(8,128)S(1)}, u32[]{:S(2)}, u32[]{:S(2)}) %collective-permute-start.11) | collective-permute-done | bytes 32800 | tf_op jit(solution)/shard_map/ppermute | solution.py:29
  50.2 1.6 %collective-permute-start.12 = (f32[64,128]{1,0:T(8,128)S(1)}, f32[64,128]{1,0:T(8,128)S(1)}, u32[]{:S(2)}, u32[]{:S(2)}) collective-permute-start(f32[64,128]{1,0:T(8,128)S(1)} %add.77), channel_id=1, source_target_pairs={{0,16},{4,20},{8,24},{12,28},{16,0},{20,4},{24,8},{28,12},{1,17},{... | collective-permute-start | bytes 98312 | tf_op jit(solution)/shard_map/ppermute | solution.py:29
  51.9 2.2 %collective-permute-start.15 = (f32[64,128]{0,1:T(8,128)S(1)}, f32[64,128]{0,1:T(8,128)S(1)}, u32[]{:S(2)}, u32[]{:S(2)}) collective-permute-start(f32[64,128]{0,1:T(8,128)S(1)} %add.80), channel_id=1, source_target_pairs={{0,16},{4,20},{8,24},{12,28},{16,0},{20,4},{24,8},{28,12},{1,17},{... | collective-permute-start | bytes 98312 | tf_op jit(solution)/shard_map/ppermute | solution.py:29
  54.1 0.9 %collective-permute-done.12 = f32[64,128]{1,0:T(8,128)S(1)} collective-permute-done((f32[64,128]{1,0:T(8,128)S(1)}, f32[64,128]{1,0:T(8,128)S(1)}, u32[]{:S(2)}, u32[]{:S(2)}) %collective-permute-start.12) | collective-permute-done | bytes 32800 | tf_op jit(solution)/shard_map/ppermute | solution.py:29
  55.0 0.6 add.78.head_ref
  55.6 6.8 %shard_map.18 = f32[64,64]{1,0:T(8,128)} custom-call(f32[64,128]{1,0:T(8,128)} %add.78.head_ref), custom_call_target="tpu_custom_call" | custom-call | tf_op jit(solution)/shard_map/pallas_call | solution.py:61
  62.4 1.1 %convolution_subtract_fusion.1 = f32[64,768]{1,0:T(8,128)S(1)} fusion(f32[64,64]{1,0:T(8,128)} %shard_map.18, f32[64,768]{1,0:T(8,128)S(1)} %fusion.1, s32[768]{0:T(1024)S(1)} %fusion.33), kind=kOutput, calls=%fused_computation.2 | convolution fusion | flops 37896192 | bytes 412672 | tf_op jit(solution)/shard_map/dot_general | solution.py:15
  66.8 1.1 %fusion = f32[1,64,768]{2,1,0:T(8,128)} fusion(f32[64,768]{1,0:T(8,128)S(1)} %convolution_subtract_fusion.3, f32[64,64]{1,0:T(8,128)S(1)} %fusion.11, f32[64,768]{1,0:T(8,128)S(1)} %convolution_subtract_fusion.1), kind=kOutput, calls=%fused_computation.1 | convolution fusion | flops 37797888 | bytes 606208 | tf_op jit(solution)/shard_map/dot_general | solution.py:159
  (84 shorter events, 9.5 us)
Async XLA Ops:
  0.0 1.4 %copy-start = (f32[1,64,768]{2,1,0:T(8,128)S(1)}, f32[1,64,768]{2,1,0:T(8,128)}, u32[]{:S(2)}) copy-start(f32[1,64,768]{2,1,0:T(8,128)} %param.1) | copy-start | bytes 589828
  1.5 6.6 %collective-permute-start = (f32[64,128]{1,0:T(8,128)S(1)}, f32[64,128]{1,0:T(8,128)S(1)}, u32[]{:S(2)}, u32[]{:S(2)}) collective-permute-start(f32[64,128]{1,0:T(8,128)S(1)} %pad_maximum_fusion.2), channel_id=1, source_target_pairs={{0,2},{4,6},{8,10},{12,14},{16,18},{20,22},{24,26},{28,30}} | collective-permute-start | bytes 98312 | tf_op jit(solution)/shard_map/ppermute | solution.py:85
  6.4 5.2 %collective-permute-start.5 = (f32[64,768]{1,0:T(8,128)S(1)}, f32[64,768]{1,0:T(8,128)S(1)}, u32[]{:S(2)}, u32[]{:S(2)}) collective-permute-start(f32[64,768]{1,0:T(8,128)S(1)} %bitcast.79), channel_id=1, source_target_pairs={{0,2},{1,3},{4,6},{5,7},{8,10},{9,11},{12,14},{13,15},{16,18},{17,... | collective-permute-start | bytes 589832 | tf_op jit(solution)/shard_map/ppermute | solution.py:71
  8.1 3.5 %collective-permute-start.1 = (f32[64,128]{1,0:T(8,128)S(1)}, f32[64,128]{1,0:T(8,128)S(1)}, u32[]{:S(2)}, u32[]{:S(2)}) collective-permute-start(f32[64,128]{1,0:T(8,128)S(1)} %broadcast_select_fusion.5), channel_id=1, source_target_pairs={{0,1},{2,3},{4,5},{6,7},{8,9},{10,11},{12,13},{14,15},{16,17},{18,... | collective-permute-start | bytes 98312 | tf_op jit(solution)/shard_map/ppermute | solution.py:85
  11.6 5.7 %collective-permute-start.6 = (f32[64,768]{1,0:T(8,128)S(1)}, f32[64,768]{1,0:T(8,128)S(1)}, u32[]{:S(2)}, u32[]{:S(2)}) collective-permute-start(f32[64,768]{1,0:T(8,128)S(1)} %broadcast_select_fusion), channel_id=1, source_target_pairs={{0,1},{1,0},{2,3},{3,2},{4,5},{5,4},{6,7},{7,6},{8,9},{9,8},{10,11... | collective-permute-start | bytes 589832 | tf_op jit(solution)/shard_map/ppermute | solution.py:76
  11.7 4.0 %collective-permute-start.2 = (f32[64,128]{1,0:T(8,128)S(1)}, f32[64,128]{1,0:T(8,128)S(1)}, u32[]{:S(2)}, u32[]{:S(2)}) collective-permute-start(f32[64,128]{1,0:T(8,128)S(1)} %broadcast_select_fusion.6), channel_id=1, source_target_pairs={{0,4},{4,0},{8,12},{12,8},{16,20},{20,16},{24,28},{28,24},{1,5},{5... | collective-permute-start | bytes 98312 | tf_op jit(solution)/shard_map/ppermute | solution.py:29
  15.6 3.9 %collective-permute-start.3 = (f32[64,128]{1,0:T(8,128)S(1)}, f32[64,128]{1,0:T(8,128)S(1)}, u32[]{:S(2)}, u32[]{:S(2)}) collective-permute-start(f32[64,128]{1,0:T(8,128)S(1)} %add.68), channel_id=1, source_target_pairs={{0,8},{4,12},{8,0},{12,4},{16,24},{20,28},{24,16},{28,20},{1,9},{5... | collective-permute-start | bytes 98312 | tf_op jit(solution)/shard_map/ppermute | solution.py:29
  17.8 5.0 %collective-permute-start.7 = (f32[64,256]{0,1:T(8,128)S(1)}, f32[64,256]{0,1:T(8,128)S(1)}, u32[]{:S(2)}, u32[]{:S(2)}) collective-permute-start(f32[64,256]{0,1:T(8,128)S(1)} %pad_maximum_fusion), channel_id=1, source_target_pairs={{0,4},{4,0},{8,12},{12,8},{16,20},{20,16},{24,28},{28,24},{1,5},{5... | collective-permute-start | bytes 196616 | tf_op jit(solution)/shard_map/ppermute | solution.py:29
  19.6 4.9 %collective-permute-start.4 = (f32[64,128]{1,0:T(8,128)S(1)}, f32[64,128]{1,0:T(8,128)S(1)}, u32[]{:S(2)}, u32[]{:S(2)}) collective-permute-start(f32[64,128]{1,0:T(8,128)S(1)} %add.69), channel_id=1, source_target_pairs={{0,16},{4,20},{8,24},{12,28},{16,0},{20,4},{24,8},{28,12},{1,17},{... | collective-permute-start | bytes 98312 | tf_op jit(solution)/shard_map/ppermute | solution.py:29
  22.8 9.1 %collective-permute-start.8 = (f32[64,256]{0,1:T(8,128)S(1)}, f32[64,256]{0,1:T(8,128)S(1)}, u32[]{:S(2)}, u32[]{:S(2)}) collective-permute-start(f32[64,256]{0,1:T(8,128)S(1)} %fusion.43), channel_id=1, source_target_pairs={{0,8},{4,12},{8,0},{12,4},{16,24},{20,28},{24,16},{28,20},{1,9},{5... | collective-permute-start | bytes 196616 | tf_op jit(solution)/shard_map/ppermute | solution.py:29
  31.9 2.6 %copy-start.1 = (f32[64,64]{1,0:T(8,128)S(1)}, f32[64,64]{1,0:T(8,128)}, u32[]{:S(2)}) copy-start(f32[64,64]{1,0:T(8,128)} %shard_map.17) | copy-start | bytes 49156
  31.9 2.6 %copy-start.3 = (f32[64,128]{1,0:T(8,128)S(1)}, f32[64,128]{1,0:T(8,128)}, u32[]{:S(2)}) copy-start(f32[64,128]{1,0:T(8,128)} %add.70.head_ref) | copy-start | bytes 98308
  31.9 7.3 %collective-permute-start.9 = (f32[64,256]{0,1:T(8,128)S(1)}, f32[64,256]{0,1:T(8,128)S(1)}, u32[]{:S(2)}, u32[]{:S(2)}) collective-permute-start(f32[64,256]{0,1:T(8,128)S(1)} %add.72), channel_id=1, source_target_pairs={{0,16},{4,20},{8,24},{12,28},{16,0},{20,4},{24,8},{28,12},{1,17},{... | collective-permute-start | bytes 196616 | tf_op jit(solution)/shard_map/ppermute | solution.py:29
  41.7 3.9 %collective-permute-start.10 = (f32[64,128]{1,0:T(8,128)S(1)}, f32[64,128]{1,0:T(8,128)S(1)}, u32[]{:S(2)}, u32[]{:S(2)}) collective-permute-start(f32[64,128]{1,0:T(8,128)S(1)} %pad_maximum_fusion.3), channel_id=1, source_target_pairs={{0,4},{4,0},{8,12},{12,8},{16,20},{20,16},{24,28},{28,24},{1,5},{5... | collective-permute-start | bytes 98312 | tf_op jit(solution)/shard_map/ppermute | solution.py:29
  43.2 4.3 %collective-permute-start.13 = (f32[64,128]{0,1:T(8,128)S(1)}, f32[64,128]{0,1:T(8,128)S(1)}, u32[]{:S(2)}, u32[]{:S(2)}) collective-permute-start(f32[64,128]{0,1:T(8,128)S(1)} %pad_maximum_fusion.1), channel_id=1, source_target_pairs={{0,4},{4,0},{8,12},{12,8},{16,20},{20,16},{24,28},{28,24},{1,5},{5... | collective-permute-start | bytes 98312 | tf_op jit(solution)/shard_map/ppermute | solution.py:29
  45.7 4.5 %collective-permute-start.11 = (f32[64,128]{1,0:T(8,128)S(1)}, f32[64,128]{1,0:T(8,128)S(1)}, u32[]{:S(2)}, u32[]{:S(2)}) collective-permute-start(f32[64,128]{1,0:T(8,128)S(1)} %fusion.117), channel_id=1, source_target_pairs={{0,8},{4,12},{8,0},{12,4},{16,24},{20,28},{24,16},{28,20},{1,9},{5... | collective-permute-start | bytes 98312 | tf_op jit(solution)/shard_map/ppermute | solution.py:29
  47.5 4.3 %collective-permute-start.14 = (f32[64,128]{0,1:T(8,128)S(1)}, f32[64,128]{0,1:T(8,128)S(1)}, u32[]{:S(2)}, u32[]{:S(2)}) collective-permute-start(f32[64,128]{0,1:T(8,128)S(1)} %fusion.42), channel_id=1, source_target_pairs={{0,8},{4,12},{8,0},{12,4},{16,24},{20,28},{24,16},{28,20},{1,9},{5... | collective-permute-start | bytes 98312 | tf_op jit(solution)/shard_map/ppermute | solution.py:29
  50.2 4.8 %collective-permute-start.12 = (f32[64,128]{1,0:T(8,128)S(1)}, f32[64,128]{1,0:T(8,128)S(1)}, u32[]{:S(2)}, u32[]{:S(2)}) collective-permute-start(f32[64,128]{1,0:T(8,128)S(1)} %add.77), channel_id=1, source_target_pairs={{0,16},{4,20},{8,24},{12,28},{16,0},{20,4},{24,8},{28,12},{1,17},{... | collective-permute-start | bytes 98312 | tf_op jit(solution)/shard_map/ppermute | solution.py:29
  51.9 12.0 %collective-permute-start.15 = (f32[64,128]{0,1:T(8,128)S(1)}, f32[64,128]{0,1:T(8,128)S(1)}, u32[]{:S(2)}, u32[]{:S(2)}) collective-permute-start(f32[64,128]{0,1:T(8,128)S(1)} %add.80), channel_id=1, source_target_pairs={{0,16},{4,20},{8,24},{12,28},{16,0},{20,4},{24,8},{28,12},{1,17},{... | collective-permute-start | bytes 98312 | tf_op jit(solution)/shard_map/ppermute | solution.py:29
  62.4 1.1 %copy-start.2 = (f32[64,64]{1,0:T(8,128)S(1)}, f32[64,64]{1,0:T(8,128)}, u32[]{:S(2)}) copy-start(f32[64,64]{1,0:T(8,128)} %shard_map.18) | copy-start | bytes 49156
  62.4 1.2 %copy-start.4 = (f32[64,128]{1,0:T(8,128)S(1)}, f32[64,128]{1,0:T(8,128)}, u32[]{:S(2)}) copy-start(f32[64,128]{1,0:T(8,128)} %add.78.head_ref) | copy-start | bytes 98308
